TPU v7x, 256 devices: a whole 4x4x8 slice. The times are simulated.
256 devices in a mesh: asset: 16 (over y, z_hi), earn: 4 (over x), age: 4 (over z_lo, core).
Axes of the slice: x: 4, y: 4, z: 8 (z_hi: 4, z_lo: 2; z = z_hi * 2 + z_lo), core: 2. Of those that a mesh axis runs over, the one named last changes fastest.
Arguments:
- values: float32 [8, 32, 512, 512], P('age', 'earn', 'asset'), may hold values from -6 to 6
- utility: float32 [8, 32, 512, 512], P('age', 'earn', 'asset'), may hold values from -6 to 6
- earn_prob: float32 [5, 32], P(None, 'earn'), may hold values from 0.1 to 1
- support_start: int32 [32], P('earn'), may hold values from 0 to 27, as said below
- liquid_offset: int32 [32, 512], P('earn'), may hold values from 0 to 508
- liquid_weight: float32 [4, 32, 512], P(None, 'earn'), may hold values from 0.05 to 0.45
- illiquid_offset: int32 [32, 512], P('earn'), may hold values from 0 to 508
- illiquid_weight: float32 [4, 32, 512], P(None, 'earn'), may hold values from 0.05 to 0.45
Outputs:
- updated: float32 [8, 32, 512, 512], P('age', 'earn', 'asset')
Inputs may be any that keep to these rules, and one draw needn't show every extreme that they name: support_start[e] lies between e - 4 and e, and support_start[e] + 4 is a valid state.
All inputs are finite; a program needn't handle non-finite values.
Results may differ from a plain program's by a relative error of at most 0.00005.
Values sent between devices are 32-bit elements; how exact they have to be, the bound alone decides.
No kernel may reach another device: no remote copies, remote signals or barrier semaphores. Data moves between devices by JAX's collectives and lax.ppermute only.
A program may use at most 64 MiB of HBM per device.

v0:
```python
import jax
import jax.numpy as jnp
from jax import lax
from jax.sharding import PartitionSpec as P

REACH = 4
BAND = 4
ITERS = 2


DISCOUNT = 0.96
PRECISE = lax.Precision.HIGHEST


def extended(cells, sides, width):
    for axis, dim in sides:
        count = lax.axis_size(axis)
        ends = count - 1
        head = lax.slice_in_dim(cells, 0, width, axis=dim)
        tail = lax.slice_in_dim(cells, cells.shape[dim] - width, cells.shape[dim], axis=dim)
        cells = jnp.concatenate(
            [
                lax.ppermute(tail, axis, [(i, (i + 1) % count) for i in range(ends)]),
                cells,
                lax.ppermute(head, axis, [((i + 1) % count, i) for i in range(ends)]),
            ],
            axis=dim,
        )
    return cells


def passed_along(value, axis, by):
    count = lax.axis_size(axis)
    pairs = [(i, i + by) for i in range(count) if 0 <= i + by < count]
    return lax.ppermute(value, axis, pairs)


def band_matrix(offset, weight):
    extent = offset.shape[1]
    positions = jnp.arange(extent, dtype=jnp.int32)
    matrix = jnp.zeros((offset.shape[0], extent, extent), jnp.float32)
    for number in range(BAND):
        matrix = matrix + jnp.where(
            positions[None, :, None] == (offset + number)[:, None, :],
            weight[number][:, None, :],
            0.0,
        )
    return matrix


def expectation(stacked, earn_prob, support_start):
    padded = extended(stacked, (("earn", 1),), REACH)
    states_here = stacked.shape[1]
    first_state = lax.axis_index("earn") * states_here
    slots = jnp.arange(states_here + 2 * REACH, dtype=jnp.int32)
    prob_sum = jnp.sum(earn_prob, axis=0)
    mixing = jnp.zeros((states_here, states_here + 2 * REACH), jnp.float32)
    for number in range(REACH + 1):
        target = support_start + number - first_state + REACH
        mixing = mixing + jnp.where(
            slots[None, :] == target[:, None], (earn_prob[number] / prob_sum)[:, None], 0.0
        )
    return jnp.einsum("ij,tjxy->tixy", mixing, padded, precision=PRECISE)


def continuation(current, earn_prob, support_start):
    arrived = passed_along(current[:1], "age", -1)
    return expectation(jnp.concatenate([current[1:], arrived], axis=0), earn_prob, support_start)


def along_lanes(stacked, matrix):
    return jnp.einsum("terc,ecn->tern", stacked, matrix, precision=lax.Precision.HIGH)


def flipped(stacked):
    ages, states, rows, lanes = stacked.shape
    count = lax.axis_size("asset")
    piece = lanes // count
    flat = stacked.reshape(ages * states * rows, lanes).T.reshape(count, piece, ages * states * rows)
    got = lax.all_to_all(flat, "asset", 0, 0, tiled=True)
    got = got.reshape(count, piece, ages, states, rows)
    return jnp.transpose(got, (2, 3, 1, 0, 4)).reshape(ages, states, piece, count * rows)


def local(
    values,
    utility,
    earn_prob,
    support_start,
    liquid_offset,
    liquid_weight,
    illiquid_offset,
    illiquid_weight,
):
    liquid_map = band_matrix(liquid_offset, liquid_weight)
    illiquid_map = band_matrix(illiquid_offset, illiquid_weight)

    expected = continuation(values, earn_prob, support_start)
    saved = along_lanes(expected, liquid_map)
    adjusted = along_lanes(flipped(saved), illiquid_map)
    current = flipped(utility) + DISCOUNT * adjusted

    expected = continuation(current, earn_prob, support_start)
    moved = along_lanes(expected, illiquid_map)
    adjusted = along_lanes(flipped(moved), liquid_map)
    return utility + DISCOUNT * adjusted


def solution(mesh):
    return jax.shard_map(
        local,
        mesh=mesh,
        in_specs=(
            P("age", "earn", "asset", None),
            P("age", "earn", "asset", None),
            P(None, "earn"),
            P("earn"),
            P("earn", None),
            P(None, "earn", None),
            P("earn", None),
            P(None, "earn", None),
        ),
        out_specs=P("age", "earn", "asset", None),
        check_vma=False,
    )
```

profile of v0, /device:TPU:1, one launch (start us, length us, event | category | flops | bytes accessed | tf_op | source)
XLA Modules:
  0.0 191.2 jit_solution(13986124427959020285)
XLA Ops:
  1.6 5.1 %collective-permute-start = (f32[1,8,32,512]{3,1,2,0:T(8,128)S(1)}, f32[1,8,32,512]{3,1,2,0:T(8,128)S(1)}, u32[]{:S(2)}, u32[]{:S(2)}) collective-permute-start(f32[1,8,32,512]{3,1,2,0:T(8,128)S(1)} %copy.40), channel_id=1, source_target_pairs={{1,0},{2,1},{3,2},{5,4},{6,5},{7,6},{9,8},{10,9},{11,10},{13,12},{... | collective-permute-start | bytes 1572872 | tf_op jit(solution)/shard_map/ppermute | solution.py:35
  6.8 2.6 %copy.21 = f32[512,512]{1,0:T(8,128)} copy(f32[512,512]{0,1:T(8,128)} %bitcast.114) | data formatting | bytes 2097152 | tf_op jit(solution)/shard_map/transpose | solution.py:79
  9.3 9.2 %all-to-all-start = ((f32[16,32,512]{2,1,0:T(8,128)}), f32[16,32,512]{2,1,0:T(8,128)S(1)}, u32[]{:S(2)}, u32[]{:S(2)}) async-start(f32[16,32,512]{2,1,0:T(8,128)} %bitcast.14), calls=%async_computation | async-start | bytes 2097152 | tf_op jit(solution)/shard_map/all_to_all | solution.py:80
  19.2 3.1 %collective-permute-start.1 = (f32[2,4,32,512]{3,1,2,0:T(4,128)S(1)}, f32[2,4,32,512]{3,1,2,0:T(4,128)S(1)}, u32[]{:S(2)}, u32[]{:S(2)}) collective-permute-start(f32[2,4,32,512]{3,1,2,0:T(4,128)S(1)} %get-tuple-element.9), channel_id=1, source_target_pairs={{0,4},{4,8},{8,12},{1,5},{5,9},{9,13},{2,6},{6,10},{10,14},{3,7},{... | collective-permute-start | bytes 1572872 | tf_op jit(solution)/shard_map/ppermute | solution.py:23
  23.7 10.2 %collective-permute-done.1 = f32[2,4,32,512]{3,1,2,0:T(4,128)S(1)} collective-permute-done((f32[2,4,32,512]{3,1,2,0:T(4,128)S(1)}, f32[2,4,32,512]{3,1,2,0:T(4,128)S(1)}, u32[]{:S(2)}, u32[]{:S(2)}) %collective-permute-start.1) | collective-permute-done | bytes 524320 | tf_op jit(solution)/shard_map/ppermute | solution.py:23
  33.9 3.9 %collective-permute-done.2 = f32[2,4,32,512]{3,1,2,0:T(4,128)S(1)} collective-permute-done((f32[2,4,32,512]{3,1,2,0:T(4,128)S(1)}, f32[2,4,32,512]{3,1,2,0:T(4,128)S(1)}, u32[]{:S(2)}, u32[]{:S(2)}) %collective-permute-start.2) | collective-permute-done | bytes 524320 | tf_op jit(solution)/shard_map/ppermute | solution.py:25
  39.4 7.5 %fusion.61 = f32[2,8,32,512]{3,2,0,1:T(8,128)S(1)} fusion(f32[8,512]{1,0:T(8,128)S(1)} %get-tuple-element.15, s32[8,512]{1,0:T(8,128)S(1)} %get-tuple-element.22, f32[8,512]{1,0:T(8,128)S(1)} %get-tuple-element.16, s32[8,512]{1,0:T(8,128)S(1)} %get-tuple-element.23, f32[8,512]{1,0:T(8,128)S(1)} %get-tuple-element.14, s32[8,512]{1,0:T(8,128)S(1)} %get-tuple-element.21, ...), kind=kOutput, calls=%fused_computation.66 | convolution fusion | flops 828375040 | bytes 2228224 | tf_op jit(solution)/shard_map/terc,ecn->tern/dot_general | solution.py:72
  48.4 8.8 %all-to-all-start.1 = ((f32[16,32,512]{2,1,0:T(8,128)}), f32[16,32,512]{2,1,0:T(8,128)S(1)}, u32[]{:S(2)}, u32[]{:S(2)}) async-start(f32[16,32,512]{2,1,0:T(8,128)} %bitcast.29), calls=%async_computation.1 | async-start | bytes 2097152 | tf_op jit(solution)/shard_map/all_to_all | solution.py:80
  59.7 6.6 %copy.22 = f32[2,8,32,16,32]{4,3,2,0,1:T(8,128)} copy(f32[2,8,32,16,32]{4,1,0,2,3:T(8,128)} %bitcast.108) | data formatting | bytes 2097152 | tf_op jit(solution)/shard_map/transpose | solution.py:82
  66.3 3.5 %reshape.95 = f32[2,8,32,512]{3,2,0,1:T(8,128)S(1)} reshape(f32[2,8,32,16,32]{4,3,2,0,1:T(8,128)} %copy.22) | data formatting | bytes 2097152 | tf_op jit(solution)/shard_map/reshape | solution.py:82
  69.9 14.3 %all-to-all-done.1 = f32[16,32,512]{2,1,0:T(8,128)S(1)} async-done(((f32[16,32,512]{2,1,0:T(8,128)}), f32[16,32,512]{2,1,0:T(8,128)S(1)}, u32[]{:S(2)}, u32[]{:S(2)}) %all-to-all-start.1) | async-done | bytes 1048608 | tf_op jit(solution)/shard_map/all_to_all | solution.py:80
  86.7 6.6 %copy.28 = f32[2,8,32,16,32]{4,3,2,0,1:T(8,128)} copy(f32[2,8,32,16,32]{4,1,0,2,3:T(8,128)} %bitcast.109) | data formatting | bytes 2097152 | tf_op jit(solution)/shard_map/transpose | solution.py:82
  93.3 3.5 %reshape.99 = f32[2,8,32,512]{3,2,0,1:T(8,128)S(1)} reshape(f32[2,8,32,16,32]{4,3,2,0,1:T(8,128)} %copy.28) | data formatting | bytes 2097152 | tf_op jit(solution)/shard_map/reshape | solution.py:82
  96.8 6.9 %fusion.79 = f32[2,8,32,512]{3,2,0,1:T(8,128)S(1)} fusion(f32[2,8,32,512]{3,2,0,1:T(8,128)S(1)} %reshape.95, f32[2,8,32,512]{3,2,0,1:T(8,128)S(1)} %reshape.99, f32[8,512]{1,0:T(8,128)S(1)} %get-tuple-element.19, s32[8,512]{1,0:T(8,128)S(1)} %get-tuple-element.25, f32[8,512]{1,0:T(8,128)S(1)} %get-tuple-element.20, s32[8,512]{1,0:T(8,128)S(1)} %get-tuple-element.26, ...), kind=kOutput, calls=%fused_computation.72 | convolution fusion | flops 828899328 | bytes 3276800 | tf_op jit(solution)/shard_map/terc,ecn->tern/dot_general | solution.py:72
  103.8 5.2 %collective-permute-start.3 = (f32[1,8,32,512]{3,2,0,1:T(8,128)S(1)}, f32[1,8,32,512]{3,2,0,1:T(8,128)S(1)}, u32[]{:S(2)}, u32[]{:S(2)}) collective-permute-start(f32[1,8,32,512]{3,2,0,1:T(8,128)S(1)} %get-tuple-element.8), channel_id=1, source_target_pairs={{1,0},{2,1},{3,2},{5,4},{6,5},{7,6},{9,8},{10,9},{11,10},{13,12},{... | collective-permute-start | bytes 1572872 | tf_op jit(solution)/shard_map/ppermute | solution.py:35
  109.0 5.3 %collective-permute-done.3 = f32[1,8,32,512]{3,2,0,1:T(8,128)S(1)} collective-permute-done((f32[1,8,32,512]{3,2,0,1:T(8,128)S(1)}, f32[1,8,32,512]{3,2,0,1:T(8,128)S(1)}, u32[]{:S(2)}, u32[]{:S(2)}) %collective-permute-start.3) | collective-permute-done | bytes 524320 | tf_op jit(solution)/shard_map/ppermute | solution.py:35
  114.4 3.3 %collective-permute-start.4 = (f32[2,4,32,512]{3,2,0,1:T(8,128)S(1)}, f32[2,4,32,512]{3,2,0,1:T(8,128)S(1)}, u32[]{:S(2)}, u32[]{:S(2)}) collective-permute-start(f32[2,4,32,512]{3,2,0,1:T(8,128)S(1)} %get-tuple-element.5), channel_id=1, source_target_pairs={{0,4},{4,8},{8,12},{1,5},{5,9},{9,13},{2,6},{6,10},{10,14},{3,7},{... | collective-permute-start | bytes 1572872 | tf_op jit(solution)/shard_map/ppermute | solution.py:23
  119.0 7.2 %collective-permute-done.4 = f32[2,4,32,512]{3,2,0,1:T(8,128)S(1)} collective-permute-done((f32[2,4,32,512]{3,2,0,1:T(8,128)S(1)}, f32[2,4,32,512]{3,2,0,1:T(8,128)S(1)}, u32[]{:S(2)}, u32[]{:S(2)}) %collective-permute-start.4) | collective-permute-done | bytes 524320 | tf_op jit(solution)/shard_map/ppermute | solution.py:23
  126.2 4.3 %collective-permute-done.5 = f32[2,4,32,512]{3,2,0,1:T(8,128)S(1)} collective-permute-done((f32[2,4,32,512]{3,2,0,1:T(8,128)S(1)}, f32[2,4,32,512]{3,2,0,1:T(8,128)S(1)}, u32[]{:S(2)}, u32[]{:S(2)}) %collective-permute-start.5) | collective-permute-done | bytes 524320 | tf_op jit(solution)/shard_map/ppermute | solution.py:25
  133.3 7.5 %fusion.58 = f32[2,8,32,512]{3,2,0,1:T(8,128)S(1)} fusion(f32[8,512]{1,0:T(8,128)S(1)} %get-tuple-element.19, s32[8,512]{1,0:T(8,128)S(1)} %get-tuple-element.25, f32[8,512]{1,0:T(8,128)S(1)} %get-tuple-element.20, s32[8,512]{1,0:T(8,128)S(1)} %get-tuple-element.26, f32[8,512]{1,0:T(8,128)S(1)} %get-tuple-element.18, s32[8,512]{1,0:T(8,128)S(1)} %get-tuple-element.24, ...), kind=kOutput, calls=%fused_computation.65 | convolution fusion | flops 828375040 | bytes 2228224 | tf_op jit(solution)/shard_map/terc,ecn->tern/dot_general | solution.py:72
  141.2 29.3 %all_to_all.15 = f32[16,32,512]{2,1,0:T(8,128)S(1)} all-to-all(f32[16,32,512]{2,1,0:T(8,128)S(1)} %bitcast.113), channel_id=1, replica_groups=mesh['asset'=16,'earn'=4,'age'=4] {'asset'}, dimensions={0} | all-to-all | bytes 2097152 | tf_op jit(solution)/shard_map/all_to_all | solution.py:80
  173.0 6.6 %copy.33 = f32[2,8,32,16,32]{4,3,2,0,1:T(8,128)} copy(f32[2,8,32,16,32]{4,1,0,2,3:T(8,128)} %bitcast.110) | data formatting | bytes 2097152 | tf_op jit(solution)/shard_map/transpose | solution.py:82
  179.6 3.6 %reshape.103 = f32[2,8,32,512]{3,2,0,1:T(8,128)S(1)} reshape(f32[2,8,32,16,32]{4,3,2,0,1:T(8,128)} %copy.33) | data formatting | bytes 2097152 | tf_op jit(solution)/shard_map/reshape | solution.py:82
  183.3 6.8 %fusion.76 = f32[2,8,32,512]{3,2,0,1:T(8,128)S(1)} fusion(f32[2,8,32,512]{3,2,0,1:T(8,128)S(1)} %reshape.103, f32[8,512]{1,0:T(8,128)S(1)} %get-tuple-element.15, s32[8,512]{1,0:T(8,128)S(1)} %get-tuple-element.22, f32[8,512]{1,0:T(8,128)S(1)} %get-tuple-element.16, s32[8,512]{1,0:T(8,128)S(1)} %get-tuple-element.23, f32[8,512]{1,0:T(8,128)S(1)} %get-tuple-element.14, ...), kind=kOutput, calls=%fused_computation.71 | convolution fusion | flops 828899328 | bytes 3276800 | tf_op jit(solution)/shard_map/terc,ecn->tern/dot_general | solution.py:72
  (43 shorter events, 19.7 us)
Async XLA Ops:
  0.0 18.6 %copy-start.5 = (f32[5,8]{1,0:T(8,128)S(1)}, f32[5,8]{1,0:T(8,128)}, u32[]{:S(2)}) copy-start(f32[5,8]{1,0:T(8,128)} %param.10) | copy-start | bytes 484
  1.6 17.3 %collective-permute-start = (f32[1,8,32,512]{3,1,2,0:T(8,128)S(1)}, f32[1,8,32,512]{3,1,2,0:T(8,128)S(1)}, u32[]{:S(2)}, u32[]{:S(2)}) collective-permute-start(f32[1,8,32,512]{3,1,2,0:T(8,128)S(1)} %copy.40), channel_id=1, source_target_pairs={{1,0},{2,1},{3,2},{5,4},{6,5},{7,6},{9,8},{10,9},{11,10},{13,12},{... | collective-permute-start | bytes 1572872 | tf_op jit(solution)/shard_map/ppermute | solution.py:35
  6.7 16.9 %copy-start.6 = (s32[8]{0:T(128)S(1)}, s32[8]{0:T(128)}, u32[]{:S(2)}) copy-start(s32[8]{0:T(128)} %param.11) | copy-start | bytes 100
  6.8 16.9 %copy-start.4 = (s32[8,512]{1,0:T(8,128)S(1)}, s32[8,512]{1,0:T(8,128)}, u32[]{:S(2)}) copy-start(s32[8,512]{1,0:T(8,128)} %param.12) | copy-start | bytes 49156
  6.8 16.9 %copy-start.1 = (f32[4,8,512]{2,1,0:T(8,128)S(1)}, f32[4,8,512]{2,1,0:T(8,128)}, u32[]{:S(2)}) copy-start(f32[4,8,512]{2,1,0:T(8,128)} %param.13) | copy-start | bytes 196612
  9.3 39.0 %all-to-all-start = ((f32[16,32,512]{2,1,0:T(8,128)}), f32[16,32,512]{2,1,0:T(8,128)S(1)}, u32[]{:S(2)}, u32[]{:S(2)}) async-start(f32[16,32,512]{2,1,0:T(8,128)} %bitcast.14), calls=%async_computation | async-start | bytes 2097152 | tf_op jit(solution)/shard_map/all_to_all | solution.py:80
  19.2 14.7 %collective-permute-start.1 = (f32[2,4,32,512]{3,1,2,0:T(4,128)S(1)}, f32[2,4,32,512]{3,1,2,0:T(4,128)S(1)}, u32[]{:S(2)}, u32[]{:S(2)}) collective-permute-start(f32[2,4,32,512]{3,1,2,0:T(4,128)S(1)} %get-tuple-element.9), channel_id=1, source_target_pairs={{0,4},{4,8},{8,12},{1,5},{5,9},{9,13},{2,6},{6,10},{10,14},{3,7},{... | collective-permute-start | bytes 1572872 | tf_op jit(solution)/shard_map/ppermute | solution.py:23
  22.3 15.4 %collective-permute-start.2 = (f32[2,4,32,512]{3,1,2,0:T(4,128)S(1)}, f32[2,4,32,512]{3,1,2,0:T(4,128)S(1)}, u32[]{:S(2)}, u32[]{:S(2)}) collective-permute-start(f32[2,4,32,512]{3,1,2,0:T(4,128)S(1)} %get-tuple-element.10), channel_id=1, source_target_pairs={{4,0},{8,4},{12,8},{5,1},{9,5},{13,9},{6,2},{10,6},{14,10},{7,3},{... | collective-permute-start | bytes 1572872 | tf_op jit(solution)/shard_map/ppermute | solution.py:25
  46.9 10.3 %copy-start.3 = (s32[8,512]{1,0:T(8,128)S(1)}, s32[8,512]{1,0:T(8,128)}, u32[]{:S(2)}) copy-start(s32[8,512]{1,0:T(8,128)} %param.14) | copy-start | bytes 49156
  46.9 10.3 %copy-start.2 = (f32[4,8,512]{2,1,0:T(8,128)S(1)}, f32[4,8,512]{2,1,0:T(8,128)}, u32[]{:S(2)}) copy-start(f32[4,8,512]{2,1,0:T(8,128)} %param.15) | copy-start | bytes 196612
  48.4 35.8 %all-to-all-start.1 = ((f32[16,32,512]{2,1,0:T(8,128)}), f32[16,32,512]{2,1,0:T(8,128)S(1)}, u32[]{:S(2)}, u32[]{:S(2)}) async-start(f32[16,32,512]{2,1,0:T(8,128)} %bitcast.29), calls=%async_computation.1 | async-start | bytes 2097152 | tf_op jit(solution)/shard_map/all_to_all | solution.py:80
  103.8 10.5 %collective-permute-start.3 = (f32[1,8,32,512]{3,2,0,1:T(8,128)S(1)}, f32[1,8,32,512]{3,2,0,1:T(8,128)S(1)}, u32[]{:S(2)}, u32[]{:S(2)}) collective-permute-start(f32[1,8,32,512]{3,2,0,1:T(8,128)S(1)} %get-tuple-element.8), channel_id=1, source_target_pairs={{1,0},{2,1},{3,2},{5,4},{6,5},{7,6},{9,8},{10,9},{11,10},{13,12},{... | collective-permute-start | bytes 1572872 | tf_op jit(solution)/shard_map/ppermute | solution.py:35
  114.4 11.9 %collective-permute-start.4 = (f32[2,4,32,512]{3,2,0,1:T(8,128)S(1)}, f32[2,4,32,512]{3,2,0,1:T(8,128)S(1)}, u32[]{:S(2)}, u32[]{:S(2)}) collective-permute-start(f32[2,4,32,512]{3,2,0,1:T(8,128)S(1)} %get-tuple-element.5), channel_id=1, source_target_pairs={{0,4},{4,8},{8,12},{1,5},{5,9},{9,13},{2,6},{6,10},{10,14},{3,7},{... | collective-permute-start | bytes 1572872 | tf_op jit(solution)/shard_map/ppermute | solution.py:23
  117.7 12.9 %collective-permute-start.5 = (f32[2,4,32,512]{3,2,0,1:T(8,128)S(1)}, f32[2,4,32,512]{3,2,0,1:T(8,128)S(1)}, u32[]{:S(2)}, u32[]{:S(2)}) collective-permute-start(f32[2,4,32,512]{3,2,0,1:T(8,128)S(1)} %get-tuple-element.6), channel_id=1, source_target_pairs={{4,0},{8,4},{12,8},{5,1},{9,5},{13,9},{6,2},{10,6},{14,10},{7,3},{... | collective-permute-start | bytes 1572872 | tf_op jit(solution)/shard_map/ppermute | solution.py:25
  179.6 3.6 %copy-start = (f32[2,8,32,512]{3,2,1,0:T(8,128)S(1)}, f32[2,8,32,512]{3,2,1,0:T(8,128)}, u32[]{:S(2)}) copy-start(f32[2,8,32,512]{3,2,1,0:T(8,128)} %param.9) | copy-start | bytes 3145732
where the time goes:
time: 192 us; the launch traced here: 191 us
  local copies, waits for them, and re-layouts  45.9 us (24%)
  waiting for transfers between devices  45.2 us (24%)
  starting transfers between devices  37.4 us (19%)
  matrix products  32.7 us (17%)
  blocking collectives  29.3 us (15%)
    all_to_all x1, blocking collectives, flipped(): got = lax.all_to_all(flat, 'asset', 0, 0, tiled=True)  29.3 us
    dot_general x4, matrix products, along_lanes(): jnp.einsum('terc,ecn->tern', stacked, matrix, precision=lax.Precision.HIGH)  28.7 us
    transpose x3, local copies, waits for them, and re-layouts, flipped(): jnp.transpose(got, (2, 3, 1, 0, 4))  19.8 us
    all_to_all x2, starting transfers between devices, flipped(): got = lax.all_to_all(flat, 'asset', 0, 0, tiled=True)  18 us
    ppermute x2, waiting for transfers between devices, extended(): lax.ppermute(tail, axis, [(i, (i + 1) % count) for i in range(ends)])  17.4 us
    all_to_all x2, waiting for transfers between devices, flipped(): got = lax.all_to_all(flat, 'asset', 0, 0, tiled=True)  14.3 us
    reshape x3, local copies, waits for them, and re-layouts, flipped(): jnp.transpose(got, (2, 3, 1, 0, 4))  10.7 us
    ppermute x2, starting transfers between devices, passed_along(): return lax.ppermute(value, axis, pairs)  10.3 us
  transfers between devices with their start and end apart: 8, of which 6 were waited for; matrix products, arithmetic and copies ran while one was open for 14% of the time, Pallas kernels for 0%

commit v1 on v0

--- a/solution.py
+++ b/solution.py
@@ -1,6 +1,8 @@
 import jax
 import jax.numpy as jnp
 from jax import lax
+from jax.experimental import pallas as pl
+from jax.experimental.pallas import tpu as pltpu
 from jax.sharding import PartitionSpec as P
 
 REACH = 4
@@ -72,14 +74,46 @@
     return jnp.einsum("terc,ecn->tern", stacked, matrix, precision=lax.Precision.HIGH)
 
 
+def _gather_kernel(src_ref, dst_ref):
+    count, piece, lanes = src_ref.shape
+    slabs = dst_ref.shape[0]
+    width = lanes // slabs
+    lane = lax.broadcasted_iota(jnp.int32, (piece, lanes), 1)
+    for w in range(count // slabs):
+        outs = [None] * slabs
+        for u in range(slabs):
+            x = src_ref[w * slabs + u]
+            keep = (lane >= u * width) & (lane < (u + 1) * width)
+            for s in range(slabs):
+                shift = ((u - s) * width) % lanes
+                y = pltpu.roll(x, shift, 1) if shift else x
+                outs[s] = y if u == 0 else jnp.where(keep, y, outs[s])
+        for s in range(slabs):
+            dst_ref[s, :, pl.ds(w * lanes, lanes)] = outs[s]
+
+
+def regroup(got):
+    count, piece, lanes = got.shape
+    width = lanes // count
+    slabs = 128 // width
+    nbytes = got.size * got.dtype.itemsize
+    return pl.pallas_call(
+        _gather_kernel,
+        grid=(lanes // 128,),
+        in_specs=[pl.BlockSpec((count, piece, 128), lambda k: (0, 0, k))],
+        out_specs=pl.BlockSpec((slabs, piece, count * width), lambda k: (k, 0, 0)),
+        out_shape=jax.ShapeDtypeStruct((lanes // width, piece, count * width), got.dtype),
+        cost_estimate=pl.CostEstimate(flops=0, transcendentals=0, bytes_accessed=2 * nbytes),
+    )(got)
+
+
 def flipped(stacked):
     ages, states, rows, lanes = stacked.shape
     count = lax.axis_size("asset")
     piece = lanes // count
     flat = stacked.reshape(ages * states * rows, lanes).T.reshape(count, piece, ages * states * rows)
     got = lax.all_to_all(flat, "asset", 0, 0, tiled=True)
-    got = got.reshape(count, piece, ages, states, rows)
-    return jnp.transpose(got, (2, 3, 1, 0, 4)).reshape(ages, states, piece, count * rows)
+    return regroup(got).reshape(ages, states, piece, count * rows)
 
 
 def local(

time: 192 us -> 177 us (0.922)
  local copies, waits for them, and re-layouts: 45.9 us -> 6.67 us
  Pallas kernels: 0 us -> 11.6 us
  waiting for transfers between devices: 45.2 us -> 54 us
  matrix products: 32.7 us -> 36 us
    transpose x3 -> x0, local copies, waits for them, and re-layouts: 19.8 us -> none  [flipped(): jnp.transpose(got, (2, 3, 1, 0, 4))]
    reshape x6 -> x1, local copies, waits for them, and re-layouts: 18.2 us -> 1.31 us  [flipped(): stacked.reshape(ages * states * rows, lanes)]
    pallas_call x0 -> x3, Pallas kernels: none -> 11.6 us  [regroup(): pl.pallas_call(_gather_kernel, grid=(lanes // 128,), in_specs=[pl.BlockSp...]
    all_to_all x2, waiting for transfers between devices: 14.3 us -> 23 us  [flipped(): got = lax.all_to_all(flat, 'asset', 0, 0, tiled=True)]
    transpose x3 -> x2, local copies, waits for them, and re-layouts: 4.28 us -> 1.63 us  [flipped(): stacked.reshape(ages * states * rows, lanes)]
    dot_general x4, matrix products: 28.7 us -> 31.1 us  [along_lanes(): jnp.einsum('terc,ecn->tern', stacked, matrix, precision=lax.Precision.HIGH)]
  transfers between devices with their start and end apart: 8 -> 8, of which waited for: 6 -> 6; matrix products, arithmetic and copies ran while one was open for 14% -> 7% of each run, Pallas kernels for 0% -> 2%
where the time goes in v1:
time: 177 us
  waiting for transfers between devices  54 us (31%)
  starting transfers between devices  37.3 us (21%)
  matrix products  36 us (20%)
  blocking collectives  30.1 us (17%)
  Pallas kernels  11.6 us (7%)
  local copies, waits for them, and re-layouts  6.67 us (4%)
    dot_general x4, matrix products, along_lanes(): jnp.einsum('terc,ecn->tern', stacked, matrix, precision=lax.Precision.HIGH)  31.1 us
    all_to_all x1, blocking collectives, flipped(): got = lax.all_to_all(flat, 'asset', 0, 0, tiled=True)  30.1 us
    all_to_all x2, waiting for transfers between devices, flipped(): got = lax.all_to_all(flat, 'asset', 0, 0, tiled=True)  23 us
    all_to_all x2, starting transfers between devices, flipped(): got = lax.all_to_all(flat, 'asset', 0, 0, tiled=True)  18.1 us
    ppermute x2, waiting for transfers between devices, extended(): lax.ppermute(tail, axis, [(i, (i + 1) % count) for i in range(ends)])  17.6 us
    pallas_call x3, Pallas kernels, regroup(): pl.pallas_call(_gather_kernel, grid=(lanes // 128,), in_specs=[pl.BlockSp...  11.6 us
    ppermute x2, starting transfers between devices, passed_along(): return lax.ppermute(value, axis, pairs)  10.3 us
    ppermute x2, waiting for transfers between devices, extended(): lax.ppermute(head, axis, [((i + 1) % count, i) for i in range(ends)])  7.99 us
  transfers between devices with their start and end apart: 8, of which 6 were waited for; matrix products, arithmetic and copies ran while one was open for 7% of the time, Pallas kernels for 2%

profile of v1, /device:TPU:1, one launch (start us, length us, event | category | flops | bytes accessed | tf_op | source)
XLA Modules:
  0.0 176.6 jit_solution(2105633822046312381)
XLA Ops:
  0.0 1.4 fusion.111
  1.4 5.1 %collective-permute-start = (f32[1,8,32,512]{3,2,1,0:T(8,128)S(1)}, f32[1,8,32,512]{3,2,1,0:T(8,128)S(1)}, u32[]{:S(2)}, u32[]{:S(2)}) collective-permute-start(f32[1,8,32,512]{3,2,1,0:T(8,128)S(1)} %get-tuple-element.12), channel_id=1, source_target_pairs={{1,0},{2,1},{3,2},{5,4},{6,5},{7,6},{9,8},{10,9},{11,10},{13,12},{... | collective-permute-start | bytes 1572872 | tf_op jit(solution)/shard_map/ppermute | solution.py:37
  6.5 1.3 copy.15
  7.8 9.3 %all-to-all-start = ((f32[16,32,512]{2,1,0:T(8,128)}), f32[16,32,512]{2,1,0:T(8,128)S(1)}, u32[]{:S(2)}, u32[]{:S(2)}) async-start(f32[16,32,512]{2,1,0:T(8,128)} %bitcast.14), calls=%async_computation | async-start | bytes 2097152 | tf_op jit(solution)/shard_map/all_to_all | solution.py:115
  17.4 3.1 %collective-permute-start.1 = (f32[2,4,32,512]{3,2,1,0:T(8,128)S(1)}, f32[2,4,32,512]{3,2,1,0:T(8,128)S(1)}, u32[]{:S(2)}, u32[]{:S(2)}) collective-permute-start(f32[2,4,32,512]{3,2,1,0:T(8,128)S(1)} %get-tuple-element.9), channel_id=1, source_target_pairs={{0,4},{4,8},{8,12},{1,5},{5,9},{9,13},{2,6},{6,10},{10,14},{3,7},{... | collective-permute-start | bytes 1572872 | tf_op jit(solution)/shard_map/ppermute | solution.py:25
  21.9 10.2 %collective-permute-done.1 = f32[2,4,32,512]{3,2,1,0:T(8,128)S(1)} collective-permute-done((f32[2,4,32,512]{3,2,1,0:T(8,128)S(1)}, f32[2,4,32,512]{3,2,1,0:T(8,128)S(1)}, u32[]{:S(2)}, u32[]{:S(2)}) %collective-permute-start.1) | collective-permute-done | bytes 524320 | tf_op jit(solution)/shard_map/ppermute | solution.py:25
  32.1 3.9 %collective-permute-done.2 = f32[2,4,32,512]{3,2,1,0:T(8,128)S(1)} collective-permute-done((f32[2,4,32,512]{3,2,1,0:T(8,128)S(1)}, f32[2,4,32,512]{3,2,1,0:T(8,128)S(1)}, u32[]{:S(2)}, u32[]{:S(2)}) %collective-permute-start.2) | collective-permute-done | bytes 524320 | tf_op jit(solution)/shard_map/ppermute | solution.py:27
  36.1 2.4 %fusion.46 = f32[2,32,512,8]{2,3,1,0:T(8,128)S(1)} fusion(f32[2,16,32,512]{3,2,1,0:T(8,128)S(1)} %pad_maximum_fusion, f32[8]{0:T(128)S(1)} %get-tuple-element.28, s32[8]{0:T(128)S(1)} %get-tuple-element.35, f32[8]{0:T(128)S(1)} %get-tuple-element.29, s32[8]{0:T(128)S(1)} %get-tuple-element.36, f32[8]{0:T(128)S(1)} %get-tuple-element.30, ...), kind=kOutput, calls=%fused_computation.58 | convolution fusion | flops 50333440 | bytes 3146048 | tf_op jit(solution)/shard_map/ij,tjxy->tixy/dot_general | solution.py:65
  38.6 7.5 %fusion.51 = f32[2,8,32,512]{3,2,0,1:T(8,128)S(1)} fusion(f32[8,512]{1,0:T(8,128)S(1)} %get-tuple-element.19, s32[8,512]{1,0:T(8,128)S(1)} %get-tuple-element.25, f32[8,512]{1,0:T(8,128)S(1)} %get-tuple-element.20, s32[8,512]{1,0:T(8,128)S(1)} %get-tuple-element.26, f32[8,512]{1,0:T(8,128)S(1)} %get-tuple-element.18, s32[8,512]{1,0:T(8,128)S(1)} %get-tuple-element.24, ...), kind=kOutput, calls=%fused_computation.61 | convolution fusion | flops 828375040 | bytes 2228224 | tf_op jit(solution)/shard_map/terc,ecn->tern/dot_general | solution.py:74
  47.5 8.8 %all-to-all-start.1 = ((f32[16,32,512]{2,1,0:T(8,128)}), f32[16,32,512]{2,1,0:T(8,128)S(1)}, u32[]{:S(2)}, u32[]{:S(2)}) async-start(f32[16,32,512]{2,1,0:T(8,128)} %bitcast.29), calls=%async_computation.1 | async-start | bytes 2097152 | tf_op jit(solution)/shard_map/all_to_all | solution.py:115
  56.4 3.9 %shard_map.82 = f32[16,32,512]{2,1,0:T(8,128)} custom-call(f32[16,32,512]{2,1,0:T(8,128)} %copy-done), custom_call_target="tpu_custom_call" | custom-call | bytes 2097152 | tf_op jit(solution)/shard_map/pallas_call | solution.py:100
  60.2 23.0 %all-to-all-done.1.src_ref = f32[16,32,512]{2,1,0:T(8,128)S(1)} async-done(((f32[16,32,512]{2,1,0:T(8,128)}), f32[16,32,512]{2,1,0:T(8,128)S(1)}, u32[]{:S(2)}, u32[]{:S(2)}) %all-to-all-start.1) | async-done | bytes 1048608 | tf_op jit(solution)/shard_map/all_to_all | solution.py:115
  84.3 3.8 %shard_map.83 = f32[16,32,512]{2,1,0:T(8,128)} custom-call(f32[16,32,512]{2,1,0:T(8,128)} %copy-done.1), custom_call_target="tpu_custom_call" | custom-call | bytes 2097152 | tf_op jit(solution)/shard_map/pallas_call | solution.py:100
  88.1 8.1 %fusion.69 = f32[2,8,32,512]{3,2,0,1:T(8,128)S(1)} fusion(f32[8,512]{1,0:T(8,128)S(1)} %get-tuple-element.15, s32[8,512]{1,0:T(8,128)S(1)} %get-tuple-element.22, f32[8,512]{1,0:T(8,128)S(1)} %get-tuple-element.16, s32[8,512]{1,0:T(8,128)S(1)} %get-tuple-element.23, f32[8,512]{1,0:T(8,128)S(1)} %get-tuple-element.14, s32[8,512]{1,0:T(8,128)S(1)} %get-tuple-element.21, ...), kind=kOutput, calls=%fused_computation.67 | convolution fusion | flops 828899328 | bytes 3276800 | tf_op jit(solution)/shard_map/terc,ecn->tern/dot_general | solution.py:74
  96.3 5.2 %collective-permute-start.3 = (f32[1,8,32,512]{3,2,0,1:T(8,128)S(1)}, f32[1,8,32,512]{3,2,0,1:T(8,128)S(1)}, u32[]{:S(2)}, u32[]{:S(2)}) collective-permute-start(f32[1,8,32,512]{3,2,0,1:T(8,128)S(1)} %get-tuple-element.8), channel_id=1, source_target_pairs={{1,0},{2,1},{3,2},{5,4},{6,5},{7,6},{9,8},{10,9},{11,10},{13,12},{... | collective-permute-start | bytes 1572872 | tf_op jit(solution)/shard_map/ppermute | solution.py:37
  101.5 5.3 %collective-permute-done.3 = f32[1,8,32,512]{3,2,0,1:T(8,128)S(1)} collective-permute-done((f32[1,8,32,512]{3,2,0,1:T(8,128)S(1)}, f32[1,8,32,512]{3,2,0,1:T(8,128)S(1)}, u32[]{:S(2)}, u32[]{:S(2)}) %collective-permute-start.3) | collective-permute-done | bytes 524320 | tf_op jit(solution)/shard_map/ppermute | solution.py:37
  106.9 3.1 %collective-permute-start.4 = (f32[2,4,32,512]{3,2,0,1:T(8,128)S(1)}, f32[2,4,32,512]{3,2,0,1:T(8,128)S(1)}, u32[]{:S(2)}, u32[]{:S(2)}) collective-permute-start(f32[2,4,32,512]{3,2,0,1:T(8,128)S(1)} %get-tuple-element.5), channel_id=1, source_target_pairs={{0,4},{4,8},{8,12},{1,5},{5,9},{9,13},{2,6},{6,10},{10,14},{3,7},{... | collective-permute-start | bytes 1572872 | tf_op jit(solution)/shard_map/ppermute | solution.py:25
  111.3 7.4 %collective-permute-done.4 = f32[2,4,32,512]{3,2,0,1:T(8,128)S(1)} collective-permute-done((f32[2,4,32,512]{3,2,0,1:T(8,128)S(1)}, f32[2,4,32,512]{3,2,0,1:T(8,128)S(1)}, u32[]{:S(2)}, u32[]{:S(2)}) %collective-permute-start.4) | collective-permute-done | bytes 524320 | tf_op jit(solution)/shard_map/ppermute | solution.py:25
  118.7 4.1 %collective-permute-done.5 = f32[2,4,32,512]{3,2,0,1:T(8,128)S(1)} collective-permute-done((f32[2,4,32,512]{3,2,0,1:T(8,128)S(1)}, f32[2,4,32,512]{3,2,0,1:T(8,128)S(1)}, u32[]{:S(2)}, u32[]{:S(2)}) %collective-permute-start.5) | collective-permute-done | bytes 524320 | tf_op jit(solution)/shard_map/ppermute | solution.py:27
  123.1 2.4 %fusion.44 = f32[2,32,512,8]{2,3,1,0:T(8,128)S(1)} fusion(f32[2,16,32,512]{3,2,0,1:T(8,128)S(1)} %pad_maximum_fusion.1, f32[8]{0:T(128)S(1)} %get-tuple-element.28, s32[8]{0:T(128)S(1)} %get-tuple-element.35, f32[8]{0:T(128)S(1)} %get-tuple-element.29, s32[8]{0:T(128)S(1)} %get-tuple-element.36, f32[8]{0:T(128)S(1)} %get-tuple-element.30, ...), kind=kOutput, calls=%fused_computation.56 | convolution fusion | flops 50333440 | bytes 3146048 | tf_op jit(solution)/shard_map/ij,tjxy->tixy/dot_general | solution.py:65
  125.6 7.5 %fusion.48 = f32[2,8,32,512]{3,2,0,1:T(8,128)S(1)} fusion(f32[8,512]{1,0:T(8,128)S(1)} %get-tuple-element.15, s32[8,512]{1,0:T(8,128)S(1)} %get-tuple-element.22, f32[8,512]{1,0:T(8,128)S(1)} %get-tuple-element.16, s32[8,512]{1,0:T(8,128)S(1)} %get-tuple-element.23, f32[8,512]{1,0:T(8,128)S(1)} %get-tuple-element.14, s32[8,512]{1,0:T(8,128)S(1)} %get-tuple-element.21, ...), kind=kOutput, calls=%fused_computation.60 | convolution fusion | flops 828375040 | bytes 2228224 | tf_op jit(solution)/shard_map/terc,ecn->tern/dot_general | solution.py:74
  133.5 30.1 %all_to_all.15.src_ref = f32[16,32,512]{2,1,0:T(8,128)} all-to-all(f32[16,32,512]{2,1,0:T(8,128)S(1)} %bitcast.98), channel_id=1, replica_groups=mesh['asset'=16,'earn'=4,'age'=4] {'asset'}, dimensions={0} | all-to-all | bytes 2097152 | tf_op jit(solution)/shard_map/all_to_all | solution.py:115
  163.6 3.9 %shard_map.84 = f32[16,32,512]{2,1,0:T(8,128)} custom-call(f32[16,32,512]{2,1,0:T(8,128)} %all_to_all.15.src_ref), custom_call_target="tpu_custom_call" | custom-call | bytes 2097152 | tf_op jit(solution)/shard_map/pallas_call | solution.py:100
  167.5 8.1 %fusion.66 = f32[2,8,32,512]{3,2,0,1:T(8,128)S(1)} fusion(f32[8,512]{1,0:T(8,128)S(1)} %get-tuple-element.19, s32[8,512]{1,0:T(8,128)S(1)} %get-tuple-element.25, f32[8,512]{1,0:T(8,128)S(1)} %get-tuple-element.20, s32[8,512]{1,0:T(8,128)S(1)} %get-tuple-element.26, f32[8,512]{1,0:T(8,128)S(1)} %get-tuple-element.18, s32[8,512]{1,0:T(8,128)S(1)} %get-tuple-element.24, ...), kind=kOutput, calls=%fused_computation.66 | convolution fusion | flops 828899328 | bytes 3276800 | tf_op jit(solution)/shard_map/terc,ecn->tern/dot_general | solution.py:74
  (43 shorter events, 7.3 us)
Async XLA Ops:
  0.0 6.5 %copy-start.2 = (f32[2,8,32,512]{3,2,1,0:T(8,128)S(1)}, f32[2,8,32,512]{3,2,1,0:T(8,128)}, u32[]{:S(2)}) copy-start(f32[2,8,32,512]{3,2,1,0:T(8,128)} %param.9) | copy-start | bytes 3145732
  1.4 15.9 %collective-permute-start = (f32[1,8,32,512]{3,2,1,0:T(8,128)S(1)}, f32[1,8,32,512]{3,2,1,0:T(8,128)S(1)}, u32[]{:S(2)}, u32[]{:S(2)}) collective-permute-start(f32[1,8,32,512]{3,2,1,0:T(8,128)S(1)} %get-tuple-element.12), channel_id=1, source_target_pairs={{1,0},{2,1},{3,2},{5,4},{6,5},{7,6},{9,8},{10,9},{11,10},{13,12},{... | collective-permute-start | bytes 1572872 | tf_op jit(solution)/shard_map/ppermute | solution.py:37
  6.5 10.7 %copy-start.9 = (f32[5,8]{1,0:T(8,128)S(1)}, f32[5,8]{1,0:T(8,128)}, u32[]{:S(2)}) copy-start(f32[5,8]{1,0:T(8,128)} %param.10) | copy-start | bytes 484
  7.8 14.0 %copy-start.10 = (s32[8]{0:T(128)S(1)}, s32[8]{0:T(128)}, u32[]{:S(2)}) copy-start(s32[8]{0:T(128)} %param.11) | copy-start | bytes 100
  7.8 14.0 %copy-start.8 = (s32[8,512]{1,0:T(8,128)S(1)}, s32[8,512]{1,0:T(8,128)}, u32[]{:S(2)}) copy-start(s32[8,512]{1,0:T(8,128)} %param.12) | copy-start | bytes 49156
  7.8 14.0 %copy-start.5 = (f32[4,8,512]{2,1,0:T(8,128)S(1)}, f32[4,8,512]{2,1,0:T(8,128)}, u32[]{:S(2)}) copy-start(f32[4,8,512]{2,1,0:T(8,128)} %param.13) | copy-start | bytes 196612
  7.8 39.7 %all-to-all-start = ((f32[16,32,512]{2,1,0:T(8,128)}), f32[16,32,512]{2,1,0:T(8,128)S(1)}, u32[]{:S(2)}, u32[]{:S(2)}) async-start(f32[16,32,512]{2,1,0:T(8,128)} %bitcast.14), calls=%async_computation | async-start | bytes 2097152 | tf_op jit(solution)/shard_map/all_to_all | solution.py:115
  17.4 14.7 %collective-permute-start.1 = (f32[2,4,32,512]{3,2,1,0:T(8,128)S(1)}, f32[2,4,32,512]{3,2,1,0:T(8,128)S(1)}, u32[]{:S(2)}, u32[]{:S(2)}) collective-permute-start(f32[2,4,32,512]{3,2,1,0:T(8,128)S(1)} %get-tuple-element.9), channel_id=1, source_target_pairs={{0,4},{4,8},{8,12},{1,5},{5,9},{9,13},{2,6},{6,10},{10,14},{3,7},{... | collective-permute-start | bytes 1572872 | tf_op jit(solution)/shard_map/ppermute | solution.py:25
  20.5 15.4 %collective-permute-start.2 = (f32[2,4,32,512]{3,2,1,0:T(8,128)S(1)}, f32[2,4,32,512]{3,2,1,0:T(8,128)S(1)}, u32[]{:S(2)}, u32[]{:S(2)}) collective-permute-start(f32[2,4,32,512]{3,2,1,0:T(8,128)S(1)} %get-tuple-element.10), channel_id=1, source_target_pairs={{4,0},{8,4},{12,8},{5,1},{9,5},{13,9},{6,2},{10,6},{14,10},{7,3},{... | collective-permute-start | bytes 1572872 | tf_op jit(solution)/shard_map/ppermute | solution.py:27
  46.2 10.1 %copy-start.7 = (s32[8,512]{1,0:T(8,128)S(1)}, s32[8,512]{1,0:T(8,128)}, u32[]{:S(2)}) copy-start(s32[8,512]{1,0:T(8,128)} %param.14) | copy-start | bytes 49156
  46.2 10.1 %copy-start.6 = (f32[4,8,512]{2,1,0:T(8,128)S(1)}, f32[4,8,512]{2,1,0:T(8,128)}, u32[]{:S(2)}) copy-start(f32[4,8,512]{2,1,0:T(8,128)} %param.15) | copy-start | bytes 196612
  47.5 8.8 %copy-start = (f32[16,32,512]{2,1,0:T(8,128)}, f32[16,32,512]{2,1,0:T(8,128)S(1)}, u32[]{:S(2)}) copy-start(f32[16,32,512]{2,1,0:T(8,128)S(1)} %all-to-all-done.src_ref) | copy-start | bytes 3145732
  47.5 35.8 %all-to-all-start.1 = ((f32[16,32,512]{2,1,0:T(8,128)}), f32[16,32,512]{2,1,0:T(8,128)S(1)}, u32[]{:S(2)}, u32[]{:S(2)}) async-start(f32[16,32,512]{2,1,0:T(8,128)} %bitcast.29), calls=%async_computation.1 | async-start | bytes 2097152 | tf_op jit(solution)/shard_map/all_to_all | solution.py:115
  60.2 27.9 %copy-start.4 = (f32[16,32,512]{2,1,0:T(8,128)S(1)}, f32[16,32,512]{2,1,0:T(8,128)}, u32[]{:S(2)}) copy-start(f32[16,32,512]{2,1,0:T(8,128)} %shard_map.82) | copy-start | bytes 3145732
  83.3 1.0 copy-start.1
  96.3 10.5 %collective-permute-start.3 = (f32[1,8,32,512]{3,2,0,1:T(8,128)S(1)}, f32[1,8,32,512]{3,2,0,1:T(8,128)S(1)}, u32[]{:S(2)}, u32[]{:S(2)}) collective-permute-start(f32[1,8,32,512]{3,2,0,1:T(8,128)S(1)} %get-tuple-element.8), channel_id=1, source_target_pairs={{1,0},{2,1},{3,2},{5,4},{6,5},{7,6},{9,8},{10,9},{11,10},{13,12},{... | collective-permute-start | bytes 1572872 | tf_op jit(solution)/shard_map/ppermute | solution.py:37
  106.9 11.9 %collective-permute-start.4 = (f32[2,4,32,512]{3,2,0,1:T(8,128)S(1)}, f32[2,4,32,512]{3,2,0,1:T(8,128)S(1)}, u32[]{:S(2)}, u32[]{:S(2)}) collective-permute-start(f32[2,4,32,512]{3,2,0,1:T(8,128)S(1)} %get-tuple-element.5), channel_id=1, source_target_pairs={{0,4},{4,8},{8,12},{1,5},{5,9},{9,13},{2,6},{6,10},{10,14},{3,7},{... | collective-permute-start | bytes 1572872 | tf_op jit(solution)/shard_map/ppermute | solution.py:25
  110.0 12.9 %collective-permute-start.5 = (f32[2,4,32,512]{3,2,0,1:T(8,128)S(1)}, f32[2,4,32,512]{3,2,0,1:T(8,128)S(1)}, u32[]{:S(2)}, u32[]{:S(2)}) collective-permute-start(f32[2,4,32,512]{3,2,0,1:T(8,128)S(1)} %get-tuple-element.6), channel_id=1, source_target_pairs={{4,0},{8,4},{12,8},{5,1},{9,5},{13,9},{6,2},{10,6},{14,10},{7,3},{... | collective-permute-start | bytes 1572872 | tf_op jit(solution)/shard_map/ppermute | solution.py:27
  133.5 34.0 %copy-start.3 = (f32[2,8,32,512]{3,2,1,0:T(8,128)S(1)}, f32[2,8,32,512]{3,2,1,0:T(8,128)}, u32[]{:S(2)}) copy-start(f32[2,8,32,512]{3,2,1,0:T(8,128)} %param.9) | copy-start | bytes 3145732

commit v2 on v1

--- a/solution.py
+++ b/solution.py
@@ -128,6 +128,7 @@
 ):
     liquid_map = band_matrix(liquid_offset, liquid_weight)
     illiquid_map = band_matrix(illiquid_offset, illiquid_weight)
+    liquid_map, illiquid_map = lax.optimization_barrier((liquid_map, illiquid_map))
 
     expected = continuation(values, earn_prob, support_start)
     saved = along_lanes(expected, liquid_map)

time: 177 us -> 186 us (1.051)
  the two profiles are of different devices: /device:TPU:1 before, /device:TPU:5 now
where the time goes in v2:
time: 186 us; the launch traced here: 185 us
  waiting for transfers between devices  54.9 us (30%)
  starting transfers between devices  35.1 us (19%)
  blocking collectives  28.1 us (15%)
  matrix products  27 us (15%)
  other arithmetic  18.5 us (10%)
  Pallas kernels  11.6 us (6%)
  local copies, waits for them, and re-layouts  9.36 us (5%)
    ppermute x2, waiting for transfers between devices, passed_along(): return lax.ppermute(value, axis, pairs)  33.8 us
    all_to_all x1, blocking collectives, flipped(): got = lax.all_to_all(flat, 'asset', 0, 0, tiled=True)  28.1 us
    dot_general x4, matrix products, along_lanes(): jnp.einsum('terc,ecn->tern', stacked, matrix, precision=lax.Precision.HIGH)  22.1 us
    all_to_all x2, starting transfers between devices, flipped(): got = lax.all_to_all(flat, 'asset', 0, 0, tiled=True)  19.3 us
    add x1, other arithmetic, band_matrix(): matrix + jnp.where(positions[None, :, None] == (offset + number)[:, None,...  15.3 us
    all_to_all x2, waiting for transfers between devices, flipped(): got = lax.all_to_all(flat, 'asset', 0, 0, tiled=True)  13.1 us
    pallas_call x3, Pallas kernels, regroup(): pl.pallas_call(_gather_kernel, grid=(lanes // 128,), in_specs=[pl.BlockSp...  11.6 us
    ppermute x2, starting transfers between devices, extended(): lax.ppermute(tail, axis, [(i, (i + 1) % count) for i in range(ends)])  6.43 us
  transfers between devices with their start and end apart: 8, of which 5 were waited for; matrix products, arithmetic and copies ran while one was open for 17% of the time, Pallas kernels for 2%

profile of v2, /device:TPU:5, one launch (start us, length us, event | category | flops | bytes accessed | tf_op | source)
XLA Modules:
  0.0 184.9 jit_solution(5917892368307145131)
XLA Ops:
  0.0 2.5 %copy.15 = f32[512,512]{0,1:T(8,128)} copy(f32[512,512]{1,0:T(8,128)} %bitcast.101) | data formatting | bytes 2097152 | tf_op jit(solution)/shard_map/reshape | solution.py:114
  2.6 10.9 %all-to-all-start = ((f32[16,32,512]{2,1,0:T(8,128)}), f32[16,32,512]{2,1,0:T(8,128)S(1)}, u32[]{:S(2)}, u32[]{:S(2)}) async-start(f32[16,32,512]{2,1,0:T(8,128)} %bitcast.14), calls=%async_computation | async-start | bytes 2097152 | tf_op jit(solution)/shard_map/all_to_all | solution.py:115
  14.8 2.9 %collective-permute-start = (f32[1,8,32,512]{3,2,1,0:T(8,128)S(1)}, f32[1,8,32,512]{3,2,1,0:T(8,128)S(1)}, u32[]{:S(2)}, u32[]{:S(2)}) collective-permute-start(f32[1,8,32,512]{3,2,1,0:T(8,128)S(1)} %get-tuple-element.16), channel_id=1, source_target_pairs={{1,0},{2,1},{3,2},{5,4},{6,5},{7,6},{9,8},{10,9},{11,10},{13,12},{... | collective-permute-start | bytes 1572872 | tf_op jit(solution)/shard_map/ppermute | solution.py:37
  20.6 23.1 %collective-permute-done = f32[1,8,32,512]{3,2,1,0:T(8,128)S(1)} collective-permute-done((f32[1,8,32,512]{3,2,1,0:T(8,128)S(1)}, f32[1,8,32,512]{3,2,1,0:T(8,128)S(1)}, u32[]{:S(2)}, u32[]{:S(2)}) %collective-permute-start) | collective-permute-done | bytes 524320 | tf_op jit(solution)/shard_map/ppermute | solution.py:37
  43.8 2.8 %collective-permute-start.1 = (f32[2,4,32,512]{3,2,1,0:T(8,128)S(1)}, f32[2,4,32,512]{3,2,1,0:T(8,128)}, u32[]{:S(2)}, u32[]{:S(2)}) collective-permute-start(f32[2,4,32,512]{3,2,1,0:T(8,128)S(1)} %get-tuple-element.13), channel_id=1, source_target_pairs={{0,4},{4,8},{8,12},{1,5},{5,9},{9,13},{2,6},{6,10},{10,14},{3,7},{... | collective-permute-start | bytes 1572872 | tf_op jit(solution)/shard_map/ppermute | solution.py:25
  46.6 2.5 %collective-permute-start.2 = (f32[2,4,32,512]{3,2,1,0:T(8,128)S(1)}, f32[2,4,32,512]{3,2,1,0:T(8,128)}, u32[]{:S(2)}, u32[]{:S(2)}) collective-permute-start(f32[2,4,32,512]{3,2,1,0:T(8,128)S(1)} %get-tuple-element.14), channel_id=1, source_target_pairs={{4,0},{8,4},{12,8},{5,1},{9,5},{13,9},{6,2},{10,6},{14,10},{7,3},{... | collective-permute-start | bytes 1572872 | tf_op jit(solution)/shard_map/ppermute | solution.py:27
  49.1 15.3 %select_add_fusion = (f32[8,512,512]{2,1,0:T(8,128)}, f32[8,512,512]{2,1,0:T(8,128)}) fusion(f32[8,512]{1,0:T(8,128)S(1)} %get-tuple-element.19, s32[8,512]{1,0:T(8,128)S(1)} %get-tuple-element.26, f32[8,512]{1,0:T(8,128)S(1)} %get-tuple-element.20, s32[8,512]{1,0:T(8,128)S(1)} %get-tuple-element.27, f32[8,512]{1,0:T(8,128)S(1)} %get-tuple-element.18, ...), kind=kLoop, calls=%fused_computation.8 | loop fusion | flops 46137344 | bytes 17039360 | tf_op jit(solution)/shard_map/add | solution.py:45
  65.9 2.4 %fusion.10 = f32[2,32,512,8]{2,3,1,0:T(8,128)S(1)} fusion(f32[2,16,32,512]{3,2,1,0:T(8,128)S(1)} %pad_maximum_fusion, f32[8]{0:T(128)S(1)} %get-tuple-element.32, s32[8]{0:T(128)S(1)} %get-tuple-element.39, f32[8]{0:T(128)S(1)} %get-tuple-element.33, s32[8]{0:T(128)S(1)} %get-tuple-element.40, f32[8]{0:T(128)S(1)} %get-tuple-element.34, ...), kind=kOutput, calls=%fused_computation.22 | convolution fusion | flops 50333440 | bytes 3146048 | tf_op jit(solution)/shard_map/ij,tjxy->tixy/dot_general | solution.py:65
  68.3 6.4 %fusion.15 = f32[2,8,32,512]{3,2,0,1:T(8,128)S(1)} fusion(f32[8,512,512]{2,1,0:T(8,128)} %get-tuple-element.7, f32[2,32,512,8]{2,3,1,0:T(8,128)S(1)} %fusion.10), kind=kOutput, calls=%fused_computation.25 | convolution fusion | flops 805306368 | bytes 10485760 | tf_op jit(solution)/shard_map/terc,ecn->tern/dot_general | solution.py:74
  76.2 8.4 %all-to-all-start.1 = ((f32[16,32,512]{2,1,0:T(8,128)}), f32[16,32,512]{2,1,0:T(8,128)S(1)}, u32[]{:S(2)}, u32[]{:S(2)}) async-start(f32[16,32,512]{2,1,0:T(8,128)} %bitcast.29), calls=%async_computation.1 | async-start | bytes 2097152 | tf_op jit(solution)/shard_map/all_to_all | solution.py:115
  84.5 3.9 %shard_map.82 = f32[16,32,512]{2,1,0:T(8,128)} custom-call(f32[16,32,512]{2,1,0:T(8,128)} %copy-done), custom_call_target="tpu_custom_call" | custom-call | bytes 2097152 | tf_op jit(solution)/shard_map/pallas_call | solution.py:100
  88.4 13.1 %all-to-all-done.1.src_ref = f32[16,32,512]{2,1,0:T(8,128)S(1)} async-done(((f32[16,32,512]{2,1,0:T(8,128)}), f32[16,32,512]{2,1,0:T(8,128)S(1)}, u32[]{:S(2)}, u32[]{:S(2)}) %all-to-all-start.1) | async-done | bytes 1048608 | tf_op jit(solution)/shard_map/all_to_all | solution.py:115
  102.4 3.9 %shard_map.83 = f32[16,32,512]{2,1,0:T(8,128)} custom-call(f32[16,32,512]{2,1,0:T(8,128)} %copy-done.1), custom_call_target="tpu_custom_call" | custom-call | bytes 2097152 | tf_op jit(solution)/shard_map/pallas_call | solution.py:100
  106.3 6.6 %fusion.24 = f32[2,8,32,512]{3,2,0,1:T(8,128)S(1)} fusion(f32[8,512,512]{2,1,0:T(8,128)} %get-tuple-element.8, f32[2,8,32,512]{3,2,1,0:T(8,128)} %bitcast.102, f32[2,8,32,512]{3,2,1,0:T(8,128)} %bitcast.103), kind=kOutput, calls=%fused_computation.28 | convolution fusion | flops 805830656 | bytes 11534336 | tf_op jit(solution)/shard_map/terc,ecn->tern/dot_general | solution.py:74
  113.1 2.2 %collective-permute-start.3 = (f32[1,8,32,512]{3,2,0,1:T(8,128)S(1)}, f32[1,8,32,512]{3,2,0,1:T(8,128)S(1)}, u32[]{:S(2)}, u32[]{:S(2)}) collective-permute-start(f32[1,8,32,512]{3,2,0,1:T(8,128)S(1)} %get-tuple-element.12), channel_id=1, source_target_pairs={{1,0},{2,1},{3,2},{5,4},{6,5},{7,6},{9,8},{10,9},{11,10},{13,12},{... | collective-permute-start | bytes 1572872 | tf_op jit(solution)/shard_map/ppermute | solution.py:37
  115.2 10.8 %collective-permute-done.3 = f32[1,8,32,512]{3,2,0,1:T(8,128)S(1)} collective-permute-done((f32[1,8,32,512]{3,2,0,1:T(8,128)S(1)}, f32[1,8,32,512]{3,2,0,1:T(8,128)S(1)}, u32[]{:S(2)}, u32[]{:S(2)}) %collective-permute-start.3) | collective-permute-done | bytes 524320 | tf_op jit(solution)/shard_map/ppermute | solution.py:37
  126.1 3.6 %collective-permute-start.4 = (f32[2,4,32,512]{3,2,0,1:T(8,128)S(1)}, f32[2,4,32,512]{3,2,0,1:T(8,128)S(1)}, u32[]{:S(2)}, u32[]{:S(2)}) collective-permute-start(f32[2,4,32,512]{3,2,0,1:T(8,128)S(1)} %get-tuple-element.9), channel_id=1, source_target_pairs={{0,4},{4,8},{8,12},{1,5},{5,9},{9,13},{2,6},{6,10},{10,14},{3,7},{... | collective-permute-start | bytes 1572872 | tf_op jit(solution)/shard_map/ppermute | solution.py:25
  131.7 4.4 %collective-permute-done.4 = f32[2,4,32,512]{3,2,0,1:T(8,128)S(1)} collective-permute-done((f32[2,4,32,512]{3,2,0,1:T(8,128)S(1)}, f32[2,4,32,512]{3,2,0,1:T(8,128)S(1)}, u32[]{:S(2)}, u32[]{:S(2)}) %collective-permute-start.4) | collective-permute-done | bytes 524320 | tf_op jit(solution)/shard_map/ppermute | solution.py:25
  136.1 3.6 %collective-permute-done.5 = f32[2,4,32,512]{3,2,0,1:T(8,128)S(1)} collective-permute-done((f32[2,4,32,512]{3,2,0,1:T(8,128)S(1)}, f32[2,4,32,512]{3,2,0,1:T(8,128)S(1)}, u32[]{:S(2)}, u32[]{:S(2)}) %collective-permute-start.5) | collective-permute-done | bytes 524320 | tf_op jit(solution)/shard_map/ppermute | solution.py:27
  139.9 2.4 %fusion.8 = f32[2,32,512,8]{2,3,1,0:T(8,128)S(1)} fusion(f32[2,16,32,512]{3,2,0,1:T(8,128)S(1)} %pad_maximum_fusion.1, f32[8]{0:T(128)S(1)} %get-tuple-element.32, s32[8]{0:T(128)S(1)} %get-tuple-element.39, f32[8]{0:T(128)S(1)} %get-tuple-element.33, s32[8]{0:T(128)S(1)} %get-tuple-element.40, f32[8]{0:T(128)S(1)} %get-tuple-element.34, ...), kind=kOutput, calls=%fused_computation.20 | convolution fusion | flops 50333440 | bytes 3146048 | tf_op jit(solution)/shard_map/ij,tjxy->tixy/dot_general | solution.py:65
  142.4 2.9 %fusion.12 = f32[2,8,32,512]{3,2,0,1:T(8,128)S(1)} fusion(f32[8,512,512]{2,1,0:T(8,128)S(1)} %bitcast.97, f32[2,32,512,8]{2,3,1,0:T(8,128)S(1)} %fusion.8), kind=kOutput, calls=%fused_computation.24 | convolution fusion | flops 805306368 | bytes 10485760 | tf_op jit(solution)/shard_map/terc,ecn->tern/dot_general | solution.py:74
  145.7 28.1 %all_to_all.15.src_ref = f32[16,32,512]{2,1,0:T(8,128)} all-to-all(f32[16,32,512]{2,1,0:T(8,128)S(1)} %bitcast.100), channel_id=1, replica_groups=mesh['asset'=16,'earn'=4,'age'=4] {'asset'}, dimensions={0} | all-to-all | bytes 2097152 | tf_op jit(solution)/shard_map/all_to_all | solution.py:115
  173.8 3.9 %shard_map.84 = f32[16,32,512]{2,1,0:T(8,128)} custom-call(f32[16,32,512]{2,1,0:T(8,128)} %all_to_all.15.src_ref), custom_call_target="tpu_custom_call" | custom-call | bytes 2097152 | tf_op jit(solution)/shard_map/pallas_call | solution.py:100
  177.6 6.1 %fusion.33 = f32[2,8,32,512]{3,2,0,1:T(8,128)S(1)} fusion(f32[8,512,512]{2,1,0:T(8,128)} %get-tuple-element.7, f32[2,8,32,512]{3,2,1,0:T(8,128)S(1)} %copy-done.2, f32[2,8,32,512]{3,2,1,0:T(8,128)} %bitcast.104), kind=kOutput, calls=%fused_computation.31 | convolution fusion | flops 805830656 | bytes 11534336 | tf_op jit(solution)/shard_map/terc,ecn->tern/dot_general | solution.py:74
  (41 shorter events, 12.0 us)
Async XLA Ops:
  0.0 49.1 %copy-start.4 = (s32[8,512]{1,0:T(8,128)S(1)}, s32[8,512]{1,0:T(8,128)}, u32[]{:S(2)}) copy-start(s32[8,512]{1,0:T(8,128)} %param.12) | copy-start | bytes 49156
  0.0 49.1 %copy-start.3 = (s32[8,512]{1,0:T(8,128)S(1)}, s32[8,512]{1,0:T(8,128)}, u32[]{:S(2)}) copy-start(s32[8,512]{1,0:T(8,128)} %param.14) | copy-start | bytes 49156
  2.6 73.6 %all-to-all-start = ((f32[16,32,512]{2,1,0:T(8,128)}), f32[16,32,512]{2,1,0:T(8,128)S(1)}, u32[]{:S(2)}, u32[]{:S(2)}) async-start(f32[16,32,512]{2,1,0:T(8,128)} %bitcast.14), calls=%async_computation | async-start | bytes 2097152 | tf_op jit(solution)/shard_map/all_to_all | solution.py:115
  14.8 28.9 %collective-permute-start = (f32[1,8,32,512]{3,2,1,0:T(8,128)S(1)}, f32[1,8,32,512]{3,2,1,0:T(8,128)S(1)}, u32[]{:S(2)}, u32[]{:S(2)}) collective-permute-start(f32[1,8,32,512]{3,2,1,0:T(8,128)S(1)} %get-tuple-element.16), channel_id=1, source_target_pairs={{1,0},{2,1},{3,2},{5,4},{6,5},{7,6},{9,8},{10,9},{11,10},{13,12},{... | collective-permute-start | bytes 1572872 | tf_op jit(solution)/shard_map/ppermute | solution.py:37
  43.8 20.7 %collective-permute-start.1 = (f32[2,4,32,512]{3,2,1,0:T(8,128)S(1)}, f32[2,4,32,512]{3,2,1,0:T(8,128)}, u32[]{:S(2)}, u32[]{:S(2)}) collective-permute-start(f32[2,4,32,512]{3,2,1,0:T(8,128)S(1)} %get-tuple-element.13), channel_id=1, source_target_pairs={{0,4},{4,8},{8,12},{1,5},{5,9},{9,13},{2,6},{6,10},{10,14},{3,7},{... | collective-permute-start | bytes 1572872 | tf_op jit(solution)/shard_map/ppermute | solution.py:25
  46.6 17.9 %collective-permute-start.2 = (f32[2,4,32,512]{3,2,1,0:T(8,128)S(1)}, f32[2,4,32,512]{3,2,1,0:T(8,128)}, u32[]{:S(2)}, u32[]{:S(2)}) collective-permute-start(f32[2,4,32,512]{3,2,1,0:T(8,128)S(1)} %get-tuple-element.14), channel_id=1, source_target_pairs={{4,0},{8,4},{12,8},{5,1},{9,5},{13,9},{6,2},{10,6},{14,10},{7,3},{... | collective-permute-start | bytes 1572872 | tf_op jit(solution)/shard_map/ppermute | solution.py:27
  49.1 15.3 %copy-start.5 = (f32[5,8]{1,0:T(8,128)S(1)}, f32[5,8]{1,0:T(8,128)}, u32[]{:S(2)}) copy-start(f32[5,8]{1,0:T(8,128)} %param.10) | copy-start | bytes 484
  49.1 15.3 %copy-start.6 = (s32[8]{0:T(128)S(1)}, s32[8]{0:T(128)}, u32[]{:S(2)}) copy-start(s32[8]{0:T(128)} %param.11) | copy-start | bytes 100
  76.2 8.4 %copy-start = (f32[16,32,512]{2,1,0:T(8,128)}, f32[16,32,512]{2,1,0:T(8,128)S(1)}, u32[]{:S(2)}) copy-start(f32[16,32,512]{2,1,0:T(8,128)S(1)} %all-to-all-done.src_ref) | copy-start | bytes 3145732
  76.2 25.3 %all-to-all-start.1 = ((f32[16,32,512]{2,1,0:T(8,128)}), f32[16,32,512]{2,1,0:T(8,128)S(1)}, u32[]{:S(2)}, u32[]{:S(2)}) async-start(f32[16,32,512]{2,1,0:T(8,128)} %bitcast.29), calls=%async_computation.1 | async-start | bytes 2097152 | tf_op jit(solution)/shard_map/all_to_all | solution.py:115
  101.5 1.0 copy-start.1
  106.3 36.0 %slice-start = ((s8[8388608]{0:T(1024)(128)(4,1)}), s8[4194304]{0:T(1024)(128)(4,1)S(1)}, s32[]{:S(2)}) async-start(s8[8388608]{0:T(1024)(128)(4,1)} %bitcast.96), calls=%async_computation.3 | async-start | bytes 8388608
  112.9 29.4 %slice-start.1 = ((s8[8388608]{0:T(1024)(128)(4,1)}), s8[4194304]{0:T(1024)(128)(4,1)S(1)}, s32[]{:S(2)}) async-start(s8[8388608]{0:T(1024)(128)(4,1)} %bitcast.96), calls=%async_computation.4 | async-start | bytes 8388608
  113.1 13.0 %collective-permute-start.3 = (f32[1,8,32,512]{3,2,0,1:T(8,128)S(1)}, f32[1,8,32,512]{3,2,0,1:T(8,128)S(1)}, u32[]{:S(2)}, u32[]{:S(2)}) collective-permute-start(f32[1,8,32,512]{3,2,0,1:T(8,128)S(1)} %get-tuple-element.12), channel_id=1, source_target_pairs={{1,0},{2,1},{3,2},{5,4},{6,5},{7,6},{9,8},{10,9},{11,10},{13,12},{... | collective-permute-start | bytes 1572872 | tf_op jit(solution)/shard_map/ppermute | solution.py:37
  126.1 9.9 %collective-permute-start.4 = (f32[2,4,32,512]{3,2,0,1:T(8,128)S(1)}, f32[2,4,32,512]{3,2,0,1:T(8,128)S(1)}, u32[]{:S(2)}, u32[]{:S(2)}) collective-permute-start(f32[2,4,32,512]{3,2,0,1:T(8,128)S(1)} %get-tuple-element.9), channel_id=1, source_target_pairs={{0,4},{4,8},{8,12},{1,5},{5,9},{9,13},{2,6},{6,10},{10,14},{3,7},{... | collective-permute-start | bytes 1572872 | tf_op jit(solution)/shard_map/ppermute | solution.py:25
  129.7 9.9 %collective-permute-start.5 = (f32[2,4,32,512]{3,2,0,1:T(8,128)S(1)}, f32[2,4,32,512]{3,2,0,1:T(8,128)S(1)}, u32[]{:S(2)}, u32[]{:S(2)}) collective-permute-start(f32[2,4,32,512]{3,2,0,1:T(8,128)S(1)} %get-tuple-element.10), channel_id=1, source_target_pairs={{4,0},{8,4},{12,8},{5,1},{9,5},{13,9},{6,2},{10,6},{14,10},{7,3},{... | collective-permute-start | bytes 1572872 | tf_op jit(solution)/shard_map/ppermute | solution.py:27
  142.3 35.3 %copy-start.2 = (f32[2,8,32,512]{3,2,1,0:T(8,128)S(1)}, f32[2,8,32,512]{3,2,1,0:T(8,128)}, u32[]{:S(2)}) copy-start(f32[2,8,32,512]{3,2,1,0:T(8,128)} %param.9) | copy-start | bytes 3145732

commit v3 on v1

--- a/solution.py
+++ b/solution.py
@@ -14,29 +14,6 @@
 PRECISE = lax.Precision.HIGHEST
 
 
-def extended(cells, sides, width):
-    for axis, dim in sides:
-        count = lax.axis_size(axis)
-        ends = count - 1
-        head = lax.slice_in_dim(cells, 0, width, axis=dim)
-        tail = lax.slice_in_dim(cells, cells.shape[dim] - width, cells.shape[dim], axis=dim)
-        cells = jnp.concatenate(
-            [
-                lax.ppermute(tail, axis, [(i, (i + 1) % count) for i in range(ends)]),
-                cells,
-                lax.ppermute(head, axis, [((i + 1) % count, i) for i in range(ends)]),
-            ],
-            axis=dim,
-        )
-    return cells
-
-
-def passed_along(value, axis, by):
-    count = lax.axis_size(axis)
-    pairs = [(i, i + by) for i in range(count) if 0 <= i + by < count]
-    return lax.ppermute(value, axis, pairs)
-
-
 def band_matrix(offset, weight):
     extent = offset.shape[1]
     positions = jnp.arange(extent, dtype=jnp.int32)
@@ -50,9 +27,36 @@
     return matrix
 
 
-def expectation(stacked, earn_prob, support_start):
-    padded = extended(stacked, (("earn", 1),), REACH)
-    states_here = stacked.shape[1]
+def neighbours(current):
+    states = current.shape[1]
+    ages = lax.axis_size("age")
+    earns = lax.axis_size("earn")
+    axes = ("earn", "age")
+
+    def moved(value, by_earn, by_age):
+        pairs = []
+        for e in range(earns):
+            for a in range(ages):
+                te, ta = e + by_earn, a + by_age
+                if 0 <= te < earns and 0 <= ta < ages:
+                    pairs.append((e * ages + a, te * ages + ta))
+        return lax.ppermute(value, axes, pairs)
+
+    head = slice(0, REACH)
+    tail = slice(states - REACH, states)
+    here = jnp.concatenate(
+        [moved(current[1:, tail], 1, 0), current[1:], moved(current[1:, head], -1, 0)], axis=1
+    )
+    above = jnp.concatenate(
+        [moved(current[:1, tail], 1, -1), moved(current[:1], 0, -1), moved(current[:1, head], -1, -1)],
+        axis=1,
+    )
+    return jnp.concatenate([here, above], axis=0)
+
+
+def continuation(current, earn_prob, support_start):
+    padded = neighbours(current)
+    states_here = current.shape[1]
     first_state = lax.axis_index("earn") * states_here
     slots = jnp.arange(states_here + 2 * REACH, dtype=jnp.int32)
     prob_sum = jnp.sum(earn_prob, axis=0)
@@ -63,11 +67,6 @@
             slots[None, :] == target[:, None], (earn_prob[number] / prob_sum)[:, None], 0.0
         )
     return jnp.einsum("ij,tjxy->tixy", mixing, padded, precision=PRECISE)
-
-
-def continuation(current, earn_prob, support_start):
-    arrived = passed_along(current[:1], "age", -1)
-    return expectation(jnp.concatenate([current[1:], arrived], axis=0), earn_prob, support_start)
 
 
 def along_lanes(stacked, matrix):

time: 177 us -> 177 us (level)
  the two profiles are of different devices: /device:TPU:1 before, /device:TPU:34 now
where the time goes in v3:
time: 177 us; the launch traced here: 176 us
  starting transfers between devices  42.7 us (24%)
  waiting for transfers between devices  41.9 us (24%)
  matrix products  36 us (20%)
  blocking collectives  32.4 us (18%)
  Pallas kernels  11.6 us (7%)
  local copies, waits for them, and re-layouts  8.28 us (5%)
  other arithmetic  2.37 us (1%)
    all_to_all x2, waiting for transfers between devices, flipped(): got = lax.all_to_all(flat, 'asset', 0, 0, tiled=True)  35.2 us
    all_to_all x1, blocking collectives, flipped(): got = lax.all_to_all(flat, 'asset', 0, 0, tiled=True)  32.4 us
    dot_general x4, matrix products, along_lanes(): jnp.einsum('terc,ecn->tern', stacked, matrix, precision=lax.Precision.HIGH)  31.1 us
    ppermute x10, starting transfers between devices, moved(): return lax.ppermute(value, axes, pairs)  25.2 us
    all_to_all x2, starting transfers between devices, flipped(): got = lax.all_to_all(flat, 'asset', 0, 0, tiled=True)  17.5 us
    pallas_call x3, Pallas kernels, regroup(): pl.pallas_call(_gather_kernel, grid=(lanes // 128,), in_specs=[pl.BlockSp...  11.6 us
    ppermute x10, waiting for transfers between devices, moved(): return lax.ppermute(value, axes, pairs)  6.66 us
    dot_general x2, matrix products, continuation(): return jnp.einsum('ij,tjxy->tixy', mixing, padded, precision=PRECISE)  4.85 us
  transfers between devices with their start and end apart: 12, of which 5 were waited for; matrix products, arithmetic and copies ran while one was open for 8% of the time, Pallas kernels for 2%

profile of v3, /device:TPU:34, one launch (start us, length us, event | category | flops | bytes accessed | tf_op | source)
XLA Modules:
  0.0 175.8 jit_solution(3493136632555185780)
XLA Ops:
  0.0 2.3 %fusion.110 = (f32[1,4,32,512]{3,2,1,0:T(8,128)}, f32[1,4,32,512]{3,2,1,0:T(8,128)}, f32[1,4,32,512]{3,2,1,0:T(8,128)}, f32[1,4,32,512]{3,2,1,0:T(8,128)}) fusion(f32[2,8,32,512]{3,2,1,0:T(8,128)} %param.8), kind=kLoop, calls=%fused_computation.136 | loop fusion | bytes 2097152 | tf_op jit(solution)/shard_map/slice | solution.py:48
  2.3 3.4 %collective-permute-start = (f32[1,4,32,512]{3,2,1,0:T(8,128)}, f32[1,4,32,512]{3,2,1,0:T(8,128)S(1)}, u32[]{:S(2)}, u32[]{:S(2)}) collective-permute-start(f32[1,4,32,512]{3,2,1,0:T(8,128)} %get-tuple-element.11), channel_id=1, source_target_pairs={{0,4},{1,5},{2,6},{3,7},{4,8},{5,9},{6,10},{7,11},{8,12},{9,13},{1... | collective-permute-start | bytes 786440 | tf_op jit(solution)/shard_map/ppermute | solution.py:43
  5.7 2.5 %collective-permute-start.1 = (f32[1,4,32,512]{3,2,1,0:T(8,128)}, f32[1,4,32,512]{3,2,1,0:T(8,128)}, u32[]{:S(2)}, u32[]{:S(2)}) collective-permute-start(f32[1,4,32,512]{3,2,1,0:T(8,128)} %get-tuple-element.13), channel_id=1, source_target_pairs={{4,0},{5,1},{6,2},{7,3},{8,4},{9,5},{10,6},{11,7},{12,8},{13,9},{1... | collective-permute-start | bytes 786440 | tf_op jit(solution)/shard_map/ppermute | solution.py:43
  8.2 1.9 %collective-permute-start.2 = (f32[1,4,32,512]{3,2,1,0:T(8,128)}, f32[1,4,32,512]{3,2,1,0:T(8,128)}, u32[]{:S(2)}, u32[]{:S(2)}) collective-permute-start(f32[1,4,32,512]{3,2,1,0:T(8,128)} %get-tuple-element.12), channel_id=1, source_target_pairs={{1,4},{2,5},{3,6},{5,8},{6,9},{7,10},{9,12},{10,13},{11,14},{17,20... | collective-permute-start | bytes 786440 | tf_op jit(solution)/shard_map/ppermute | solution.py:43
  10.1 3.9 %collective-permute-start.4 = (f32[1,4,32,512]{3,2,1,0:T(8,128)}, f32[1,4,32,512]{3,2,1,0:T(8,128)}, u32[]{:S(2)}, u32[]{:S(2)}) collective-permute-start(f32[1,4,32,512]{3,2,1,0:T(8,128)} %get-tuple-element.14), channel_id=1, source_target_pairs={{5,0},{6,1},{7,2},{9,4},{10,5},{11,6},{13,8},{14,9},{15,10},{21,16... | collective-permute-start | bytes 786440 | tf_op jit(solution)/shard_map/ppermute | solution.py:43
  14.1 1.9 %collective-permute-start.3 = (f32[1,8,32,512]{3,2,1,0:T(8,128)S(1)}, f32[1,8,32,512]{3,2,1,0:T(8,128)}, u32[]{:S(2)}, u32[]{:S(2)}) collective-permute-start(f32[1,8,32,512]{3,2,1,0:T(8,128)S(1)} %get-tuple-element.16), channel_id=1, source_target_pairs={{1,0},{2,1},{3,2},{5,4},{6,5},{7,6},{9,8},{10,9},{11,10},{13,12},{... | collective-permute-start | bytes 1572872 | tf_op jit(solution)/shard_map/ppermute | solution.py:43
  17.4 11.2 %all-to-all-start = ((f32[16,32,512]{2,1,0:T(8,128)}), f32[16,32,512]{2,1,0:T(8,128)S(1)}, u32[]{:S(2)}, u32[]{:S(2)}) async-start(f32[16,32,512]{2,1,0:T(8,128)} %bitcast.14), calls=%async_computation | async-start | bytes 2097152 | tf_op jit(solution)/shard_map/all_to_all | solution.py:114
  31.1 2.4 %fusion.46 = f32[2,32,512,8]{2,3,1,0:T(8,128)S(1)} fusion(f32[2,16,32,512]{3,2,1,0:T(8,128)S(1)} %maximum_maximum_fusion, f32[8]{0:T(128)S(1)} %copy-done.27, s32[8]{0:T(128)S(1)} %get-tuple-element.39, f32[8]{0:T(128)S(1)} %copy-done.28, s32[8]{0:T(128)S(1)} %get-tuple-element.40, f32[8]{0:T(128)S(1)} %copy-done.29, s32[8]{0:T(128)S(1)} %get-tuple-element.37, ...), kind=kOutput, calls=%fused_computation.58 | convolution fusion | flops 50333440 | bytes 3146048 | tf_op jit(solution)/shard_map/ij,tjxy->tixy/dot_general | solution.py:69
  33.5 7.5 %fusion.51 = f32[2,8,32,512]{3,2,0,1:T(8,128)S(1)} fusion(f32[8,512]{1,0:T(8,128)S(1)} %get-tuple-element.23, s32[8,512]{1,0:T(8,128)S(1)} %get-tuple-element.29, f32[8,512]{1,0:T(8,128)S(1)} %get-tuple-element.24, s32[8,512]{1,0:T(8,128)S(1)} %get-tuple-element.30, f32[8,512]{1,0:T(8,128)S(1)} %get-tuple-element.22, s32[8,512]{1,0:T(8,128)S(1)} %get-tuple-element.28, ...), kind=kOutput, calls=%fused_computation.61 | convolution fusion | flops 828375040 | bytes 2228224 | tf_op jit(solution)/shard_map/terc,ecn->tern/dot_general | solution.py:73
  42.5 13.3 %all-to-all-done.src_ref = f32[16,32,512]{2,1,0:T(8,128)S(1)} async-done(((f32[16,32,512]{2,1,0:T(8,128)}), f32[16,32,512]{2,1,0:T(8,128)S(1)}, u32[]{:S(2)}, u32[]{:S(2)}) %all-to-all-start) | async-done | bytes 1048608 | tf_op jit(solution)/shard_map/all_to_all | solution.py:114
  55.8 6.3 %all-to-all-start.1 = ((f32[16,32,512]{2,1,0:T(8,128)}), f32[16,32,512]{2,1,0:T(8,128)S(1)}, u32[]{:S(2)}, u32[]{:S(2)}) async-start(f32[16,32,512]{2,1,0:T(8,128)} %bitcast.29), calls=%async_computation.1 | async-start | bytes 2097152 | tf_op jit(solution)/shard_map/all_to_all | solution.py:114
  62.1 3.9 %shard_map.82 = f32[16,32,512]{2,1,0:T(8,128)} custom-call(f32[16,32,512]{2,1,0:T(8,128)} %copy-done.1), custom_call_target="tpu_custom_call" | custom-call | bytes 2097152 | tf_op jit(solution)/shard_map/pallas_call | solution.py:99
  66.0 21.9 %all-to-all-done.1.src_ref = f32[16,32,512]{2,1,0:T(8,128)S(1)} async-done(((f32[16,32,512]{2,1,0:T(8,128)}), f32[16,32,512]{2,1,0:T(8,128)S(1)}, u32[]{:S(2)}, u32[]{:S(2)}) %all-to-all-start.1) | async-done | bytes 1048608 | tf_op jit(solution)/shard_map/all_to_all | solution.py:114
  88.9 3.8 %shard_map.83 = f32[16,32,512]{2,1,0:T(8,128)} custom-call(f32[16,32,512]{2,1,0:T(8,128)} %copy-done.2), custom_call_target="tpu_custom_call" | custom-call | bytes 2097152 | tf_op jit(solution)/shard_map/pallas_call | solution.py:99
  92.8 8.1 %fusion.69 = f32[2,8,32,512]{3,2,0,1:T(8,128)S(1)} fusion(f32[8,512]{1,0:T(8,128)S(1)} %get-tuple-element.19, s32[8,512]{1,0:T(8,128)S(1)} %get-tuple-element.26, f32[8,512]{1,0:T(8,128)S(1)} %get-tuple-element.20, s32[8,512]{1,0:T(8,128)S(1)} %get-tuple-element.27, f32[8,512]{1,0:T(8,128)S(1)} %get-tuple-element.18, s32[8,512]{1,0:T(8,128)S(1)} %get-tuple-element.25, ...), kind=kOutput, calls=%fused_computation.67 | convolution fusion | flops 828899328 | bytes 3276800 | tf_op jit(solution)/shard_map/terc,ecn->tern/dot_general | solution.py:73
  103.0 2.6 %collective-permute-start.5 = (f32[1,4,32,512]{3,2,0,1:T(8,128)S(1)}, f32[1,4,32,512]{3,2,0,1:T(8,128)S(1)}, u32[]{:S(2)}, u32[]{:S(2)}) collective-permute-start(f32[1,4,32,512]{3,2,0,1:T(8,128)S(1)} %get-tuple-element.5), channel_id=1, source_target_pairs={{0,4},{1,5},{2,6},{3,7},{4,8},{5,9},{6,10},{7,11},{8,12},{9,13},{1... | collective-permute-start | bytes 786440 | tf_op jit(solution)/shard_map/ppermute | solution.py:43
  105.5 3.3 %collective-permute-start.6 = (f32[1,4,32,512]{3,2,0,1:T(8,128)S(1)}, f32[1,4,32,512]{3,2,0,1:T(8,128)S(1)}, u32[]{:S(2)}, u32[]{:S(2)}) collective-permute-start(f32[1,4,32,512]{3,2,0,1:T(8,128)S(1)} %get-tuple-element.8), channel_id=1, source_target_pairs={{4,0},{5,1},{6,2},{7,3},{8,4},{9,5},{10,6},{11,7},{12,8},{13,9},{1... | collective-permute-start | bytes 786440 | tf_op jit(solution)/shard_map/ppermute | solution.py:43
  113.6 3.4 %collective-permute-done.6 = f32[1,4,32,512]{3,2,0,1:T(8,128)S(1)} collective-permute-done((f32[1,4,32,512]{3,2,0,1:T(8,128)S(1)}, f32[1,4,32,512]{3,2,0,1:T(8,128)S(1)}, u32[]{:S(2)}, u32[]{:S(2)}) %collective-permute-start.6) | collective-permute-done | bytes 262176 | tf_op jit(solution)/shard_map/ppermute | solution.py:43
  117.0 2.4 %collective-permute-done.9 = f32[1,4,32,512]{3,2,0,1:T(8,128)S(1)} collective-permute-done((f32[1,4,32,512]{3,2,0,1:T(8,128)S(1)}, f32[1,4,32,512]{3,2,0,1:T(8,128)S(1)}, u32[]{:S(2)}, u32[]{:S(2)}) %collective-permute-start.9) | collective-permute-done | bytes 262176 | tf_op jit(solution)/shard_map/ppermute | solution.py:43
  120.0 2.4 %fusion.44 = f32[2,32,512,8]{2,3,1,0:T(8,128)S(1)} fusion(f32[2,16,32,512]{3,2,0,1:T(8,128)S(1)} %maximum_maximum_fusion.1, f32[8]{0:T(128)S(1)} %copy-done.27, s32[8]{0:T(128)S(1)} %copy-done.23, f32[8]{0:T(128)S(1)} %copy-done.28, s32[8]{0:T(128)S(1)} %copy-done.25, f32[8]{0:T(128)S(1)} %copy-done.29, s32[8]{0:T(128)S(1)} %copy-done.19, ...), kind=kOutput, calls=%fused_computation.56 | convolution fusion | flops 50333440 | bytes 3146048 | tf_op jit(solution)/shard_map/ij,tjxy->tixy/dot_general | solution.py:69
  122.4 7.5 %fusion.48 = f32[2,8,32,512]{3,2,0,1:T(8,128)S(1)} fusion(f32[8,512]{1,0:T(8,128)S(1)} %get-tuple-element.19, s32[8,512]{1,0:T(8,128)S(1)} %get-tuple-element.26, f32[8,512]{1,0:T(8,128)S(1)} %get-tuple-element.20, s32[8,512]{1,0:T(8,128)S(1)} %get-tuple-element.27, f32[8,512]{1,0:T(8,128)S(1)} %get-tuple-element.18, s32[8,512]{1,0:T(8,128)S(1)} %get-tuple-element.25, ...), kind=kOutput, calls=%fused_computation.60 | convolution fusion | flops 828375040 | bytes 2228224 | tf_op jit(solution)/shard_map/terc,ecn->tern/dot_general | solution.py:73
  130.4 32.4 %all_to_all.15.src_ref = f32[16,32,512]{2,1,0:T(8,128)} all-to-all(f32[16,32,512]{2,1,0:T(8,128)S(1)} %bitcast.98), channel_id=1, replica_groups=mesh['asset'=16,'earn'=4,'age'=4] {'asset'}, dimensions={0} | all-to-all | bytes 2097152 | tf_op jit(solution)/shard_map/all_to_all | solution.py:114
  162.8 3.9 %shard_map.84 = f32[16,32,512]{2,1,0:T(8,128)} custom-call(f32[16,32,512]{2,1,0:T(8,128)} %all_to_all.15.src_ref), custom_call_target="tpu_custom_call" | custom-call | bytes 2097152 | tf_op jit(solution)/shard_map/pallas_call | solution.py:99
  166.7 8.1 %fusion.66 = f32[2,8,32,512]{3,2,0,1:T(8,128)S(1)} fusion(f32[8,512]{1,0:T(8,128)S(1)} %copy-done.12, s32[8,512]{1,0:T(8,128)S(1)} %get-tuple-element.29, f32[8,512]{1,0:T(8,128)S(1)} %copy-done.14, s32[8,512]{1,0:T(8,128)S(1)} %get-tuple-element.30, f32[8,512]{1,0:T(8,128)S(1)} %copy-done.10, s32[8,512]{1,0:T(8,128)S(1)} %get-tuple-element.28, ...), kind=kOutput, calls=%fused_computation.66 | convolution fusion | flops 828899328 | bytes 3276800 | tf_op jit(solution)/shard_map/terc,ecn->tern/dot_general | solution.py:73
  (93 shorter events, 15.0 us)
Async XLA Ops:
  0.0 14.0 %copy-start = (f32[2,8,32,512]{3,2,1,0:T(8,128)S(1)}, f32[2,8,32,512]{3,2,1,0:T(8,128)}, u32[]{:S(2)}) copy-start(f32[2,8,32,512]{3,2,1,0:T(8,128)} %param.8) | copy-start | bytes 3145732
  0.0 16.0 %copy-start.3 = (f32[2,8,32,512]{3,2,1,0:T(8,128)S(1)}, f32[2,8,32,512]{3,2,1,0:T(8,128)}, u32[]{:S(2)}) copy-start(f32[2,8,32,512]{3,2,1,0:T(8,128)} %param.9) | copy-start | bytes 3145732
  2.3 27.1 %collective-permute-start = (f32[1,4,32,512]{3,2,1,0:T(8,128)}, f32[1,4,32,512]{3,2,1,0:T(8,128)S(1)}, u32[]{:S(2)}, u32[]{:S(2)}) collective-permute-start(f32[1,4,32,512]{3,2,1,0:T(8,128)} %get-tuple-element.11), channel_id=1, source_target_pairs={{0,4},{1,5},{2,6},{3,7},{4,8},{5,9},{6,10},{7,11},{8,12},{9,13},{1... | collective-permute-start | bytes 786440 | tf_op jit(solution)/shard_map/ppermute | solution.py:43
  5.7 23.7 %collective-permute-start.1 = (f32[1,4,32,512]{3,2,1,0:T(8,128)}, f32[1,4,32,512]{3,2,1,0:T(8,128)}, u32[]{:S(2)}, u32[]{:S(2)}) collective-permute-start(f32[1,4,32,512]{3,2,1,0:T(8,128)} %get-tuple-element.13), channel_id=1, source_target_pairs={{4,0},{5,1},{6,2},{7,3},{8,4},{9,5},{10,6},{11,7},{12,8},{13,9},{1... | collective-permute-start | bytes 786440 | tf_op jit(solution)/shard_map/ppermute | solution.py:43
  8.2 21.2 %collective-permute-start.2 = (f32[1,4,32,512]{3,2,1,0:T(8,128)}, f32[1,4,32,512]{3,2,1,0:T(8,128)}, u32[]{:S(2)}, u32[]{:S(2)}) collective-permute-start(f32[1,4,32,512]{3,2,1,0:T(8,128)} %get-tuple-element.12), channel_id=1, source_target_pairs={{1,4},{2,5},{3,6},{5,8},{6,9},{7,10},{9,12},{10,13},{11,14},{17,20... | collective-permute-start | bytes 786440 | tf_op jit(solution)/shard_map/ppermute | solution.py:43
  10.1 19.3 %collective-permute-start.4 = (f32[1,4,32,512]{3,2,1,0:T(8,128)}, f32[1,4,32,512]{3,2,1,0:T(8,128)}, u32[]{:S(2)}, u32[]{:S(2)}) collective-permute-start(f32[1,4,32,512]{3,2,1,0:T(8,128)} %get-tuple-element.14), channel_id=1, source_target_pairs={{5,0},{6,1},{7,2},{9,4},{10,5},{11,6},{13,8},{14,9},{15,10},{21,16... | collective-permute-start | bytes 786440 | tf_op jit(solution)/shard_map/ppermute | solution.py:43
  14.1 15.3 %collective-permute-start.3 = (f32[1,8,32,512]{3,2,1,0:T(8,128)S(1)}, f32[1,8,32,512]{3,2,1,0:T(8,128)}, u32[]{:S(2)}, u32[]{:S(2)}) collective-permute-start(f32[1,8,32,512]{3,2,1,0:T(8,128)S(1)} %get-tuple-element.16), channel_id=1, source_target_pairs={{1,0},{2,1},{3,2},{5,4},{6,5},{7,6},{9,8},{10,9},{11,10},{13,12},{... | collective-permute-start | bytes 1572872 | tf_op jit(solution)/shard_map/ppermute | solution.py:43
  16.1 12.6 %copy-start.8 = (s32[8,512]{1,0:T(8,128)S(1)}, s32[8,512]{1,0:T(8,128)}, u32[]{:S(2)}) copy-start(s32[8,512]{1,0:T(8,128)} %param.12) | copy-start | bytes 49156
  16.1 12.6 %copy-start.15 = (f32[5,8]{1,0:T(8,128)S(1)}, f32[5,8]{1,0:T(8,128)}, u32[]{:S(2)}) copy-start(f32[5,8]{1,0:T(8,128)} %param.10) | copy-start | bytes 484
  16.1 13.2 %copy-start.31 = (s32[8]{0:T(128)S(1)}, s32[8]{0:T(128)}, u32[]{:S(2)}) copy-start(s32[8]{0:T(128)} %param.11) | copy-start | bytes 100
  16.1 13.2 %copy-start.5 = (f32[4,8,512]{2,1,0:T(8,128)S(1)}, f32[4,8,512]{2,1,0:T(8,128)}, u32[]{:S(2)}) copy-start(f32[4,8,512]{2,1,0:T(8,128)} %param.13) | copy-start | bytes 196612
  17.4 38.4 %all-to-all-start = ((f32[16,32,512]{2,1,0:T(8,128)}), f32[16,32,512]{2,1,0:T(8,128)S(1)}, u32[]{:S(2)}, u32[]{:S(2)}) async-start(f32[16,32,512]{2,1,0:T(8,128)} %bitcast.14), calls=%async_computation | async-start | bytes 2097152 | tf_op jit(solution)/shard_map/all_to_all | solution.py:114
  41.1 21.0 %copy-start.7 = (s32[8,512]{1,0:T(8,128)S(1)}, s32[8,512]{1,0:T(8,128)}, u32[]{:S(2)}) copy-start(s32[8,512]{1,0:T(8,128)} %param.14) | copy-start | bytes 49156
  41.1 21.0 %copy-start.6 = (f32[4,8,512]{2,1,0:T(8,128)S(1)}, f32[4,8,512]{2,1,0:T(8,128)}, u32[]{:S(2)}) copy-start(f32[4,8,512]{2,1,0:T(8,128)} %param.15) | copy-start | bytes 196612
  55.8 32.2 %all-to-all-start.1 = ((f32[16,32,512]{2,1,0:T(8,128)}), f32[16,32,512]{2,1,0:T(8,128)S(1)}, u32[]{:S(2)}, u32[]{:S(2)}) async-start(f32[16,32,512]{2,1,0:T(8,128)} %bitcast.29), calls=%async_computation.1 | async-start | bytes 2097152 | tf_op jit(solution)/shard_map/all_to_all | solution.py:114
  66.0 26.7 %copy-start.4 = (f32[16,32,512]{2,1,0:T(8,128)S(1)}, f32[16,32,512]{2,1,0:T(8,128)}, u32[]{:S(2)}) copy-start(f32[16,32,512]{2,1,0:T(8,128)} %shard_map.82) | copy-start | bytes 3145732
  100.9 18.4 %collective-permute-start.8 = (f32[1,8,32,512]{3,2,0,1:T(8,128)S(1)}, f32[1,8,32,512]{3,2,0,1:T(8,128)S(1)}, u32[]{:S(2)}, u32[]{:S(2)}) collective-permute-start(f32[1,8,32,512]{3,2,0,1:T(8,128)S(1)} %get-tuple-element.10), channel_id=1, source_target_pairs={{1,0},{2,1},{3,2},{5,4},{6,5},{7,6},{9,8},{10,9},{11,10},{13,12},{... | collective-permute-start | bytes 1572872 | tf_op jit(solution)/shard_map/ppermute | solution.py:43
  103.0 10.6 %collective-permute-start.5 = (f32[1,4,32,512]{3,2,0,1:T(8,128)S(1)}, f32[1,4,32,512]{3,2,0,1:T(8,128)S(1)}, u32[]{:S(2)}, u32[]{:S(2)}) collective-permute-start(f32[1,4,32,512]{3,2,0,1:T(8,128)S(1)} %get-tuple-element.5), channel_id=1, source_target_pairs={{0,4},{1,5},{2,6},{3,7},{4,8},{5,9},{6,10},{7,11},{8,12},{9,13},{1... | collective-permute-start | bytes 786440 | tf_op jit(solution)/shard_map/ppermute | solution.py:43
  105.5 11.4 %collective-permute-start.6 = (f32[1,4,32,512]{3,2,0,1:T(8,128)S(1)}, f32[1,4,32,512]{3,2,0,1:T(8,128)S(1)}, u32[]{:S(2)}, u32[]{:S(2)}) collective-permute-start(f32[1,4,32,512]{3,2,0,1:T(8,128)S(1)} %get-tuple-element.8), channel_id=1, source_target_pairs={{4,0},{5,1},{6,2},{7,3},{8,4},{9,5},{10,6},{11,7},{12,8},{13,9},{1... | collective-permute-start | bytes 786440 | tf_op jit(solution)/shard_map/ppermute | solution.py:43
  108.8 8.1 %collective-permute-start.7 = (f32[1,4,32,512]{3,2,0,1:T(8,128)S(1)}, f32[1,4,32,512]{3,2,0,1:T(8,128)S(1)}, u32[]{:S(2)}, u32[]{:S(2)}) collective-permute-start(f32[1,4,32,512]{3,2,0,1:T(8,128)S(1)} %get-tuple-element.7), channel_id=1, source_target_pairs={{1,4},{2,5},{3,6},{5,8},{6,9},{7,10},{9,12},{10,13},{11,14},{17,20... | collective-permute-start | bytes 786440 | tf_op jit(solution)/shard_map/ppermute | solution.py:43
  110.8 8.6 %collective-permute-start.9 = (f32[1,4,32,512]{3,2,0,1:T(8,128)S(1)}, f32[1,4,32,512]{3,2,0,1:T(8,128)S(1)}, u32[]{:S(2)}, u32[]{:S(2)}) collective-permute-start(f32[1,4,32,512]{3,2,0,1:T(8,128)S(1)} %get-tuple-element.6), channel_id=1, source_target_pairs={{5,0},{6,1},{7,2},{9,4},{10,5},{11,6},{13,8},{14,9},{15,10},{21,16... | collective-permute-start | bytes 786440 | tf_op jit(solution)/shard_map/ppermute | solution.py:43
  130.4 36.3 %copy-start.10 = (f32[8,512]{1,0:T(8,128)S(1)}, f32[8,512]{1,0:T(8,128)}, u32[]{:S(2)}) copy-start(f32[8,512]{1,0:T(8,128)} %copy-done.9) | copy-start | bytes 49156
  130.4 36.3 %copy-start.12 = (f32[8,512]{1,0:T(8,128)S(1)}, f32[8,512]{1,0:T(8,128)}, u32[]{:S(2)}) copy-start(f32[8,512]{1,0:T(8,128)} %copy-done.11) | copy-start | bytes 49156
  130.4 36.3 %copy-start.14 = (f32[8,512]{1,0:T(8,128)S(1)}, f32[8,512]{1,0:T(8,128)}, u32[]{:S(2)}) copy-start(f32[8,512]{1,0:T(8,128)} %copy-done.13) | copy-start | bytes 49156
  (20 other events, 38.9 us)

commit v4 on v3

--- a/solution.py
+++ b/solution.py
@@ -75,32 +75,31 @@
 
 def _gather_kernel(src_ref, dst_ref):
     count, piece, lanes = src_ref.shape
-    slabs = dst_ref.shape[0]
-    width = lanes // slabs
-    lane = lax.broadcasted_iota(jnp.int32, (piece, lanes), 1)
-    for w in range(count // slabs):
-        outs = [None] * slabs
-        for u in range(slabs):
-            x = src_ref[w * slabs + u]
-            keep = (lane >= u * width) & (lane < (u + 1) * width)
+    width = dst_ref.shape[2] // count
+    slabs = 128 // width
+    lane = lax.broadcasted_iota(jnp.int32, (piece, 128), 1)
+    for k in range(lanes // 128):
+        for w in range(count // slabs):
+            outs = [None] * slabs
+            for u in range(slabs):
+                x = src_ref[w * slabs + u, :, pl.ds(k * 128, 128)]
+                keep = (lane >= u * width) & (lane < (u + 1) * width)
+                for s in range(slabs):
+                    shift = ((u - s) * width) % 128
+                    y = pltpu.roll(x, shift, 1) if shift else x
+                    outs[s] = y if u == 0 else jnp.where(keep, y, outs[s])
             for s in range(slabs):
-                shift = ((u - s) * width) % lanes
-                y = pltpu.roll(x, shift, 1) if shift else x
-                outs[s] = y if u == 0 else jnp.where(keep, y, outs[s])
-        for s in range(slabs):
-            dst_ref[s, :, pl.ds(w * lanes, lanes)] = outs[s]
+                dst_ref[k * slabs + s, :, pl.ds(w * 128, 128)] = outs[s]
 
 
 def regroup(got):
     count, piece, lanes = got.shape
     width = lanes // count
-    slabs = 128 // width
     nbytes = got.size * got.dtype.itemsize
     return pl.pallas_call(
         _gather_kernel,
-        grid=(lanes // 128,),
-        in_specs=[pl.BlockSpec((count, piece, 128), lambda k: (0, 0, k))],
-        out_specs=pl.BlockSpec((slabs, piece, count * width), lambda k: (k, 0, 0)),
+        in_specs=[pl.BlockSpec(memory_space=pltpu.VMEM)],
+        out_specs=pl.BlockSpec(memory_space=pltpu.VMEM),
         out_shape=jax.ShapeDtypeStruct((lanes // width, piece, count * width), got.dtype),
         cost_estimate=pl.CostEstimate(flops=0, transcendentals=0, bytes_accessed=2 * nbytes),
     )(got)

time: 177 us -> 175 us (0.989)
  Pallas kernels: 11.6 us -> 9.25 us
    pallas_call x3, Pallas kernels: 11.6 us -> 9.25 us  [regroup(): pl.pallas_call(_gather_kernel, in_specs=[pl.BlockSpec(memory_space=pltpu....]
  transfers between devices with their start and end apart: 12 -> 12, of which waited for: 5 -> 5; matrix products, arithmetic and copies ran while one was open for 8% -> 9% of each run, Pallas kernels for 2% -> 2%
where the time goes in v4:
time: 175 us; the launch traced here: 174 us
  starting transfers between devices  42.9 us (25%)
  waiting for transfers between devices  42.4 us (24%)
  matrix products  36 us (21%)
  blocking collectives  32.4 us (19%)
  Pallas kernels  9.25 us (5%)
  local copies, waits for them, and re-layouts  8.28 us (5%)
  other arithmetic  2.37 us (1%)
    all_to_all x2, waiting for transfers between devices, flipped(): got = lax.all_to_all(flat, 'asset', 0, 0, tiled=True)  36 us
    all_to_all x1, blocking collectives, flipped(): got = lax.all_to_all(flat, 'asset', 0, 0, tiled=True)  32.4 us
    dot_general x4, matrix products, along_lanes(): jnp.einsum('terc,ecn->tern', stacked, matrix, precision=lax.Precision.HIGH)  31.1 us
    ppermute x10, starting transfers between devices, moved(): return lax.ppermute(value, axes, pairs)  25.4 us
    all_to_all x2, starting transfers between devices, flipped(): got = lax.all_to_all(flat, 'asset', 0, 0, tiled=True)  17.5 us
    pallas_call x3, Pallas kernels, regroup(): pl.pallas_call(_gather_kernel, in_specs=[pl.BlockSpec(memory_space=pltpu....  9.25 us
    ppermute x10, waiting for transfers between devices, moved(): return lax.ppermute(value, axes, pairs)  6.44 us
    dot_general x2, matrix products, continuation(): return jnp.einsum('ij,tjxy->tixy', mixing, padded, precision=PRECISE)  4.85 us
  transfers between devices with their start and end apart: 12, of which 5 were waited for; matrix products, arithmetic and copies ran while one was open for 9% of the time, Pallas kernels for 2%

profile of v4, /device:TPU:34, one launch (start us, length us, event | category | flops | bytes accessed | tf_op | source)
XLA Modules:
  0.0 174.3 jit_solution(7626566982906098978)
XLA Ops:
  0.0 2.3 %fusion.110 = (f32[1,4,32,512]{3,2,1,0:T(8,128)}, f32[1,4,32,512]{3,2,1,0:T(8,128)}, f32[1,4,32,512]{3,2,1,0:T(8,128)}, f32[1,4,32,512]{3,2,1,0:T(8,128)}) fusion(f32[2,8,32,512]{3,2,1,0:T(8,128)} %param.8), kind=kLoop, calls=%fused_computation.136 | loop fusion | bytes 2097152 | tf_op jit(solution)/shard_map/slice | solution.py:48
  2.3 3.4 %collective-permute-start = (f32[1,4,32,512]{3,2,1,0:T(8,128)}, f32[1,4,32,512]{3,2,1,0:T(8,128)S(1)}, u32[]{:S(2)}, u32[]{:S(2)}) collective-permute-start(f32[1,4,32,512]{3,2,1,0:T(8,128)} %get-tuple-element.11), channel_id=1, source_target_pairs={{0,4},{1,5},{2,6},{3,7},{4,8},{5,9},{6,10},{7,11},{8,12},{9,13},{1... | collective-permute-start | bytes 786440 | tf_op jit(solution)/shard_map/ppermute | solution.py:43
  5.7 2.5 %collective-permute-start.1 = (f32[1,4,32,512]{3,2,1,0:T(8,128)}, f32[1,4,32,512]{3,2,1,0:T(8,128)}, u32[]{:S(2)}, u32[]{:S(2)}) collective-permute-start(f32[1,4,32,512]{3,2,1,0:T(8,128)} %get-tuple-element.13), channel_id=1, source_target_pairs={{4,0},{5,1},{6,2},{7,3},{8,4},{9,5},{10,6},{11,7},{12,8},{13,9},{1... | collective-permute-start | bytes 786440 | tf_op jit(solution)/shard_map/ppermute | solution.py:43
  8.2 1.9 %collective-permute-start.2 = (f32[1,4,32,512]{3,2,1,0:T(8,128)}, f32[1,4,32,512]{3,2,1,0:T(8,128)}, u32[]{:S(2)}, u32[]{:S(2)}) collective-permute-start(f32[1,4,32,512]{3,2,1,0:T(8,128)} %get-tuple-element.12), channel_id=1, source_target_pairs={{1,4},{2,5},{3,6},{5,8},{6,9},{7,10},{9,12},{10,13},{11,14},{17,20... | collective-permute-start | bytes 786440 | tf_op jit(solution)/shard_map/ppermute | solution.py:43
  10.1 3.9 %collective-permute-start.4 = (f32[1,4,32,512]{3,2,1,0:T(8,128)}, f32[1,4,32,512]{3,2,1,0:T(8,128)}, u32[]{:S(2)}, u32[]{:S(2)}) collective-permute-start(f32[1,4,32,512]{3,2,1,0:T(8,128)} %get-tuple-element.14), channel_id=1, source_target_pairs={{5,0},{6,1},{7,2},{9,4},{10,5},{11,6},{13,8},{14,9},{15,10},{21,16... | collective-permute-start | bytes 786440 | tf_op jit(solution)/shard_map/ppermute | solution.py:43
  17.4 11.2 %all-to-all-start = ((f32[16,32,512]{2,1,0:T(8,128)}), f32[16,32,512]{2,1,0:T(8,128)S(1)}, u32[]{:S(2)}, u32[]{:S(2)}) async-start(f32[16,32,512]{2,1,0:T(8,128)} %bitcast.14), calls=%async_computation | async-start | bytes 2097152 | tf_op jit(solution)/shard_map/all_to_all | solution.py:113
  31.1 2.4 %fusion.46 = f32[2,32,512,8]{2,3,1,0:T(8,128)S(1)} fusion(f32[2,16,32,512]{3,2,1,0:T(8,128)S(1)} %maximum_maximum_fusion, f32[8]{0:T(128)S(1)} %copy-done.27, s32[8]{0:T(128)S(1)} %get-tuple-element.39, f32[8]{0:T(128)S(1)} %copy-done.28, s32[8]{0:T(128)S(1)} %get-tuple-element.40, f32[8]{0:T(128)S(1)} %copy-done.29, s32[8]{0:T(128)S(1)} %get-tuple-element.37, ...), kind=kOutput, calls=%fused_computation.58 | convolution fusion | flops 50333440 | bytes 3146048 | tf_op jit(solution)/shard_map/ij,tjxy->tixy/dot_general | solution.py:69
  33.5 7.5 %fusion.51 = f32[2,8,32,512]{3,2,0,1:T(8,128)S(1)} fusion(f32[8,512]{1,0:T(8,128)S(1)} %get-tuple-element.23, s32[8,512]{1,0:T(8,128)S(1)} %get-tuple-element.29, f32[8,512]{1,0:T(8,128)S(1)} %get-tuple-element.24, s32[8,512]{1,0:T(8,128)S(1)} %get-tuple-element.30, f32[8,512]{1,0:T(8,128)S(1)} %get-tuple-element.22, s32[8,512]{1,0:T(8,128)S(1)} %get-tuple-element.28, ...), kind=kOutput, calls=%fused_computation.61 | convolution fusion | flops 828375040 | bytes 2228224 | tf_op jit(solution)/shard_map/terc,ecn->tern/dot_general | solution.py:73
  42.5 13.3 %all-to-all-done.src_ref = f32[16,32,512]{2,1,0:T(8,128)S(1)} async-done(((f32[16,32,512]{2,1,0:T(8,128)}), f32[16,32,512]{2,1,0:T(8,128)S(1)}, u32[]{:S(2)}, u32[]{:S(2)}) %all-to-all-start) | async-done | bytes 1048608 | tf_op jit(solution)/shard_map/all_to_all | solution.py:113
  55.8 6.3 %all-to-all-start.1 = ((f32[16,32,512]{2,1,0:T(8,128)}), f32[16,32,512]{2,1,0:T(8,128)S(1)}, u32[]{:S(2)}, u32[]{:S(2)}) async-start(f32[16,32,512]{2,1,0:T(8,128)} %bitcast.29), calls=%async_computation.1 | async-start | bytes 2097152 | tf_op jit(solution)/shard_map/all_to_all | solution.py:113
  62.1 3.1 %shard_map.82 = f32[16,32,512]{2,1,0:T(8,128)} custom-call(f32[16,32,512]{2,1,0:T(8,128)} %copy-done.1), custom_call_target="tpu_custom_call" | custom-call | bytes 2097152 | tf_op jit(solution)/shard_map/pallas_call | solution.py:99
  65.2 22.7 %all-to-all-done.1.src_ref = f32[16,32,512]{2,1,0:T(8,128)S(1)} async-done(((f32[16,32,512]{2,1,0:T(8,128)}), f32[16,32,512]{2,1,0:T(8,128)S(1)}, u32[]{:S(2)}, u32[]{:S(2)}) %all-to-all-start.1) | async-done | bytes 1048608 | tf_op jit(solution)/shard_map/all_to_all | solution.py:113
  88.9 3.1 %shard_map.83 = f32[16,32,512]{2,1,0:T(8,128)} custom-call(f32[16,32,512]{2,1,0:T(8,128)} %copy-done.2), custom_call_target="tpu_custom_call" | custom-call | bytes 2097152 | tf_op jit(solution)/shard_map/pallas_call | solution.py:99
  92.0 8.1 %fusion.69 = f32[2,8,32,512]{3,2,0,1:T(8,128)S(1)} fusion(f32[8,512]{1,0:T(8,128)S(1)} %get-tuple-element.19, s32[8,512]{1,0:T(8,128)S(1)} %get-tuple-element.26, f32[8,512]{1,0:T(8,128)S(1)} %get-tuple-element.20, s32[8,512]{1,0:T(8,128)S(1)} %get-tuple-element.27, f32[8,512]{1,0:T(8,128)S(1)} %get-tuple-element.18, s32[8,512]{1,0:T(8,128)S(1)} %get-tuple-element.25, ...), kind=kOutput, calls=%fused_computation.67 | convolution fusion | flops 828899328 | bytes 3276800 | tf_op jit(solution)/shard_map/terc,ecn->tern/dot_general | solution.py:73
  102.2 2.6 %collective-permute-start.5 = (f32[1,4,32,512]{3,2,0,1:T(8,128)S(1)}, f32[1,4,32,512]{3,2,0,1:T(8,128)S(1)}, u32[]{:S(2)}, u32[]{:S(2)}) collective-permute-start(f32[1,4,32,512]{3,2,0,1:T(8,128)S(1)} %get-tuple-element.5), channel_id=1, source_target_pairs={{0,4},{1,5},{2,6},{3,7},{4,8},{5,9},{6,10},{7,11},{8,12},{9,13},{1... | collective-permute-start | bytes 786440 | tf_op jit(solution)/shard_map/ppermute | solution.py:43
  104.8 3.3 %collective-permute-start.6 = (f32[1,4,32,512]{3,2,0,1:T(8,128)S(1)}, f32[1,4,32,512]{3,2,0,1:T(8,128)S(1)}, u32[]{:S(2)}, u32[]{:S(2)}) collective-permute-start(f32[1,4,32,512]{3,2,0,1:T(8,128)S(1)} %get-tuple-element.8), channel_id=1, source_target_pairs={{4,0},{5,1},{6,2},{7,3},{8,4},{9,5},{10,6},{11,7},{12,8},{13,9},{1... | collective-permute-start | bytes 786440 | tf_op jit(solution)/shard_map/ppermute | solution.py:43
  110.0 2.1 %collective-permute-start.9 = (f32[1,4,32,512]{3,2,0,1:T(8,128)S(1)}, f32[1,4,32,512]{3,2,0,1:T(8,128)S(1)}, u32[]{:S(2)}, u32[]{:S(2)}) collective-permute-start(f32[1,4,32,512]{3,2,0,1:T(8,128)S(1)} %get-tuple-element.6), channel_id=1, source_target_pairs={{5,0},{6,1},{7,2},{9,4},{10,5},{11,6},{13,8},{14,9},{15,10},{21,16... | collective-permute-start | bytes 786440 | tf_op jit(solution)/shard_map/ppermute | solution.py:43
  112.8 3.4 %collective-permute-done.6 = f32[1,4,32,512]{3,2,0,1:T(8,128)S(1)} collective-permute-done((f32[1,4,32,512]{3,2,0,1:T(8,128)S(1)}, f32[1,4,32,512]{3,2,0,1:T(8,128)S(1)}, u32[]{:S(2)}, u32[]{:S(2)}) %collective-permute-start.6) | collective-permute-done | bytes 262176 | tf_op jit(solution)/shard_map/ppermute | solution.py:43
  116.2 2.4 %collective-permute-done.9 = f32[1,4,32,512]{3,2,0,1:T(8,128)S(1)} collective-permute-done((f32[1,4,32,512]{3,2,0,1:T(8,128)S(1)}, f32[1,4,32,512]{3,2,0,1:T(8,128)S(1)}, u32[]{:S(2)}, u32[]{:S(2)}) %collective-permute-start.9) | collective-permute-done | bytes 262176 | tf_op jit(solution)/shard_map/ppermute | solution.py:43
  119.2 2.4 %fusion.44 = f32[2,32,512,8]{2,3,1,0:T(8,128)S(1)} fusion(f32[2,16,32,512]{3,2,0,1:T(8,128)S(1)} %maximum_maximum_fusion.1, f32[8]{0:T(128)S(1)} %copy-done.27, s32[8]{0:T(128)S(1)} %copy-done.23, f32[8]{0:T(128)S(1)} %copy-done.28, s32[8]{0:T(128)S(1)} %copy-done.25, f32[8]{0:T(128)S(1)} %copy-done.29, s32[8]{0:T(128)S(1)} %copy-done.19, ...), kind=kOutput, calls=%fused_computation.56 | convolution fusion | flops 50333440 | bytes 3146048 | tf_op jit(solution)/shard_map/ij,tjxy->tixy/dot_general | solution.py:69
  121.7 7.5 %fusion.48 = f32[2,8,32,512]{3,2,0,1:T(8,128)S(1)} fusion(f32[8,512]{1,0:T(8,128)S(1)} %get-tuple-element.19, s32[8,512]{1,0:T(8,128)S(1)} %get-tuple-element.26, f32[8,512]{1,0:T(8,128)S(1)} %get-tuple-element.20, s32[8,512]{1,0:T(8,128)S(1)} %get-tuple-element.27, f32[8,512]{1,0:T(8,128)S(1)} %get-tuple-element.18, s32[8,512]{1,0:T(8,128)S(1)} %get-tuple-element.25, ...), kind=kOutput, calls=%fused_computation.60 | convolution fusion | flops 828375040 | bytes 2228224 | tf_op jit(solution)/shard_map/terc,ecn->tern/dot_general | solution.py:73
  129.6 32.4 %all_to_all.15.src_ref = f32[16,32,512]{2,1,0:T(8,128)} all-to-all(f32[16,32,512]{2,1,0:T(8,128)S(1)} %bitcast.98), channel_id=1, replica_groups=mesh['asset'=16,'earn'=4,'age'=4] {'asset'}, dimensions={0} | all-to-all | bytes 2097152 | tf_op jit(solution)/shard_map/all_to_all | solution.py:113
  162.0 3.1 %shard_map.84 = f32[16,32,512]{2,1,0:T(8,128)} custom-call(f32[16,32,512]{2,1,0:T(8,128)} %all_to_all.15.src_ref), custom_call_target="tpu_custom_call" | custom-call | bytes 2097152 | tf_op jit(solution)/shard_map/pallas_call | solution.py:99
  165.1 8.1 %fusion.66 = f32[2,8,32,512]{3,2,0,1:T(8,128)S(1)} fusion(f32[8,512]{1,0:T(8,128)S(1)} %copy-done.12, s32[8,512]{1,0:T(8,128)S(1)} %get-tuple-element.29, f32[8,512]{1,0:T(8,128)S(1)} %copy-done.14, s32[8,512]{1,0:T(8,128)S(1)} %get-tuple-element.30, f32[8,512]{1,0:T(8,128)S(1)} %copy-done.10, s32[8,512]{1,0:T(8,128)S(1)} %get-tuple-element.28, ...), kind=kOutput, calls=%fused_computation.66 | convolution fusion | flops 828899328 | bytes 3276800 | tf_op jit(solution)/shard_map/terc,ecn->tern/dot_general | solution.py:73
  (93 shorter events, 14.8 us)
Async XLA Ops:
  0.0 14.0 %copy-start = (f32[2,8,32,512]{3,2,1,0:T(8,128)S(1)}, f32[2,8,32,512]{3,2,1,0:T(8,128)}, u32[]{:S(2)}) copy-start(f32[2,8,32,512]{3,2,1,0:T(8,128)} %param.8) | copy-start | bytes 3145732
  0.0 16.0 %copy-start.3 = (f32[2,8,32,512]{3,2,1,0:T(8,128)S(1)}, f32[2,8,32,512]{3,2,1,0:T(8,128)}, u32[]{:S(2)}) copy-start(f32[2,8,32,512]{3,2,1,0:T(8,128)} %param.9) | copy-start | bytes 3145732
  2.3 27.1 %collective-permute-start = (f32[1,4,32,512]{3,2,1,0:T(8,128)}, f32[1,4,32,512]{3,2,1,0:T(8,128)S(1)}, u32[]{:S(2)}, u32[]{:S(2)}) collective-permute-start(f32[1,4,32,512]{3,2,1,0:T(8,128)} %get-tuple-element.11), channel_id=1, source_target_pairs={{0,4},{1,5},{2,6},{3,7},{4,8},{5,9},{6,10},{7,11},{8,12},{9,13},{1... | collective-permute-start | bytes 786440 | tf_op jit(solution)/shard_map/ppermute | solution.py:43
  5.7 23.7 %collective-permute-start.1 = (f32[1,4,32,512]{3,2,1,0:T(8,128)}, f32[1,4,32,512]{3,2,1,0:T(8,128)}, u32[]{:S(2)}, u32[]{:S(2)}) collective-permute-start(f32[1,4,32,512]{3,2,1,0:T(8,128)} %get-tuple-element.13), channel_id=1, source_target_pairs={{4,0},{5,1},{6,2},{7,3},{8,4},{9,5},{10,6},{11,7},{12,8},{13,9},{1... | collective-permute-start | bytes 786440 | tf_op jit(solution)/shard_map/ppermute | solution.py:43
  8.2 21.2 %collective-permute-start.2 = (f32[1,4,32,512]{3,2,1,0:T(8,128)}, f32[1,4,32,512]{3,2,1,0:T(8,128)}, u32[]{:S(2)}, u32[]{:S(2)}) collective-permute-start(f32[1,4,32,512]{3,2,1,0:T(8,128)} %get-tuple-element.12), channel_id=1, source_target_pairs={{1,4},{2,5},{3,6},{5,8},{6,9},{7,10},{9,12},{10,13},{11,14},{17,20... | collective-permute-start | bytes 786440 | tf_op jit(solution)/shard_map/ppermute | solution.py:43
  10.1 19.3 %collective-permute-start.4 = (f32[1,4,32,512]{3,2,1,0:T(8,128)}, f32[1,4,32,512]{3,2,1,0:T(8,128)}, u32[]{:S(2)}, u32[]{:S(2)}) collective-permute-start(f32[1,4,32,512]{3,2,1,0:T(8,128)} %get-tuple-element.14), channel_id=1, source_target_pairs={{5,0},{6,1},{7,2},{9,4},{10,5},{11,6},{13,8},{14,9},{15,10},{21,16... | collective-permute-start | bytes 786440 | tf_op jit(solution)/shard_map/ppermute | solution.py:43
  14.1 15.3 %collective-permute-start.3 = (f32[1,8,32,512]{3,2,1,0:T(8,128)S(1)}, f32[1,8,32,512]{3,2,1,0:T(8,128)}, u32[]{:S(2)}, u32[]{:S(2)}) collective-permute-start(f32[1,8,32,512]{3,2,1,0:T(8,128)S(1)} %get-tuple-element.16), channel_id=1, source_target_pairs={{1,0},{2,1},{3,2},{5,4},{6,5},{7,6},{9,8},{10,9},{11,10},{13,12},{... | collective-permute-start | bytes 1572872 | tf_op jit(solution)/shard_map/ppermute | solution.py:43
  16.1 12.6 %copy-start.8 = (s32[8,512]{1,0:T(8,128)S(1)}, s32[8,512]{1,0:T(8,128)}, u32[]{:S(2)}) copy-start(s32[8,512]{1,0:T(8,128)} %param.12) | copy-start | bytes 49156
  16.1 12.6 %copy-start.15 = (f32[5,8]{1,0:T(8,128)S(1)}, f32[5,8]{1,0:T(8,128)}, u32[]{:S(2)}) copy-start(f32[5,8]{1,0:T(8,128)} %param.10) | copy-start | bytes 484
  16.1 13.2 %copy-start.31 = (s32[8]{0:T(128)S(1)}, s32[8]{0:T(128)}, u32[]{:S(2)}) copy-start(s32[8]{0:T(128)} %param.11) | copy-start | bytes 100
  16.1 13.2 %copy-start.5 = (f32[4,8,512]{2,1,0:T(8,128)S(1)}, f32[4,8,512]{2,1,0:T(8,128)}, u32[]{:S(2)}) copy-start(f32[4,8,512]{2,1,0:T(8,128)} %param.13) | copy-start | bytes 196612
  17.4 38.4 %all-to-all-start = ((f32[16,32,512]{2,1,0:T(8,128)}), f32[16,32,512]{2,1,0:T(8,128)S(1)}, u32[]{:S(2)}, u32[]{:S(2)}) async-start(f32[16,32,512]{2,1,0:T(8,128)} %bitcast.14), calls=%async_computation | async-start | bytes 2097152 | tf_op jit(solution)/shard_map/all_to_all | solution.py:113
  41.1 21.0 %copy-start.7 = (s32[8,512]{1,0:T(8,128)S(1)}, s32[8,512]{1,0:T(8,128)}, u32[]{:S(2)}) copy-start(s32[8,512]{1,0:T(8,128)} %param.14) | copy-start | bytes 49156
  41.1 21.0 %copy-start.6 = (f32[4,8,512]{2,1,0:T(8,128)S(1)}, f32[4,8,512]{2,1,0:T(8,128)}, u32[]{:S(2)}) copy-start(f32[4,8,512]{2,1,0:T(8,128)} %param.15) | copy-start | bytes 196612
  55.8 32.2 %all-to-all-start.1 = ((f32[16,32,512]{2,1,0:T(8,128)}), f32[16,32,512]{2,1,0:T(8,128)S(1)}, u32[]{:S(2)}, u32[]{:S(2)}) async-start(f32[16,32,512]{2,1,0:T(8,128)} %bitcast.29), calls=%async_computation.1 | async-start | bytes 2097152 | tf_op jit(solution)/shard_map/all_to_all | solution.py:113
  65.2 26.7 %copy-start.4 = (f32[16,32,512]{2,1,0:T(8,128)S(1)}, f32[16,32,512]{2,1,0:T(8,128)}, u32[]{:S(2)}) copy-start(f32[16,32,512]{2,1,0:T(8,128)} %shard_map.82) | copy-start | bytes 3145732
  100.2 18.4 %collective-permute-start.8 = (f32[1,8,32,512]{3,2,0,1:T(8,128)S(1)}, f32[1,8,32,512]{3,2,0,1:T(8,128)S(1)}, u32[]{:S(2)}, u32[]{:S(2)}) collective-permute-start(f32[1,8,32,512]{3,2,0,1:T(8,128)S(1)} %get-tuple-element.10), channel_id=1, source_target_pairs={{1,0},{2,1},{3,2},{5,4},{6,5},{7,6},{9,8},{10,9},{11,10},{13,12},{... | collective-permute-start | bytes 1572872 | tf_op jit(solution)/shard_map/ppermute | solution.py:43
  102.2 10.6 %collective-permute-start.5 = (f32[1,4,32,512]{3,2,0,1:T(8,128)S(1)}, f32[1,4,32,512]{3,2,0,1:T(8,128)S(1)}, u32[]{:S(2)}, u32[]{:S(2)}) collective-permute-start(f32[1,4,32,512]{3,2,0,1:T(8,128)S(1)} %get-tuple-element.5), channel_id=1, source_target_pairs={{0,4},{1,5},{2,6},{3,7},{4,8},{5,9},{6,10},{7,11},{8,12},{9,13},{1... | collective-permute-start | bytes 786440 | tf_op jit(solution)/shard_map/ppermute | solution.py:43
  104.8 11.4 %collective-permute-start.6 = (f32[1,4,32,512]{3,2,0,1:T(8,128)S(1)}, f32[1,4,32,512]{3,2,0,1:T(8,128)S(1)}, u32[]{:S(2)}, u32[]{:S(2)}) collective-permute-start(f32[1,4,32,512]{3,2,0,1:T(8,128)S(1)} %get-tuple-element.8), channel_id=1, source_target_pairs={{4,0},{5,1},{6,2},{7,3},{8,4},{9,5},{10,6},{11,7},{12,8},{13,9},{1... | collective-permute-start | bytes 786440 | tf_op jit(solution)/shard_map/ppermute | solution.py:43
  108.1 8.1 %collective-permute-start.7 = (f32[1,4,32,512]{3,2,0,1:T(8,128)S(1)}, f32[1,4,32,512]{3,2,0,1:T(8,128)S(1)}, u32[]{:S(2)}, u32[]{:S(2)}) collective-permute-start(f32[1,4,32,512]{3,2,0,1:T(8,128)S(1)} %get-tuple-element.7), channel_id=1, source_target_pairs={{1,4},{2,5},{3,6},{5,8},{6,9},{7,10},{9,12},{10,13},{11,14},{17,20... | collective-permute-start | bytes 786440 | tf_op jit(solution)/shard_map/ppermute | solution.py:43
  110.0 8.6 %collective-permute-start.9 = (f32[1,4,32,512]{3,2,0,1:T(8,128)S(1)}, f32[1,4,32,512]{3,2,0,1:T(8,128)S(1)}, u32[]{:S(2)}, u32[]{:S(2)}) collective-permute-start(f32[1,4,32,512]{3,2,0,1:T(8,128)S(1)} %get-tuple-element.6), channel_id=1, source_target_pairs={{5,0},{6,1},{7,2},{9,4},{10,5},{11,6},{13,8},{14,9},{15,10},{21,16... | collective-permute-start | bytes 786440 | tf_op jit(solution)/shard_map/ppermute | solution.py:43
  129.6 35.5 %copy-start.10 = (f32[8,512]{1,0:T(8,128)S(1)}, f32[8,512]{1,0:T(8,128)}, u32[]{:S(2)}) copy-start(f32[8,512]{1,0:T(8,128)} %copy-done.9) | copy-start | bytes 49156
  129.6 35.5 %copy-start.12 = (f32[8,512]{1,0:T(8,128)S(1)}, f32[8,512]{1,0:T(8,128)}, u32[]{:S(2)}) copy-start(f32[8,512]{1,0:T(8,128)} %copy-done.11) | copy-start | bytes 49156
  129.6 35.5 %copy-start.14 = (f32[8,512]{1,0:T(8,128)S(1)}, f32[8,512]{1,0:T(8,128)}, u32[]{:S(2)}) copy-start(f32[8,512]{1,0:T(8,128)} %copy-done.13) | copy-start | bytes 49156
  (20 other events, 38.9 us)

commit v5 on v4

--- a/solution.py
+++ b/solution.py
@@ -130,9 +130,9 @@
     expected = continuation(values, earn_prob, support_start)
     saved = along_lanes(expected, liquid_map)
     adjusted = along_lanes(flipped(saved), illiquid_map)
-    current = flipped(utility) + DISCOUNT * adjusted
 
-    expected = continuation(current, earn_prob, support_start)
+    carried = flipped(continuation(utility, earn_prob, support_start))
+    expected = carried + DISCOUNT * continuation(adjusted, earn_prob, support_start)
     moved = along_lanes(expected, illiquid_map)
     adjusted = along_lanes(flipped(moved), liquid_map)
     return utility + DISCOUNT * adjusted

time: 175 us -> 186 us (1.063)
  the two profiles are of different devices: /device:TPU:34 before, /device:TPU:1 now
where the time goes in v5:
time: 186 us; the launch traced here: 185 us
  starting transfers between devices  53.2 us (29%)
  matrix products  37.7 us (20%)
  blocking collectives  37.2 us (20%)
  waiting for transfers between devices  32.8 us (18%)
  local copies, waits for them, and re-layouts  12.1 us (7%)
  Pallas kernels  9.24 us (5%)
  other arithmetic  2.2 us (1%)
    all_to_all x1, blocking collectives, flipped(): got = lax.all_to_all(flat, 'asset', 0, 0, tiled=True)  37.2 us
    ppermute x15, starting transfers between devices, moved(): return lax.ppermute(value, axes, pairs)  33.2 us
    ppermute x15, waiting for transfers between devices, moved(): return lax.ppermute(value, axes, pairs)  32.8 us
    dot_general x4, matrix products, along_lanes(): jnp.einsum('terc,ecn->tern', stacked, matrix, precision=lax.Precision.HIGH)  31.2 us
    all_to_all x2, starting transfers between devices, flipped(): got = lax.all_to_all(flat, 'asset', 0, 0, tiled=True)  20 us
    pallas_call x3, Pallas kernels, regroup(): pl.pallas_call(_gather_kernel, in_specs=[pl.BlockSpec(memory_space=pltpu....  9.24 us
    dot_general x3, matrix products, continuation(): return jnp.einsum('ij,tjxy->tixy', mixing, padded, precision=PRECISE)  6.46 us
  transfers between devices with their start and end apart: 17, of which 6 were waited for; matrix products, arithmetic and copies ran while one was open for 9% of the time, Pallas kernels for 3%

profile of v5, /device:TPU:1, one launch (start us, length us, event | category | flops | bytes accessed | tf_op | source)
XLA Modules:
  0.0 185.5 jit_solution(5372463144091605645)
XLA Ops:
  0.0 2.1 %fusion.100 = (f32[1,4,32,512]{3,2,1,0:T(8,128)}, f32[1,4,32,512]{3,2,1,0:T(8,128)S(1)}, f32[1,4,32,512]{3,2,1,0:T(8,128)S(1)}, f32[1,4,32,512]{3,2,1,0:T(8,128)S(1)}) fusion(f32[2,8,32,512]{3,2,1,0:T(8,128)} %param.8), kind=kLoop, calls=%fused_computation.130 | loop fusion | bytes 2097152 | tf_op jit(solution)/shard_map/slice | solution.py:48
  2.1 3.9 %collective-permute-start.5 = (f32[1,4,32,512]{3,2,1,0:T(8,128)}, f32[1,4,32,512]{3,2,1,0:T(8,128)S(1)}, u32[]{:S(2)}, u32[]{:S(2)}) collective-permute-start(f32[1,4,32,512]{3,2,1,0:T(8,128)} %get-tuple-element.17), channel_id=1, source_target_pairs={{0,4},{1,5},{2,6},{3,7},{4,8},{5,9},{6,10},{7,11},{8,12},{9,13},{1... | collective-permute-start | bytes 786440 | tf_op jit(solution)/shard_map/ppermute | solution.py:43
  7.4 5.1 %collective-permute-start.7 = (f32[1,4,32,512]{3,2,1,0:T(8,128)S(1)}, f32[1,4,32,512]{3,2,1,0:T(8,128)S(1)}, u32[]{:S(2)}, u32[]{:S(2)}) collective-permute-start(f32[1,4,32,512]{3,2,1,0:T(8,128)S(1)} %get-tuple-element.18), channel_id=1, source_target_pairs={{1,4},{2,5},{3,6},{5,8},{6,9},{7,10},{9,12},{10,13},{11,14},{17,20... | collective-permute-start | bytes 786440 | tf_op jit(solution)/shard_map/ppermute | solution.py:43
  13.9 1.9 %collective-permute-start.8 = (f32[1,8,32,512]{3,2,1,0:T(8,128)S(1)}, f32[1,8,32,512]{3,2,1,0:T(8,128)S(1)}, u32[]{:S(2)}, u32[]{:S(2)}) collective-permute-start(f32[1,8,32,512]{3,2,1,0:T(8,128)S(1)} %get-tuple-element.22), channel_id=1, source_target_pairs={{1,0},{2,1},{3,2},{5,4},{6,5},{7,6},{9,8},{10,9},{11,10},{13,12},{... | collective-permute-start | bytes 1572872 | tf_op jit(solution)/shard_map/ppermute | solution.py:43
  16.6 2.0 %collective-permute-done.7 = f32[1,4,32,512]{3,2,1,0:T(8,128)S(1)} collective-permute-done((f32[1,4,32,512]{3,2,1,0:T(8,128)S(1)}, f32[1,4,32,512]{3,2,1,0:T(8,128)S(1)}, u32[]{:S(2)}, u32[]{:S(2)}) %collective-permute-start.7) | collective-permute-done | bytes 262176 | tf_op jit(solution)/shard_map/ppermute | solution.py:43
  18.6 2.6 %collective-permute-done.9 = f32[1,4,32,512]{3,2,1,0:T(8,128)S(1)} collective-permute-done((f32[1,4,32,512]{3,2,1,0:T(8,128)S(1)}, f32[1,4,32,512]{3,2,1,0:T(8,128)S(1)}, u32[]{:S(2)}, u32[]{:S(2)}) %collective-permute-start.9) | collective-permute-done | bytes 262176 | tf_op jit(solution)/shard_map/ppermute | solution.py:43
  21.2 3.2 %collective-permute-done.8 = f32[1,8,32,512]{3,2,1,0:T(8,128)S(1)} collective-permute-done((f32[1,8,32,512]{3,2,1,0:T(8,128)S(1)}, f32[1,8,32,512]{3,2,1,0:T(8,128)S(1)}, u32[]{:S(2)}, u32[]{:S(2)}) %collective-permute-start.8) | collective-permute-done | bytes 524320 | tf_op jit(solution)/shard_map/ppermute | solution.py:43
  25.1 2.4 %fusion.58 = f32[2,32,512,8]{2,3,1,0:T(8,128)S(1)} fusion(f32[2,16,32,512]{3,2,1,0:T(8,128)S(1)} %maximum_maximum_fusion, f32[8]{0:T(128)S(1)} %copy-done.41, s32[8]{0:T(128)S(1)} %get-tuple-element.45, f32[8]{0:T(128)S(1)} %copy-done.43, s32[8]{0:T(128)S(1)} %get-tuple-element.46, f32[8]{0:T(128)S(1)} %copy-done.45, s32[8]{0:T(128)S(1)} %get-tuple-element.43, ...), kind=kOutput, calls=%fused_computation.70 | convolution fusion | flops 50333440 | bytes 3146048 | tf_op jit(solution)/shard_map/ij,tjxy->tixy/dot_general | solution.py:69
  27.5 7.5 %fusion.69 = f32[2,8,32,512]{3,2,0,1:T(8,128)S(1)} fusion(f32[8,512]{1,0:T(8,128)S(1)} %get-tuple-element.29, s32[8,512]{1,0:T(8,128)S(1)} %get-tuple-element.35, f32[8,512]{1,0:T(8,128)S(1)} %get-tuple-element.30, s32[8,512]{1,0:T(8,128)S(1)} %get-tuple-element.36, f32[8,512]{1,0:T(8,128)S(1)} %get-tuple-element.28, s32[8,512]{1,0:T(8,128)S(1)} %get-tuple-element.34, ...), kind=kOutput, calls=%fused_computation.75 | convolution fusion | flops 828375040 | bytes 2228224 | tf_op jit(solution)/shard_map/terc,ecn->tern/dot_general | solution.py:73
  36.5 10.9 %all-to-all-start.1 = ((f32[16,32,512]{2,1,0:T(8,128)}), f32[16,32,512]{2,1,0:T(8,128)S(1)}, u32[]{:S(2)}, u32[]{:S(2)}) async-start(f32[16,32,512]{2,1,0:T(8,128)} %bitcast.31), calls=%async_computation.1 | async-start | bytes 2097152 | tf_op jit(solution)/shard_map/all_to_all | solution.py:113
  50.1 4.6 %collective-permute-start = (f32[1,4,32,512]{3,1,2,0:T(4,128)S(1)}, f32[1,4,32,512]{3,1,2,0:T(4,128)S(1)}, u32[]{:S(2)}, u32[]{:S(2)}) collective-permute-start(f32[1,4,32,512]{3,1,2,0:T(4,128)S(1)} %copy.44), channel_id=1, source_target_pairs={{0,4},{1,5},{2,6},{3,7},{4,8},{5,9},{6,10},{7,11},{8,12},{9,13},{1... | collective-permute-start | bytes 786440 | tf_op jit(solution)/shard_map/ppermute | solution.py:43
  59.7 2.6 %collective-permute-done.1 = f32[1,4,32,512]{3,1,2,0:T(4,128)S(1)} collective-permute-done((f32[1,4,32,512]{3,1,2,0:T(4,128)S(1)}, f32[1,4,32,512]{3,1,2,0:T(4,128)S(1)}, u32[]{:S(2)}, u32[]{:S(2)}) %collective-permute-start.1) | collective-permute-done | bytes 262176 | tf_op jit(solution)/shard_map/ppermute | solution.py:43
  62.2 16.3 %collective-permute-done.4 = f32[1,4,32,512]{3,1,2,0:T(4,128)S(1)} collective-permute-done((f32[1,4,32,512]{3,1,2,0:T(4,128)S(1)}, f32[1,4,32,512]{3,1,2,0:T(4,128)S(1)}, u32[]{:S(2)}, u32[]{:S(2)}) %collective-permute-start.4) | collective-permute-done | bytes 262176 | tf_op jit(solution)/shard_map/ppermute | solution.py:43
  82.1 9.1 %all-to-all-start = ((f32[16,32,512]{2,1,0:T(8,128)}), f32[16,32,512]{2,1,0:T(8,128)S(1)}, u32[]{:S(2)}, u32[]{:S(2)}) async-start(f32[16,32,512]{2,1,0:T(8,128)} %bitcast.22), calls=%async_computation | async-start | bytes 2097152 | tf_op jit(solution)/shard_map/all_to_all | solution.py:113
  91.3 3.1 %shard_map.83 = f32[16,32,512]{2,1,0:T(8,128)} custom-call(f32[16,32,512]{2,1,0:T(8,128)} %copy-done.2), custom_call_target="tpu_custom_call" | custom-call | bytes 2097152 | tf_op jit(solution)/shard_map/pallas_call | solution.py:99
  94.4 8.0 %fusion.63 = f32[2,8,32,512]{3,2,0,1:T(8,128)S(1)} fusion(f32[8,512]{1,0:T(8,128)S(1)} %get-tuple-element.25, s32[8,512]{1,0:T(8,128)S(1)} %get-tuple-element.32, f32[8,512]{1,0:T(8,128)S(1)} %get-tuple-element.26, s32[8,512]{1,0:T(8,128)S(1)} %get-tuple-element.33, f32[8,512]{1,0:T(8,128)S(1)} %get-tuple-element.24, s32[8,512]{1,0:T(8,128)S(1)} %get-tuple-element.31, ...), kind=kOutput, calls=%fused_computation.73 | convolution fusion | flops 828375040 | bytes 2228224 | tf_op jit(solution)/shard_map/terc,ecn->tern/dot_general | solution.py:73
  106.3 3.1 %collective-permute-start.10 = (f32[1,4,32,512]{3,2,0,1:T(8,128)}, f32[1,4,32,512]{3,2,0,1:T(8,128)S(1)}, u32[]{:S(2)}, u32[]{:S(2)}) collective-permute-start(f32[1,4,32,512]{3,2,0,1:T(8,128)} %get-tuple-element.11), channel_id=1, source_target_pairs={{0,4},{1,5},{2,6},{3,7},{4,8},{5,9},{6,10},{7,11},{8,12},{9,13},{1... | collective-permute-start | bytes 786440 | tf_op jit(solution)/shard_map/ppermute | solution.py:43
  114.5 3.1 %shard_map.82 = f32[16,32,512]{2,1,0:T(8,128)} custom-call(f32[16,32,512]{2,1,0:T(8,128)} %copy-done.3), custom_call_target="tpu_custom_call" | custom-call | bytes 2097152 | tf_op jit(solution)/shard_map/pallas_call | solution.py:99
  117.6 6.2 %collective-permute-done.14 = f32[1,4,32,512]{3,2,0,1:T(8,128)S(1)} collective-permute-done((f32[1,4,32,512]{3,2,0,1:T(8,128)S(1)}, f32[1,4,32,512]{3,2,0,1:T(8,128)S(1)}, u32[]{:S(2)}, u32[]{:S(2)}) %collective-permute-start.14) | collective-permute-done | bytes 262176 | tf_op jit(solution)/shard_map/ppermute | solution.py:43
  125.4 2.4 %fusion.56 = f32[2,32,512,8]{2,3,1,0:T(8,128)S(1)} fusion(f32[2,16,32,512]{3,2,0,1:T(8,128)S(1)} %maximum_maximum_fusion.1, f32[8]{0:T(128)S(1)} %copy-done.42, s32[8]{0:T(128)S(1)} %copy-done.35, f32[8]{0:T(128)S(1)} %copy-done.44, s32[8]{0:T(128)S(1)} %copy-done.38, f32[8]{0:T(128)S(1)} %copy-done.46, s32[8]{0:T(128)S(1)} %copy-done.29, ...), kind=kOutput, calls=%fused_computation.68 | convolution fusion | flops 50333440 | bytes 3146048 | tf_op jit(solution)/shard_map/ij,tjxy->tixy/dot_general | solution.py:69
  127.9 7.6 %fusion.66 = f32[2,8,32,512]{3,2,0,1:T(8,128)S(1)} fusion(f32[8,512]{1,0:T(8,128)S(1)} %copy-done.20, s32[8,512]{1,0:T(8,128)S(1)} %get-tuple-element.32, f32[8,512]{1,0:T(8,128)S(1)} %copy-done.22, s32[8,512]{1,0:T(8,128)S(1)} %get-tuple-element.33, f32[8,512]{1,0:T(8,128)S(1)} %copy-done.18, s32[8,512]{1,0:T(8,128)S(1)} %get-tuple-element.31, ...), kind=kOutput, calls=%fused_computation.74 | convolution fusion | flops 828899328 | bytes 3276800 | tf_op jit(solution)/shard_map/terc,ecn->tern/dot_general | solution.py:73
  136.0 37.2 %all_to_all.15.src_ref = f32[16,32,512]{2,1,0:T(8,128)} all-to-all(f32[16,32,512]{2,1,0:T(8,128)S(1)} %bitcast.97), channel_id=1, replica_groups=mesh['asset'=16,'earn'=4,'age'=4] {'asset'}, dimensions={0} | all-to-all | bytes 2097152 | tf_op jit(solution)/shard_map/all_to_all | solution.py:113
  173.2 3.1 %shard_map.84 = f32[16,32,512]{2,1,0:T(8,128)} custom-call(f32[16,32,512]{2,1,0:T(8,128)} %all_to_all.15.src_ref), custom_call_target="tpu_custom_call" | custom-call | bytes 2097152 | tf_op jit(solution)/shard_map/pallas_call | solution.py:99
  176.3 8.1 %fusion.78 = f32[2,8,32,512]{3,2,0,1:T(8,128)S(1)} fusion(f32[8,512]{1,0:T(8,128)S(1)} %copy-done.12, s32[8,512]{1,0:T(8,128)S(1)} %get-tuple-element.35, f32[8,512]{1,0:T(8,128)S(1)} %copy-done.14, s32[8,512]{1,0:T(8,128)S(1)} %get-tuple-element.36, f32[8,512]{1,0:T(8,128)S(1)} %copy-done.10, s32[8,512]{1,0:T(8,128)S(1)} %get-tuple-element.34, ...), kind=kOutput, calls=%fused_computation.78 | convolution fusion | flops 828899328 | bytes 3276800 | tf_op jit(solution)/shard_map/terc,ecn->tern/dot_general | solution.py:73
  (149 shorter events, 28.4 us)
Async XLA Ops:
  2.1 14.5 %collective-permute-start.5 = (f32[1,4,32,512]{3,2,1,0:T(8,128)}, f32[1,4,32,512]{3,2,1,0:T(8,128)S(1)}, u32[]{:S(2)}, u32[]{:S(2)}) collective-permute-start(f32[1,4,32,512]{3,2,1,0:T(8,128)} %get-tuple-element.17), channel_id=1, source_target_pairs={{0,4},{1,5},{2,6},{3,7},{4,8},{5,9},{6,10},{7,11},{8,12},{9,13},{1... | collective-permute-start | bytes 786440 | tf_op jit(solution)/shard_map/ppermute | solution.py:43
  6.1 10.6 %collective-permute-start.6 = (f32[1,4,32,512]{3,2,1,0:T(8,128)S(1)}, f32[1,4,32,512]{3,2,1,0:T(8,128)S(1)}, u32[]{:S(2)}, u32[]{:S(2)}) collective-permute-start(f32[1,4,32,512]{3,2,1,0:T(8,128)S(1)} %get-tuple-element.19), channel_id=1, source_target_pairs={{4,0},{5,1},{6,2},{7,3},{8,4},{9,5},{10,6},{11,7},{12,8},{13,9},{1... | collective-permute-start | bytes 786440 | tf_op jit(solution)/shard_map/ppermute | solution.py:43
  7.4 11.2 %collective-permute-start.7 = (f32[1,4,32,512]{3,2,1,0:T(8,128)S(1)}, f32[1,4,32,512]{3,2,1,0:T(8,128)S(1)}, u32[]{:S(2)}, u32[]{:S(2)}) collective-permute-start(f32[1,4,32,512]{3,2,1,0:T(8,128)S(1)} %get-tuple-element.18), channel_id=1, source_target_pairs={{1,4},{2,5},{3,6},{5,8},{6,9},{7,10},{9,12},{10,13},{11,14},{17,20... | collective-permute-start | bytes 786440 | tf_op jit(solution)/shard_map/ppermute | solution.py:43
  12.5 8.7 %collective-permute-start.9 = (f32[1,4,32,512]{3,2,1,0:T(8,128)S(1)}, f32[1,4,32,512]{3,2,1,0:T(8,128)S(1)}, u32[]{:S(2)}, u32[]{:S(2)}) collective-permute-start(f32[1,4,32,512]{3,2,1,0:T(8,128)S(1)} %get-tuple-element.20), channel_id=1, source_target_pairs={{5,0},{6,1},{7,2},{9,4},{10,5},{11,6},{13,8},{14,9},{15,10},{21,16... | collective-permute-start | bytes 786440 | tf_op jit(solution)/shard_map/ppermute | solution.py:43
  13.9 10.5 %collective-permute-start.8 = (f32[1,8,32,512]{3,2,1,0:T(8,128)S(1)}, f32[1,8,32,512]{3,2,1,0:T(8,128)S(1)}, u32[]{:S(2)}, u32[]{:S(2)}) collective-permute-start(f32[1,8,32,512]{3,2,1,0:T(8,128)S(1)} %get-tuple-element.22), channel_id=1, source_target_pairs={{1,0},{2,1},{3,2},{5,4},{6,5},{7,6},{9,8},{10,9},{11,10},{13,12},{... | collective-permute-start | bytes 1572872 | tf_op jit(solution)/shard_map/ppermute | solution.py:43
  36.5 45.7 %all-to-all-start.1 = ((f32[16,32,512]{2,1,0:T(8,128)}), f32[16,32,512]{2,1,0:T(8,128)S(1)}, u32[]{:S(2)}, u32[]{:S(2)}) async-start(f32[16,32,512]{2,1,0:T(8,128)} %bitcast.31), calls=%async_computation.1 | async-start | bytes 2097152 | tf_op jit(solution)/shard_map/all_to_all | solution.py:113
  47.8 30.7 %collective-permute-start.3 = (f32[1,8,32,512]{3,1,2,0:T(8,128)S(1)}, f32[1,8,32,512]{3,1,2,0:T(8,128)S(1)}, u32[]{:S(2)}, u32[]{:S(2)}) collective-permute-start(f32[1,8,32,512]{3,1,2,0:T(8,128)S(1)} %copy.48), channel_id=1, source_target_pairs={{1,0},{2,1},{3,2},{5,4},{6,5},{7,6},{9,8},{10,9},{11,10},{13,12},{... | collective-permute-start | bytes 1572872 | tf_op jit(solution)/shard_map/ppermute | solution.py:43
  50.1 9.6 %collective-permute-start = (f32[1,4,32,512]{3,1,2,0:T(4,128)S(1)}, f32[1,4,32,512]{3,1,2,0:T(4,128)S(1)}, u32[]{:S(2)}, u32[]{:S(2)}) collective-permute-start(f32[1,4,32,512]{3,1,2,0:T(4,128)S(1)} %copy.44), channel_id=1, source_target_pairs={{0,4},{1,5},{2,6},{3,7},{4,8},{5,9},{6,10},{7,11},{8,12},{9,13},{1... | collective-permute-start | bytes 786440 | tf_op jit(solution)/shard_map/ppermute | solution.py:43
  54.8 7.4 %collective-permute-start.1 = (f32[1,4,32,512]{3,1,2,0:T(4,128)S(1)}, f32[1,4,32,512]{3,1,2,0:T(4,128)S(1)}, u32[]{:S(2)}, u32[]{:S(2)}) collective-permute-start(f32[1,4,32,512]{3,1,2,0:T(4,128)S(1)} %copy.46), channel_id=1, source_target_pairs={{4,0},{5,1},{6,2},{7,3},{8,4},{9,5},{10,6},{11,7},{12,8},{13,9},{1... | collective-permute-start | bytes 786440 | tf_op jit(solution)/shard_map/ppermute | solution.py:43
  56.3 5.9 %collective-permute-start.2 = (f32[1,4,32,512]{3,1,2,0:T(4,128)S(1)}, f32[1,4,32,512]{3,1,2,0:T(4,128)S(1)}, u32[]{:S(2)}, u32[]{:S(2)}) collective-permute-start(f32[1,4,32,512]{3,1,2,0:T(4,128)S(1)} %copy.47), channel_id=1, source_target_pairs={{1,4},{2,5},{3,6},{5,8},{6,9},{7,10},{9,12},{10,13},{11,14},{17,20... | collective-permute-start | bytes 786440 | tf_op jit(solution)/shard_map/ppermute | solution.py:43
  57.8 20.7 %collective-permute-start.4 = (f32[1,4,32,512]{3,1,2,0:T(4,128)S(1)}, f32[1,4,32,512]{3,1,2,0:T(4,128)S(1)}, u32[]{:S(2)}, u32[]{:S(2)}) collective-permute-start(f32[1,4,32,512]{3,1,2,0:T(4,128)S(1)} %copy.49), channel_id=1, source_target_pairs={{5,0},{6,1},{7,2},{9,4},{10,5},{11,6},{13,8},{14,9},{15,10},{21,16... | collective-permute-start | bytes 786440 | tf_op jit(solution)/shard_map/ppermute | solution.py:43
  59.6 34.8 %copy-start.15 = (f32[8,512]{1,0:T(8,128)}, f32[8,512]{1,0:T(8,128)S(1)}, u32[]{:S(2)}) copy-start(f32[8,512]{1,0:T(8,128)S(1)} %get-tuple-element.23) | copy-start | bytes 49156
  59.6 34.7 %copy-start.17 = (f32[8,512]{1,0:T(8,128)}, f32[8,512]{1,0:T(8,128)S(1)}, u32[]{:S(2)}) copy-start(f32[8,512]{1,0:T(8,128)S(1)} %get-tuple-element.24) | copy-start | bytes 49156
  59.6 34.7 %copy-start.19 = (f32[8,512]{1,0:T(8,128)}, f32[8,512]{1,0:T(8,128)S(1)}, u32[]{:S(2)}) copy-start(f32[8,512]{1,0:T(8,128)S(1)} %get-tuple-element.25) | copy-start | bytes 49156
  59.6 34.7 %copy-start.21 = (f32[8,512]{1,0:T(8,128)}, f32[8,512]{1,0:T(8,128)S(1)}, u32[]{:S(2)}) copy-start(f32[8,512]{1,0:T(8,128)S(1)} %get-tuple-element.26) | copy-start | bytes 49156
  82.1 31.4 %all-to-all-start = ((f32[16,32,512]{2,1,0:T(8,128)}), f32[16,32,512]{2,1,0:T(8,128)S(1)}, u32[]{:S(2)}, u32[]{:S(2)}) async-start(f32[16,32,512]{2,1,0:T(8,128)} %bitcast.22), calls=%async_computation | async-start | bytes 2097152 | tf_op jit(solution)/shard_map/all_to_all | solution.py:113
  103.5 20.3 %collective-permute-start.13 = (f32[1,8,32,512]{3,2,0,1:T(8,128)}, f32[1,8,32,512]{3,2,0,1:T(8,128)}, u32[]{:S(2)}, u32[]{:S(2)}) collective-permute-start(f32[1,8,32,512]{3,2,0,1:T(8,128)} %get-tuple-element.16), channel_id=1, source_target_pairs={{1,0},{2,1},{3,2},{5,4},{6,5},{7,6},{9,8},{10,9},{11,10},{13,12},{... | collective-permute-start | bytes 1572872 | tf_op jit(solution)/shard_map/ppermute | solution.py:43
  106.3 11.3 %collective-permute-start.10 = (f32[1,4,32,512]{3,2,0,1:T(8,128)}, f32[1,4,32,512]{3,2,0,1:T(8,128)S(1)}, u32[]{:S(2)}, u32[]{:S(2)}) collective-permute-start(f32[1,4,32,512]{3,2,0,1:T(8,128)} %get-tuple-element.11), channel_id=1, source_target_pairs={{0,4},{1,5},{2,6},{3,7},{4,8},{5,9},{6,10},{7,11},{8,12},{9,13},{1... | collective-permute-start | bytes 786440 | tf_op jit(solution)/shard_map/ppermute | solution.py:43
  109.4 8.2 %collective-permute-start.11 = (f32[1,4,32,512]{3,2,0,1:T(8,128)}, f32[1,4,32,512]{3,2,0,1:T(8,128)S(1)}, u32[]{:S(2)}, u32[]{:S(2)}) collective-permute-start(f32[1,4,32,512]{3,2,0,1:T(8,128)} %get-tuple-element.14), channel_id=1, source_target_pairs={{4,0},{5,1},{6,2},{7,3},{8,4},{9,5},{10,6},{11,7},{12,8},{13,9},{1... | collective-permute-start | bytes 786440 | tf_op jit(solution)/shard_map/ppermute | solution.py:43
  110.7 6.9 %collective-permute-start.12 = (f32[1,4,32,512]{3,2,0,1:T(8,128)}, f32[1,4,32,512]{3,2,0,1:T(8,128)S(1)}, u32[]{:S(2)}, u32[]{:S(2)}) collective-permute-start(f32[1,4,32,512]{3,2,0,1:T(8,128)} %get-tuple-element.13), channel_id=1, source_target_pairs={{1,4},{2,5},{3,6},{5,8},{6,9},{7,10},{9,12},{10,13},{11,14},{17,20... | collective-permute-start | bytes 786440 | tf_op jit(solution)/shard_map/ppermute | solution.py:43
  112.0 11.8 %collective-permute-start.14 = (f32[1,4,32,512]{3,2,0,1:T(8,128)S(1)}, f32[1,4,32,512]{3,2,0,1:T(8,128)S(1)}, u32[]{:S(2)}, u32[]{:S(2)}) collective-permute-start(f32[1,4,32,512]{3,2,0,1:T(8,128)S(1)} %get-tuple-element.12), channel_id=1, source_target_pairs={{5,0},{6,1},{7,2},{9,4},{10,5},{11,6},{13,8},{14,9},{15,10},{21,16... | collective-permute-start | bytes 786440 | tf_op jit(solution)/shard_map/ppermute | solution.py:43
  136.0 40.3 %copy-start.10 = (f32[8,512]{1,0:T(8,128)S(1)}, f32[8,512]{1,0:T(8,128)}, u32[]{:S(2)}) copy-start(f32[8,512]{1,0:T(8,128)} %copy-done.9) | copy-start | bytes 49156
  136.0 40.3 %copy-start.12 = (f32[8,512]{1,0:T(8,128)S(1)}, f32[8,512]{1,0:T(8,128)}, u32[]{:S(2)}) copy-start(f32[8,512]{1,0:T(8,128)} %copy-done.11) | copy-start | bytes 49156
  136.0 40.3 %copy-start.14 = (f32[8,512]{1,0:T(8,128)S(1)}, f32[8,512]{1,0:T(8,128)}, u32[]{:S(2)}) copy-start(f32[8,512]{1,0:T(8,128)} %copy-done.13) | copy-start | bytes 49156
  (43 other events, 368.1 us)

commit v6 on v4

--- a/solution.py
+++ b/solution.py
@@ -66,7 +66,7 @@
         mixing = mixing + jnp.where(
             slots[None, :] == target[:, None], (earn_prob[number] / prob_sum)[:, None], 0.0
         )
-    return jnp.einsum("ij,tjxy->tixy", mixing, padded, precision=PRECISE)
+    return jnp.einsum("ij,tjxy->tixy", mixing, padded, precision=lax.Precision.HIGH)
 
 
 def along_lanes(stacked, matrix):

time: 175 us -> 175 us (level)
  transfers between devices with their start and end apart: 12 -> 12, of which waited for: 5 -> 5; matrix products, arithmetic and copies ran while one was open for 9% -> 8% of each run, Pallas kernels for 2% -> 2%
where the time goes in v6:
time: 175 us; the launch traced here: 174 us
  waiting for transfers between devices  43.3 us (25%)
  starting transfers between devices  42.7 us (24%)
  matrix products  34.7 us (20%)
  blocking collectives  32.4 us (19%)
  Pallas kernels  9.25 us (5%)
  local copies, waits for them, and re-layouts  8.28 us (5%)
  other arithmetic  2.37 us (1%)
    all_to_all x2, waiting for transfers between devices, flipped(): got = lax.all_to_all(flat, 'asset', 0, 0, tiled=True)  36.4 us
    all_to_all x1, blocking collectives, flipped(): got = lax.all_to_all(flat, 'asset', 0, 0, tiled=True)  32.4 us
    dot_general x4, matrix products, along_lanes(): jnp.einsum('terc,ecn->tern', stacked, matrix, precision=lax.Precision.HIGH)  31.2 us
    ppermute x10, starting transfers between devices, moved(): return lax.ppermute(value, axes, pairs)  25.2 us
    all_to_all x2, starting transfers between devices, flipped(): got = lax.all_to_all(flat, 'asset', 0, 0, tiled=True)  17.5 us
    pallas_call x3, Pallas kernels, regroup(): pl.pallas_call(_gather_kernel, in_specs=[pl.BlockSpec(memory_space=pltpu....  9.25 us
    ppermute x10, waiting for transfers between devices, moved(): return lax.ppermute(value, axes, pairs)  6.89 us
    dot_general x2, matrix products, continuation(): jnp.einsum('ij,tjxy->tixy', mixing, padded, precision=lax.Precision.HIGH)  3.56 us
  transfers between devices with their start and end apart: 12, of which 5 were waited for; matrix products, arithmetic and copies ran while one was open for 8% of the time, Pallas kernels for 2%

profile of v6, /device:TPU:34, one launch (start us, length us, event | category | flops | bytes accessed | tf_op | source)
XLA Modules:
  0.0 173.6 jit_solution(11133227889894990002)
XLA Ops:
  0.0 2.3 %fusion.110 = (f32[1,4,32,512]{3,2,1,0:T(8,128)}, f32[1,4,32,512]{3,2,1,0:T(8,128)}, f32[1,4,32,512]{3,2,1,0:T(8,128)}, f32[1,4,32,512]{3,2,1,0:T(8,128)}) fusion(f32[2,8,32,512]{3,2,1,0:T(8,128)} %param.8), kind=kLoop, calls=%fused_computation.136 | loop fusion | bytes 2097152 | tf_op jit(solution)/shard_map/slice | solution.py:48
  2.3 3.4 %collective-permute-start = (f32[1,4,32,512]{3,2,1,0:T(8,128)}, f32[1,4,32,512]{3,2,1,0:T(8,128)S(1)}, u32[]{:S(2)}, u32[]{:S(2)}) collective-permute-start(f32[1,4,32,512]{3,2,1,0:T(8,128)} %get-tuple-element.11), channel_id=1, source_target_pairs={{0,4},{1,5},{2,6},{3,7},{4,8},{5,9},{6,10},{7,11},{8,12},{9,13},{1... | collective-permute-start | bytes 786440 | tf_op jit(solution)/shard_map/ppermute | solution.py:43
  5.7 2.5 %collective-permute-start.1 = (f32[1,4,32,512]{3,2,1,0:T(8,128)}, f32[1,4,32,512]{3,2,1,0:T(8,128)}, u32[]{:S(2)}, u32[]{:S(2)}) collective-permute-start(f32[1,4,32,512]{3,2,1,0:T(8,128)} %get-tuple-element.13), channel_id=1, source_target_pairs={{4,0},{5,1},{6,2},{7,3},{8,4},{9,5},{10,6},{11,7},{12,8},{13,9},{1... | collective-permute-start | bytes 786440 | tf_op jit(solution)/shard_map/ppermute | solution.py:43
  8.2 1.9 %collective-permute-start.2 = (f32[1,4,32,512]{3,2,1,0:T(8,128)}, f32[1,4,32,512]{3,2,1,0:T(8,128)}, u32[]{:S(2)}, u32[]{:S(2)}) collective-permute-start(f32[1,4,32,512]{3,2,1,0:T(8,128)} %get-tuple-element.12), channel_id=1, source_target_pairs={{1,4},{2,5},{3,6},{5,8},{6,9},{7,10},{9,12},{10,13},{11,14},{17,20... | collective-permute-start | bytes 786440 | tf_op jit(solution)/shard_map/ppermute | solution.py:43
  10.1 3.9 %collective-permute-start.4 = (f32[1,4,32,512]{3,2,1,0:T(8,128)}, f32[1,4,32,512]{3,2,1,0:T(8,128)}, u32[]{:S(2)}, u32[]{:S(2)}) collective-permute-start(f32[1,4,32,512]{3,2,1,0:T(8,128)} %get-tuple-element.14), channel_id=1, source_target_pairs={{5,0},{6,1},{7,2},{9,4},{10,5},{11,6},{13,8},{14,9},{15,10},{21,16... | collective-permute-start | bytes 786440 | tf_op jit(solution)/shard_map/ppermute | solution.py:43
  14.1 1.9 %collective-permute-start.3 = (f32[1,8,32,512]{3,2,1,0:T(8,128)S(1)}, f32[1,8,32,512]{3,2,1,0:T(8,128)}, u32[]{:S(2)}, u32[]{:S(2)}) collective-permute-start(f32[1,8,32,512]{3,2,1,0:T(8,128)S(1)} %get-tuple-element.16), channel_id=1, source_target_pairs={{1,0},{2,1},{3,2},{5,4},{6,5},{7,6},{9,8},{10,9},{11,10},{13,12},{... | collective-permute-start | bytes 1572872 | tf_op jit(solution)/shard_map/ppermute | solution.py:43
  17.4 11.2 %all-to-all-start = ((f32[16,32,512]{2,1,0:T(8,128)}), f32[16,32,512]{2,1,0:T(8,128)S(1)}, u32[]{:S(2)}, u32[]{:S(2)}) async-start(f32[16,32,512]{2,1,0:T(8,128)} %bitcast.14), calls=%async_computation | async-start | bytes 2097152 | tf_op jit(solution)/shard_map/all_to_all | solution.py:113
  32.9 7.5 %fusion.51 = f32[2,8,32,512]{3,2,0,1:T(8,128)S(1)} fusion(f32[8,512]{1,0:T(8,128)S(1)} %get-tuple-element.23, s32[8,512]{1,0:T(8,128)S(1)} %get-tuple-element.29, f32[8,512]{1,0:T(8,128)S(1)} %get-tuple-element.24, s32[8,512]{1,0:T(8,128)S(1)} %get-tuple-element.30, f32[8,512]{1,0:T(8,128)S(1)} %get-tuple-element.22, s32[8,512]{1,0:T(8,128)S(1)} %get-tuple-element.28, ...), kind=kOutput, calls=%fused_computation.61 | convolution fusion | flops 828375040 | bytes 2228224 | tf_op jit(solution)/shard_map/terc,ecn->tern/dot_general | solution.py:73
  41.8 14.0 %all-to-all-done.src_ref = f32[16,32,512]{2,1,0:T(8,128)S(1)} async-done(((f32[16,32,512]{2,1,0:T(8,128)}), f32[16,32,512]{2,1,0:T(8,128)S(1)}, u32[]{:S(2)}, u32[]{:S(2)}) %all-to-all-start) | async-done | bytes 1048608 | tf_op jit(solution)/shard_map/all_to_all | solution.py:113
  55.8 6.3 %all-to-all-start.1 = ((f32[16,32,512]{2,1,0:T(8,128)}), f32[16,32,512]{2,1,0:T(8,128)S(1)}, u32[]{:S(2)}, u32[]{:S(2)}) async-start(f32[16,32,512]{2,1,0:T(8,128)} %bitcast.29), calls=%async_computation.1 | async-start | bytes 2097152 | tf_op jit(solution)/shard_map/all_to_all | solution.py:113
  62.1 3.1 %shard_map.82 = f32[16,32,512]{2,1,0:T(8,128)} custom-call(f32[16,32,512]{2,1,0:T(8,128)} %copy-done.1), custom_call_target="tpu_custom_call" | custom-call | bytes 2097152 | tf_op jit(solution)/shard_map/pallas_call | solution.py:99
  65.2 22.4 %all-to-all-done.1.src_ref = f32[16,32,512]{2,1,0:T(8,128)S(1)} async-done(((f32[16,32,512]{2,1,0:T(8,128)}), f32[16,32,512]{2,1,0:T(8,128)S(1)}, u32[]{:S(2)}, u32[]{:S(2)}) %all-to-all-start.1) | async-done | bytes 1048608 | tf_op jit(solution)/shard_map/all_to_all | solution.py:113
  88.7 3.1 %shard_map.83 = f32[16,32,512]{2,1,0:T(8,128)} custom-call(f32[16,32,512]{2,1,0:T(8,128)} %copy-done.2), custom_call_target="tpu_custom_call" | custom-call | bytes 2097152 | tf_op jit(solution)/shard_map/pallas_call | solution.py:99
  91.7 8.1 %fusion.69 = f32[2,8,32,512]{3,2,0,1:T(8,128)S(1)} fusion(f32[8,512]{1,0:T(8,128)S(1)} %get-tuple-element.19, s32[8,512]{1,0:T(8,128)S(1)} %get-tuple-element.26, f32[8,512]{1,0:T(8,128)S(1)} %get-tuple-element.20, s32[8,512]{1,0:T(8,128)S(1)} %get-tuple-element.27, f32[8,512]{1,0:T(8,128)S(1)} %get-tuple-element.18, s32[8,512]{1,0:T(8,128)S(1)} %get-tuple-element.25, ...), kind=kOutput, calls=%fused_computation.67 | convolution fusion | flops 828899328 | bytes 3276800 | tf_op jit(solution)/shard_map/terc,ecn->tern/dot_general | solution.py:73
  99.9 1.9 %collective-permute-start.8 = (f32[1,8,32,512]{3,2,0,1:T(8,128)S(1)}, f32[1,8,32,512]{3,2,0,1:T(8,128)S(1)}, u32[]{:S(2)}, u32[]{:S(2)}) collective-permute-start(f32[1,8,32,512]{3,2,0,1:T(8,128)S(1)} %get-tuple-element.10), channel_id=1, source_target_pairs={{1,0},{2,1},{3,2},{5,4},{6,5},{7,6},{9,8},{10,9},{11,10},{13,12},{... | collective-permute-start | bytes 1572872 | tf_op jit(solution)/shard_map/ppermute | solution.py:43
  101.9 2.8 %collective-permute-start.5 = (f32[1,4,32,512]{3,2,0,1:T(8,128)S(1)}, f32[1,4,32,512]{3,2,0,1:T(8,128)S(1)}, u32[]{:S(2)}, u32[]{:S(2)}) collective-permute-start(f32[1,4,32,512]{3,2,0,1:T(8,128)S(1)} %get-tuple-element.5), channel_id=1, source_target_pairs={{0,4},{1,5},{2,6},{3,7},{4,8},{5,9},{6,10},{7,11},{8,12},{9,13},{1... | collective-permute-start | bytes 786440 | tf_op jit(solution)/shard_map/ppermute | solution.py:43
  104.8 3.1 %collective-permute-start.6 = (f32[1,4,32,512]{3,2,0,1:T(8,128)S(1)}, f32[1,4,32,512]{3,2,0,1:T(8,128)S(1)}, u32[]{:S(2)}, u32[]{:S(2)}) collective-permute-start(f32[1,4,32,512]{3,2,0,1:T(8,128)S(1)} %get-tuple-element.8), channel_id=1, source_target_pairs={{4,0},{5,1},{6,2},{7,3},{8,4},{9,5},{10,6},{11,7},{12,8},{13,9},{1... | collective-permute-start | bytes 786440 | tf_op jit(solution)/shard_map/ppermute | solution.py:43
  107.8 1.9 %collective-permute-start.7 = (f32[1,4,32,512]{3,2,0,1:T(8,128)S(1)}, f32[1,4,32,512]{3,2,0,1:T(8,128)S(1)}, u32[]{:S(2)}, u32[]{:S(2)}) collective-permute-start(f32[1,4,32,512]{3,2,0,1:T(8,128)S(1)} %get-tuple-element.7), channel_id=1, source_target_pairs={{1,4},{2,5},{3,6},{5,8},{6,9},{7,10},{9,12},{10,13},{11,14},{17,20... | collective-permute-start | bytes 786440 | tf_op jit(solution)/shard_map/ppermute | solution.py:43
  112.6 3.6 %collective-permute-done.6 = f32[1,4,32,512]{3,2,0,1:T(8,128)S(1)} collective-permute-done((f32[1,4,32,512]{3,2,0,1:T(8,128)S(1)}, f32[1,4,32,512]{3,2,0,1:T(8,128)S(1)}, u32[]{:S(2)}, u32[]{:S(2)}) %collective-permute-start.6) | collective-permute-done | bytes 262176 | tf_op jit(solution)/shard_map/ppermute | solution.py:43
  116.2 2.4 %collective-permute-done.9 = f32[1,4,32,512]{3,2,0,1:T(8,128)S(1)} collective-permute-done((f32[1,4,32,512]{3,2,0,1:T(8,128)S(1)}, f32[1,4,32,512]{3,2,0,1:T(8,128)S(1)}, u32[]{:S(2)}, u32[]{:S(2)}) %collective-permute-start.9) | collective-permute-done | bytes 262176 | tf_op jit(solution)/shard_map/ppermute | solution.py:43
  121.0 7.5 %fusion.48 = f32[2,8,32,512]{3,2,0,1:T(8,128)S(1)} fusion(f32[8,512]{1,0:T(8,128)S(1)} %get-tuple-element.19, s32[8,512]{1,0:T(8,128)S(1)} %get-tuple-element.26, f32[8,512]{1,0:T(8,128)S(1)} %get-tuple-element.20, s32[8,512]{1,0:T(8,128)S(1)} %get-tuple-element.27, f32[8,512]{1,0:T(8,128)S(1)} %get-tuple-element.18, s32[8,512]{1,0:T(8,128)S(1)} %get-tuple-element.25, ...), kind=kOutput, calls=%fused_computation.60 | convolution fusion | flops 828375040 | bytes 2228224 | tf_op jit(solution)/shard_map/terc,ecn->tern/dot_general | solution.py:73
  129.0 32.4 %all_to_all.15.src_ref = f32[16,32,512]{2,1,0:T(8,128)} all-to-all(f32[16,32,512]{2,1,0:T(8,128)S(1)} %bitcast.98), channel_id=1, replica_groups=mesh['asset'=16,'earn'=4,'age'=4] {'asset'}, dimensions={0} | all-to-all | bytes 2097152 | tf_op jit(solution)/shard_map/all_to_all | solution.py:113
  161.4 3.1 %shard_map.84 = f32[16,32,512]{2,1,0:T(8,128)} custom-call(f32[16,32,512]{2,1,0:T(8,128)} %all_to_all.15.src_ref), custom_call_target="tpu_custom_call" | custom-call | bytes 2097152 | tf_op jit(solution)/shard_map/pallas_call | solution.py:99
  164.5 8.1 %fusion.66 = f32[2,8,32,512]{3,2,0,1:T(8,128)S(1)} fusion(f32[8,512]{1,0:T(8,128)S(1)} %copy-done.12, s32[8,512]{1,0:T(8,128)S(1)} %get-tuple-element.29, f32[8,512]{1,0:T(8,128)S(1)} %copy-done.14, s32[8,512]{1,0:T(8,128)S(1)} %get-tuple-element.30, f32[8,512]{1,0:T(8,128)S(1)} %copy-done.10, s32[8,512]{1,0:T(8,128)S(1)} %get-tuple-element.28, ...), kind=kOutput, calls=%fused_computation.66 | convolution fusion | flops 828899328 | bytes 3276800 | tf_op jit(solution)/shard_map/terc,ecn->tern/dot_general | solution.py:73
  (93 shorter events, 14.7 us)
Async XLA Ops:
  0.0 14.0 %copy-start = (f32[2,8,32,512]{3,2,1,0:T(8,128)S(1)}, f32[2,8,32,512]{3,2,1,0:T(8,128)}, u32[]{:S(2)}) copy-start(f32[2,8,32,512]{3,2,1,0:T(8,128)} %param.8) | copy-start | bytes 3145732
  0.0 16.0 %copy-start.3 = (f32[2,8,32,512]{3,2,1,0:T(8,128)S(1)}, f32[2,8,32,512]{3,2,1,0:T(8,128)}, u32[]{:S(2)}) copy-start(f32[2,8,32,512]{3,2,1,0:T(8,128)} %param.9) | copy-start | bytes 3145732
  2.3 27.1 %collective-permute-start = (f32[1,4,32,512]{3,2,1,0:T(8,128)}, f32[1,4,32,512]{3,2,1,0:T(8,128)S(1)}, u32[]{:S(2)}, u32[]{:S(2)}) collective-permute-start(f32[1,4,32,512]{3,2,1,0:T(8,128)} %get-tuple-element.11), channel_id=1, source_target_pairs={{0,4},{1,5},{2,6},{3,7},{4,8},{5,9},{6,10},{7,11},{8,12},{9,13},{1... | collective-permute-start | bytes 786440 | tf_op jit(solution)/shard_map/ppermute | solution.py:43
  5.7 23.7 %collective-permute-start.1 = (f32[1,4,32,512]{3,2,1,0:T(8,128)}, f32[1,4,32,512]{3,2,1,0:T(8,128)}, u32[]{:S(2)}, u32[]{:S(2)}) collective-permute-start(f32[1,4,32,512]{3,2,1,0:T(8,128)} %get-tuple-element.13), channel_id=1, source_target_pairs={{4,0},{5,1},{6,2},{7,3},{8,4},{9,5},{10,6},{11,7},{12,8},{13,9},{1... | collective-permute-start | bytes 786440 | tf_op jit(solution)/shard_map/ppermute | solution.py:43
  8.2 21.2 %collective-permute-start.2 = (f32[1,4,32,512]{3,2,1,0:T(8,128)}, f32[1,4,32,512]{3,2,1,0:T(8,128)}, u32[]{:S(2)}, u32[]{:S(2)}) collective-permute-start(f32[1,4,32,512]{3,2,1,0:T(8,128)} %get-tuple-element.12), channel_id=1, source_target_pairs={{1,4},{2,5},{3,6},{5,8},{6,9},{7,10},{9,12},{10,13},{11,14},{17,20... | collective-permute-start | bytes 786440 | tf_op jit(solution)/shard_map/ppermute | solution.py:43
  10.1 19.3 %collective-permute-start.4 = (f32[1,4,32,512]{3,2,1,0:T(8,128)}, f32[1,4,32,512]{3,2,1,0:T(8,128)}, u32[]{:S(2)}, u32[]{:S(2)}) collective-permute-start(f32[1,4,32,512]{3,2,1,0:T(8,128)} %get-tuple-element.14), channel_id=1, source_target_pairs={{5,0},{6,1},{7,2},{9,4},{10,5},{11,6},{13,8},{14,9},{15,10},{21,16... | collective-permute-start | bytes 786440 | tf_op jit(solution)/shard_map/ppermute | solution.py:43
  14.1 15.3 %collective-permute-start.3 = (f32[1,8,32,512]{3,2,1,0:T(8,128)S(1)}, f32[1,8,32,512]{3,2,1,0:T(8,128)}, u32[]{:S(2)}, u32[]{:S(2)}) collective-permute-start(f32[1,8,32,512]{3,2,1,0:T(8,128)S(1)} %get-tuple-element.16), channel_id=1, source_target_pairs={{1,0},{2,1},{3,2},{5,4},{6,5},{7,6},{9,8},{10,9},{11,10},{13,12},{... | collective-permute-start | bytes 1572872 | tf_op jit(solution)/shard_map/ppermute | solution.py:43
  16.1 12.6 %copy-start.8 = (s32[8,512]{1,0:T(8,128)S(1)}, s32[8,512]{1,0:T(8,128)}, u32[]{:S(2)}) copy-start(s32[8,512]{1,0:T(8,128)} %param.12) | copy-start | bytes 49156
  16.1 12.6 %copy-start.15 = (f32[5,8]{1,0:T(8,128)S(1)}, f32[5,8]{1,0:T(8,128)}, u32[]{:S(2)}) copy-start(f32[5,8]{1,0:T(8,128)} %param.10) | copy-start | bytes 484
  16.1 13.2 %copy-start.31 = (s32[8]{0:T(128)S(1)}, s32[8]{0:T(128)}, u32[]{:S(2)}) copy-start(s32[8]{0:T(128)} %param.11) | copy-start | bytes 100
  16.1 13.2 %copy-start.5 = (f32[4,8,512]{2,1,0:T(8,128)S(1)}, f32[4,8,512]{2,1,0:T(8,128)}, u32[]{:S(2)}) copy-start(f32[4,8,512]{2,1,0:T(8,128)} %param.13) | copy-start | bytes 196612
  17.4 38.4 %all-to-all-start = ((f32[16,32,512]{2,1,0:T(8,128)}), f32[16,32,512]{2,1,0:T(8,128)S(1)}, u32[]{:S(2)}, u32[]{:S(2)}) async-start(f32[16,32,512]{2,1,0:T(8,128)} %bitcast.14), calls=%async_computation | async-start | bytes 2097152 | tf_op jit(solution)/shard_map/all_to_all | solution.py:113
  40.5 21.6 %copy-start.7 = (s32[8,512]{1,0:T(8,128)S(1)}, s32[8,512]{1,0:T(8,128)}, u32[]{:S(2)}) copy-start(s32[8,512]{1,0:T(8,128)} %param.14) | copy-start | bytes 49156
  40.5 21.6 %copy-start.6 = (f32[4,8,512]{2,1,0:T(8,128)S(1)}, f32[4,8,512]{2,1,0:T(8,128)}, u32[]{:S(2)}) copy-start(f32[4,8,512]{2,1,0:T(8,128)} %param.15) | copy-start | bytes 196612
  55.8 31.9 %all-to-all-start.1 = ((f32[16,32,512]{2,1,0:T(8,128)}), f32[16,32,512]{2,1,0:T(8,128)S(1)}, u32[]{:S(2)}, u32[]{:S(2)}) async-start(f32[16,32,512]{2,1,0:T(8,128)} %bitcast.29), calls=%async_computation.1 | async-start | bytes 2097152 | tf_op jit(solution)/shard_map/all_to_all | solution.py:113
  65.2 26.5 %copy-start.4 = (f32[16,32,512]{2,1,0:T(8,128)S(1)}, f32[16,32,512]{2,1,0:T(8,128)}, u32[]{:S(2)}) copy-start(f32[16,32,512]{2,1,0:T(8,128)} %shard_map.82) | copy-start | bytes 3145732
  99.9 18.6 %collective-permute-start.8 = (f32[1,8,32,512]{3,2,0,1:T(8,128)S(1)}, f32[1,8,32,512]{3,2,0,1:T(8,128)S(1)}, u32[]{:S(2)}, u32[]{:S(2)}) collective-permute-start(f32[1,8,32,512]{3,2,0,1:T(8,128)S(1)} %get-tuple-element.10), channel_id=1, source_target_pairs={{1,0},{2,1},{3,2},{5,4},{6,5},{7,6},{9,8},{10,9},{11,10},{13,12},{... | collective-permute-start | bytes 1572872 | tf_op jit(solution)/shard_map/ppermute | solution.py:43
  101.9 10.6 %collective-permute-start.5 = (f32[1,4,32,512]{3,2,0,1:T(8,128)S(1)}, f32[1,4,32,512]{3,2,0,1:T(8,128)S(1)}, u32[]{:S(2)}, u32[]{:S(2)}) collective-permute-start(f32[1,4,32,512]{3,2,0,1:T(8,128)S(1)} %get-tuple-element.5), channel_id=1, source_target_pairs={{0,4},{1,5},{2,6},{3,7},{4,8},{5,9},{6,10},{7,11},{8,12},{9,13},{1... | collective-permute-start | bytes 786440 | tf_op jit(solution)/shard_map/ppermute | solution.py:43
  104.8 11.4 %collective-permute-start.6 = (f32[1,4,32,512]{3,2,0,1:T(8,128)S(1)}, f32[1,4,32,512]{3,2,0,1:T(8,128)S(1)}, u32[]{:S(2)}, u32[]{:S(2)}) collective-permute-start(f32[1,4,32,512]{3,2,0,1:T(8,128)S(1)} %get-tuple-element.8), channel_id=1, source_target_pairs={{4,0},{5,1},{6,2},{7,3},{8,4},{9,5},{10,6},{11,7},{12,8},{13,9},{1... | collective-permute-start | bytes 786440 | tf_op jit(solution)/shard_map/ppermute | solution.py:43
  107.8 8.4 %collective-permute-start.7 = (f32[1,4,32,512]{3,2,0,1:T(8,128)S(1)}, f32[1,4,32,512]{3,2,0,1:T(8,128)S(1)}, u32[]{:S(2)}, u32[]{:S(2)}) collective-permute-start(f32[1,4,32,512]{3,2,0,1:T(8,128)S(1)} %get-tuple-element.7), channel_id=1, source_target_pairs={{1,4},{2,5},{3,6},{5,8},{6,9},{7,10},{9,12},{10,13},{11,14},{17,20... | collective-permute-start | bytes 786440 | tf_op jit(solution)/shard_map/ppermute | solution.py:43
  109.7 8.8 %collective-permute-start.9 = (f32[1,4,32,512]{3,2,0,1:T(8,128)S(1)}, f32[1,4,32,512]{3,2,0,1:T(8,128)S(1)}, u32[]{:S(2)}, u32[]{:S(2)}) collective-permute-start(f32[1,4,32,512]{3,2,0,1:T(8,128)S(1)} %get-tuple-element.6), channel_id=1, source_target_pairs={{5,0},{6,1},{7,2},{9,4},{10,5},{11,6},{13,8},{14,9},{15,10},{21,16... | collective-permute-start | bytes 786440 | tf_op jit(solution)/shard_map/ppermute | solution.py:43
  129.0 35.5 %copy-start.10 = (f32[8,512]{1,0:T(8,128)S(1)}, f32[8,512]{1,0:T(8,128)}, u32[]{:S(2)}) copy-start(f32[8,512]{1,0:T(8,128)} %copy-done.9) | copy-start | bytes 49156
  129.0 35.5 %copy-start.12 = (f32[8,512]{1,0:T(8,128)S(1)}, f32[8,512]{1,0:T(8,128)}, u32[]{:S(2)}) copy-start(f32[8,512]{1,0:T(8,128)} %copy-done.11) | copy-start | bytes 49156
  129.0 35.5 %copy-start.14 = (f32[8,512]{1,0:T(8,128)S(1)}, f32[8,512]{1,0:T(8,128)}, u32[]{:S(2)}) copy-start(f32[8,512]{1,0:T(8,128)} %copy-done.13) | copy-start | bytes 49156
  (20 other events, 36.9 us)

commit v7 on v6

--- a/solution.py
+++ b/solution.py
@@ -124,13 +124,18 @@
     illiquid_offset,
     illiquid_weight,
 ):
-    liquid_map = band_matrix(liquid_offset, liquid_weight)
-    illiquid_map = band_matrix(illiquid_offset, illiquid_weight)
-
     expected = continuation(values, earn_prob, support_start)
-    saved = along_lanes(expected, liquid_map)
+    saved = along_lanes(expected, band_matrix(liquid_offset, liquid_weight))
+    saved, illiquid_offset, illiquid_weight = lax.optimization_barrier(
+        (saved, illiquid_offset, illiquid_weight)
+    )
+    illiquid_map = lax.optimization_barrier(band_matrix(illiquid_offset, illiquid_weight))
     adjusted = along_lanes(flipped(saved), illiquid_map)
     current = flipped(utility) + DISCOUNT * adjusted
+    current, liquid_offset, liquid_weight = lax.optimization_barrier(
+        (current, liquid_offset, liquid_weight)
+    )
+    liquid_map = lax.optimization_barrier(band_matrix(liquid_offset, liquid_weight))
 
     expected = continuation(current, earn_prob, support_start)
     moved = along_lanes(expected, illiquid_map)

time: 175 us -> 174 us (level)
  the two profiles are of different devices: /device:TPU:34 before, /device:TPU:1 now
where the time goes in v7:
time: 174 us; the launch traced here: 173 us
  waiting for transfers between devices  53.6 us (31%)
  starting transfers between devices  52.9 us (30%)
  matrix products  27.5 us (16%)
  other arithmetic  16.9 us (10%)
  local copies, waits for them, and re-layouts  12.1 us (7%)
  Pallas kernels  9.23 us (5%)
    all_to_all x3, waiting for transfers between devices, flipped(): got = lax.all_to_all(flat, 'asset', 0, 0, tiled=True)  39.6 us
    ppermute x10, starting transfers between devices, moved(): return lax.ppermute(value, axes, pairs)  29.5 us
    all_to_all x3, starting transfers between devices, flipped(): got = lax.all_to_all(flat, 'asset', 0, 0, tiled=True)  23.4 us
    dot_general x4, matrix products, along_lanes(): jnp.einsum('terc,ecn->tern', stacked, matrix, precision=lax.Precision.HIGH)  23.3 us
    add x2, other arithmetic, band_matrix(): matrix + jnp.where(positions[None, :, None] == (offset + number)[:, None,...  14.2 us
    ppermute x10, waiting for transfers between devices, moved(): return lax.ppermute(value, axes, pairs)  14 us
    pallas_call x3, Pallas kernels, regroup(): pl.pallas_call(_gather_kernel, in_specs=[pl.BlockSpec(memory_space=pltpu....  9.23 us
    dot_general x2, matrix products, continuation(): jnp.einsum('ij,tjxy->tixy', mixing, padded, precision=lax.Precision.HIGH)  4.24 us
  transfers between devices with their start and end apart: 13, of which 5 were waited for; matrix products, arithmetic and copies ran while one was open for 18% of the time, Pallas kernels for 2%

profile of v7, /device:TPU:1, one launch (start us, length us, event | category | flops | bytes accessed | tf_op | source)
XLA Modules:
  0.0 172.8 jit_solution(12339513543808129999)
XLA Ops:
  0.0 2.3 %fusion.87 = (f32[1,4,32,512]{3,2,1,0:T(8,128)}, f32[1,4,32,512]{3,2,1,0:T(8,128)}, f32[1,4,32,512]{3,2,1,0:T(8,128)}, f32[1,4,32,512]{3,2,1,0:T(8,128)}) fusion(f32[2,8,32,512]{3,2,1,0:T(8,128)} %param.8), kind=kLoop, calls=%fused_computation.124 | loop fusion | bytes 2097152 | tf_op jit(solution)/shard_map/slice | solution.py:48
  2.3 3.9 %collective-permute-start = (f32[1,4,32,512]{3,2,1,0:T(8,128)}, f32[1,4,32,512]{3,2,1,0:T(8,128)S(1)}, u32[]{:S(2)}, u32[]{:S(2)}) collective-permute-start(f32[1,4,32,512]{3,2,1,0:T(8,128)} %get-tuple-element.23), channel_id=1, source_target_pairs={{0,4},{1,5},{2,6},{3,7},{4,8},{5,9},{6,10},{7,11},{8,12},{9,13},{1... | collective-permute-start | bytes 786440 | tf_op jit(solution)/shard_map/ppermute | solution.py:43
  7.5 5.1 %collective-permute-start.2 = (f32[1,4,32,512]{3,2,1,0:T(8,128)}, f32[1,4,32,512]{3,2,1,0:T(8,128)S(1)}, u32[]{:S(2)}, u32[]{:S(2)}) collective-permute-start(f32[1,4,32,512]{3,2,1,0:T(8,128)} %get-tuple-element.24), channel_id=1, source_target_pairs={{1,4},{2,5},{3,6},{5,8},{6,9},{7,10},{9,12},{10,13},{11,14},{17,20... | collective-permute-start | bytes 786440 | tf_op jit(solution)/shard_map/ppermute | solution.py:43
  17.2 2.5 %copy.15 = f32[512,512]{0,1:T(8,128)} copy(f32[512,512]{1,0:T(8,128)} %bitcast.111) | data formatting | bytes 2097152 | tf_op jit(solution)/shard_map/reshape | solution.py:112
  19.7 10.9 %all-to-all-start = ((f32[16,32,512]{2,1,0:T(8,128)}), f32[16,32,512]{2,1,0:T(8,128)S(1)}, u32[]{:S(2)}, u32[]{:S(2)}) async-start(f32[16,32,512]{2,1,0:T(8,128)} %bitcast.2), calls=%async_computation | async-start | bytes 2097152 | tf_op jit(solution)/shard_map/all_to_all | solution.py:113
  33.2 2.5 %fusion.26 = f32[2,32,512,8]{2,3,1,0:T(8,128)S(1)} fusion(f32[2,16,32,512]{3,2,1,0:T(8,128)S(1)} %maximum_maximum_fusion, f32[8]{0:T(128)} %get-tuple-element.51, s32[8]{0:T(128)S(1)} %get-tuple-element.58, f32[8]{0:T(128)} %get-tuple-element.52, s32[8]{0:T(128)S(1)} %get-tuple-element.59, f32[8]{0:T(128)} %get-tuple-element.53, ...), kind=kOutput, calls=%fused_computation.42 | convolution fusion | flops 25167616 | bytes 3146048 | tf_op jit(solution)/shard_map/ij,tjxy->tixy/dot_general | solution.py:69
  35.6 7.4 %fusion.31 = f32[2,8,32,512]{3,2,0,1:T(8,128)S(1)} fusion(f32[8,512]{1,0:T(8,128)S(1)} %get-tuple-element.40, s32[8,512]{1,0:T(8,128)S(1)} %get-tuple-element.49, f32[8,512]{1,0:T(8,128)S(1)} %get-tuple-element.38, s32[8,512]{1,0:T(8,128)S(1)} %get-tuple-element.48, f32[8,512]{1,0:T(8,128)S(1)} %get-tuple-element.39, s32[8,512]{1,0:T(8,128)S(1)} %get-tuple-element.47, ...), kind=kOutput, calls=%fused_computation.45 | convolution fusion | flops 828375040 | bytes 2228224 | tf_op jit(solution)/shard_map/terc,ecn->tern/dot_general | solution.py:73
  44.5 8.0 %all-to-all-done.src_ref = f32[16,32,512]{2,1,0:T(8,128)S(1)} async-done(((f32[16,32,512]{2,1,0:T(8,128)}), f32[16,32,512]{2,1,0:T(8,128)S(1)}, u32[]{:S(2)}, u32[]{:S(2)}) %all-to-all-start) | async-done | bytes 1048608 | tf_op jit(solution)/shard_map/all_to_all | solution.py:113
  52.6 8.0 %all-to-all-start.1 = ((f32[16,32,512]{2,1,0:T(8,128)}), f32[16,32,512]{2,1,0:T(8,128)S(1)}, u32[]{:S(2)}, u32[]{:S(2)}) async-start(f32[16,32,512]{2,1,0:T(8,128)} %bitcast.27), calls=%async_computation.1 | async-start | bytes 2097152 | tf_op jit(solution)/shard_map/all_to_all | solution.py:113
  60.6 7.1 %select_add_fusion.1 = f32[8,512,512]{2,1,0:T(8,128)} fusion(f32[8,512]{1,0:T(8,128)S(1)} %get-tuple-element.34, s32[8,512]{1,0:T(8,128)S(1)} %get-tuple-element.45, f32[8,512]{1,0:T(8,128)S(1)} %get-tuple-element.35, s32[8,512]{1,0:T(8,128)S(1)} %get-tuple-element.46, f32[8,512]{1,0:T(8,128)S(1)} %get-tuple-element.36, s32[8,512]{1,0:T(8,128)S(1)} %get-tuple-element.44, ...), kind=kLoop, calls=%fused_computation.12 | loop fusion | flops 23068672 | bytes 8519680 | tf_op jit(solution)/shard_map/add | solution.py:22
  67.7 3.1 %shard_map.82 = f32[16,32,512]{2,1,0:T(8,128)} custom-call(f32[16,32,512]{2,1,0:T(8,128)} %copy-done), custom_call_target="tpu_custom_call" | custom-call | bytes 2097152 | tf_op jit(solution)/shard_map/pallas_call | solution.py:99
  70.8 9.7 %all-to-all-done.1.src_ref = f32[16,32,512]{2,1,0:T(8,128)S(1)} async-done(((f32[16,32,512]{2,1,0:T(8,128)}), f32[16,32,512]{2,1,0:T(8,128)S(1)}, u32[]{:S(2)}, u32[]{:S(2)}) %all-to-all-start.1) | async-done | bytes 1048608 | tf_op jit(solution)/shard_map/all_to_all | solution.py:113
  81.4 3.1 %shard_map.83 = f32[16,32,512]{2,1,0:T(8,128)} custom-call(f32[16,32,512]{2,1,0:T(8,128)} %copy-done.1), custom_call_target="tpu_custom_call" | custom-call | bytes 2097152 | tf_op jit(solution)/shard_map/pallas_call | solution.py:99
  84.6 6.7 %fusion.40 = f32[2,8,32,512]{3,2,0,1:T(8,128)S(1)} fusion(f32[8,512,512]{2,1,0:T(8,128)} %select_add_fusion.1, f32[2,8,32,512]{3,2,1,0:T(8,128)} %bitcast.112, f32[2,8,32,512]{3,2,1,0:T(8,128)} %bitcast.113), kind=kOutput, calls=%fused_computation.48 | convolution fusion | flops 805830656 | bytes 11534336 | tf_op jit(solution)/shard_map/terc,ecn->tern/dot_general | solution.py:73
  93.6 8.1 %collective-permute-start.5 = (f32[1,4,32,512]{3,2,0,1:T(8,128)S(1)}, f32[1,4,32,512]{3,2,0,1:T(8,128)S(1)}, u32[]{:S(2)}, u32[]{:S(2)}) collective-permute-start(f32[1,4,32,512]{3,2,0,1:T(8,128)S(1)} %get-tuple-element.17), channel_id=1, source_target_pairs={{0,4},{1,5},{2,6},{3,7},{4,8},{5,9},{6,10},{7,11},{8,12},{9,13},{1... | collective-permute-start | bytes 786440 | tf_op jit(solution)/shard_map/ppermute | solution.py:43
  103.0 3.1 %collective-permute-start.7 = (f32[1,4,32,512]{3,2,0,1:T(8,128)S(1)}, f32[1,4,32,512]{3,2,0,1:T(8,128)S(1)}, u32[]{:S(2)}, u32[]{:S(2)}) collective-permute-start(f32[1,4,32,512]{3,2,0,1:T(8,128)S(1)} %get-tuple-element.19), channel_id=1, source_target_pairs={{1,4},{2,5},{3,6},{5,8},{6,9},{7,10},{9,12},{10,13},{11,14},{17,20... | collective-permute-start | bytes 786440 | tf_op jit(solution)/shard_map/ppermute | solution.py:43
  107.4 3.6 %collective-permute-done.6 = f32[1,4,32,512]{3,2,0,1:T(8,128)S(1)} collective-permute-done((f32[1,4,32,512]{3,2,0,1:T(8,128)S(1)}, f32[1,4,32,512]{3,2,0,1:T(8,128)S(1)}, u32[]{:S(2)}, u32[]{:S(2)}) %collective-permute-start.6) | collective-permute-done | bytes 262176 | tf_op jit(solution)/shard_map/ppermute | solution.py:43
  111.0 10.4 %collective-permute-done.9 = f32[1,4,32,512]{3,2,0,1:T(8,128)S(1)} collective-permute-done((f32[1,4,32,512]{3,2,0,1:T(8,128)S(1)}, f32[1,4,32,512]{3,2,0,1:T(8,128)S(1)}, u32[]{:S(2)}, u32[]{:S(2)}) %collective-permute-start.9) | collective-permute-done | bytes 262176 | tf_op jit(solution)/shard_map/ppermute | solution.py:43
  123.6 3.1 %fusion.28 = f32[2,8,32,512]{3,2,0,1:T(8,128)S(1)} fusion(f32[8,512,512]{2,1,0:T(8,128)S(1)} %bitcast.108, f32[2,32,512,8]{2,3,1,0:T(8,128)S(1)} %fusion.24), kind=kOutput, calls=%fused_computation.44 | convolution fusion | flops 805306368 | bytes 10485760 | tf_op jit(solution)/shard_map/terc,ecn->tern/dot_general | solution.py:73
  128.1 4.5 %all-to-all-start.2 = ((f32[16,32,512]{2,1,0:T(8,128)}), f32[16,32,512]{2,1,0:T(8,128)S(1)}, u32[]{:S(2)}, u32[]{:S(2)}) async-start(f32[16,32,512]{2,1,0:T(8,128)} %bitcast.42), calls=%async_computation.2 | async-start | bytes 2097152 | tf_op jit(solution)/shard_map/all_to_all | solution.py:113
  132.6 7.1 %select_add_fusion = f32[8,512,512]{2,1,0:T(8,128)} fusion(f32[8,512]{1,0:T(8,128)S(1)} %get-tuple-element.30, s32[8,512]{1,0:T(8,128)S(1)} %get-tuple-element.42, f32[8,512]{1,0:T(8,128)S(1)} %get-tuple-element.31, s32[8,512]{1,0:T(8,128)S(1)} %get-tuple-element.43, f32[8,512]{1,0:T(8,128)S(1)} %get-tuple-element.32, s32[8,512]{1,0:T(8,128)S(1)} %get-tuple-element.41, ...), kind=kLoop, calls=%fused_computation.8 | loop fusion | flops 23068672 | bytes 8519680 | tf_op jit(solution)/shard_map/add | solution.py:22
  139.7 21.9 %all-to-all-done.2.src_ref = f32[16,32,512]{2,1,0:T(8,128)S(1)} async-done(((f32[16,32,512]{2,1,0:T(8,128)}), f32[16,32,512]{2,1,0:T(8,128)S(1)}, u32[]{:S(2)}, u32[]{:S(2)}) %all-to-all-start.2) | async-done | bytes 1048608 | tf_op jit(solution)/shard_map/all_to_all | solution.py:113
  162.5 3.1 %shard_map.84 = f32[16,32,512]{2,1,0:T(8,128)} custom-call(f32[16,32,512]{2,1,0:T(8,128)} %copy-done.2), custom_call_target="tpu_custom_call" | custom-call | bytes 2097152 | tf_op jit(solution)/shard_map/pallas_call | solution.py:99
  165.6 6.1 %fusion.49 = f32[2,8,32,512]{3,2,0,1:T(8,128)S(1)} fusion(f32[8,512,512]{2,1,0:T(8,128)} %select_add_fusion, f32[2,8,32,512]{3,2,1,0:T(8,128)S(1)} %copy-done.3, f32[2,8,32,512]{3,2,1,0:T(8,128)} %bitcast.114), kind=kOutput, calls=%fused_computation.51 | convolution fusion | flops 805830656 | bytes 11534336 | tf_op jit(solution)/shard_map/terc,ecn->tern/dot_general | solution.py:73
  (71 shorter events, 21.1 us)
Async XLA Ops:
  0.0 30.6 %copy-start.8 = (f32[5,8]{1,0:T(8,128)S(1)}, f32[5,8]{1,0:T(8,128)}, u32[]{:S(2)}) copy-start(f32[5,8]{1,0:T(8,128)} %param.10) | copy-start | bytes 484
  0.0 31.9 %copy-start.4 = (f32[4,8,512]{2,1,0:T(8,128)S(1)}, f32[4,8,512]{2,1,0:T(8,128)}, u32[]{:S(2)}) copy-start(f32[4,8,512]{2,1,0:T(8,128)} %param.13) | copy-start | bytes 196612
  2.3 29.7 %collective-permute-start = (f32[1,4,32,512]{3,2,1,0:T(8,128)}, f32[1,4,32,512]{3,2,1,0:T(8,128)S(1)}, u32[]{:S(2)}, u32[]{:S(2)}) collective-permute-start(f32[1,4,32,512]{3,2,1,0:T(8,128)} %get-tuple-element.23), channel_id=1, source_target_pairs={{0,4},{1,5},{2,6},{3,7},{4,8},{5,9},{6,10},{7,11},{8,12},{9,13},{1... | collective-permute-start | bytes 786440 | tf_op jit(solution)/shard_map/ppermute | solution.py:43
  6.2 25.8 %collective-permute-start.1 = (f32[1,4,32,512]{3,2,1,0:T(8,128)}, f32[1,4,32,512]{3,2,1,0:T(8,128)S(1)}, u32[]{:S(2)}, u32[]{:S(2)}) collective-permute-start(f32[1,4,32,512]{3,2,1,0:T(8,128)} %get-tuple-element.25), channel_id=1, source_target_pairs={{4,0},{5,1},{6,2},{7,3},{8,4},{9,5},{10,6},{11,7},{12,8},{13,9},{1... | collective-permute-start | bytes 786440 | tf_op jit(solution)/shard_map/ppermute | solution.py:43
  7.5 24.5 %collective-permute-start.2 = (f32[1,4,32,512]{3,2,1,0:T(8,128)}, f32[1,4,32,512]{3,2,1,0:T(8,128)S(1)}, u32[]{:S(2)}, u32[]{:S(2)}) collective-permute-start(f32[1,4,32,512]{3,2,1,0:T(8,128)} %get-tuple-element.24), channel_id=1, source_target_pairs={{1,4},{2,5},{3,6},{5,8},{6,9},{7,10},{9,12},{10,13},{11,14},{17,20... | collective-permute-start | bytes 786440 | tf_op jit(solution)/shard_map/ppermute | solution.py:43
  12.6 19.4 %collective-permute-start.4 = (f32[1,4,32,512]{3,2,1,0:T(8,128)}, f32[1,4,32,512]{3,2,1,0:T(8,128)}, u32[]{:S(2)}, u32[]{:S(2)}) collective-permute-start(f32[1,4,32,512]{3,2,1,0:T(8,128)} %get-tuple-element.26), channel_id=1, source_target_pairs={{5,0},{6,1},{7,2},{9,4},{10,5},{11,6},{13,8},{14,9},{15,10},{21,16... | collective-permute-start | bytes 786440 | tf_op jit(solution)/shard_map/ppermute | solution.py:43
  15.2 16.8 %collective-permute-start.3 = (f32[1,8,32,512]{3,2,1,0:T(8,128)S(1)}, f32[1,8,32,512]{3,2,1,0:T(8,128)S(1)}, u32[]{:S(2)}, u32[]{:S(2)}) collective-permute-start(f32[1,8,32,512]{3,2,1,0:T(8,128)S(1)} %get-tuple-element.28), channel_id=1, source_target_pairs={{1,0},{2,1},{3,2},{5,4},{6,5},{7,6},{9,8},{10,9},{11,10},{13,12},{... | collective-permute-start | bytes 1572872 | tf_op jit(solution)/shard_map/ppermute | solution.py:43
  19.7 32.9 %all-to-all-start = ((f32[16,32,512]{2,1,0:T(8,128)}), f32[16,32,512]{2,1,0:T(8,128)S(1)}, u32[]{:S(2)}, u32[]{:S(2)}) async-start(f32[16,32,512]{2,1,0:T(8,128)} %bitcast.2), calls=%async_computation | async-start | bytes 2097152 | tf_op jit(solution)/shard_map/all_to_all | solution.py:113
  52.6 27.9 %all-to-all-start.1 = ((f32[16,32,512]{2,1,0:T(8,128)}), f32[16,32,512]{2,1,0:T(8,128)S(1)}, u32[]{:S(2)}, u32[]{:S(2)}) async-start(f32[16,32,512]{2,1,0:T(8,128)} %bitcast.27), calls=%async_computation.1 | async-start | bytes 2097152 | tf_op jit(solution)/shard_map/all_to_all | solution.py:113
  84.5 37.2 %copy-start.10 = (s32[8]{0:T(128)S(1)}, s32[8]{0:T(128)}, u32[]{:S(2)}) copy-start(s32[8]{0:T(128)} %copy-done.9) | copy-start | bytes 100
  84.5 37.2 %copy-start.11 = (f32[8]{0:T(128)S(1)}, f32[8]{0:T(128)}, u32[]{:S(2)}) copy-start(f32[8]{0:T(128)} %get-tuple-element.50) | copy-start | bytes 100
  84.5 37.2 %copy-start.12 = (f32[8]{0:T(128)S(1)}, f32[8]{0:T(128)}, u32[]{:S(2)}) copy-start(f32[8]{0:T(128)} %get-tuple-element.51) | copy-start | bytes 100
  84.5 37.2 %copy-start.13 = (f32[8]{0:T(128)S(1)}, f32[8]{0:T(128)}, u32[]{:S(2)}) copy-start(f32[8]{0:T(128)} %get-tuple-element.52) | copy-start | bytes 100
  84.5 37.2 %copy-start.14 = (f32[8]{0:T(128)S(1)}, f32[8]{0:T(128)}, u32[]{:S(2)}) copy-start(f32[8]{0:T(128)} %get-tuple-element.53) | copy-start | bytes 100
  84.5 37.2 %copy-start.15 = (f32[8]{0:T(128)S(1)}, f32[8]{0:T(128)}, u32[]{:S(2)}) copy-start(f32[8]{0:T(128)} %get-tuple-element.54) | copy-start | bytes 100
  84.6 39.0 %slice-start = ((s8[8388608]{0:T(1024)(128)(4,1)}), s8[4194304]{0:T(1024)(128)(4,1)S(1)}, s32[]{:S(2)}) async-start(s8[8388608]{0:T(1024)(128)(4,1)} %bitcast.107), calls=%async_computation.3 | async-start | bytes 8388608
  91.2 32.3 %slice-start.1 = ((s8[8388608]{0:T(1024)(128)(4,1)}), s8[4194304]{0:T(1024)(128)(4,1)S(1)}, s32[]{:S(2)}) async-start(s8[8388608]{0:T(1024)(128)(4,1)} %bitcast.107), calls=%async_computation.4 | async-start | bytes 8388608
  91.3 30.1 %collective-permute-start.8 = (f32[1,8,32,512]{3,2,0,1:T(8,128)S(1)}, f32[1,8,32,512]{3,2,0,1:T(8,128)S(1)}, u32[]{:S(2)}, u32[]{:S(2)}) collective-permute-start(f32[1,8,32,512]{3,2,0,1:T(8,128)S(1)} %get-tuple-element.22), channel_id=1, source_target_pairs={{1,0},{2,1},{3,2},{5,4},{6,5},{7,6},{9,8},{10,9},{11,10},{13,12},{... | collective-permute-start | bytes 1572872 | tf_op jit(solution)/shard_map/ppermute | solution.py:43
  93.6 13.8 %collective-permute-start.5 = (f32[1,4,32,512]{3,2,0,1:T(8,128)S(1)}, f32[1,4,32,512]{3,2,0,1:T(8,128)S(1)}, u32[]{:S(2)}, u32[]{:S(2)}) collective-permute-start(f32[1,4,32,512]{3,2,0,1:T(8,128)S(1)} %get-tuple-element.17), channel_id=1, source_target_pairs={{0,4},{1,5},{2,6},{3,7},{4,8},{5,9},{6,10},{7,11},{8,12},{9,13},{1... | collective-permute-start | bytes 786440 | tf_op jit(solution)/shard_map/ppermute | solution.py:43
  101.7 9.4 %collective-permute-start.6 = (f32[1,4,32,512]{3,2,0,1:T(8,128)S(1)}, f32[1,4,32,512]{3,2,0,1:T(8,128)S(1)}, u32[]{:S(2)}, u32[]{:S(2)}) collective-permute-start(f32[1,4,32,512]{3,2,0,1:T(8,128)S(1)} %get-tuple-element.20), channel_id=1, source_target_pairs={{4,0},{5,1},{6,2},{7,3},{8,4},{9,5},{10,6},{11,7},{12,8},{13,9},{1... | collective-permute-start | bytes 786440 | tf_op jit(solution)/shard_map/ppermute | solution.py:43
  103.0 8.1 %collective-permute-start.7 = (f32[1,4,32,512]{3,2,0,1:T(8,128)S(1)}, f32[1,4,32,512]{3,2,0,1:T(8,128)S(1)}, u32[]{:S(2)}, u32[]{:S(2)}) collective-permute-start(f32[1,4,32,512]{3,2,0,1:T(8,128)S(1)} %get-tuple-element.19), channel_id=1, source_target_pairs={{1,4},{2,5},{3,6},{5,8},{6,9},{7,10},{9,12},{10,13},{11,14},{17,20... | collective-permute-start | bytes 786440 | tf_op jit(solution)/shard_map/ppermute | solution.py:43
  106.1 15.3 %collective-permute-start.9 = (f32[1,4,32,512]{3,2,0,1:T(8,128)S(1)}, f32[1,4,32,512]{3,2,0,1:T(8,128)S(1)}, u32[]{:S(2)}, u32[]{:S(2)}) collective-permute-start(f32[1,4,32,512]{3,2,0,1:T(8,128)S(1)} %get-tuple-element.18), channel_id=1, source_target_pairs={{5,0},{6,1},{7,2},{9,4},{10,5},{11,6},{13,8},{14,9},{15,10},{21,16... | collective-permute-start | bytes 786440 | tf_op jit(solution)/shard_map/ppermute | solution.py:43
  126.6 39.0 %copy-start.3 = (f32[2,8,32,512]{3,2,1,0:T(8,128)S(1)}, f32[2,8,32,512]{3,2,1,0:T(8,128)}, u32[]{:S(2)}) copy-start(f32[2,8,32,512]{3,2,1,0:T(8,128)} %param.9) | copy-start | bytes 3145732
  128.1 33.5 %all-to-all-start.2 = ((f32[16,32,512]{2,1,0:T(8,128)}), f32[16,32,512]{2,1,0:T(8,128)S(1)}, u32[]{:S(2)}, u32[]{:S(2)}) async-start(f32[16,32,512]{2,1,0:T(8,128)} %bitcast.42), calls=%async_computation.2 | async-start | bytes 2097152 | tf_op jit(solution)/shard_map/all_to_all | solution.py:113
  (7 other events, 108.8 us)

commit v8 on v6

--- a/solution.py
+++ b/solution.py
@@ -124,11 +124,14 @@
     illiquid_offset,
     illiquid_weight,
 ):
-    liquid_map = band_matrix(liquid_offset, liquid_weight)
-    illiquid_map = band_matrix(illiquid_offset, illiquid_weight)
-
     expected = continuation(values, earn_prob, support_start)
-    saved = along_lanes(expected, liquid_map)
+    saved = along_lanes(expected, band_matrix(liquid_offset, liquid_weight))
+    saved, illiquid_offset, illiquid_weight, liquid_offset, liquid_weight = lax.optimization_barrier(
+        (saved, illiquid_offset, illiquid_weight, liquid_offset, liquid_weight)
+    )
+    illiquid_map, liquid_map = lax.optimization_barrier(
+        (band_matrix(illiquid_offset, illiquid_weight), band_matrix(liquid_offset, liquid_weight))
+    )
     adjusted = along_lanes(flipped(saved), illiquid_map)
     current = flipped(utility) + DISCOUNT * adjusted
 

time: 175 us -> 173 us (0.989)
  waiting for transfers between devices: 43.3 us -> 22 us
  other arithmetic: 2.37 us -> 19.9 us
  matrix products: 34.7 us -> 28.2 us
  starting transfers between devices: 42.7 us -> 46.5 us
  local copies, waits for them, and re-layouts: 8.28 us -> 10.9 us
    all_to_all x2, waiting for transfers between devices: 36.4 us -> 1.85 us  [flipped(): got = lax.all_to_all(flat, 'asset', 0, 0, tiled=True)]
    add x0 -> x1, other arithmetic: none -> 15.2 us  [band_matrix(): matrix + jnp.where(positions[None, :, None] == (offset + number)[:, None,...]
    ppermute x10, waiting for transfers between devices: 6.89 us -> 20.1 us  [moved(): return lax.ppermute(value, axes, pairs)]
    dot_general x4, matrix products: 31.2 us -> 24 us  [along_lanes(): jnp.einsum('terc,ecn->tern', stacked, matrix, precision=lax.Precision.HIGH)]
    ppermute x10, starting transfers between devices: 25.2 us -> 27.2 us  [moved(): return lax.ppermute(value, axes, pairs)]
    all_to_all x2, starting transfers between devices: 17.5 us -> 19.3 us  [flipped(): got = lax.all_to_all(flat, 'asset', 0, 0, tiled=True)]
  transfers between devices with their start and end apart: 12 -> 12, of which waited for: 5 -> 7; matrix products, arithmetic and copies ran while one was open for 8% -> 21% of each run, Pallas kernels for 2% -> 2%
where the time goes in v8:
time: 173 us; the launch traced here: 171 us
  starting transfers between devices  46.5 us (27%)
  blocking collectives  33.3 us (19%)
  matrix products  28.2 us (16%)
  waiting for transfers between devices  22 us (13%)
  other arithmetic  19.9 us (12%)
  local copies, waits for them, and re-layouts  10.9 us (6%)
  Pallas kernels  9.25 us (5%)
    all_to_all x1, blocking collectives, flipped(): got = lax.all_to_all(flat, 'asset', 0, 0, tiled=True)  33.3 us
    ppermute x10, starting transfers between devices, moved(): return lax.ppermute(value, axes, pairs)  27.2 us
    dot_general x4, matrix products, along_lanes(): jnp.einsum('terc,ecn->tern', stacked, matrix, precision=lax.Precision.HIGH)  24 us
    ppermute x10, waiting for transfers between devices, moved(): return lax.ppermute(value, axes, pairs)  20.1 us
    all_to_all x2, starting transfers between devices, flipped(): got = lax.all_to_all(flat, 'asset', 0, 0, tiled=True)  19.3 us
    add x1, other arithmetic, band_matrix(): matrix + jnp.where(positions[None, :, None] == (offset + number)[:, None,...  15.2 us
    pallas_call x3, Pallas kernels, regroup(): pl.pallas_call(_gather_kernel, in_specs=[pl.BlockSpec(memory_space=pltpu....  9.25 us
    dot_general x2, matrix products, continuation(): jnp.einsum('ij,tjxy->tixy', mixing, padded, precision=lax.Precision.HIGH)  4.24 us
  transfers between devices with their start and end apart: 12, of which 7 were waited for; matrix products, arithmetic and copies ran while one was open for 21% of the time, Pallas kernels for 2%

profile of v8, /device:TPU:34, one launch (start us, length us, event | category | flops | bytes accessed | tf_op | source)
XLA Modules:
  0.0 170.6 jit_solution(15029299072530957728)
XLA Ops:
  0.0 2.6 %copy.15 = f32[512,512]{0,1:T(8,128)} copy(f32[512,512]{1,0:T(8,128)} %bitcast.112) | data formatting | bytes 2097152 | tf_op jit(solution)/shard_map/reshape | solution.py:112
  2.6 10.3 %all-to-all-start = ((f32[16,32,512]{2,1,0:T(8,128)}), f32[16,32,512]{2,1,0:T(8,128)S(1)}, u32[]{:S(2)}, u32[]{:S(2)}) async-start(f32[16,32,512]{2,1,0:T(8,128)} %bitcast.29), calls=%async_computation | async-start | bytes 2097152 | tf_op jit(solution)/shard_map/all_to_all | solution.py:113
  15.1 3.4 %collective-permute-start = (f32[1,4,32,512]{3,2,1,0:T(8,128)}, f32[1,4,32,512]{3,2,1,0:T(8,128)S(1)}, u32[]{:S(2)}, u32[]{:S(2)}) collective-permute-start(f32[1,4,32,512]{3,2,1,0:T(8,128)} %get-tuple-element.25), channel_id=1, source_target_pairs={{0,4},{1,5},{2,6},{3,7},{4,8},{5,9},{6,10},{7,11},{8,12},{9,13},{1... | collective-permute-start | bytes 786440 | tf_op jit(solution)/shard_map/ppermute | solution.py:43
  18.5 2.4 %collective-permute-start.2 = (f32[1,4,32,512]{3,2,1,0:T(8,128)}, f32[1,4,32,512]{3,2,1,0:T(8,128)S(1)}, u32[]{:S(2)}, u32[]{:S(2)}) collective-permute-start(f32[1,4,32,512]{3,2,1,0:T(8,128)} %get-tuple-element.26), channel_id=1, source_target_pairs={{1,4},{2,5},{3,6},{5,8},{6,9},{7,10},{9,12},{10,13},{11,14},{17,20... | collective-permute-start | bytes 786440 | tf_op jit(solution)/shard_map/ppermute | solution.py:43
  20.9 2.7 %collective-permute-start.1 = (f32[1,4,32,512]{3,2,1,0:T(8,128)}, f32[1,4,32,512]{3,2,1,0:T(8,128)S(1)}, u32[]{:S(2)}, u32[]{:S(2)}) collective-permute-start(f32[1,4,32,512]{3,2,1,0:T(8,128)} %get-tuple-element.27), channel_id=1, source_target_pairs={{4,0},{5,1},{6,2},{7,3},{8,4},{9,5},{10,6},{11,7},{12,8},{13,9},{1... | collective-permute-start | bytes 786440 | tf_op jit(solution)/shard_map/ppermute | solution.py:43
  27.1 2.8 %collective-permute-start.3 = (f32[1,8,32,512]{3,2,1,0:T(8,128)S(1)}, f32[1,8,32,512]{3,2,1,0:T(8,128)S(1)}, u32[]{:S(2)}, u32[]{:S(2)}) collective-permute-start(f32[1,8,32,512]{3,2,1,0:T(8,128)S(1)} %get-tuple-element.30), channel_id=1, source_target_pairs={{1,0},{2,1},{3,2},{5,4},{6,5},{7,6},{9,8},{10,9},{11,10},{13,12},{... | collective-permute-start | bytes 1572872 | tf_op jit(solution)/shard_map/ppermute | solution.py:43
  34.0 4.4 %collective-permute-done.2 = f32[1,4,32,512]{3,2,1,0:T(8,128)S(1)} collective-permute-done((f32[1,4,32,512]{3,2,1,0:T(8,128)}, f32[1,4,32,512]{3,2,1,0:T(8,128)S(1)}, u32[]{:S(2)}, u32[]{:S(2)}) %collective-permute-start.2) | collective-permute-done | bytes 262176 | tf_op jit(solution)/shard_map/ppermute | solution.py:43
  38.4 2.8 %collective-permute-done.4 = f32[1,4,32,512]{3,2,1,0:T(8,128)} collective-permute-done((f32[1,4,32,512]{3,2,1,0:T(8,128)}, f32[1,4,32,512]{3,2,1,0:T(8,128)}, u32[]{:S(2)}, u32[]{:S(2)}) %collective-permute-start.4) | collective-permute-done | bytes 262176 | tf_op jit(solution)/shard_map/ppermute | solution.py:43
  41.2 5.5 %collective-permute-done.3 = f32[1,8,32,512]{3,2,1,0:T(8,128)S(1)} collective-permute-done((f32[1,8,32,512]{3,2,1,0:T(8,128)S(1)}, f32[1,8,32,512]{3,2,1,0:T(8,128)S(1)}, u32[]{:S(2)}, u32[]{:S(2)}) %collective-permute-start.3) | collective-permute-done | bytes 524320 | tf_op jit(solution)/shard_map/ppermute | solution.py:43
  47.8 2.5 %fusion.26 = f32[2,32,512,8]{2,3,1,0:T(8,128)S(1)} fusion(f32[2,16,32,512]{3,2,1,0:T(8,128)S(1)} %maximum_maximum_fusion, f32[8]{0:T(128)} %get-tuple-element.53, s32[8]{0:T(128)S(1)} %get-tuple-element.60, f32[8]{0:T(128)} %get-tuple-element.54, s32[8]{0:T(128)S(1)} %get-tuple-element.61, f32[8]{0:T(128)} %get-tuple-element.55, ...), kind=kOutput, calls=%fused_computation.42 | convolution fusion | flops 25167616 | bytes 3146048 | tf_op jit(solution)/shard_map/ij,tjxy->tixy/dot_general | solution.py:69
  50.3 8.3 %fusion.31 = f32[2,8,32,512]{3,2,0,1:T(8,128)S(1)} fusion(f32[8,512]{1,0:T(8,128)} %get-tuple-element.42, s32[8,512]{1,0:T(8,128)S(1)} %get-tuple-element.51, f32[8,512]{1,0:T(8,128)} %get-tuple-element.40, s32[8,512]{1,0:T(8,128)S(1)} %get-tuple-element.50, f32[8,512]{1,0:T(8,128)} %get-tuple-element.41, s32[8,512]{1,0:T(8,128)S(1)} %get-tuple-element.49, ...), kind=kOutput, calls=%fused_computation.45 | convolution fusion | flops 828375040 | bytes 2228224 | tf_op jit(solution)/shard_map/terc,ecn->tern/dot_general | solution.py:73
  60.1 9.0 %all-to-all-start.1 = ((f32[16,32,512]{2,1,0:T(8,128)}), f32[16,32,512]{2,1,0:T(8,128)S(1)}, u32[]{:S(2)}, u32[]{:S(2)}) async-start(f32[16,32,512]{2,1,0:T(8,128)} %bitcast.34), calls=%async_computation.1 | async-start | bytes 2097152 | tf_op jit(solution)/shard_map/all_to_all | solution.py:113
  69.1 15.2 %select_add_fusion = (f32[8,512,512]{2,1,0:T(8,128)}, f32[8,512,512]{2,1,0:T(8,128)}) fusion(f32[8,512]{1,0:T(8,128)S(1)} %get-tuple-element.32, s32[8,512]{1,0:T(8,128)S(1)} %get-tuple-element.44, f32[8,512]{1,0:T(8,128)S(1)} %get-tuple-element.33, s32[8,512]{1,0:T(8,128)S(1)} %get-tuple-element.45, f32[8,512]{1,0:T(8,128)S(1)} %get-tuple-element.34, ...), kind=kLoop, calls=%fused_computation.8 | loop fusion | flops 46137344 | bytes 17039360 | tf_op jit(solution)/shard_map/add | solution.py:22
  84.3 3.1 %shard_map.82 = f32[16,32,512]{2,1,0:T(8,128)} custom-call(f32[16,32,512]{2,1,0:T(8,128)} %copy-done), custom_call_target="tpu_custom_call" | custom-call | bytes 2097152 | tf_op jit(solution)/shard_map/pallas_call | solution.py:99
  90.2 3.1 %shard_map.83 = f32[16,32,512]{2,1,0:T(8,128)} custom-call(f32[16,32,512]{2,1,0:T(8,128)} %copy-done.1), custom_call_target="tpu_custom_call" | custom-call | bytes 2097152 | tf_op jit(solution)/shard_map/pallas_call | solution.py:99
  93.4 6.6 %fusion.40 = f32[2,8,32,512]{3,2,0,1:T(8,128)S(1)} fusion(f32[8,512,512]{2,1,0:T(8,128)} %get-tuple-element.17, f32[2,8,32,512]{3,2,1,0:T(8,128)} %bitcast.113, f32[2,8,32,512]{3,2,1,0:T(8,128)} %bitcast.114), kind=kOutput, calls=%fused_computation.48 | convolution fusion | flops 805830656 | bytes 11534336 | tf_op jit(solution)/shard_map/terc,ecn->tern/dot_general | solution.py:73
  100.2 2.7 %collective-permute-start.8 = (f32[1,8,32,512]{3,2,0,1:T(8,128)S(1)}, f32[1,8,32,512]{3,2,0,1:T(8,128)S(1)}, u32[]{:S(2)}, u32[]{:S(2)}) collective-permute-start(f32[1,8,32,512]{3,2,0,1:T(8,128)S(1)} %get-tuple-element.24), channel_id=1, source_target_pairs={{1,0},{2,1},{3,2},{5,4},{6,5},{7,6},{9,8},{10,9},{11,10},{13,12},{... | collective-permute-start | bytes 1572872 | tf_op jit(solution)/shard_map/ppermute | solution.py:43
  103.0 3.8 %collective-permute-start.5 = (f32[1,4,32,512]{3,2,0,1:T(8,128)S(1)}, f32[1,4,32,512]{3,2,0,1:T(8,128)S(1)}, u32[]{:S(2)}, u32[]{:S(2)}) collective-permute-start(f32[1,4,32,512]{3,2,0,1:T(8,128)S(1)} %get-tuple-element.19), channel_id=1, source_target_pairs={{0,4},{1,5},{2,6},{3,7},{4,8},{5,9},{6,10},{7,11},{8,12},{9,13},{1... | collective-permute-start | bytes 786440 | tf_op jit(solution)/shard_map/ppermute | solution.py:43
  110.7 3.3 %collective-permute-start.6 = (f32[1,4,32,512]{3,2,0,1:T(8,128)S(1)}, f32[1,4,32,512]{3,2,0,1:T(8,128)S(1)}, u32[]{:S(2)}, u32[]{:S(2)}) collective-permute-start(f32[1,4,32,512]{3,2,0,1:T(8,128)S(1)} %get-tuple-element.22), channel_id=1, source_target_pairs={{4,0},{5,1},{6,2},{7,3},{8,4},{9,5},{10,6},{11,7},{12,8},{13,9},{1... | collective-permute-start | bytes 786440 | tf_op jit(solution)/shard_map/ppermute | solution.py:43
  116.5 5.0 %collective-permute-done.6 = f32[1,4,32,512]{3,2,0,1:T(8,128)S(1)} collective-permute-done((f32[1,4,32,512]{3,2,0,1:T(8,128)S(1)}, f32[1,4,32,512]{3,2,0,1:T(8,128)S(1)}, u32[]{:S(2)}, u32[]{:S(2)}) %collective-permute-start.6) | collective-permute-done | bytes 262176 | tf_op jit(solution)/shard_map/ppermute | solution.py:43
  123.6 2.9 %fusion.28 = f32[2,8,32,512]{3,2,0,1:T(8,128)S(1)} fusion(f32[8,512,512]{2,1,0:T(8,128)S(1)} %bitcast.108, f32[2,32,512,8]{2,3,1,0:T(8,128)S(1)} %fusion.24), kind=kOutput, calls=%fused_computation.44 | convolution fusion | flops 805306368 | bytes 10485760 | tf_op jit(solution)/shard_map/terc,ecn->tern/dot_general | solution.py:73
  127.0 33.3 %all_to_all.15.src_ref = f32[16,32,512]{2,1,0:T(8,128)} all-to-all(f32[16,32,512]{2,1,0:T(8,128)S(1)} %bitcast.111), channel_id=1, replica_groups=mesh['asset'=16,'earn'=4,'age'=4] {'asset'}, dimensions={0} | all-to-all | bytes 2097152 | tf_op jit(solution)/shard_map/all_to_all | solution.py:113
  160.3 3.1 %shard_map.84 = f32[16,32,512]{2,1,0:T(8,128)} custom-call(f32[16,32,512]{2,1,0:T(8,128)} %all_to_all.15.src_ref), custom_call_target="tpu_custom_call" | custom-call | bytes 2097152 | tf_op jit(solution)/shard_map/pallas_call | solution.py:99
  163.4 6.1 %fusion.49 = f32[2,8,32,512]{3,2,0,1:T(8,128)S(1)} fusion(f32[8,512,512]{2,1,0:T(8,128)} %get-tuple-element.16, f32[2,8,32,512]{3,2,1,0:T(8,128)S(1)} %copy-done.2, f32[2,8,32,512]{3,2,1,0:T(8,128)} %bitcast.115), kind=kOutput, calls=%fused_computation.51 | convolution fusion | flops 805830656 | bytes 11534336 | tf_op jit(solution)/shard_map/terc,ecn->tern/dot_general | solution.py:73
  (81 shorter events, 25.0 us)
Async XLA Ops:
  0.0 29.9 %copy-start.3 = (f32[4,8,512]{2,1,0:T(8,128)S(1)}, f32[4,8,512]{2,1,0:T(8,128)}, u32[]{:S(2)}) copy-start(f32[4,8,512]{2,1,0:T(8,128)} %param.13) | copy-start | bytes 196612
  0.0 30.6 %copy-start.4 = (s32[8,512]{1,0:T(8,128)S(1)}, s32[8,512]{1,0:T(8,128)}, u32[]{:S(2)}) copy-start(s32[8,512]{1,0:T(8,128)} %param.12) | copy-start | bytes 49156
  2.6 57.5 %all-to-all-start = ((f32[16,32,512]{2,1,0:T(8,128)}), f32[16,32,512]{2,1,0:T(8,128)S(1)}, u32[]{:S(2)}, u32[]{:S(2)}) async-start(f32[16,32,512]{2,1,0:T(8,128)} %bitcast.29), calls=%async_computation | async-start | bytes 2097152 | tf_op jit(solution)/shard_map/all_to_all | solution.py:113
  15.1 18.9 %collective-permute-start = (f32[1,4,32,512]{3,2,1,0:T(8,128)}, f32[1,4,32,512]{3,2,1,0:T(8,128)S(1)}, u32[]{:S(2)}, u32[]{:S(2)}) collective-permute-start(f32[1,4,32,512]{3,2,1,0:T(8,128)} %get-tuple-element.25), channel_id=1, source_target_pairs={{0,4},{1,5},{2,6},{3,7},{4,8},{5,9},{6,10},{7,11},{8,12},{9,13},{1... | collective-permute-start | bytes 786440 | tf_op jit(solution)/shard_map/ppermute | solution.py:43
  18.5 19.9 %collective-permute-start.2 = (f32[1,4,32,512]{3,2,1,0:T(8,128)}, f32[1,4,32,512]{3,2,1,0:T(8,128)S(1)}, u32[]{:S(2)}, u32[]{:S(2)}) collective-permute-start(f32[1,4,32,512]{3,2,1,0:T(8,128)} %get-tuple-element.26), channel_id=1, source_target_pairs={{1,4},{2,5},{3,6},{5,8},{6,9},{7,10},{9,12},{10,13},{11,14},{17,20... | collective-permute-start | bytes 786440 | tf_op jit(solution)/shard_map/ppermute | solution.py:43
  20.9 17.5 %collective-permute-start.1 = (f32[1,4,32,512]{3,2,1,0:T(8,128)}, f32[1,4,32,512]{3,2,1,0:T(8,128)S(1)}, u32[]{:S(2)}, u32[]{:S(2)}) collective-permute-start(f32[1,4,32,512]{3,2,1,0:T(8,128)} %get-tuple-element.27), channel_id=1, source_target_pairs={{4,0},{5,1},{6,2},{7,3},{8,4},{9,5},{10,6},{11,7},{12,8},{13,9},{1... | collective-permute-start | bytes 786440 | tf_op jit(solution)/shard_map/ppermute | solution.py:43
  23.7 17.5 %collective-permute-start.4 = (f32[1,4,32,512]{3,2,1,0:T(8,128)}, f32[1,4,32,512]{3,2,1,0:T(8,128)}, u32[]{:S(2)}, u32[]{:S(2)}) collective-permute-start(f32[1,4,32,512]{3,2,1,0:T(8,128)} %get-tuple-element.28), channel_id=1, source_target_pairs={{5,0},{6,1},{7,2},{9,4},{10,5},{11,6},{13,8},{14,9},{15,10},{21,16... | collective-permute-start | bytes 786440 | tf_op jit(solution)/shard_map/ppermute | solution.py:43
  27.1 19.6 %collective-permute-start.3 = (f32[1,8,32,512]{3,2,1,0:T(8,128)S(1)}, f32[1,8,32,512]{3,2,1,0:T(8,128)S(1)}, u32[]{:S(2)}, u32[]{:S(2)}) collective-permute-start(f32[1,8,32,512]{3,2,1,0:T(8,128)S(1)} %get-tuple-element.30), channel_id=1, source_target_pairs={{1,0},{2,1},{3,2},{5,4},{6,5},{7,6},{9,8},{10,9},{11,10},{13,12},{... | collective-permute-start | bytes 1572872 | tf_op jit(solution)/shard_map/ppermute | solution.py:43
  60.1 29.2 %all-to-all-start.1 = ((f32[16,32,512]{2,1,0:T(8,128)}), f32[16,32,512]{2,1,0:T(8,128)S(1)}, u32[]{:S(2)}, u32[]{:S(2)}) async-start(f32[16,32,512]{2,1,0:T(8,128)} %bitcast.34), calls=%async_computation.1 | async-start | bytes 2097152 | tf_op jit(solution)/shard_map/all_to_all | solution.py:113
  93.3 28.4 %copy-start.12 = (s32[8]{0:T(128)S(1)}, s32[8]{0:T(128)}, u32[]{:S(2)}) copy-start(s32[8]{0:T(128)} %copy-done.11) | copy-start | bytes 100
  93.3 28.4 %copy-start.14 = (s32[8]{0:T(128)S(1)}, s32[8]{0:T(128)}, u32[]{:S(2)}) copy-start(s32[8]{0:T(128)} %copy-done.13) | copy-start | bytes 100
  93.3 28.4 %copy-start.16 = (s32[8]{0:T(128)S(1)}, s32[8]{0:T(128)}, u32[]{:S(2)}) copy-start(s32[8]{0:T(128)} %copy-done.15) | copy-start | bytes 100
  93.4 28.4 %copy-start.17 = (f32[8]{0:T(128)S(1)}, f32[8]{0:T(128)}, u32[]{:S(2)}) copy-start(f32[8]{0:T(128)} %get-tuple-element.52) | copy-start | bytes 100
  93.4 28.4 %copy-start.18 = (f32[8]{0:T(128)S(1)}, f32[8]{0:T(128)}, u32[]{:S(2)}) copy-start(f32[8]{0:T(128)} %get-tuple-element.53) | copy-start | bytes 100
  93.4 28.4 %copy-start.19 = (f32[8]{0:T(128)S(1)}, f32[8]{0:T(128)}, u32[]{:S(2)}) copy-start(f32[8]{0:T(128)} %get-tuple-element.54) | copy-start | bytes 100
  93.4 28.4 %copy-start.20 = (f32[8]{0:T(128)S(1)}, f32[8]{0:T(128)}, u32[]{:S(2)}) copy-start(f32[8]{0:T(128)} %get-tuple-element.55) | copy-start | bytes 100
  93.4 28.4 %copy-start.21 = (f32[8]{0:T(128)S(1)}, f32[8]{0:T(128)}, u32[]{:S(2)}) copy-start(f32[8]{0:T(128)} %get-tuple-element.56) | copy-start | bytes 100
  93.4 30.2 %slice-start = ((s8[8388608]{0:T(1024)(128)(4,1)}), s8[4194304]{0:T(1024)(128)(4,1)S(1)}, s32[]{:S(2)}) async-start(s8[8388608]{0:T(1024)(128)(4,1)} %bitcast.107), calls=%async_computation.3 | async-start | bytes 8388608
  100.2 21.3 %collective-permute-start.8 = (f32[1,8,32,512]{3,2,0,1:T(8,128)S(1)}, f32[1,8,32,512]{3,2,0,1:T(8,128)S(1)}, u32[]{:S(2)}, u32[]{:S(2)}) collective-permute-start(f32[1,8,32,512]{3,2,0,1:T(8,128)S(1)} %get-tuple-element.24), channel_id=1, source_target_pairs={{1,0},{2,1},{3,2},{5,4},{6,5},{7,6},{9,8},{10,9},{11,10},{13,12},{... | collective-permute-start | bytes 1572872 | tf_op jit(solution)/shard_map/ppermute | solution.py:43
  103.0 11.0 %collective-permute-start.5 = (f32[1,4,32,512]{3,2,0,1:T(8,128)S(1)}, f32[1,4,32,512]{3,2,0,1:T(8,128)S(1)}, u32[]{:S(2)}, u32[]{:S(2)}) collective-permute-start(f32[1,4,32,512]{3,2,0,1:T(8,128)S(1)} %get-tuple-element.19), channel_id=1, source_target_pairs={{0,4},{1,5},{2,6},{3,7},{4,8},{5,9},{6,10},{7,11},{8,12},{9,13},{1... | collective-permute-start | bytes 786440 | tf_op jit(solution)/shard_map/ppermute | solution.py:43
  106.8 7.7 %collective-permute-start.9 = (f32[1,4,32,512]{3,2,0,1:T(8,128)S(1)}, f32[1,4,32,512]{3,2,0,1:T(8,128)S(1)}, u32[]{:S(2)}, u32[]{:S(2)}) collective-permute-start(f32[1,4,32,512]{3,2,0,1:T(8,128)S(1)} %get-tuple-element.20), channel_id=1, source_target_pairs={{5,0},{6,1},{7,2},{9,4},{10,5},{11,6},{13,8},{14,9},{15,10},{21,16... | collective-permute-start | bytes 786440 | tf_op jit(solution)/shard_map/ppermute | solution.py:43
  108.8 7.7 %collective-permute-start.7 = (f32[1,4,32,512]{3,2,0,1:T(8,128)S(1)}, f32[1,4,32,512]{3,2,0,1:T(8,128)S(1)}, u32[]{:S(2)}, u32[]{:S(2)}) collective-permute-start(f32[1,4,32,512]{3,2,0,1:T(8,128)S(1)} %get-tuple-element.21), channel_id=1, source_target_pairs={{1,4},{2,5},{3,6},{5,8},{6,9},{7,10},{9,12},{10,13},{11,14},{17,20... | collective-permute-start | bytes 786440 | tf_op jit(solution)/shard_map/ppermute | solution.py:43
  110.7 10.7 %collective-permute-start.6 = (f32[1,4,32,512]{3,2,0,1:T(8,128)S(1)}, f32[1,4,32,512]{3,2,0,1:T(8,128)S(1)}, u32[]{:S(2)}, u32[]{:S(2)}) collective-permute-start(f32[1,4,32,512]{3,2,0,1:T(8,128)S(1)} %get-tuple-element.22), channel_id=1, source_target_pairs={{4,0},{5,1},{6,2},{7,3},{8,4},{9,5},{10,6},{11,7},{12,8},{13,9},{1... | collective-permute-start | bytes 786440 | tf_op jit(solution)/shard_map/ppermute | solution.py:43
  123.6 39.7 %copy-start.2 = (f32[2,8,32,512]{3,2,1,0:T(8,128)S(1)}, f32[2,8,32,512]{3,2,1,0:T(8,128)}, u32[]{:S(2)}) copy-start(f32[2,8,32,512]{3,2,1,0:T(8,128)} %param.9) | copy-start | bytes 3145732
  (12 other events, 248.4 us)

commit v9 on v8

--- a/solution.py
+++ b/solution.py
@@ -51,11 +51,15 @@
         [moved(current[:1, tail], 1, -1), moved(current[:1], 0, -1), moved(current[:1, head], -1, -1)],
         axis=1,
     )
-    return jnp.concatenate([here, above], axis=0)
+    return here, above
 
 
 def continuation(current, earn_prob, support_start):
-    padded = neighbours(current)
+    return jnp.concatenate(mixed(current, earn_prob, support_start), axis=0)
+
+
+def mixed(current, earn_prob, support_start):
+    chunks = neighbours(current)
     states_here = current.shape[1]
     first_state = lax.axis_index("earn") * states_here
     slots = jnp.arange(states_here + 2 * REACH, dtype=jnp.int32)
@@ -66,7 +70,9 @@
         mixing = mixing + jnp.where(
             slots[None, :] == target[:, None], (earn_prob[number] / prob_sum)[:, None], 0.0
         )
-    return jnp.einsum("ij,tjxy->tixy", mixing, padded, precision=lax.Precision.HIGH)
+    return tuple(
+        jnp.einsum("ij,tjxy->tixy", mixing, padded, precision=lax.Precision.HIGH) for padded in chunks
+    )
 
 
 def along_lanes(stacked, matrix):
@@ -92,9 +98,8 @@
                 dst_ref[k * slabs + s, :, pl.ds(w * 128, 128)] = outs[s]
 
 
-def regroup(got):
+def regroup(got, width):
     count, piece, lanes = got.shape
-    width = lanes // count
     nbytes = got.size * got.dtype.itemsize
     return pl.pallas_call(
         _gather_kernel,
@@ -111,7 +116,7 @@
     piece = lanes // count
     flat = stacked.reshape(ages * states * rows, lanes).T.reshape(count, piece, ages * states * rows)
     got = lax.all_to_all(flat, "asset", 0, 0, tiled=True)
-    return regroup(got).reshape(ages, states, piece, count * rows)
+    return regroup(got, rows).reshape(ages, states, piece, count * rows)
 
 
 def local(
@@ -135,9 +140,8 @@
     adjusted = along_lanes(flipped(saved), illiquid_map)
     current = flipped(utility) + DISCOUNT * adjusted
 
-    expected = continuation(current, earn_prob, support_start)
-    moved = along_lanes(expected, illiquid_map)
-    adjusted = along_lanes(flipped(moved), liquid_map)
+    back = [flipped(along_lanes(part, illiquid_map)) for part in mixed(current, earn_prob, support_start)]
+    adjusted = along_lanes(jnp.concatenate(back, axis=0), liquid_map)
     return utility + DISCOUNT * adjusted
 
 

time: 173 us -> 180 us (1.040)
  blocking collectives: 33.3 us -> 0 us
  waiting for transfers between devices: 22 us -> 39 us
  starting transfers between devices: 46.5 us -> 58.5 us
  matrix products: 28.2 us -> 34.8 us
  local copies, waits for them, and re-layouts: 10.9 us -> 15.3 us
    all_to_all x1 -> x0, blocking collectives: 33.3 us -> none  [flipped(): got = lax.all_to_all(flat, 'asset', 0, 0, tiled=True)]
    all_to_all x2 -> x4, waiting for transfers between devices: 1.85 us -> 23.3 us  [flipped(): got = lax.all_to_all(flat, 'asset', 0, 0, tiled=True)]
    all_to_all x2 -> x4, starting transfers between devices: 19.3 us -> 29.6 us  [flipped(): got = lax.all_to_all(flat, 'asset', 0, 0, tiled=True)]
    dot_general x4 -> x5, matrix products: 24 us -> 29.6 us  [along_lanes(): jnp.einsum('terc,ecn->tern', stacked, matrix, precision=lax.Precision.HIGH)]
    ppermute x10, waiting for transfers between devices: 20.1 us -> 15.7 us  [moved(): return lax.ppermute(value, axes, pairs)]
    unnamed x48 -> x60, local copies, waits for them, and re-layouts: 1.07 us -> 5.3 us
    reshape x1 -> x3, local copies, waits for them, and re-layouts: 2.56 us -> 4.63 us  [flipped(): stacked.reshape(ages * states * rows, lanes)]
    pallas_call x3 -> x4, Pallas kernels: 9.25 us -> 10.8 us  [regroup(): pl.pallas_call(_gather_kernel, in_specs=[pl.BlockSpec(memory_space=pltpu....]
  transfers between devices with their start and end apart: 12 -> 14, of which waited for: 7 -> 8; matrix products, arithmetic and copies ran while one was open for 21% -> 28% of each run, Pallas kernels for 2% -> 3%
where the time goes in v9:
time: 180 us; the launch traced here: 177 us
  starting transfers between devices  58.5 us (32%)
  waiting for transfers between devices  39 us (22%)
  matrix products  34.8 us (19%)
  other arithmetic  18.3 us (10%)
  local copies, waits for them, and re-layouts  15.3 us (8%)
  Pallas kernels  10.8 us (6%)
    all_to_all x4, starting transfers between devices, flipped(): got = lax.all_to_all(flat, 'asset', 0, 0, tiled=True)  29.6 us
    dot_general x5, matrix products, along_lanes(): jnp.einsum('terc,ecn->tern', stacked, matrix, precision=lax.Precision.HIGH)  29.6 us
    ppermute x10, starting transfers between devices, moved(): return lax.ppermute(value, axes, pairs)  28.9 us
    all_to_all x4, waiting for transfers between devices, flipped(): got = lax.all_to_all(flat, 'asset', 0, 0, tiled=True)  23.3 us
    ppermute x10, waiting for transfers between devices, moved(): return lax.ppermute(value, axes, pairs)  15.7 us
    add x1, other arithmetic, band_matrix(): matrix + jnp.where(positions[None, :, None] == (offset + number)[:, None,...  15.2 us
    pallas_call x4, Pallas kernels, regroup(): pl.pallas_call(_gather_kernel, in_specs=[pl.BlockSpec(memory_space=pltpu....  10.8 us
    unnamed x60, local copies, waits for them, and re-layouts  5.3 us
  transfers between devices with their start and end apart: 14, of which 8 were waited for; matrix products, arithmetic and copies ran while one was open for 28% of the time, Pallas kernels for 3%

profile of v9, /device:TPU:34, one launch (start us, length us, event | category | flops | bytes accessed | tf_op | source)
XLA Modules:
  0.0 177.4 jit_solution(7423679950293613290)
XLA Ops:
  0.0 2.6 %copy.35 = f32[512,512]{0,1:T(8,128)} copy(f32[512,512]{1,0:T(8,128)} %bitcast.145) | data formatting | bytes 2097152 | tf_op jit(solution)/shard_map/reshape | solution.py:117
  2.6 10.3 %all-to-all-start = ((f32[16,32,512]{2,1,0:T(8,128)}), f32[16,32,512]{2,1,0:T(8,128)S(1)}, u32[]{:S(2)}, u32[]{:S(2)}) async-start(f32[16,32,512]{2,1,0:T(8,128)} %bitcast.31), calls=%async_computation | async-start | bytes 2097152 | tf_op jit(solution)/shard_map/all_to_all | solution.py:118
  20.1 4.2 %collective-permute-start.2 = (f32[1,4,32,512]{3,1,2,0:T(4,128)}, f32[1,4,32,512]{3,1,2,0:T(4,128)}, u32[]{:S(2)}, u32[]{:S(2)}) collective-permute-start(f32[1,4,32,512]{3,1,2,0:T(4,128)} %copy.55), channel_id=1, source_target_pairs={{1,4},{2,5},{3,6},{5,8},{6,9},{7,10},{9,12},{10,13},{11,14},{17,20... | collective-permute-start | bytes 786440 | tf_op jit(solution)/shard_map/ppermute | solution.py:43
  25.2 4.1 %collective-permute-start = (f32[1,4,32,512]{3,1,2,0:T(4,128)}, f32[1,4,32,512]{3,1,2,0:T(4,128)}, u32[]{:S(2)}, u32[]{:S(2)}) collective-permute-start(f32[1,4,32,512]{3,1,2,0:T(4,128)} %copy.52), channel_id=1, source_target_pairs={{0,4},{1,5},{2,6},{3,7},{4,8},{5,9},{6,10},{7,11},{8,12},{9,13},{1... | collective-permute-start | bytes 786440 | tf_op jit(solution)/shard_map/ppermute | solution.py:43
  38.3 2.9 %collective-permute-done.2 = f32[1,4,32,512]{3,1,2,0:T(4,128)} collective-permute-done((f32[1,4,32,512]{3,1,2,0:T(4,128)}, f32[1,4,32,512]{3,1,2,0:T(4,128)}, u32[]{:S(2)}, u32[]{:S(2)}) %collective-permute-start.2) | collective-permute-done | bytes 262176 | tf_op jit(solution)/shard_map/ppermute | solution.py:43
  41.2 5.5 %collective-permute-done.3 = f32[1,8,32,512]{3,1,2,0:T(8,128)} collective-permute-done((f32[1,8,32,512]{3,1,2,0:T(8,128)S(1)}, f32[1,8,32,512]{3,1,2,0:T(8,128)}, u32[]{:S(2)}, u32[]{:S(2)}) %collective-permute-start.3) | collective-permute-done | bytes 524320 | tf_op jit(solution)/shard_map/ppermute | solution.py:43
  48.7 8.3 %fusion.22 = f32[2,8,32,512]{3,2,0,1:T(8,128)S(1)} fusion(f32[8,512]{1,0:T(8,128)} %get-tuple-element.42, s32[8,512]{1,0:T(8,128)S(1)} %get-tuple-element.51, f32[8,512]{1,0:T(8,128)} %get-tuple-element.40, s32[8,512]{1,0:T(8,128)S(1)} %get-tuple-element.50, f32[8,512]{1,0:T(8,128)} %get-tuple-element.41, s32[8,512]{1,0:T(8,128)S(1)} %get-tuple-element.49, ...), kind=kOutput, calls=%fused_computation.36 | convolution fusion | flops 828375040 | bytes 2228224 | tf_op jit(solution)/shard_map/terc,ecn->tern/dot_general | solution.py:79
  58.5 9.0 %all-to-all-start.1 = ((f32[16,32,512]{2,1,0:T(8,128)}), f32[16,32,512]{2,1,0:T(8,128)S(1)}, u32[]{:S(2)}, u32[]{:S(2)}) async-start(f32[16,32,512]{2,1,0:T(8,128)} %bitcast.37), calls=%async_computation.1 | async-start | bytes 2097152 | tf_op jit(solution)/shard_map/all_to_all | solution.py:118
  67.4 15.2 %select_add_fusion = (f32[8,512,512]{2,1,0:T(8,128)}, f32[8,512,512]{2,1,0:T(8,128)}) fusion(f32[8,512]{1,0:T(8,128)S(1)} %get-tuple-element.32, s32[8,512]{1,0:T(8,128)S(1)} %get-tuple-element.44, f32[8,512]{1,0:T(8,128)S(1)} %get-tuple-element.33, s32[8,512]{1,0:T(8,128)S(1)} %get-tuple-element.45, f32[8,512]{1,0:T(8,128)S(1)} %get-tuple-element.34, ...), kind=kLoop, calls=%fused_computation.6 | loop fusion | flops 46137344 | bytes 17039360 | tf_op jit(solution)/shard_map/add | solution.py:22
  82.7 3.1 %shard_map.82 = f32[16,32,512]{2,1,0:T(8,128)} custom-call(f32[16,32,512]{2,1,0:T(8,128)} %copy-done.1), custom_call_target="tpu_custom_call" | custom-call | bytes 2097152 | tf_op jit(solution)/shard_map/pallas_call | solution.py:104
  87.5 3.1 %shard_map.83 = f32[16,32,512]{2,1,0:T(8,128)} custom-call(f32[16,32,512]{2,1,0:T(8,128)} %copy-done.2), custom_call_target="tpu_custom_call" | custom-call | bytes 2097152 | tf_op jit(solution)/shard_map/pallas_call | solution.py:104
  90.7 6.6 %fusion.40 = f32[2,8,32,512]{3,2,0,1:T(8,128)S(1)} fusion(f32[8,512,512]{2,1,0:T(8,128)} %get-tuple-element.17, f32[2,8,32,512]{3,2,1,0:T(8,128)} %bitcast.146, f32[2,8,32,512]{3,2,1,0:T(8,128)} %bitcast.147), kind=kOutput, calls=%fused_computation.42 | convolution fusion | flops 805830656 | bytes 11534336 | tf_op jit(solution)/shard_map/terc,ecn->tern/dot_general | solution.py:79
  98.1 3.2 %collective-permute-start.5 = (f32[1,4,32,512]{3,2,0,1:T(8,128)S(1)}, f32[1,4,32,512]{3,2,0,1:T(8,128)S(1)}, u32[]{:S(2)}, u32[]{:S(2)}) collective-permute-start(f32[1,4,32,512]{3,2,0,1:T(8,128)S(1)} %get-tuple-element.19), channel_id=1, source_target_pairs={{0,4},{1,5},{2,6},{3,7},{4,8},{5,9},{6,10},{7,11},{8,12},{9,13},{1... | collective-permute-start | bytes 786440 | tf_op jit(solution)/shard_map/ppermute | solution.py:43
  101.2 3.8 %collective-permute-start.9 = (f32[1,4,32,512]{3,2,0,1:T(8,128)}, f32[1,4,32,512]{3,2,0,1:T(8,128)S(1)}, u32[]{:S(2)}, u32[]{:S(2)}) collective-permute-start(f32[1,4,32,512]{3,2,0,1:T(8,128)} %get-tuple-element.20), channel_id=1, source_target_pairs={{5,0},{6,1},{7,2},{9,4},{10,5},{11,6},{13,8},{14,9},{15,10},{21,16... | collective-permute-start | bytes 786440 | tf_op jit(solution)/shard_map/ppermute | solution.py:43
  105.0 2.9 %collective-permute-start.7 = (f32[1,4,32,512]{3,2,0,1:T(8,128)S(1)}, f32[1,4,32,512]{3,2,0,1:T(8,128)S(1)}, u32[]{:S(2)}, u32[]{:S(2)}) collective-permute-start(f32[1,4,32,512]{3,2,0,1:T(8,128)S(1)} %get-tuple-element.21), channel_id=1, source_target_pairs={{1,4},{2,5},{3,6},{5,8},{6,9},{7,10},{9,12},{10,13},{11,14},{17,20... | collective-permute-start | bytes 786440 | tf_op jit(solution)/shard_map/ppermute | solution.py:43
  108.0 2.7 %collective-permute-start.6 = (f32[1,4,32,512]{3,2,0,1:T(8,128)S(1)}, f32[1,4,32,512]{3,2,0,1:T(8,128)S(1)}, u32[]{:S(2)}, u32[]{:S(2)}) collective-permute-start(f32[1,4,32,512]{3,2,0,1:T(8,128)S(1)} %get-tuple-element.22), channel_id=1, source_target_pairs={{4,0},{5,1},{6,2},{7,3},{8,4},{9,5},{10,6},{11,7},{12,8},{13,9},{1... | collective-permute-start | bytes 786440 | tf_op jit(solution)/shard_map/ppermute | solution.py:43
  113.0 6.0 %collective-permute-done.6 = f32[1,4,32,512]{3,2,0,1:T(8,128)S(1)} collective-permute-done((f32[1,4,32,512]{3,2,0,1:T(8,128)S(1)}, f32[1,4,32,512]{3,2,0,1:T(8,128)S(1)}, u32[]{:S(2)}, u32[]{:S(2)}) %collective-permute-start.6) | collective-permute-done | bytes 262176 | tf_op jit(solution)/shard_map/ppermute | solution.py:43
  120.1 2.6 %fusion.58 = f32[8,512,32]{1,2,0:T(8,128)S(1)} fusion(f32[8,512,512]{2,1,0:T(8,128)S(1)} %bitcast.143, f32[8,32,512]{2,0,1:T(8,128)S(1)} %convolution_bitcast_fusion.1), kind=kOutput, calls=%fused_computation.68 | convolution fusion | flops 402653184 | bytes 9437184 | tf_op jit(solution)/shard_map/terc,ecn->tern/dot_general | solution.py:79
  123.8 6.8 %all-to-all-start.2 = ((f32[16,32,256]{2,1,0:T(8,128)}), f32[16,32,256]{2,1,0:T(8,128)S(1)}, u32[]{:S(2)}, u32[]{:S(2)}) async-start(f32[16,32,256]{2,1,0:T(8,128)} %bitcast.48), calls=%async_computation.2 | async-start | bytes 1048576 | tf_op jit(solution)/shard_map/all_to_all | solution.py:118
  131.7 5.9 %fusion.56 = f32[8,512,32]{1,2,0:T(8,128)S(1)} fusion(f32[8,512,512]{2,1,0:T(8,128)} %get-tuple-element.17, f32[8,32,512]{2,0,1:T(8,128)S(1)} %convolution_bitcast_fusion), kind=kOutput, calls=%fused_computation.66 | convolution fusion | flops 402653184 | bytes 9437184 | tf_op jit(solution)/shard_map/terc,ecn->tern/dot_general | solution.py:79
  138.6 8.7 %all-to-all-done.2.src_ref = f32[16,32,256]{2,1,0:T(8,128)S(1)} async-done(((f32[16,32,256]{2,1,0:T(8,128)}), f32[16,32,256]{2,1,0:T(8,128)S(1)}, u32[]{:S(2)}, u32[]{:S(2)}) %all-to-all-start.2) | async-done | bytes 524320 | tf_op jit(solution)/shard_map/all_to_all | solution.py:118
  147.3 3.6 %all-to-all-start.3 = ((f32[16,32,256]{2,1,0:T(8,128)}), f32[16,32,256]{2,1,0:T(8,128)S(1)}, u32[]{:S(2)}, u32[]{:S(2)}) async-start(f32[16,32,256]{2,1,0:T(8,128)} %bitcast.58), calls=%async_computation.3 | async-start | bytes 1048576 | tf_op jit(solution)/shard_map/all_to_all | solution.py:118
  153.2 13.9 %all-to-all-done.3.src_ref = f32[16,32,256]{2,1,0:T(8,128)S(1)} async-done(((f32[16,32,256]{2,1,0:T(8,128)}), f32[16,32,256]{2,1,0:T(8,128)S(1)}, u32[]{:S(2)}, u32[]{:S(2)}) %all-to-all-start.3) | async-done | bytes 524320 | tf_op jit(solution)/shard_map/all_to_all | solution.py:118
  170.2 6.1 %fusion.31 = f32[2,8,32,512]{3,2,0,1:T(8,128)S(1)} fusion(f32[8,512,512]{2,1,0:T(8,128)} %get-tuple-element.16, f32[2,8,32,512]{3,2,1,0:T(8,128)S(1)} %copy-done.3, f32[1,8,32,512]{3,2,1,0:T(8,128)} %bitcast.149, f32[1,8,32,512]{3,2,1,0:T(8,128)} %bitcast.148), kind=kOutput, calls=%fused_computation.39 | convolution fusion | flops 806092800 | bytes 11534336 | tf_op jit(solution)/shard_map/terc,ecn->tern/dot_general | solution.py:79
  (101 shorter events, 35.6 us)
Async XLA Ops:
  0.0 29.3 %copy-start = (f32[2,8,32,512]{3,2,1,0:T(8,128)S(1)}, f32[2,8,32,512]{3,2,1,0:T(8,128)}, u32[]{:S(2)}) copy-start(f32[2,8,32,512]{3,2,1,0:T(8,128)} %param.8) | copy-start | bytes 3145732
  0.0 31.7 %copy-start.7 = (s32[8,512]{1,0:T(8,128)S(1)}, s32[8,512]{1,0:T(8,128)}, u32[]{:S(2)}) copy-start(s32[8,512]{1,0:T(8,128)} %param.12) | copy-start | bytes 49156
  0.0 31.7 %copy-start.6 = (f32[4,8,512]{2,1,0:T(8,128)S(1)}, f32[4,8,512]{2,1,0:T(8,128)}, u32[]{:S(2)}) copy-start(f32[4,8,512]{2,1,0:T(8,128)} %param.13) | copy-start | bytes 196612
  2.6 55.8 %all-to-all-start = ((f32[16,32,512]{2,1,0:T(8,128)}), f32[16,32,512]{2,1,0:T(8,128)S(1)}, u32[]{:S(2)}, u32[]{:S(2)}) async-start(f32[16,32,512]{2,1,0:T(8,128)} %bitcast.31), calls=%async_computation | async-start | bytes 2097152 | tf_op jit(solution)/shard_map/all_to_all | solution.py:118
  14.4 23.9 %collective-permute-start.4 = (f32[1,4,32,512]{3,1,2,0:T(4,128)S(1)}, f32[1,4,32,512]{3,1,2,0:T(4,128)}, u32[]{:S(2)}, u32[]{:S(2)}) collective-permute-start(f32[1,4,32,512]{3,1,2,0:T(4,128)S(1)} %copy.57), channel_id=1, source_target_pairs={{5,0},{6,1},{7,2},{9,4},{10,5},{11,6},{13,8},{14,9},{15,10},{21,16... | collective-permute-start | bytes 786440 | tf_op jit(solution)/shard_map/ppermute | solution.py:43
  17.3 18.2 %collective-permute-start.1 = (f32[1,4,32,512]{3,1,2,0:T(4,128)}, f32[1,4,32,512]{3,1,2,0:T(4,128)}, u32[]{:S(2)}, u32[]{:S(2)}) collective-permute-start(f32[1,4,32,512]{3,1,2,0:T(4,128)} %copy.54), channel_id=1, source_target_pairs={{4,0},{5,1},{6,2},{7,3},{8,4},{9,5},{10,6},{11,7},{12,8},{13,9},{1... | collective-permute-start | bytes 786440 | tf_op jit(solution)/shard_map/ppermute | solution.py:43
  20.1 21.1 %collective-permute-start.2 = (f32[1,4,32,512]{3,1,2,0:T(4,128)}, f32[1,4,32,512]{3,1,2,0:T(4,128)}, u32[]{:S(2)}, u32[]{:S(2)}) collective-permute-start(f32[1,4,32,512]{3,1,2,0:T(4,128)} %copy.55), channel_id=1, source_target_pairs={{1,4},{2,5},{3,6},{5,8},{6,9},{7,10},{9,12},{10,13},{11,14},{17,20... | collective-permute-start | bytes 786440 | tf_op jit(solution)/shard_map/ppermute | solution.py:43
  25.2 10.9 %collective-permute-start = (f32[1,4,32,512]{3,1,2,0:T(4,128)}, f32[1,4,32,512]{3,1,2,0:T(4,128)}, u32[]{:S(2)}, u32[]{:S(2)}) collective-permute-start(f32[1,4,32,512]{3,1,2,0:T(4,128)} %copy.52), channel_id=1, source_target_pairs={{0,4},{1,5},{2,6},{3,7},{4,8},{5,9},{6,10},{7,11},{8,12},{9,13},{1... | collective-permute-start | bytes 786440 | tf_op jit(solution)/shard_map/ppermute | solution.py:43
  29.7 17.0 %collective-permute-start.3 = (f32[1,8,32,512]{3,1,2,0:T(8,128)S(1)}, f32[1,8,32,512]{3,1,2,0:T(8,128)}, u32[]{:S(2)}, u32[]{:S(2)}) collective-permute-start(f32[1,8,32,512]{3,1,2,0:T(8,128)S(1)} %copy.56), channel_id=1, source_target_pairs={{1,0},{2,1},{3,2},{5,4},{6,5},{7,6},{9,8},{10,9},{11,10},{13,12},{... | collective-permute-start | bytes 1572872 | tf_op jit(solution)/shard_map/ppermute | solution.py:43
  58.5 28.0 %all-to-all-start.1 = ((f32[16,32,512]{2,1,0:T(8,128)}), f32[16,32,512]{2,1,0:T(8,128)S(1)}, u32[]{:S(2)}, u32[]{:S(2)}) async-start(f32[16,32,512]{2,1,0:T(8,128)} %bitcast.37), calls=%async_computation.1 | async-start | bytes 2097152 | tf_op jit(solution)/shard_map/all_to_all | solution.py:118
  90.6 29.5 %slice-start = ((s8[8388608]{0:T(1024)(128)(4,1)}), s8[4194304]{0:T(1024)(128)(4,1)S(1)}, s32[]{:S(2)}) async-start(s8[8388608]{0:T(1024)(128)(4,1)} %bitcast.142), calls=%async_computation.4 | async-start | bytes 8388608
  90.6 28.5 %copy-start.17 = (s32[8]{0:T(128)S(1)}, s32[8]{0:T(128)}, u32[]{:S(2)}) copy-start(s32[8]{0:T(128)} %copy-done.16) | copy-start | bytes 100
  90.6 28.5 %copy-start.19 = (s32[8]{0:T(128)S(1)}, s32[8]{0:T(128)}, u32[]{:S(2)}) copy-start(s32[8]{0:T(128)} %copy-done.18) | copy-start | bytes 100
  90.6 28.5 %copy-start.20 = (f32[8]{0:T(128)S(1)}, f32[8]{0:T(128)}, u32[]{:S(2)}) copy-start(f32[8]{0:T(128)} %get-tuple-element.52) | copy-start | bytes 100
  90.6 28.5 %copy-start.21 = (f32[8]{0:T(128)S(1)}, f32[8]{0:T(128)}, u32[]{:S(2)}) copy-start(f32[8]{0:T(128)} %get-tuple-element.53) | copy-start | bytes 100
  90.7 29.5 %slice-start.1 = ((s8[8388608]{0:T(1024)(128)(4,1)}), s8[4194304]{0:T(1024)(128)(4,1)S(1)}, s32[]{:S(2)}) async-start(s8[8388608]{0:T(1024)(128)(4,1)} %bitcast.142), calls=%async_computation.5 | async-start | bytes 8388608
  98.1 14.9 %collective-permute-start.5 = (f32[1,4,32,512]{3,2,0,1:T(8,128)S(1)}, f32[1,4,32,512]{3,2,0,1:T(8,128)S(1)}, u32[]{:S(2)}, u32[]{:S(2)}) collective-permute-start(f32[1,4,32,512]{3,2,0,1:T(8,128)S(1)} %get-tuple-element.19), channel_id=1, source_target_pairs={{0,4},{1,5},{2,6},{3,7},{4,8},{5,9},{6,10},{7,11},{8,12},{9,13},{1... | collective-permute-start | bytes 786440 | tf_op jit(solution)/shard_map/ppermute | solution.py:43
  101.2 29.4 %collective-permute-start.9 = (f32[1,4,32,512]{3,2,0,1:T(8,128)}, f32[1,4,32,512]{3,2,0,1:T(8,128)S(1)}, u32[]{:S(2)}, u32[]{:S(2)}) collective-permute-start(f32[1,4,32,512]{3,2,0,1:T(8,128)} %get-tuple-element.20), channel_id=1, source_target_pairs={{5,0},{6,1},{7,2},{9,4},{10,5},{11,6},{13,8},{14,9},{15,10},{21,16... | collective-permute-start | bytes 786440 | tf_op jit(solution)/shard_map/ppermute | solution.py:43
  105.0 25.6 %collective-permute-start.7 = (f32[1,4,32,512]{3,2,0,1:T(8,128)S(1)}, f32[1,4,32,512]{3,2,0,1:T(8,128)S(1)}, u32[]{:S(2)}, u32[]{:S(2)}) collective-permute-start(f32[1,4,32,512]{3,2,0,1:T(8,128)S(1)} %get-tuple-element.21), channel_id=1, source_target_pairs={{1,4},{2,5},{3,6},{5,8},{6,9},{7,10},{9,12},{10,13},{11,14},{17,20... | collective-permute-start | bytes 786440 | tf_op jit(solution)/shard_map/ppermute | solution.py:43
  108.0 11.0 %collective-permute-start.6 = (f32[1,4,32,512]{3,2,0,1:T(8,128)S(1)}, f32[1,4,32,512]{3,2,0,1:T(8,128)S(1)}, u32[]{:S(2)}, u32[]{:S(2)}) collective-permute-start(f32[1,4,32,512]{3,2,0,1:T(8,128)S(1)} %get-tuple-element.22), channel_id=1, source_target_pairs={{4,0},{5,1},{6,2},{7,3},{8,4},{9,5},{10,6},{11,7},{12,8},{13,9},{1... | collective-permute-start | bytes 786440 | tf_op jit(solution)/shard_map/ppermute | solution.py:43
  110.8 19.8 %collective-permute-start.8 = (f32[1,8,32,512]{3,2,0,1:T(8,128)S(1)}, f32[1,8,32,512]{3,2,0,1:T(8,128)S(1)}, u32[]{:S(2)}, u32[]{:S(2)}) collective-permute-start(f32[1,8,32,512]{3,2,0,1:T(8,128)S(1)} %get-tuple-element.24), channel_id=1, source_target_pairs={{1,0},{2,1},{3,2},{5,4},{6,5},{7,6},{9,8},{10,9},{11,10},{13,12},{... | collective-permute-start | bytes 1572872 | tf_op jit(solution)/shard_map/ppermute | solution.py:43
  123.8 23.5 %all-to-all-start.2 = ((f32[16,32,256]{2,1,0:T(8,128)}), f32[16,32,256]{2,1,0:T(8,128)S(1)}, u32[]{:S(2)}, u32[]{:S(2)}) async-start(f32[16,32,256]{2,1,0:T(8,128)} %bitcast.48), calls=%async_computation.2 | async-start | bytes 1048576 | tf_op jit(solution)/shard_map/all_to_all | solution.py:118
  130.6 39.6 %copy-start.3 = (f32[2,8,32,512]{3,2,1,0:T(8,128)S(1)}, f32[2,8,32,512]{3,2,1,0:T(8,128)}, u32[]{:S(2)}) copy-start(f32[2,8,32,512]{3,2,1,0:T(8,128)} %param.9) | copy-start | bytes 3145732
  147.3 19.8 %all-to-all-start.3 = ((f32[16,32,256]{2,1,0:T(8,128)}), f32[16,32,256]{2,1,0:T(8,128)S(1)}, u32[]{:S(2)}, u32[]{:S(2)}) async-start(f32[16,32,256]{2,1,0:T(8,128)} %bitcast.58), calls=%async_computation.3 | async-start | bytes 1048576 | tf_op jit(solution)/shard_map/all_to_all | solution.py:118
  (17 other events, 285.8 us)

commit v10 on v8

--- a/solution.py
+++ b/solution.py
@@ -55,8 +55,11 @@
 
 
 def continuation(current, earn_prob, support_start):
-    padded = neighbours(current)
-    states_here = current.shape[1]
+    return mix(neighbours(current), earn_prob, support_start)
+
+
+def mix(padded, earn_prob, support_start):
+    states_here = padded.shape[1] - 2 * REACH
     first_state = lax.axis_index("earn") * states_here
     slots = jnp.arange(states_here + 2 * REACH, dtype=jnp.int32)
     prob_sum = jnp.sum(earn_prob, axis=0)
@@ -124,7 +127,8 @@
     illiquid_offset,
     illiquid_weight,
 ):
-    expected = continuation(values, earn_prob, support_start)
+    padded, utility = lax.optimization_barrier((neighbours(values), utility))
+    expected = mix(padded, earn_prob, support_start)
     saved = along_lanes(expected, band_matrix(liquid_offset, liquid_weight))
     saved, illiquid_offset, illiquid_weight, liquid_offset, liquid_weight = lax.optimization_barrier(
         (saved, illiquid_offset, illiquid_weight, liquid_offset, liquid_weight)

time: 173 us -> 188 us (1.087)
  waiting for transfers between devices: 22 us -> 32.3 us
  starting transfers between devices: 46.5 us -> 55.9 us
    all_to_all x2, waiting for transfers between devices: 1.85 us -> 21.7 us  [flipped(): got = lax.all_to_all(flat, 'asset', 0, 0, tiled=True)]
    ppermute x10, starting transfers between devices: 27.2 us -> 36.9 us  [moved(): return lax.ppermute(value, axes, pairs)]
    ppermute x10, waiting for transfers between devices: 20.1 us -> 10.6 us  [moved(): return lax.ppermute(value, axes, pairs)]
  transfers between devices with their start and end apart: 12 -> 12, of which waited for: 7 -> 6; matrix products, arithmetic and copies ran while one was open for 21% -> 12% of each run, Pallas kernels for 2% -> 2%
where the time goes in v10:
time: 188 us; the launch traced here: 185 us
  starting transfers between devices  55.9 us (30%)
  waiting for transfers between devices  32.3 us (17%)
  blocking collectives  32.3 us (17%)
  matrix products  26.7 us (14%)
  other arithmetic  18.7 us (10%)
  local copies, waits for them, and re-layouts  9.47 us (5%)
  Pallas kernels  9.21 us (5%)
    ppermute x10, starting transfers between devices, moved(): return lax.ppermute(value, axes, pairs)  36.9 us
    all_to_all x1, blocking collectives, flipped(): got = lax.all_to_all(flat, 'asset', 0, 0, tiled=True)  32.3 us
    dot_general x4, matrix products, along_lanes(): jnp.einsum('terc,ecn->tern', stacked, matrix, precision=lax.Precision.HIGH)  23.2 us
    all_to_all x2, waiting for transfers between devices, flipped(): got = lax.all_to_all(flat, 'asset', 0, 0, tiled=True)  21.7 us
    all_to_all x2, starting transfers between devices, flipped(): got = lax.all_to_all(flat, 'asset', 0, 0, tiled=True)  19 us
    add x1, other arithmetic, band_matrix(): matrix + jnp.where(positions[None, :, None] == (offset + number)[:, None,...  15.3 us
    ppermute x10, waiting for transfers between devices, moved(): return lax.ppermute(value, axes, pairs)  10.6 us
    pallas_call x3, Pallas kernels, regroup(): pl.pallas_call(_gather_kernel, in_specs=[pl.BlockSpec(memory_space=pltpu....  9.21 us
  transfers between devices with their start and end apart: 12, of which 6 were waited for; matrix products, arithmetic and copies ran while one was open for 12% of the time, Pallas kernels for 2%

profile of v10, /device:TPU:34, one launch (start us, length us, event | category | flops | bytes accessed | tf_op | source)
XLA Modules:
  0.0 185.0 jit_solution(4323861273097722152)
XLA Ops:
  0.0 2.0 %fusion.88 = (f32[1,4,32,512]{3,2,1,0:T(8,128)}, f32[1,4,32,512]{3,2,1,0:T(8,128)S(1)}, f32[1,4,32,512]{3,2,1,0:T(8,128)S(1)}, f32[1,4,32,512]{3,2,1,0:T(8,128)S(1)}) fusion(f32[2,8,32,512]{3,2,1,0:T(8,128)} %param.8), kind=kLoop, calls=%fused_computation.124 | loop fusion | bytes 2097152 | tf_op jit(solution)/shard_map/slice | solution.py:48
  2.0 3.4 %collective-permute-start = (f32[1,4,32,512]{3,2,1,0:T(8,128)}, f32[1,4,32,512]{3,2,1,0:T(8,128)S(1)}, u32[]{:S(2)}, u32[]{:S(2)}) collective-permute-start(f32[1,4,32,512]{3,2,1,0:T(8,128)} %get-tuple-element.29), channel_id=1, source_target_pairs={{0,4},{1,5},{2,6},{3,7},{4,8},{5,9},{6,10},{7,11},{8,12},{9,13},{1... | collective-permute-start | bytes 786440 | tf_op jit(solution)/shard_map/ppermute | solution.py:43
  5.4 1.9 %collective-permute-start.2 = (f32[1,4,32,512]{3,2,1,0:T(8,128)S(1)}, f32[1,4,32,512]{3,2,1,0:T(8,128)S(1)}, u32[]{:S(2)}, u32[]{:S(2)}) collective-permute-start(f32[1,4,32,512]{3,2,1,0:T(8,128)S(1)} %get-tuple-element.30), channel_id=1, source_target_pairs={{1,4},{2,5},{3,6},{5,8},{6,9},{7,10},{9,12},{10,13},{11,14},{17,20... | collective-permute-start | bytes 786440 | tf_op jit(solution)/shard_map/ppermute | solution.py:43
  7.3 2.6 %collective-permute-start.1 = (f32[1,4,32,512]{3,2,1,0:T(8,128)S(1)}, f32[1,4,32,512]{3,2,1,0:T(8,128)S(1)}, u32[]{:S(2)}, u32[]{:S(2)}) collective-permute-start(f32[1,4,32,512]{3,2,1,0:T(8,128)S(1)} %get-tuple-element.31), channel_id=1, source_target_pairs={{4,0},{5,1},{6,2},{7,3},{8,4},{9,5},{10,6},{11,7},{12,8},{13,9},{1... | collective-permute-start | bytes 786440 | tf_op jit(solution)/shard_map/ppermute | solution.py:43
  13.2 2.8 %collective-permute-start.3 = (f32[1,8,32,512]{3,2,1,0:T(8,128)S(1)}, f32[1,8,32,512]{3,2,1,0:T(8,128)S(1)}, u32[]{:S(2)}, u32[]{:S(2)}) collective-permute-start(f32[1,8,32,512]{3,2,1,0:T(8,128)S(1)} %get-tuple-element.34), channel_id=1, source_target_pairs={{1,0},{2,1},{3,2},{5,4},{6,5},{7,6},{9,8},{10,9},{11,10},{13,12},{... | collective-permute-start | bytes 1572872 | tf_op jit(solution)/shard_map/ppermute | solution.py:43
  24.6 7.5 %fusion.31 = f32[2,8,32,512]{3,2,0,1:T(8,128)S(1)} fusion(f32[8,512]{1,0:T(8,128)S(1)} %get-tuple-element.46, s32[8,512]{1,0:T(8,128)S(1)} %get-tuple-element.55, f32[8,512]{1,0:T(8,128)S(1)} %get-tuple-element.44, s32[8,512]{1,0:T(8,128)S(1)} %get-tuple-element.54, f32[8,512]{1,0:T(8,128)S(1)} %get-tuple-element.45, s32[8,512]{1,0:T(8,128)S(1)} %get-tuple-element.53, ...), kind=kOutput, calls=%fused_computation.45 | convolution fusion | flops 828375040 | bytes 2228224 | tf_op jit(solution)/shard_map/terc,ecn->tern/dot_general | solution.py:76
  33.6 11.2 %all-to-all-start.1 = ((f32[16,32,512]{2,1,0:T(8,128)}), f32[16,32,512]{2,1,0:T(8,128)S(1)}, u32[]{:S(2)}, u32[]{:S(2)}) async-start(f32[16,32,512]{2,1,0:T(8,128)} %bitcast.34), calls=%async_computation.1 | async-start | bytes 2097152 | tf_op jit(solution)/shard_map/all_to_all | solution.py:116
  46.1 21.5 %all-to-all-done.1.src_ref = f32[16,32,512]{2,1,0:T(8,128)S(1)} async-done(((f32[16,32,512]{2,1,0:T(8,128)}), f32[16,32,512]{2,1,0:T(8,128)S(1)}, u32[]{:S(2)}, u32[]{:S(2)}) %all-to-all-start.1) | async-done | bytes 1048608 | tf_op jit(solution)/shard_map/all_to_all | solution.py:116
  67.7 7.8 %all-to-all-start = ((f32[16,32,512]{2,1,0:T(8,128)}), f32[16,32,512]{2,1,0:T(8,128)S(1)}, u32[]{:S(2)}, u32[]{:S(2)}) async-start(f32[16,32,512]{2,1,0:T(8,128)} %bitcast.29), calls=%async_computation | async-start | bytes 2097152 | tf_op jit(solution)/shard_map/all_to_all | solution.py:116
  75.6 15.3 %select_add_fusion = (f32[8,512,512]{2,1,0:T(8,128)}, f32[8,512,512]{2,1,0:T(8,128)}) fusion(f32[8,512]{1,0:T(8,128)S(1)} %get-tuple-element.36, s32[8,512]{1,0:T(8,128)S(1)} %get-tuple-element.48, f32[8,512]{1,0:T(8,128)S(1)} %get-tuple-element.37, s32[8,512]{1,0:T(8,128)S(1)} %get-tuple-element.49, f32[8,512]{1,0:T(8,128)S(1)} %get-tuple-element.38, ...), kind=kLoop, calls=%fused_computation.8 | loop fusion | flops 46137344 | bytes 17039360 | tf_op jit(solution)/shard_map/add | solution.py:22
  90.8 3.1 %shard_map.83 = f32[16,32,512]{2,1,0:T(8,128)} custom-call(f32[16,32,512]{2,1,0:T(8,128)} %copy-done), custom_call_target="tpu_custom_call" | custom-call | bytes 2097152 | tf_op jit(solution)/shard_map/pallas_call | solution.py:102
  95.0 3.1 %shard_map.82 = f32[16,32,512]{2,1,0:T(8,128)} custom-call(f32[16,32,512]{2,1,0:T(8,128)} %copy-done.1), custom_call_target="tpu_custom_call" | custom-call | bytes 2097152 | tf_op jit(solution)/shard_map/pallas_call | solution.py:102
  98.0 6.6 %fusion.40 = f32[2,8,32,512]{3,2,0,1:T(8,128)S(1)} fusion(f32[8,512,512]{2,1,0:T(8,128)} %get-tuple-element.21, f32[2,8,32,512]{3,2,1,0:T(8,128)} %bitcast.114, f32[2,8,32,512]{3,2,1,0:T(8,128)} %bitcast.113), kind=kOutput, calls=%fused_computation.48 | convolution fusion | flops 805830656 | bytes 11534336 | tf_op jit(solution)/shard_map/terc,ecn->tern/dot_general | solution.py:76
  104.8 11.7 %collective-permute-start.8 = (f32[1,8,32,512]{3,2,0,1:T(8,128)S(1)}, f32[1,8,32,512]{3,2,0,1:T(8,128)S(1)}, u32[]{:S(2)}, u32[]{:S(2)}) collective-permute-start(f32[1,8,32,512]{3,2,0,1:T(8,128)S(1)} %get-tuple-element.28), channel_id=1, source_target_pairs={{1,0},{2,1},{3,2},{5,4},{6,5},{7,6},{9,8},{10,9},{11,10},{13,12},{... | collective-permute-start | bytes 1572872 | tf_op jit(solution)/shard_map/ppermute | solution.py:43
  116.6 3.7 %collective-permute-start.5 = (f32[1,4,32,512]{3,2,0,1:T(8,128)S(1)}, f32[1,4,32,512]{3,2,0,1:T(8,128)S(1)}, u32[]{:S(2)}, u32[]{:S(2)}) collective-permute-start(f32[1,4,32,512]{3,2,0,1:T(8,128)S(1)} %get-tuple-element.23), channel_id=1, source_target_pairs={{0,4},{1,5},{2,6},{3,7},{4,8},{5,9},{6,10},{7,11},{8,12},{9,13},{1... | collective-permute-start | bytes 786440 | tf_op jit(solution)/shard_map/ppermute | solution.py:43
  120.3 3.5 %collective-permute-start.9 = (f32[1,4,32,512]{3,2,0,1:T(8,128)S(1)}, f32[1,4,32,512]{3,2,0,1:T(8,128)S(1)}, u32[]{:S(2)}, u32[]{:S(2)}) collective-permute-start(f32[1,4,32,512]{3,2,0,1:T(8,128)S(1)} %get-tuple-element.24), channel_id=1, source_target_pairs={{5,0},{6,1},{7,2},{9,4},{10,5},{11,6},{13,8},{14,9},{15,10},{21,16... | collective-permute-start | bytes 786440 | tf_op jit(solution)/shard_map/ppermute | solution.py:43
  123.9 2.1 %collective-permute-start.7 = (f32[1,4,32,512]{3,2,0,1:T(8,128)S(1)}, f32[1,4,32,512]{3,2,0,1:T(8,128)S(1)}, u32[]{:S(2)}, u32[]{:S(2)}) collective-permute-start(f32[1,4,32,512]{3,2,0,1:T(8,128)S(1)} %get-tuple-element.25), channel_id=1, source_target_pairs={{1,4},{2,5},{3,6},{5,8},{6,9},{7,10},{9,12},{10,13},{11,14},{17,20... | collective-permute-start | bytes 786440 | tf_op jit(solution)/shard_map/ppermute | solution.py:43
  126.0 3.2 %collective-permute-start.6 = (f32[1,4,32,512]{3,2,0,1:T(8,128)S(1)}, f32[1,4,32,512]{3,2,0,1:T(8,128)S(1)}, u32[]{:S(2)}, u32[]{:S(2)}) collective-permute-start(f32[1,4,32,512]{3,2,0,1:T(8,128)S(1)} %get-tuple-element.26), channel_id=1, source_target_pairs={{4,0},{5,1},{6,2},{7,3},{8,4},{9,5},{10,6},{11,7},{12,8},{13,9},{1... | collective-permute-start | bytes 786440 | tf_op jit(solution)/shard_map/ppermute | solution.py:43
  129.2 2.3 %collective-permute-done.7 = f32[1,4,32,512]{3,2,0,1:T(8,128)S(1)} collective-permute-done((f32[1,4,32,512]{3,2,0,1:T(8,128)S(1)}, f32[1,4,32,512]{3,2,0,1:T(8,128)S(1)}, u32[]{:S(2)}, u32[]{:S(2)}) %collective-permute-start.7) | collective-permute-done | bytes 262176 | tf_op jit(solution)/shard_map/ppermute | solution.py:43
  131.6 5.4 %collective-permute-done.6 = f32[1,4,32,512]{3,2,0,1:T(8,128)S(1)} collective-permute-done((f32[1,4,32,512]{3,2,0,1:T(8,128)S(1)}, f32[1,4,32,512]{3,2,0,1:T(8,128)S(1)}, u32[]{:S(2)}, u32[]{:S(2)}) %collective-permute-start.6) | collective-permute-done | bytes 262176 | tf_op jit(solution)/shard_map/ppermute | solution.py:43
  139.1 2.9 %fusion.28 = f32[2,8,32,512]{3,2,0,1:T(8,128)S(1)} fusion(f32[8,512,512]{2,1,0:T(8,128)S(1)} %bitcast.108, f32[2,32,512,8]{2,3,1,0:T(8,128)S(1)} %fusion.24), kind=kOutput, calls=%fused_computation.44 | convolution fusion | flops 805306368 | bytes 10485760 | tf_op jit(solution)/shard_map/terc,ecn->tern/dot_general | solution.py:76
  142.4 32.3 %all_to_all.15.src_ref = f32[16,32,512]{2,1,0:T(8,128)} all-to-all(f32[16,32,512]{2,1,0:T(8,128)S(1)} %bitcast.111), channel_id=1, replica_groups=mesh['asset'=16,'earn'=4,'age'=4] {'asset'}, dimensions={0} | all-to-all | bytes 2097152 | tf_op jit(solution)/shard_map/all_to_all | solution.py:116
  174.7 3.1 %shard_map.84 = f32[16,32,512]{2,1,0:T(8,128)} custom-call(f32[16,32,512]{2,1,0:T(8,128)} %all_to_all.15.src_ref), custom_call_target="tpu_custom_call" | custom-call | bytes 2097152 | tf_op jit(solution)/shard_map/pallas_call | solution.py:102
  177.8 6.1 %copy_add_fusion = f32[2,8,32,512]{3,2,0,1:T(8,128)S(1)} fusion(f32[2,8,32,512]{3,2,1,0:T(8,128)S(1)} %copy-done.2, f32[2,8,32,512]{3,2,1,0:T(8,128)} %bitcast.115, f32[8,512,512]{2,1,0:T(8,128)} %get-tuple-element.20), kind=kOutput, calls=%fused_computation.55 | convolution fusion | flops 805830656 | bytes 11534336 | tf_op jit(solution)/shard_map/terc,ecn->tern/dot_general | solution.py:76
  (51 shorter events, 19.4 us)
Async XLA Ops:
  0.0 24.6 %copy-start.4 = (s32[8,512]{1,0:T(8,128)S(1)}, s32[8,512]{1,0:T(8,128)}, u32[]{:S(2)}) copy-start(s32[8,512]{1,0:T(8,128)} %param.12) | copy-start | bytes 49156
  2.0 17.7 %collective-permute-start = (f32[1,4,32,512]{3,2,1,0:T(8,128)}, f32[1,4,32,512]{3,2,1,0:T(8,128)S(1)}, u32[]{:S(2)}, u32[]{:S(2)}) collective-permute-start(f32[1,4,32,512]{3,2,1,0:T(8,128)} %get-tuple-element.29), channel_id=1, source_target_pairs={{0,4},{1,5},{2,6},{3,7},{4,8},{5,9},{6,10},{7,11},{8,12},{9,13},{1... | collective-permute-start | bytes 786440 | tf_op jit(solution)/shard_map/ppermute | solution.py:43
  5.4 14.3 %collective-permute-start.2 = (f32[1,4,32,512]{3,2,1,0:T(8,128)S(1)}, f32[1,4,32,512]{3,2,1,0:T(8,128)S(1)}, u32[]{:S(2)}, u32[]{:S(2)}) collective-permute-start(f32[1,4,32,512]{3,2,1,0:T(8,128)S(1)} %get-tuple-element.30), channel_id=1, source_target_pairs={{1,4},{2,5},{3,6},{5,8},{6,9},{7,10},{9,12},{10,13},{11,14},{17,20... | collective-permute-start | bytes 786440 | tf_op jit(solution)/shard_map/ppermute | solution.py:43
  7.3 12.4 %collective-permute-start.1 = (f32[1,4,32,512]{3,2,1,0:T(8,128)S(1)}, f32[1,4,32,512]{3,2,1,0:T(8,128)S(1)}, u32[]{:S(2)}, u32[]{:S(2)}) collective-permute-start(f32[1,4,32,512]{3,2,1,0:T(8,128)S(1)} %get-tuple-element.31), channel_id=1, source_target_pairs={{4,0},{5,1},{6,2},{7,3},{8,4},{9,5},{10,6},{11,7},{12,8},{13,9},{1... | collective-permute-start | bytes 786440 | tf_op jit(solution)/shard_map/ppermute | solution.py:43
  10.0 11.2 %collective-permute-start.4 = (f32[1,4,32,512]{3,2,1,0:T(8,128)S(1)}, f32[1,4,32,512]{3,2,1,0:T(8,128)S(1)}, u32[]{:S(2)}, u32[]{:S(2)}) collective-permute-start(f32[1,4,32,512]{3,2,1,0:T(8,128)S(1)} %get-tuple-element.32), channel_id=1, source_target_pairs={{5,0},{6,1},{7,2},{9,4},{10,5},{11,6},{13,8},{14,9},{15,10},{21,16... | collective-permute-start | bytes 786440 | tf_op jit(solution)/shard_map/ppermute | solution.py:43
  13.2 9.4 %collective-permute-start.3 = (f32[1,8,32,512]{3,2,1,0:T(8,128)S(1)}, f32[1,8,32,512]{3,2,1,0:T(8,128)S(1)}, u32[]{:S(2)}, u32[]{:S(2)}) collective-permute-start(f32[1,8,32,512]{3,2,1,0:T(8,128)S(1)} %get-tuple-element.34), channel_id=1, source_target_pairs={{1,0},{2,1},{3,2},{5,4},{6,5},{7,6},{9,8},{10,9},{11,10},{13,12},{... | collective-permute-start | bytes 1572872 | tf_op jit(solution)/shard_map/ppermute | solution.py:43
  24.6 20.2 %copy-start.2 = (f32[2,8,32,512]{3,2,1,0:T(8,128)S(1)}, f32[2,8,32,512]{3,2,1,0:T(8,128)}, u32[]{:S(2)}) copy-start(f32[2,8,32,512]{3,2,1,0:T(8,128)} %param.9) | copy-start | bytes 3145732
  32.1 14.0 %copy-start.6 = (s32[8,512]{1,0:T(8,128)S(1)}, s32[8,512]{1,0:T(8,128)}, u32[]{:S(2)}) copy-start(s32[8,512]{1,0:T(8,128)} %param.14) | copy-start | bytes 49156
  32.1 14.0 %copy-start.5 = (f32[4,8,512]{2,1,0:T(8,128)S(1)}, f32[4,8,512]{2,1,0:T(8,128)}, u32[]{:S(2)}) copy-start(f32[4,8,512]{2,1,0:T(8,128)} %param.15) | copy-start | bytes 196612
  32.1 43.4 %copy-start.3 = (f32[4,8,512]{2,1,0:T(8,128)S(1)}, f32[4,8,512]{2,1,0:T(8,128)}, u32[]{:S(2)}) copy-start(f32[4,8,512]{2,1,0:T(8,128)} %param.13) | copy-start | bytes 196612
  33.6 34.1 %all-to-all-start.1 = ((f32[16,32,512]{2,1,0:T(8,128)}), f32[16,32,512]{2,1,0:T(8,128)S(1)}, u32[]{:S(2)}, u32[]{:S(2)}) async-start(f32[16,32,512]{2,1,0:T(8,128)} %bitcast.34), calls=%async_computation.1 | async-start | bytes 2097152 | tf_op jit(solution)/shard_map/all_to_all | solution.py:116
  67.7 23.1 %copy-start = (f32[16,32,512]{2,1,0:T(8,128)}, f32[16,32,512]{2,1,0:T(8,128)S(1)}, u32[]{:S(2)}) copy-start(f32[16,32,512]{2,1,0:T(8,128)S(1)} %all-to-all-done.1.src_ref) | copy-start | bytes 3145732
  67.7 26.3 %all-to-all-start = ((f32[16,32,512]{2,1,0:T(8,128)}), f32[16,32,512]{2,1,0:T(8,128)S(1)}, u32[]{:S(2)}, u32[]{:S(2)}) async-start(f32[16,32,512]{2,1,0:T(8,128)} %bitcast.29), calls=%async_computation | async-start | bytes 2097152 | tf_op jit(solution)/shard_map/all_to_all | solution.py:116
  94.0 1.0 copy-start.1
  98.0 41.0 %slice-start = ((s8[8388608]{0:T(1024)(128)(4,1)}), s8[4194304]{0:T(1024)(128)(4,1)S(1)}, s32[]{:S(2)}) async-start(s8[8388608]{0:T(1024)(128)(4,1)} %bitcast.107), calls=%async_computation.3 | async-start | bytes 8388608
  104.7 34.3 %slice-start.1 = ((s8[8388608]{0:T(1024)(128)(4,1)}), s8[4194304]{0:T(1024)(128)(4,1)S(1)}, s32[]{:S(2)}) async-start(s8[8388608]{0:T(1024)(128)(4,1)} %bitcast.107), calls=%async_computation.4 | async-start | bytes 8388608
  104.8 32.2 %collective-permute-start.8 = (f32[1,8,32,512]{3,2,0,1:T(8,128)S(1)}, f32[1,8,32,512]{3,2,0,1:T(8,128)S(1)}, u32[]{:S(2)}, u32[]{:S(2)}) collective-permute-start(f32[1,8,32,512]{3,2,0,1:T(8,128)S(1)} %get-tuple-element.28), channel_id=1, source_target_pairs={{1,0},{2,1},{3,2},{5,4},{6,5},{7,6},{9,8},{10,9},{11,10},{13,12},{... | collective-permute-start | bytes 1572872 | tf_op jit(solution)/shard_map/ppermute | solution.py:43
  116.6 12.6 %collective-permute-start.5 = (f32[1,4,32,512]{3,2,0,1:T(8,128)S(1)}, f32[1,4,32,512]{3,2,0,1:T(8,128)S(1)}, u32[]{:S(2)}, u32[]{:S(2)}) collective-permute-start(f32[1,4,32,512]{3,2,0,1:T(8,128)S(1)} %get-tuple-element.23), channel_id=1, source_target_pairs={{0,4},{1,5},{2,6},{3,7},{4,8},{5,9},{6,10},{7,11},{8,12},{9,13},{1... | collective-permute-start | bytes 786440 | tf_op jit(solution)/shard_map/ppermute | solution.py:43
  120.3 8.9 %collective-permute-start.9 = (f32[1,4,32,512]{3,2,0,1:T(8,128)S(1)}, f32[1,4,32,512]{3,2,0,1:T(8,128)S(1)}, u32[]{:S(2)}, u32[]{:S(2)}) collective-permute-start(f32[1,4,32,512]{3,2,0,1:T(8,128)S(1)} %get-tuple-element.24), channel_id=1, source_target_pairs={{5,0},{6,1},{7,2},{9,4},{10,5},{11,6},{13,8},{14,9},{15,10},{21,16... | collective-permute-start | bytes 786440 | tf_op jit(solution)/shard_map/ppermute | solution.py:43
  123.9 7.7 %collective-permute-start.7 = (f32[1,4,32,512]{3,2,0,1:T(8,128)S(1)}, f32[1,4,32,512]{3,2,0,1:T(8,128)S(1)}, u32[]{:S(2)}, u32[]{:S(2)}) collective-permute-start(f32[1,4,32,512]{3,2,0,1:T(8,128)S(1)} %get-tuple-element.25), channel_id=1, source_target_pairs={{1,4},{2,5},{3,6},{5,8},{6,9},{7,10},{9,12},{10,13},{11,14},{17,20... | collective-permute-start | bytes 786440 | tf_op jit(solution)/shard_map/ppermute | solution.py:43
  126.0 11.0 %collective-permute-start.6 = (f32[1,4,32,512]{3,2,0,1:T(8,128)S(1)}, f32[1,4,32,512]{3,2,0,1:T(8,128)S(1)}, u32[]{:S(2)}, u32[]{:S(2)}) collective-permute-start(f32[1,4,32,512]{3,2,0,1:T(8,128)S(1)} %get-tuple-element.26), channel_id=1, source_target_pairs={{4,0},{5,1},{6,2},{7,3},{8,4},{9,5},{10,6},{11,7},{12,8},{13,9},{1... | collective-permute-start | bytes 786440 | tf_op jit(solution)/shard_map/ppermute | solution.py:43

commit v11 on v10

--- a/solution.py
+++ b/solution.py
@@ -51,11 +51,11 @@
         [moved(current[:1, tail], 1, -1), moved(current[:1], 0, -1), moved(current[:1, head], -1, -1)],
         axis=1,
     )
-    return jnp.concatenate([here, above], axis=0)
+    return here, above
 
 
 def continuation(current, earn_prob, support_start):
-    return mix(neighbours(current), earn_prob, support_start)
+    return jnp.concatenate([mix(part, earn_prob, support_start) for part in neighbours(current)], axis=0)
 
 
 def mix(padded, earn_prob, support_start):
@@ -127,15 +127,14 @@
     illiquid_offset,
     illiquid_weight,
 ):
-    padded, utility = lax.optimization_barrier((neighbours(values), utility))
-    expected = mix(padded, earn_prob, support_start)
-    saved = along_lanes(expected, band_matrix(liquid_offset, liquid_weight))
-    saved, illiquid_offset, illiquid_weight, liquid_offset, liquid_weight = lax.optimization_barrier(
-        (saved, illiquid_offset, illiquid_weight, liquid_offset, liquid_weight)
+    liquid_map = lax.optimization_barrier(band_matrix(liquid_offset, liquid_weight))
+    saved = jnp.concatenate(
+        [along_lanes(mix(part, earn_prob, support_start), liquid_map) for part in neighbours(values)], axis=0
     )
-    illiquid_map, liquid_map = lax.optimization_barrier(
-        (band_matrix(illiquid_offset, illiquid_weight), band_matrix(liquid_offset, liquid_weight))
+    saved, illiquid_offset, illiquid_weight = lax.optimization_barrier(
+        (saved, illiquid_offset, illiquid_weight)
     )
+    illiquid_map = lax.optimization_barrier(band_matrix(illiquid_offset, illiquid_weight))
     adjusted = along_lanes(flipped(saved), illiquid_map)
     current = flipped(utility) + DISCOUNT * adjusted
 

time: 188 us -> 167 us (0.89)
  starting transfers between devices: 55.9 us -> 46 us
  waiting for transfers between devices: 32.3 us -> 25 us
  other arithmetic: 18.7 us -> 14.5 us
  blocking collectives: 32.3 us -> 28.7 us
  matrix products: 26.7 us -> 29.8 us
  local copies, waits for them, and re-layouts: 9.47 us -> 11.4 us
    ppermute x10, starting transfers between devices: 36.9 us -> 26 us  [moved(): return lax.ppermute(value, axes, pairs)]
    all_to_all x2, waiting for transfers between devices: 21.7 us -> 17.6 us  [flipped(): got = lax.all_to_all(flat, 'asset', 0, 0, tiled=True)]
    all_to_all x1, blocking collectives: 32.3 us -> 28.7 us  [flipped(): got = lax.all_to_all(flat, 'asset', 0, 0, tiled=True)]
    unnamed x18 -> x32, local copies, waits for them, and re-layouts: 1.01 us -> 4.43 us
    ppermute x10, waiting for transfers between devices: 10.6 us -> 7.4 us  [moved(): return lax.ppermute(value, axes, pairs)]
    reshape x1 -> x2, local copies, waits for them, and re-layouts: 1.31 us -> 3.92 us  [flipped(): stacked.reshape(ages * states * rows, lanes)]
    dot_general x2 -> x4, matrix products: 3.56 us -> 5.19 us  [mix(): jnp.einsum('ij,tjxy->tixy', mixing, padded, precision=lax.Precision.HIGH)]
    dot_general x4 -> x5, matrix products: 23.2 us -> 24.6 us  [along_lanes(): jnp.einsum('terc,ecn->tern', stacked, matrix, precision=lax.Precision.HIGH)]
  transfers between devices with their start and end apart: 12 -> 12, of which waited for: 6 -> 4; matrix products, arithmetic and copies ran while one was open for 12% -> 20% of each run, Pallas kernels for 2% -> 2%
where the time goes in v11:
time: 167 us; the launch traced here: 165 us
  starting transfers between devices  46 us (28%)
  matrix products  29.8 us (18%)
  blocking collectives  28.7 us (17%)
  waiting for transfers between devices  25 us (15%)
  other arithmetic  14.5 us (9%)
  local copies, waits for them, and re-layouts  11.4 us (7%)
  Pallas kernels  9.2 us (6%)
    all_to_all x1, blocking collectives, flipped(): got = lax.all_to_all(flat, 'asset', 0, 0, tiled=True)  28.7 us
    ppermute x10, starting transfers between devices, moved(): return lax.ppermute(value, axes, pairs)  26 us
    dot_general x5, matrix products, along_lanes(): jnp.einsum('terc,ecn->tern', stacked, matrix, precision=lax.Precision.HIGH)  24.6 us
    all_to_all x2, starting transfers between devices, flipped(): got = lax.all_to_all(flat, 'asset', 0, 0, tiled=True)  19.9 us
    all_to_all x2, waiting for transfers between devices, flipped(): got = lax.all_to_all(flat, 'asset', 0, 0, tiled=True)  17.6 us
    add x2, other arithmetic, band_matrix(): matrix + jnp.where(positions[None, :, None] == (offset + number)[:, None,...  14.1 us
    pallas_call x3, Pallas kernels, regroup(): pl.pallas_call(_gather_kernel, in_specs=[pl.BlockSpec(memory_space=pltpu....  9.2 us
    ppermute x10, waiting for transfers between devices, moved(): return lax.ppermute(value, axes, pairs)  7.4 us
  transfers between devices with their start and end apart: 12, of which 4 were waited for; matrix products, arithmetic and copies ran while one was open for 20% of the time, Pallas kernels for 2%

profile of v11, /device:TPU:34, one launch (start us, length us, event | category | flops | bytes accessed | tf_op | source)
XLA Modules:
  0.0 165.1 jit_solution(14452136750221455716)
XLA Ops:
  0.0 2.6 %copy.35 = f32[512,512]{0,1:T(8,128)} copy(f32[512,512]{1,0:T(8,128)} %bitcast.131) | data formatting | bytes 2097152 | tf_op jit(solution)/shard_map/reshape | solution.py:115
  2.6 10.3 %all-to-all-start = ((f32[16,32,512]{2,1,0:T(8,128)}), f32[16,32,512]{2,1,0:T(8,128)S(1)}, u32[]{:S(2)}, u32[]{:S(2)}) async-start(f32[16,32,512]{2,1,0:T(8,128)} %bitcast.32), calls=%async_computation | async-start | bytes 2097152 | tf_op jit(solution)/shard_map/all_to_all | solution.py:116
  14.4 2.0 %collective-permute-start.4 = (f32[1,4,32,512]{3,1,2,0:T(4,128)S(1)}, f32[1,4,32,512]{3,1,2,0:T(4,128)}, u32[]{:S(2)}, u32[]{:S(2)}) collective-permute-start(f32[1,4,32,512]{3,1,2,0:T(4,128)S(1)} %copy.54), channel_id=1, source_target_pairs={{5,0},{6,1},{7,2},{9,4},{10,5},{11,6},{13,8},{14,9},{15,10},{21,16... | collective-permute-start | bytes 786440 | tf_op jit(solution)/shard_map/ppermute | solution.py:43
  20.2 4.2 %collective-permute-start.2 = (f32[1,4,32,512]{3,1,2,0:T(4,128)}, f32[1,4,32,512]{3,1,2,0:T(4,128)}, u32[]{:S(2)}, u32[]{:S(2)}) collective-permute-start(f32[1,4,32,512]{3,1,2,0:T(4,128)} %copy.52), channel_id=1, source_target_pairs={{1,4},{2,5},{3,6},{5,8},{6,9},{7,10},{9,12},{10,13},{11,14},{17,20... | collective-permute-start | bytes 786440 | tf_op jit(solution)/shard_map/ppermute | solution.py:43
  25.2 4.1 %collective-permute-start = (f32[1,4,32,512]{3,1,2,0:T(4,128)}, f32[1,4,32,512]{3,1,2,0:T(4,128)}, u32[]{:S(2)}, u32[]{:S(2)}) collective-permute-start(f32[1,4,32,512]{3,1,2,0:T(4,128)} %copy.49), channel_id=1, source_target_pairs={{0,4},{1,5},{2,6},{3,7},{4,8},{5,9},{6,10},{7,11},{8,12},{9,13},{1... | collective-permute-start | bytes 786440 | tf_op jit(solution)/shard_map/ppermute | solution.py:43
  29.7 1.9 %collective-permute-start.3 = (f32[1,8,32,512]{3,1,2,0:T(8,128)S(1)}, f32[1,8,32,512]{3,1,2,0:T(8,128)S(1)}, u32[]{:S(2)}, u32[]{:S(2)}) collective-permute-start(f32[1,8,32,512]{3,1,2,0:T(8,128)S(1)} %copy.53), channel_id=1, source_target_pairs={{1,0},{2,1},{3,2},{5,4},{6,5},{7,6},{9,8},{10,9},{11,10},{13,12},{... | collective-permute-start | bytes 1572872 | tf_op jit(solution)/shard_map/ppermute | solution.py:43
  31.7 7.1 %select_add_fusion.1 = f32[8,512,512]{2,1,0:T(8,128)} fusion(f32[8,512]{1,0:T(8,128)S(1)} %get-tuple-element.29, s32[8,512]{1,0:T(8,128)S(1)} %get-tuple-element.35, f32[8,512]{1,0:T(8,128)S(1)} %get-tuple-element.30, s32[8,512]{1,0:T(8,128)S(1)} %get-tuple-element.36, f32[8,512]{1,0:T(8,128)S(1)} %get-tuple-element.28, s32[8,512]{1,0:T(8,128)S(1)} %get-tuple-element.34, ...), kind=kLoop, calls=%fused_computation.11 | loop fusion | flops 23068672 | bytes 8519680 | tf_op jit(solution)/shard_map/add | solution.py:22
  41.0 6.4 %convolution_bitcast_fusion.1 = f32[1,8,32,512]{3,2,1,0:T(8,128)S(1)} fusion(f32[8,512,512]{2,1,0:T(8,128)} %select_add_fusion.1, f32[8,32,512]{2,0,1:T(8,128)S(1)} %convolution_bitcast_fusion.5), kind=kOutput, calls=%fused_computation.24 | convolution fusion | flops 402653184 | bytes 9437184 | tf_op jit(solution)/shard_map/terc,ecn->tern/dot_general | solution.py:76
  49.0 2.5 %convolution_bitcast_fusion = f32[1,8,32,512]{3,2,1,0:T(8,128)S(1)} fusion(f32[8,512,512]{2,1,0:T(8,128)S(1)} %copy-done, f32[8,32,512]{2,0,1:T(8,128)S(1)} %convolution_bitcast_fusion.4), kind=kOutput, calls=%fused_computation.23 | convolution fusion | flops 402653184 | bytes 9437184 | tf_op jit(solution)/shard_map/terc,ecn->tern/dot_general | solution.py:76
  53.0 9.6 %all-to-all-start.1 = ((f32[16,32,512]{2,1,0:T(8,128)}), f32[16,32,512]{2,1,0:T(8,128)S(1)}, u32[]{:S(2)}, u32[]{:S(2)}) async-start(f32[16,32,512]{2,1,0:T(8,128)} %bitcast.37), calls=%async_computation.1 | async-start | bytes 2097152 | tf_op jit(solution)/shard_map/all_to_all | solution.py:116
  62.7 7.0 %select_add_fusion = f32[8,512,512]{2,1,0:T(8,128)} fusion(f32[8,512]{1,0:T(8,128)S(1)} %get-tuple-element.24, s32[8,512]{1,0:T(8,128)S(1)} %get-tuple-element.32, f32[8,512]{1,0:T(8,128)S(1)} %get-tuple-element.25, s32[8,512]{1,0:T(8,128)S(1)} %get-tuple-element.33, f32[8,512]{1,0:T(8,128)S(1)} %get-tuple-element.26, s32[8,512]{1,0:T(8,128)S(1)} %get-tuple-element.31, ...), kind=kLoop, calls=%fused_computation.6 | loop fusion | flops 23068672 | bytes 8519680 | tf_op jit(solution)/shard_map/add | solution.py:22
  69.6 3.1 %shard_map.82 = f32[16,32,512]{2,1,0:T(8,128)} custom-call(f32[16,32,512]{2,1,0:T(8,128)} %copy-done.2), custom_call_target="tpu_custom_call" | custom-call | bytes 2097152 | tf_op jit(solution)/shard_map/pallas_call | solution.py:102
  72.7 17.6 %all-to-all-done.1.src_ref = f32[16,32,512]{2,1,0:T(8,128)S(1)} async-done(((f32[16,32,512]{2,1,0:T(8,128)}), f32[16,32,512]{2,1,0:T(8,128)S(1)}, u32[]{:S(2)}, u32[]{:S(2)}) %all-to-all-start.1) | async-done | bytes 1048608 | tf_op jit(solution)/shard_map/all_to_all | solution.py:116
  91.3 3.1 %shard_map.83 = f32[16,32,512]{2,1,0:T(8,128)} custom-call(f32[16,32,512]{2,1,0:T(8,128)} %copy-done.3), custom_call_target="tpu_custom_call" | custom-call | bytes 2097152 | tf_op jit(solution)/shard_map/pallas_call | solution.py:102
  94.4 6.6 %fusion.15 = f32[2,8,32,512]{3,2,0,1:T(8,128)S(1)} fusion(f32[8,512,512]{2,1,0:T(8,128)} %select_add_fusion, f32[2,8,32,512]{3,2,1,0:T(8,128)} %bitcast.132, f32[2,8,32,512]{3,2,1,0:T(8,128)} %bitcast.133), kind=kOutput, calls=%fused_computation.19 | convolution fusion | flops 805830656 | bytes 11534336 | tf_op jit(solution)/shard_map/terc,ecn->tern/dot_general | solution.py:76
  101.1 4.1 %collective-permute-start.5 = (f32[1,4,32,512]{3,2,0,1:T(8,128)S(1)}, f32[1,4,32,512]{3,2,0,1:T(8,128)S(1)}, u32[]{:S(2)}, u32[]{:S(2)}) collective-permute-start(f32[1,4,32,512]{3,2,0,1:T(8,128)S(1)} %get-tuple-element.11), channel_id=1, source_target_pairs={{0,4},{1,5},{2,6},{3,7},{4,8},{5,9},{6,10},{7,11},{8,12},{9,13},{1... | collective-permute-start | bytes 786440 | tf_op jit(solution)/shard_map/ppermute | solution.py:43
  105.2 2.1 %collective-permute-start.6 = (f32[1,4,32,512]{3,2,0,1:T(8,128)S(1)}, f32[1,4,32,512]{3,2,0,1:T(8,128)S(1)}, u32[]{:S(2)}, u32[]{:S(2)}) collective-permute-start(f32[1,4,32,512]{3,2,0,1:T(8,128)S(1)} %get-tuple-element.14), channel_id=1, source_target_pairs={{4,0},{5,1},{6,2},{7,3},{8,4},{9,5},{10,6},{11,7},{12,8},{13,9},{1... | collective-permute-start | bytes 786440 | tf_op jit(solution)/shard_map/ppermute | solution.py:43
  113.1 2.4 %collective-permute-done.6 = f32[1,4,32,512]{3,2,0,1:T(8,128)S(1)} collective-permute-done((f32[1,4,32,512]{3,2,0,1:T(8,128)S(1)}, f32[1,4,32,512]{3,2,0,1:T(8,128)S(1)}, u32[]{:S(2)}, u32[]{:S(2)}) %collective-permute-start.6) | collective-permute-done | bytes 262176 | tf_op jit(solution)/shard_map/ppermute | solution.py:43
  116.6 2.1 %collective-permute-done.9 = f32[1,4,32,512]{3,2,0,1:T(8,128)S(1)} collective-permute-done((f32[1,4,32,512]{3,2,0,1:T(8,128)S(1)}, f32[1,4,32,512]{3,2,0,1:T(8,128)S(1)}, u32[]{:S(2)}, u32[]{:S(2)}) %collective-permute-start.9) | collective-permute-done | bytes 262176 | tf_op jit(solution)/shard_map/ppermute | solution.py:43
  118.8 2.8 %collective-permute-done.7 = f32[1,4,32,512]{3,2,0,1:T(8,128)S(1)} collective-permute-done((f32[1,4,32,512]{3,2,0,1:T(8,128)S(1)}, f32[1,4,32,512]{3,2,0,1:T(8,128)S(1)}, u32[]{:S(2)}, u32[]{:S(2)}) %collective-permute-start.7) | collective-permute-done | bytes 262176 | tf_op jit(solution)/shard_map/ppermute | solution.py:43
  122.7 2.9 %fusion.6 = f32[2,8,32,512]{3,2,0,1:T(8,128)S(1)} fusion(f32[8,512,512]{2,1,0:T(8,128)S(1)} %bitcast.127, f32[2,8,32,512]{3,1,2,0:T(8,128)S(1)} %pad_maximum_fusion.1), kind=kOutput, calls=%fused_computation.16 | convolution fusion | flops 805306368 | bytes 10485760 | tf_op jit(solution)/shard_map/terc,ecn->tern/dot_general | solution.py:76
  126.1 28.7 %all_to_all.15.src_ref = f32[16,32,512]{2,1,0:T(8,128)} all-to-all(f32[16,32,512]{2,1,0:T(8,128)S(1)} %bitcast.130), channel_id=1, replica_groups=mesh['asset'=16,'earn'=4,'age'=4] {'asset'}, dimensions={0} | all-to-all | bytes 2097152 | tf_op jit(solution)/shard_map/all_to_all | solution.py:116
  154.8 3.1 %shard_map.84 = f32[16,32,512]{2,1,0:T(8,128)} custom-call(f32[16,32,512]{2,1,0:T(8,128)} %all_to_all.15.src_ref), custom_call_target="tpu_custom_call" | custom-call | bytes 2097152 | tf_op jit(solution)/shard_map/pallas_call | solution.py:102
  157.9 6.1 %fusion.24 = f32[2,8,32,512]{3,2,0,1:T(8,128)S(1)} fusion(f32[8,512,512]{2,1,0:T(8,128)} %select_add_fusion.1, f32[2,8,32,512]{3,2,1,0:T(8,128)S(1)} %copy-done.4, f32[2,8,32,512]{3,2,1,0:T(8,128)} %bitcast.134), kind=kOutput, calls=%fused_computation.22 | convolution fusion | flops 805830656 | bytes 11534336 | tf_op jit(solution)/shard_map/terc,ecn->tern/dot_general | solution.py:76
  (68 shorter events, 22.1 us)
Async XLA Ops:
  0.0 29.3 %copy-start.1 = (f32[2,8,32,512]{3,2,1,0:T(8,128)S(1)}, f32[2,8,32,512]{3,2,1,0:T(8,128)}, u32[]{:S(2)}) copy-start(f32[2,8,32,512]{3,2,1,0:T(8,128)} %param.8) | copy-start | bytes 3145732
  0.0 31.7 %copy-start.5 = (s32[8,512]{1,0:T(8,128)S(1)}, s32[8,512]{1,0:T(8,128)}, u32[]{:S(2)}) copy-start(s32[8,512]{1,0:T(8,128)} %param.12) | copy-start | bytes 49156
  0.0 31.7 %copy-start.7 = (f32[4,8,512]{2,1,0:T(8,128)S(1)}, f32[4,8,512]{2,1,0:T(8,128)}, u32[]{:S(2)}) copy-start(f32[4,8,512]{2,1,0:T(8,128)} %param.13) | copy-start | bytes 196612
  2.6 50.3 %all-to-all-start = ((f32[16,32,512]{2,1,0:T(8,128)}), f32[16,32,512]{2,1,0:T(8,128)S(1)}, u32[]{:S(2)}, u32[]{:S(2)}) async-start(f32[16,32,512]{2,1,0:T(8,128)} %bitcast.32), calls=%async_computation | async-start | bytes 2097152 | tf_op jit(solution)/shard_map/all_to_all | solution.py:116
  12.9 25.9 %copy-start.10 = (s32[8]{0:T(128)S(1)}, s32[8]{0:T(128)}, u32[]{:S(2)}) copy-start(s32[8]{0:T(128)} %param.11) | copy-start | bytes 100
  13.0 26.2 %copy-start.9 = (f32[5,8]{1,0:T(8,128)S(1)}, f32[5,8]{1,0:T(8,128)}, u32[]{:S(2)}) copy-start(f32[5,8]{1,0:T(8,128)} %param.10) | copy-start | bytes 484
  14.4 32.9 %collective-permute-start.4 = (f32[1,4,32,512]{3,1,2,0:T(4,128)S(1)}, f32[1,4,32,512]{3,1,2,0:T(4,128)}, u32[]{:S(2)}, u32[]{:S(2)}) collective-permute-start(f32[1,4,32,512]{3,1,2,0:T(4,128)S(1)} %copy.54), channel_id=1, source_target_pairs={{5,0},{6,1},{7,2},{9,4},{10,5},{11,6},{13,8},{14,9},{15,10},{21,16... | collective-permute-start | bytes 786440 | tf_op jit(solution)/shard_map/ppermute | solution.py:43
  17.4 21.8 %collective-permute-start.1 = (f32[1,4,32,512]{3,1,2,0:T(4,128)}, f32[1,4,32,512]{3,1,2,0:T(4,128)}, u32[]{:S(2)}, u32[]{:S(2)}) collective-permute-start(f32[1,4,32,512]{3,1,2,0:T(4,128)} %copy.51), channel_id=1, source_target_pairs={{4,0},{5,1},{6,2},{7,3},{8,4},{9,5},{10,6},{11,7},{12,8},{13,9},{1... | collective-permute-start | bytes 786440 | tf_op jit(solution)/shard_map/ppermute | solution.py:43
  20.2 27.2 %collective-permute-start.2 = (f32[1,4,32,512]{3,1,2,0:T(4,128)}, f32[1,4,32,512]{3,1,2,0:T(4,128)}, u32[]{:S(2)}, u32[]{:S(2)}) collective-permute-start(f32[1,4,32,512]{3,1,2,0:T(4,128)} %copy.52), channel_id=1, source_target_pairs={{1,4},{2,5},{3,6},{5,8},{6,9},{7,10},{9,12},{10,13},{11,14},{17,20... | collective-permute-start | bytes 786440 | tf_op jit(solution)/shard_map/ppermute | solution.py:43
  25.2 14.0 %collective-permute-start = (f32[1,4,32,512]{3,1,2,0:T(4,128)}, f32[1,4,32,512]{3,1,2,0:T(4,128)}, u32[]{:S(2)}, u32[]{:S(2)}) collective-permute-start(f32[1,4,32,512]{3,1,2,0:T(4,128)} %copy.49), channel_id=1, source_target_pairs={{0,4},{1,5},{2,6},{3,7},{4,8},{5,9},{6,10},{7,11},{8,12},{9,13},{1... | collective-permute-start | bytes 786440 | tf_op jit(solution)/shard_map/ppermute | solution.py:43
  29.7 17.7 %collective-permute-start.3 = (f32[1,8,32,512]{3,1,2,0:T(8,128)S(1)}, f32[1,8,32,512]{3,1,2,0:T(8,128)S(1)}, u32[]{:S(2)}, u32[]{:S(2)}) collective-permute-start(f32[1,8,32,512]{3,1,2,0:T(8,128)S(1)} %copy.53), channel_id=1, source_target_pairs={{1,0},{2,1},{3,2},{5,4},{6,5},{7,6},{9,8},{10,9},{11,10},{13,12},{... | collective-permute-start | bytes 1572872 | tf_op jit(solution)/shard_map/ppermute | solution.py:43
  39.2 9.8 %copy-start = (f32[8,512,512]{2,1,0:T(8,128)S(1)}, f32[8,512,512]{2,1,0:T(8,128)}, u32[]{:S(2)}) copy-start(f32[8,512,512]{2,1,0:T(8,128)} %select_add_fusion.1) | copy-start | bytes 25165828
  47.4 15.3 %copy-start.6 = (s32[8,512]{1,0:T(8,128)S(1)}, s32[8,512]{1,0:T(8,128)}, u32[]{:S(2)}) copy-start(s32[8,512]{1,0:T(8,128)} %param.14) | copy-start | bytes 49156
  47.4 15.3 %copy-start.8 = (f32[4,8,512]{2,1,0:T(8,128)S(1)}, f32[4,8,512]{2,1,0:T(8,128)}, u32[]{:S(2)}) copy-start(f32[4,8,512]{2,1,0:T(8,128)} %param.15) | copy-start | bytes 196612
  53.0 16.7 %copy-start.2 = (f32[16,32,512]{2,1,0:T(8,128)}, f32[16,32,512]{2,1,0:T(8,128)S(1)}, u32[]{:S(2)}) copy-start(f32[16,32,512]{2,1,0:T(8,128)S(1)} %all-to-all-done.src_ref) | copy-start | bytes 3145732
  53.0 37.4 %all-to-all-start.1 = ((f32[16,32,512]{2,1,0:T(8,128)}), f32[16,32,512]{2,1,0:T(8,128)S(1)}, u32[]{:S(2)}, u32[]{:S(2)}) async-start(f32[16,32,512]{2,1,0:T(8,128)} %bitcast.37), calls=%async_computation.1 | async-start | bytes 2097152 | tf_op jit(solution)/shard_map/all_to_all | solution.py:116
  94.4 28.3 %slice-start = ((s8[8388608]{0:T(1024)(128)(4,1)}), s8[4194304]{0:T(1024)(128)(4,1)S(1)}, s32[]{:S(2)}) async-start(s8[8388608]{0:T(1024)(128)(4,1)} %bitcast.126), calls=%async_computation.3 | async-start | bytes 8388608
  101.0 21.7 %slice-start.1 = ((s8[8388608]{0:T(1024)(128)(4,1)}), s8[4194304]{0:T(1024)(128)(4,1)S(1)}, s32[]{:S(2)}) async-start(s8[8388608]{0:T(1024)(128)(4,1)} %bitcast.126), calls=%async_computation.4 | async-start | bytes 8388608
  101.1 12.0 %collective-permute-start.5 = (f32[1,4,32,512]{3,2,0,1:T(8,128)S(1)}, f32[1,4,32,512]{3,2,0,1:T(8,128)S(1)}, u32[]{:S(2)}, u32[]{:S(2)}) collective-permute-start(f32[1,4,32,512]{3,2,0,1:T(8,128)S(1)} %get-tuple-element.11), channel_id=1, source_target_pairs={{0,4},{1,5},{2,6},{3,7},{4,8},{5,9},{6,10},{7,11},{8,12},{9,13},{1... | collective-permute-start | bytes 786440 | tf_op jit(solution)/shard_map/ppermute | solution.py:43
  105.2 10.4 %collective-permute-start.6 = (f32[1,4,32,512]{3,2,0,1:T(8,128)S(1)}, f32[1,4,32,512]{3,2,0,1:T(8,128)S(1)}, u32[]{:S(2)}, u32[]{:S(2)}) collective-permute-start(f32[1,4,32,512]{3,2,0,1:T(8,128)S(1)} %get-tuple-element.14), channel_id=1, source_target_pairs={{4,0},{5,1},{6,2},{7,3},{8,4},{9,5},{10,6},{11,7},{12,8},{13,9},{1... | collective-permute-start | bytes 786440 | tf_op jit(solution)/shard_map/ppermute | solution.py:43
  107.3 14.2 %collective-permute-start.8 = (f32[1,8,32,512]{3,2,0,1:T(8,128)S(1)}, f32[1,8,32,512]{3,2,0,1:T(8,128)S(1)}, u32[]{:S(2)}, u32[]{:S(2)}) collective-permute-start(f32[1,8,32,512]{3,2,0,1:T(8,128)S(1)} %get-tuple-element.16), channel_id=1, source_target_pairs={{1,0},{2,1},{3,2},{5,4},{6,5},{7,6},{9,8},{10,9},{11,10},{13,12},{... | collective-permute-start | bytes 1572872 | tf_op jit(solution)/shard_map/ppermute | solution.py:43
  109.3 9.5 %collective-permute-start.9 = (f32[1,4,32,512]{3,2,0,1:T(8,128)S(1)}, f32[1,4,32,512]{3,2,0,1:T(8,128)S(1)}, u32[]{:S(2)}, u32[]{:S(2)}) collective-permute-start(f32[1,4,32,512]{3,2,0,1:T(8,128)S(1)} %get-tuple-element.12), channel_id=1, source_target_pairs={{5,0},{6,1},{7,2},{9,4},{10,5},{11,6},{13,8},{14,9},{15,10},{21,16... | collective-permute-start | bytes 786440 | tf_op jit(solution)/shard_map/ppermute | solution.py:43
  111.2 10.4 %collective-permute-start.7 = (f32[1,4,32,512]{3,2,0,1:T(8,128)S(1)}, f32[1,4,32,512]{3,2,0,1:T(8,128)S(1)}, u32[]{:S(2)}, u32[]{:S(2)}) collective-permute-start(f32[1,4,32,512]{3,2,0,1:T(8,128)S(1)} %get-tuple-element.13), channel_id=1, source_target_pairs={{1,4},{2,5},{3,6},{5,8},{6,9},{7,10},{9,12},{10,13},{11,14},{17,20... | collective-permute-start | bytes 786440 | tf_op jit(solution)/shard_map/ppermute | solution.py:43
  122.7 35.2 %copy-start.4 = (f32[2,8,32,512]{3,2,1,0:T(8,128)S(1)}, f32[2,8,32,512]{3,2,1,0:T(8,128)}, u32[]{:S(2)}) copy-start(f32[2,8,32,512]{3,2,1,0:T(8,128)} %param.9) | copy-start | bytes 3145732
  (1 other events, 1.0 us)

commit v12 on v11

--- a/solution.py
+++ b/solution.py
@@ -138,8 +138,9 @@
     adjusted = along_lanes(flipped(saved), illiquid_map)
     current = flipped(utility) + DISCOUNT * adjusted
 
-    expected = continuation(current, earn_prob, support_start)
-    moved = along_lanes(expected, illiquid_map)
+    moved = jnp.concatenate(
+        [along_lanes(mix(part, earn_prob, support_start), illiquid_map) for part in neighbours(current)], axis=0
+    )
     adjusted = along_lanes(flipped(moved), liquid_map)
     return utility + DISCOUNT * adjusted
 

time: 167 us -> 171 us (1.024)
  blocking collectives: 28.7 us -> 32.6 us
  matrix products: 29.8 us -> 32.1 us
    all_to_all x1, blocking collectives: 28.7 us -> 32.6 us  [flipped(): got = lax.all_to_all(flat, 'asset', 0, 0, tiled=True)]
    dot_general x5 -> x6, matrix products: 24.6 us -> 26.9 us  [along_lanes(): jnp.einsum('terc,ecn->tern', stacked, matrix, precision=lax.Precision.HIGH)]
    reshape x2 -> x3, local copies, waits for them, and re-layouts: 3.92 us -> 4.25 us  [flipped(): stacked.reshape(ages * states * rows, lanes)]
  transfers between devices with their start and end apart: 12 -> 12, of which waited for: 4 -> 2; matrix products, arithmetic and copies ran while one was open for 20% -> 21% of each run, Pallas kernels for 2% -> 2%
where the time goes in v12:
time: 171 us; the launch traced here: 170 us
  starting transfers between devices  45.8 us (27%)
  blocking collectives  32.6 us (19%)
  matrix products  32.1 us (19%)
  waiting for transfers between devices  23.7 us (14%)
  other arithmetic  14.5 us (8%)
  local copies, waits for them, and re-layouts  11.3 us (7%)
  Pallas kernels  9.2 us (5%)
    all_to_all x1, blocking collectives, flipped(): got = lax.all_to_all(flat, 'asset', 0, 0, tiled=True)  32.6 us
    dot_general x6, matrix products, along_lanes(): jnp.einsum('terc,ecn->tern', stacked, matrix, precision=lax.Precision.HIGH)  26.9 us
    ppermute x10, starting transfers between devices, moved(): return lax.ppermute(value, axes, pairs)  25.8 us
    all_to_all x2, starting transfers between devices, flipped(): got = lax.all_to_all(flat, 'asset', 0, 0, tiled=True)  19.9 us
    all_to_all x2, waiting for transfers between devices, flipped(): got = lax.all_to_all(flat, 'asset', 0, 0, tiled=True)  17.6 us
    add x2, other arithmetic, band_matrix(): matrix + jnp.where(positions[None, :, None] == (offset + number)[:, None,...  14.1 us
    pallas_call x3, Pallas kernels, regroup(): pl.pallas_call(_gather_kernel, in_specs=[pl.BlockSpec(memory_space=pltpu....  9.2 us
    ppermute x10, waiting for transfers between devices, moved(): return lax.ppermute(value, axes, pairs)  6.07 us
  transfers between devices with their start and end apart: 12, of which 2 were waited for; matrix products, arithmetic and copies ran while one was open for 21% of the time, Pallas kernels for 2%

profile of v12, /device:TPU:34, one launch (start us, length us, event | category | flops | bytes accessed | tf_op | source)
XLA Modules:
  0.0 169.7 jit_solution(17152138280086735510)
XLA Ops:
  0.0 2.6 %copy.17 = f32[512,512]{0,1:T(8,128)} copy(f32[512,512]{1,0:T(8,128)} %bitcast.139) | data formatting | bytes 2097152 | tf_op jit(solution)/shard_map/reshape | solution.py:115
  2.6 10.3 %all-to-all-start = ((f32[16,32,512]{2,1,0:T(8,128)}), f32[16,32,512]{2,1,0:T(8,128)S(1)}, u32[]{:S(2)}, u32[]{:S(2)}) async-start(f32[16,32,512]{2,1,0:T(8,128)} %bitcast.30), calls=%async_computation | async-start | bytes 2097152 | tf_op jit(solution)/shard_map/all_to_all | solution.py:116
  14.4 2.0 %collective-permute-start.4 = (f32[1,4,32,512]{3,1,2,0:T(4,128)S(1)}, f32[1,4,32,512]{3,1,2,0:T(4,128)}, u32[]{:S(2)}, u32[]{:S(2)}) collective-permute-start(f32[1,4,32,512]{3,1,2,0:T(4,128)S(1)} %copy.36), channel_id=1, source_target_pairs={{5,0},{6,1},{7,2},{9,4},{10,5},{11,6},{13,8},{14,9},{15,10},{21,16... | collective-permute-start | bytes 786440 | tf_op jit(solution)/shard_map/ppermute | solution.py:43
  20.2 4.2 %collective-permute-start.2 = (f32[1,4,32,512]{3,1,2,0:T(4,128)}, f32[1,4,32,512]{3,1,2,0:T(4,128)}, u32[]{:S(2)}, u32[]{:S(2)}) collective-permute-start(f32[1,4,32,512]{3,1,2,0:T(4,128)} %copy.34), channel_id=1, source_target_pairs={{1,4},{2,5},{3,6},{5,8},{6,9},{7,10},{9,12},{10,13},{11,14},{17,20... | collective-permute-start | bytes 786440 | tf_op jit(solution)/shard_map/ppermute | solution.py:43
  25.2 4.1 %collective-permute-start = (f32[1,4,32,512]{3,1,2,0:T(4,128)}, f32[1,4,32,512]{3,1,2,0:T(4,128)}, u32[]{:S(2)}, u32[]{:S(2)}) collective-permute-start(f32[1,4,32,512]{3,1,2,0:T(4,128)} %copy.31), channel_id=1, source_target_pairs={{0,4},{1,5},{2,6},{3,7},{4,8},{5,9},{6,10},{7,11},{8,12},{9,13},{1... | collective-permute-start | bytes 786440 | tf_op jit(solution)/shard_map/ppermute | solution.py:43
  29.7 1.9 %collective-permute-start.3 = (f32[1,8,32,512]{3,1,2,0:T(8,128)S(1)}, f32[1,8,32,512]{3,1,2,0:T(8,128)S(1)}, u32[]{:S(2)}, u32[]{:S(2)}) collective-permute-start(f32[1,8,32,512]{3,1,2,0:T(8,128)S(1)} %copy.35), channel_id=1, source_target_pairs={{1,0},{2,1},{3,2},{5,4},{6,5},{7,6},{9,8},{10,9},{11,10},{13,12},{... | collective-permute-start | bytes 1572872 | tf_op jit(solution)/shard_map/ppermute | solution.py:43
  31.7 7.1 %select_add_fusion.1 = f32[8,512,512]{2,1,0:T(8,128)} fusion(f32[8,512]{1,0:T(8,128)S(1)} %get-tuple-element.29, s32[8,512]{1,0:T(8,128)S(1)} %get-tuple-element.35, f32[8,512]{1,0:T(8,128)S(1)} %get-tuple-element.30, s32[8,512]{1,0:T(8,128)S(1)} %get-tuple-element.36, f32[8,512]{1,0:T(8,128)S(1)} %get-tuple-element.28, s32[8,512]{1,0:T(8,128)S(1)} %get-tuple-element.34, ...), kind=kLoop, calls=%fused_computation.9 | loop fusion | flops 23068672 | bytes 8519680 | tf_op jit(solution)/shard_map/add | solution.py:22
  41.0 6.4 %convolution_bitcast_fusion.3 = f32[1,8,32,512]{3,2,1,0:T(8,128)S(1)} fusion(f32[8,512,512]{2,1,0:T(8,128)} %select_add_fusion.1, f32[8,32,512]{2,0,1:T(8,128)S(1)} %convolution_bitcast_fusion.7), kind=kOutput, calls=%fused_computation.23 | convolution fusion | flops 402653184 | bytes 9437184 | tf_op jit(solution)/shard_map/terc,ecn->tern/dot_general | solution.py:76
  49.0 2.5 %convolution_bitcast_fusion.2 = f32[1,8,32,512]{3,2,1,0:T(8,128)S(1)} fusion(f32[8,512,512]{2,1,0:T(8,128)S(1)} %copy-done, f32[8,32,512]{2,0,1:T(8,128)S(1)} %convolution_bitcast_fusion.6), kind=kOutput, calls=%fused_computation.22 | convolution fusion | flops 402653184 | bytes 9437184 | tf_op jit(solution)/shard_map/terc,ecn->tern/dot_general | solution.py:76
  53.0 9.6 %all-to-all-start.1 = ((f32[16,32,512]{2,1,0:T(8,128)}), f32[16,32,512]{2,1,0:T(8,128)S(1)}, u32[]{:S(2)}, u32[]{:S(2)}) async-start(f32[16,32,512]{2,1,0:T(8,128)} %bitcast.36), calls=%async_computation.1 | async-start | bytes 2097152 | tf_op jit(solution)/shard_map/all_to_all | solution.py:116
  62.7 7.0 %select_add_fusion = f32[8,512,512]{2,1,0:T(8,128)} fusion(f32[8,512]{1,0:T(8,128)S(1)} %get-tuple-element.24, s32[8,512]{1,0:T(8,128)S(1)} %get-tuple-element.32, f32[8,512]{1,0:T(8,128)S(1)} %get-tuple-element.25, s32[8,512]{1,0:T(8,128)S(1)} %get-tuple-element.33, f32[8,512]{1,0:T(8,128)S(1)} %get-tuple-element.26, s32[8,512]{1,0:T(8,128)S(1)} %get-tuple-element.31, ...), kind=kLoop, calls=%fused_computation.4 | loop fusion | flops 23068672 | bytes 8519680 | tf_op jit(solution)/shard_map/add | solution.py:22
  69.6 3.1 %shard_map.82 = f32[16,32,512]{2,1,0:T(8,128)} custom-call(f32[16,32,512]{2,1,0:T(8,128)} %copy-done.2), custom_call_target="tpu_custom_call" | custom-call | bytes 2097152 | tf_op jit(solution)/shard_map/pallas_call | solution.py:102
  72.7 17.6 %all-to-all-done.1.src_ref = f32[16,32,512]{2,1,0:T(8,128)S(1)} async-done(((f32[16,32,512]{2,1,0:T(8,128)}), f32[16,32,512]{2,1,0:T(8,128)S(1)}, u32[]{:S(2)}, u32[]{:S(2)}) %all-to-all-start.1) | async-done | bytes 1048608 | tf_op jit(solution)/shard_map/all_to_all | solution.py:116
  91.3 3.1 %shard_map.83 = f32[16,32,512]{2,1,0:T(8,128)} custom-call(f32[16,32,512]{2,1,0:T(8,128)} %copy-done.3), custom_call_target="tpu_custom_call" | custom-call | bytes 2097152 | tf_op jit(solution)/shard_map/pallas_call | solution.py:102
  94.4 6.6 %fusion.19 = f32[2,8,32,512]{3,2,0,1:T(8,128)S(1)} fusion(f32[8,512,512]{2,1,0:T(8,128)} %select_add_fusion, f32[2,8,32,512]{3,2,1,0:T(8,128)} %bitcast.140, f32[2,8,32,512]{3,2,1,0:T(8,128)} %bitcast.141), kind=kOutput, calls=%fused_computation.19 | convolution fusion | flops 805830656 | bytes 11534336 | tf_op jit(solution)/shard_map/terc,ecn->tern/dot_general | solution.py:76
  101.1 3.8 %collective-permute-start.5 = (f32[1,4,32,512]{3,2,0,1:T(8,128)S(1)}, f32[1,4,32,512]{3,2,0,1:T(8,128)S(1)}, u32[]{:S(2)}, u32[]{:S(2)}) collective-permute-start(f32[1,4,32,512]{3,2,0,1:T(8,128)S(1)} %get-tuple-element.11), channel_id=1, source_target_pairs={{0,4},{1,5},{2,6},{3,7},{4,8},{5,9},{6,10},{7,11},{8,12},{9,13},{1... | collective-permute-start | bytes 786440 | tf_op jit(solution)/shard_map/ppermute | solution.py:43
  104.9 1.9 %collective-permute-start.9 = (f32[1,4,32,512]{3,2,0,1:T(8,128)S(1)}, f32[1,4,32,512]{3,2,0,1:T(8,128)S(1)}, u32[]{:S(2)}, u32[]{:S(2)}) collective-permute-start(f32[1,4,32,512]{3,2,0,1:T(8,128)S(1)} %get-tuple-element.12), channel_id=1, source_target_pairs={{5,0},{6,1},{7,2},{9,4},{10,5},{11,6},{13,8},{14,9},{15,10},{21,16... | collective-permute-start | bytes 786440 | tf_op jit(solution)/shard_map/ppermute | solution.py:43
  110.8 2.1 %collective-permute-start.8 = (f32[1,8,32,512]{3,2,0,1:T(8,128)S(1)}, f32[1,8,32,512]{3,2,0,1:T(8,128)S(1)}, u32[]{:S(2)}, u32[]{:S(2)}) collective-permute-start(f32[1,8,32,512]{3,2,0,1:T(8,128)S(1)} %get-tuple-element.16), channel_id=1, source_target_pairs={{1,0},{2,1},{3,2},{5,4},{6,5},{7,6},{9,8},{10,9},{11,10},{13,12},{... | collective-permute-start | bytes 1572872 | tf_op jit(solution)/shard_map/ppermute | solution.py:43
  112.9 6.0 %collective-permute-done.6 = f32[1,4,32,512]{3,2,0,1:T(8,128)S(1)} collective-permute-done((f32[1,4,32,512]{3,2,0,1:T(8,128)S(1)}, f32[1,4,32,512]{3,2,0,1:T(8,128)S(1)}, u32[]{:S(2)}, u32[]{:S(2)}) %collective-permute-start.6) | collective-permute-done | bytes 262176 | tf_op jit(solution)/shard_map/ppermute | solution.py:43
  120.0 2.6 %convolution_bitcast_fusion.1 = f32[1,8,32,512]{3,2,1,0:T(8,128)S(1)} fusion(f32[8,512,512]{2,1,0:T(8,128)S(1)} %bitcast.135, f32[8,32,512]{2,0,1:T(8,128)S(1)} %convolution_bitcast_fusion.5), kind=kOutput, calls=%fused_computation.21 | convolution fusion | flops 402653184 | bytes 9437184 | tf_op jit(solution)/shard_map/terc,ecn->tern/dot_general | solution.py:76
  123.8 2.5 %convolution_bitcast_fusion = f32[1,8,32,512]{3,2,1,0:T(8,128)S(1)} fusion(f32[8,512,512]{2,1,0:T(8,128)S(1)} %bitcast.135, f32[8,32,512]{2,0,1:T(8,128)S(1)} %convolution_bitcast_fusion.4), kind=kOutput, calls=%fused_computation.20 | convolution fusion | flops 402653184 | bytes 9437184 | tf_op jit(solution)/shard_map/terc,ecn->tern/dot_general | solution.py:76
  126.8 32.6 %all_to_all.15.src_ref = f32[16,32,512]{2,1,0:T(8,128)} all-to-all(f32[16,32,512]{2,1,0:T(8,128)S(1)} %bitcast.138), channel_id=1, replica_groups=mesh['asset'=16,'earn'=4,'age'=4] {'asset'}, dimensions={0} | all-to-all | bytes 2097152 | tf_op jit(solution)/shard_map/all_to_all | solution.py:116
  159.4 3.1 %shard_map.84 = f32[16,32,512]{2,1,0:T(8,128)} custom-call(f32[16,32,512]{2,1,0:T(8,128)} %all_to_all.15.src_ref), custom_call_target="tpu_custom_call" | custom-call | bytes 2097152 | tf_op jit(solution)/shard_map/pallas_call | solution.py:102
  162.5 6.1 %fusion.10 = f32[2,8,32,512]{3,2,0,1:T(8,128)S(1)} fusion(f32[8,512,512]{2,1,0:T(8,128)} %select_add_fusion.1, f32[2,8,32,512]{3,2,1,0:T(8,128)S(1)} %copy-done.4, f32[2,8,32,512]{3,2,1,0:T(8,128)} %bitcast.142), kind=kOutput, calls=%fused_computation.16 | convolution fusion | flops 805830656 | bytes 11534336 | tf_op jit(solution)/shard_map/terc,ecn->tern/dot_general | solution.py:76
  (68 shorter events, 20.1 us)
Async XLA Ops:
  0.0 29.3 %copy-start.1 = (f32[2,8,32,512]{3,2,1,0:T(8,128)S(1)}, f32[2,8,32,512]{3,2,1,0:T(8,128)}, u32[]{:S(2)}) copy-start(f32[2,8,32,512]{3,2,1,0:T(8,128)} %param.8) | copy-start | bytes 3145732
  0.0 31.7 %copy-start.5 = (s32[8,512]{1,0:T(8,128)S(1)}, s32[8,512]{1,0:T(8,128)}, u32[]{:S(2)}) copy-start(s32[8,512]{1,0:T(8,128)} %param.12) | copy-start | bytes 49156
  0.0 31.7 %copy-start.7 = (f32[4,8,512]{2,1,0:T(8,128)S(1)}, f32[4,8,512]{2,1,0:T(8,128)}, u32[]{:S(2)}) copy-start(f32[4,8,512]{2,1,0:T(8,128)} %param.13) | copy-start | bytes 196612
  2.6 50.3 %all-to-all-start = ((f32[16,32,512]{2,1,0:T(8,128)}), f32[16,32,512]{2,1,0:T(8,128)S(1)}, u32[]{:S(2)}, u32[]{:S(2)}) async-start(f32[16,32,512]{2,1,0:T(8,128)} %bitcast.30), calls=%async_computation | async-start | bytes 2097152 | tf_op jit(solution)/shard_map/all_to_all | solution.py:116
  12.9 25.9 %copy-start.10 = (s32[8]{0:T(128)S(1)}, s32[8]{0:T(128)}, u32[]{:S(2)}) copy-start(s32[8]{0:T(128)} %param.11) | copy-start | bytes 100
  13.0 26.2 %copy-start.9 = (f32[5,8]{1,0:T(8,128)S(1)}, f32[5,8]{1,0:T(8,128)}, u32[]{:S(2)}) copy-start(f32[5,8]{1,0:T(8,128)} %param.10) | copy-start | bytes 484
  14.4 32.9 %collective-permute-start.4 = (f32[1,4,32,512]{3,1,2,0:T(4,128)S(1)}, f32[1,4,32,512]{3,1,2,0:T(4,128)}, u32[]{:S(2)}, u32[]{:S(2)}) collective-permute-start(f32[1,4,32,512]{3,1,2,0:T(4,128)S(1)} %copy.36), channel_id=1, source_target_pairs={{5,0},{6,1},{7,2},{9,4},{10,5},{11,6},{13,8},{14,9},{15,10},{21,16... | collective-permute-start | bytes 786440 | tf_op jit(solution)/shard_map/ppermute | solution.py:43
  17.4 21.8 %collective-permute-start.1 = (f32[1,4,32,512]{3,1,2,0:T(4,128)}, f32[1,4,32,512]{3,1,2,0:T(4,128)}, u32[]{:S(2)}, u32[]{:S(2)}) collective-permute-start(f32[1,4,32,512]{3,1,2,0:T(4,128)} %copy.33), channel_id=1, source_target_pairs={{4,0},{5,1},{6,2},{7,3},{8,4},{9,5},{10,6},{11,7},{12,8},{13,9},{1... | collective-permute-start | bytes 786440 | tf_op jit(solution)/shard_map/ppermute | solution.py:43
  20.2 27.2 %collective-permute-start.2 = (f32[1,4,32,512]{3,1,2,0:T(4,128)}, f32[1,4,32,512]{3,1,2,0:T(4,128)}, u32[]{:S(2)}, u32[]{:S(2)}) collective-permute-start(f32[1,4,32,512]{3,1,2,0:T(4,128)} %copy.34), channel_id=1, source_target_pairs={{1,4},{2,5},{3,6},{5,8},{6,9},{7,10},{9,12},{10,13},{11,14},{17,20... | collective-permute-start | bytes 786440 | tf_op jit(solution)/shard_map/ppermute | solution.py:43
  25.2 14.0 %collective-permute-start = (f32[1,4,32,512]{3,1,2,0:T(4,128)}, f32[1,4,32,512]{3,1,2,0:T(4,128)}, u32[]{:S(2)}, u32[]{:S(2)}) collective-permute-start(f32[1,4,32,512]{3,1,2,0:T(4,128)} %copy.31), channel_id=1, source_target_pairs={{0,4},{1,5},{2,6},{3,7},{4,8},{5,9},{6,10},{7,11},{8,12},{9,13},{1... | collective-permute-start | bytes 786440 | tf_op jit(solution)/shard_map/ppermute | solution.py:43
  29.7 17.7 %collective-permute-start.3 = (f32[1,8,32,512]{3,1,2,0:T(8,128)S(1)}, f32[1,8,32,512]{3,1,2,0:T(8,128)S(1)}, u32[]{:S(2)}, u32[]{:S(2)}) collective-permute-start(f32[1,8,32,512]{3,1,2,0:T(8,128)S(1)} %copy.35), channel_id=1, source_target_pairs={{1,0},{2,1},{3,2},{5,4},{6,5},{7,6},{9,8},{10,9},{11,10},{13,12},{... | collective-permute-start | bytes 1572872 | tf_op jit(solution)/shard_map/ppermute | solution.py:43
  39.2 9.8 %copy-start = (f32[8,512,512]{2,1,0:T(8,128)S(1)}, f32[8,512,512]{2,1,0:T(8,128)}, u32[]{:S(2)}) copy-start(f32[8,512,512]{2,1,0:T(8,128)} %select_add_fusion.1) | copy-start | bytes 25165828
  47.4 15.3 %copy-start.6 = (s32[8,512]{1,0:T(8,128)S(1)}, s32[8,512]{1,0:T(8,128)}, u32[]{:S(2)}) copy-start(s32[8,512]{1,0:T(8,128)} %param.14) | copy-start | bytes 49156
  47.4 15.3 %copy-start.8 = (f32[4,8,512]{2,1,0:T(8,128)S(1)}, f32[4,8,512]{2,1,0:T(8,128)}, u32[]{:S(2)}) copy-start(f32[4,8,512]{2,1,0:T(8,128)} %param.15) | copy-start | bytes 196612
  53.0 16.7 %copy-start.2 = (f32[16,32,512]{2,1,0:T(8,128)}, f32[16,32,512]{2,1,0:T(8,128)S(1)}, u32[]{:S(2)}) copy-start(f32[16,32,512]{2,1,0:T(8,128)S(1)} %all-to-all-done.src_ref) | copy-start | bytes 3145732
  53.0 37.4 %all-to-all-start.1 = ((f32[16,32,512]{2,1,0:T(8,128)}), f32[16,32,512]{2,1,0:T(8,128)S(1)}, u32[]{:S(2)}, u32[]{:S(2)}) async-start(f32[16,32,512]{2,1,0:T(8,128)} %bitcast.36), calls=%async_computation.1 | async-start | bytes 2097152 | tf_op jit(solution)/shard_map/all_to_all | solution.py:116
  94.4 25.7 %slice-start = ((s8[8388608]{0:T(1024)(128)(4,1)}), s8[4194304]{0:T(1024)(128)(4,1)S(1)}, s32[]{:S(2)}) async-start(s8[8388608]{0:T(1024)(128)(4,1)} %bitcast.134), calls=%async_computation.3 | async-start | bytes 8388608
  94.4 25.7 %slice-start.1 = ((s8[8388608]{0:T(1024)(128)(4,1)}), s8[4194304]{0:T(1024)(128)(4,1)S(1)}, s32[]{:S(2)}) async-start(s8[8388608]{0:T(1024)(128)(4,1)} %bitcast.134), calls=%async_computation.4 | async-start | bytes 8388608
  101.1 11.8 %collective-permute-start.5 = (f32[1,4,32,512]{3,2,0,1:T(8,128)S(1)}, f32[1,4,32,512]{3,2,0,1:T(8,128)S(1)}, u32[]{:S(2)}, u32[]{:S(2)}) collective-permute-start(f32[1,4,32,512]{3,2,0,1:T(8,128)S(1)} %get-tuple-element.11), channel_id=1, source_target_pairs={{0,4},{1,5},{2,6},{3,7},{4,8},{5,9},{6,10},{7,11},{8,12},{9,13},{1... | collective-permute-start | bytes 786440 | tf_op jit(solution)/shard_map/ppermute | solution.py:43
  104.9 17.8 %collective-permute-start.9 = (f32[1,4,32,512]{3,2,0,1:T(8,128)S(1)}, f32[1,4,32,512]{3,2,0,1:T(8,128)S(1)}, u32[]{:S(2)}, u32[]{:S(2)}) collective-permute-start(f32[1,4,32,512]{3,2,0,1:T(8,128)S(1)} %get-tuple-element.12), channel_id=1, source_target_pairs={{5,0},{6,1},{7,2},{9,4},{10,5},{11,6},{13,8},{14,9},{15,10},{21,16... | collective-permute-start | bytes 786440 | tf_op jit(solution)/shard_map/ppermute | solution.py:43
  106.8 15.9 %collective-permute-start.7 = (f32[1,4,32,512]{3,2,0,1:T(8,128)S(1)}, f32[1,4,32,512]{3,2,0,1:T(8,128)S(1)}, u32[]{:S(2)}, u32[]{:S(2)}) collective-permute-start(f32[1,4,32,512]{3,2,0,1:T(8,128)S(1)} %get-tuple-element.13), channel_id=1, source_target_pairs={{1,4},{2,5},{3,6},{5,8},{6,9},{7,10},{9,12},{10,13},{11,14},{17,20... | collective-permute-start | bytes 786440 | tf_op jit(solution)/shard_map/ppermute | solution.py:43
  108.7 10.2 %collective-permute-start.6 = (f32[1,4,32,512]{3,2,0,1:T(8,128)S(1)}, f32[1,4,32,512]{3,2,0,1:T(8,128)S(1)}, u32[]{:S(2)}, u32[]{:S(2)}) collective-permute-start(f32[1,4,32,512]{3,2,0,1:T(8,128)S(1)} %get-tuple-element.14), channel_id=1, source_target_pairs={{4,0},{5,1},{6,2},{7,3},{8,4},{9,5},{10,6},{11,7},{12,8},{13,9},{1... | collective-permute-start | bytes 786440 | tf_op jit(solution)/shard_map/ppermute | solution.py:43
  110.8 11.9 %collective-permute-start.8 = (f32[1,8,32,512]{3,2,0,1:T(8,128)S(1)}, f32[1,8,32,512]{3,2,0,1:T(8,128)S(1)}, u32[]{:S(2)}, u32[]{:S(2)}) collective-permute-start(f32[1,8,32,512]{3,2,0,1:T(8,128)S(1)} %get-tuple-element.16), channel_id=1, source_target_pairs={{1,0},{2,1},{3,2},{5,4},{6,5},{7,6},{9,8},{10,9},{11,10},{13,12},{... | collective-permute-start | bytes 1572872 | tf_op jit(solution)/shard_map/ppermute | solution.py:43
  123.8 38.7 %copy-start.4 = (f32[2,8,32,512]{3,2,1,0:T(8,128)S(1)}, f32[2,8,32,512]{3,2,1,0:T(8,128)}, u32[]{:S(2)}) copy-start(f32[2,8,32,512]{3,2,1,0:T(8,128)} %param.9) | copy-start | bytes 3145732
  (1 other events, 1.0 us)

commit v13 on v11

--- a/solution.py
+++ b/solution.py
@@ -128,15 +128,18 @@
     illiquid_weight,
 ):
     liquid_map = lax.optimization_barrier(band_matrix(liquid_offset, liquid_weight))
+    here, above = neighbours(values)
+    first = mix(here, earn_prob, support_start)
+    first, utility_sent = lax.optimization_barrier((first, utility))
     saved = jnp.concatenate(
-        [along_lanes(mix(part, earn_prob, support_start), liquid_map) for part in neighbours(values)], axis=0
+        [along_lanes(first, liquid_map), along_lanes(mix(above, earn_prob, support_start), liquid_map)], axis=0
     )
     saved, illiquid_offset, illiquid_weight = lax.optimization_barrier(
         (saved, illiquid_offset, illiquid_weight)
     )
     illiquid_map = lax.optimization_barrier(band_matrix(illiquid_offset, illiquid_weight))
     adjusted = along_lanes(flipped(saved), illiquid_map)
-    current = flipped(utility) + DISCOUNT * adjusted
+    current = flipped(utility_sent) + DISCOUNT * adjusted
 
     expected = continuation(current, earn_prob, support_start)
     moved = along_lanes(expected, illiquid_map)

time: 167 us -> 179 us (1.072)
  waiting for transfers between devices: 25 us -> 43 us
  starting transfers between devices: 46 us -> 40.8 us
  matrix products: 29.8 us -> 26.2 us
    all_to_all x2, waiting for transfers between devices: 17.6 us -> 35.7 us  [flipped(): got = lax.all_to_all(flat, 'asset', 0, 0, tiled=True)]
    all_to_all x2, starting transfers between devices: 19.9 us -> 15.6 us  [flipped(): got = lax.all_to_all(flat, 'asset', 0, 0, tiled=True)]
    dot_general x5, matrix products: 24.6 us -> 20.9 us  [along_lanes(): jnp.einsum('terc,ecn->tern', stacked, matrix, precision=lax.Precision.HIGH)]
    add x2, other arithmetic: 14.1 us -> 12 us  [band_matrix(): matrix + jnp.where(positions[None, :, None] == (offset + number)[:, None,...]
    unnamed x32 -> x50, local copies, waits for them, and re-layouts: 4.43 us -> 3.07 us
  transfers between devices with their start and end apart: 12 -> 12, of which waited for: 4 -> 4; matrix products, arithmetic and copies ran while one was open for 20% -> 18% of each run, Pallas kernels for 2% -> 2%
where the time goes in v13:
time: 179 us; the launch traced here: 176 us
  waiting for transfers between devices  43 us (24%)
  starting transfers between devices  40.8 us (23%)
  blocking collectives  29.9 us (17%)
  matrix products  26.2 us (15%)
  other arithmetic  15.9 us (9%)
  local copies, waits for them, and re-layouts  10.8 us (6%)
  Pallas kernels  9.25 us (5%)
    all_to_all x2, waiting for transfers between devices, flipped(): got = lax.all_to_all(flat, 'asset', 0, 0, tiled=True)  35.7 us
    all_to_all x1, blocking collectives, flipped(): got = lax.all_to_all(flat, 'asset', 0, 0, tiled=True)  29.9 us
    ppermute x10, starting transfers between devices, moved(): return lax.ppermute(value, axes, pairs)  25.2 us
    dot_general x5, matrix products, along_lanes(): jnp.einsum('terc,ecn->tern', stacked, matrix, precision=lax.Precision.HIGH)  20.9 us
    all_to_all x2, starting transfers between devices, flipped(): got = lax.all_to_all(flat, 'asset', 0, 0, tiled=True)  15.6 us
    add x2, other arithmetic, band_matrix(): matrix + jnp.where(positions[None, :, None] == (offset + number)[:, None,...  12 us
    pallas_call x3, Pallas kernels, regroup(): pl.pallas_call(_gather_kernel, in_specs=[pl.BlockSpec(memory_space=pltpu....  9.25 us
    ppermute x10, waiting for transfers between devices, moved(): return lax.ppermute(value, axes, pairs)  7.33 us
  transfers between devices with their start and end apart: 12, of which 4 were waited for; matrix products, arithmetic and copies ran while one was open for 18% of the time, Pallas kernels for 2%

profile of v13, /device:TPU:34, one launch (start us, length us, event | category | flops | bytes accessed | tf_op | source)
XLA Modules:
  0.0 176.4 jit_solution(13257607513792957330)
XLA Ops:
  1.6 1.9 %collective-permute-start.4 = (f32[1,4,32,512]{3,1,2,0:T(4,128)S(1)}, f32[1,4,32,512]{3,1,2,0:T(4,128)}, u32[]{:S(2)}, u32[]{:S(2)}) collective-permute-start(f32[1,4,32,512]{3,1,2,0:T(4,128)S(1)} %copy.54), channel_id=1, source_target_pairs={{5,0},{6,1},{7,2},{9,4},{10,5},{11,6},{13,8},{14,9},{15,10},{21,16... | collective-permute-start | bytes 786440 | tf_op jit(solution)/shard_map/ppermute | solution.py:43
  3.7 1.9 %collective-permute-start.1 = (f32[1,4,32,512]{3,1,2,0:T(4,128)S(1)}, f32[1,4,32,512]{3,1,2,0:T(4,128)}, u32[]{:S(2)}, u32[]{:S(2)}) collective-permute-start(f32[1,4,32,512]{3,1,2,0:T(4,128)S(1)} %copy.51), channel_id=1, source_target_pairs={{4,0},{5,1},{6,2},{7,3},{8,4},{9,5},{10,6},{11,7},{12,8},{13,9},{1... | collective-permute-start | bytes 786440 | tf_op jit(solution)/shard_map/ppermute | solution.py:43
  6.5 5.1 %collective-permute-start.2 = (f32[1,4,32,512]{3,1,2,0:T(4,128)}, f32[1,4,32,512]{3,1,2,0:T(4,128)}, u32[]{:S(2)}, u32[]{:S(2)}) collective-permute-start(f32[1,4,32,512]{3,1,2,0:T(4,128)} %copy.52), channel_id=1, source_target_pairs={{1,4},{2,5},{3,6},{5,8},{6,9},{7,10},{9,12},{10,13},{11,14},{17,20... | collective-permute-start | bytes 786440 | tf_op jit(solution)/shard_map/ppermute | solution.py:43
  11.8 2.4 %collective-permute-start = (f32[1,4,32,512]{3,1,2,0:T(4,128)S(1)}, f32[1,4,32,512]{3,1,2,0:T(4,128)}, u32[]{:S(2)}, u32[]{:S(2)}) collective-permute-start(f32[1,4,32,512]{3,1,2,0:T(4,128)S(1)} %copy.49), channel_id=1, source_target_pairs={{0,4},{1,5},{2,6},{3,7},{4,8},{5,9},{6,10},{7,11},{8,12},{9,13},{1... | collective-permute-start | bytes 786440 | tf_op jit(solution)/shard_map/ppermute | solution.py:43
  15.8 1.9 %collective-permute-start.3 = (f32[1,8,32,512]{3,1,2,0:T(8,128)S(1)}, f32[1,8,32,512]{3,1,2,0:T(8,128)}, u32[]{:S(2)}, u32[]{:S(2)}) collective-permute-start(f32[1,8,32,512]{3,1,2,0:T(8,128)S(1)} %copy.53), channel_id=1, source_target_pairs={{1,0},{2,1},{3,2},{5,4},{6,5},{7,6},{9,8},{10,9},{11,10},{13,12},{... | collective-permute-start | bytes 1572872 | tf_op jit(solution)/shard_map/ppermute | solution.py:43
  25.3 11.2 %all-to-all-start = ((f32[16,32,512]{2,1,0:T(8,128)}), f32[16,32,512]{2,1,0:T(8,128)S(1)}, u32[]{:S(2)}, u32[]{:S(2)}) async-start(f32[16,32,512]{2,1,0:T(8,128)} %bitcast.32), calls=%async_computation | async-start | bytes 2097152 | tf_op jit(solution)/shard_map/all_to_all | solution.py:116
  36.6 5.0 %select_add_fusion.1 = f32[8,512,512]{2,1,0:T(8,128)S(1)} fusion(f32[8,512]{1,0:T(8,128)S(1)} %get-tuple-element.33, s32[8,512]{1,0:T(8,128)S(1)} %get-tuple-element.39, f32[8,512]{1,0:T(8,128)S(1)} %get-tuple-element.34, s32[8,512]{1,0:T(8,128)S(1)} %get-tuple-element.40, f32[8,512]{1,0:T(8,128)S(1)} %get-tuple-element.32, ...), kind=kLoop, calls=%fused_computation.11 | loop fusion | flops 23068672 | bytes 8519680 | tf_op jit(solution)/shard_map/add | solution.py:22
  41.7 2.6 %convolution_bitcast_fusion.1 = f32[1,8,32,512]{3,2,1,0:T(8,128)S(1)} fusion(f32[8,512,512]{2,1,0:T(8,128)S(1)} %select_add_fusion.1, f32[8,32,512]{2,0,1:T(8,128)S(1)} %bitcast.134), kind=kOutput, calls=%fused_computation.24 | convolution fusion | flops 402653184 | bytes 9437184 | tf_op jit(solution)/shard_map/terc,ecn->tern/dot_general | solution.py:76
  46.2 2.5 %convolution_bitcast_fusion = f32[1,8,32,512]{3,2,1,0:T(8,128)S(1)} fusion(f32[8,512,512]{2,1,0:T(8,128)S(1)} %select_add_fusion.1, f32[8,32,512]{2,0,1:T(8,128)S(1)} %convolution_bitcast_fusion.4), kind=kOutput, calls=%fused_computation.23 | convolution fusion | flops 402653184 | bytes 9437184 | tf_op jit(solution)/shard_map/terc,ecn->tern/dot_general | solution.py:76
  50.2 15.6 %all-to-all-done.src_ref = f32[16,32,512]{2,1,0:T(8,128)S(1)} async-done(((f32[16,32,512]{2,1,0:T(8,128)}), f32[16,32,512]{2,1,0:T(8,128)S(1)}, u32[]{:S(2)}, u32[]{:S(2)}) %all-to-all-start) | async-done | bytes 1048608 | tf_op jit(solution)/shard_map/all_to_all | solution.py:116
  65.8 4.4 %all-to-all-start.1 = ((f32[16,32,512]{2,1,0:T(8,128)}), f32[16,32,512]{2,1,0:T(8,128)S(1)}, u32[]{:S(2)}, u32[]{:S(2)}) async-start(f32[16,32,512]{2,1,0:T(8,128)} %bitcast.37), calls=%async_computation.1 | async-start | bytes 2097152 | tf_op jit(solution)/shard_map/all_to_all | solution.py:116
  70.3 6.9 %select_add_fusion = f32[8,512,512]{2,1,0:T(8,128)} fusion(f32[8,512]{1,0:T(8,128)S(1)} %get-tuple-element.28, s32[8,512]{1,0:T(8,128)S(1)} %get-tuple-element.36, f32[8,512]{1,0:T(8,128)S(1)} %get-tuple-element.29, s32[8,512]{1,0:T(8,128)S(1)} %get-tuple-element.37, f32[8,512]{1,0:T(8,128)S(1)} %get-tuple-element.30, s32[8,512]{1,0:T(8,128)S(1)} %get-tuple-element.35, ...), kind=kLoop, calls=%fused_computation.6 | loop fusion | flops 23068672 | bytes 8519680 | tf_op jit(solution)/shard_map/add | solution.py:22
  77.2 3.1 %shard_map.82 = f32[16,32,512]{2,1,0:T(8,128)} custom-call(f32[16,32,512]{2,1,0:T(8,128)} %copy-done.1), custom_call_target="tpu_custom_call" | custom-call | bytes 2097152 | tf_op jit(solution)/shard_map/pallas_call | solution.py:102
  80.3 20.1 %all-to-all-done.1.src_ref = f32[16,32,512]{2,1,0:T(8,128)S(1)} async-done(((f32[16,32,512]{2,1,0:T(8,128)}), f32[16,32,512]{2,1,0:T(8,128)S(1)}, u32[]{:S(2)}, u32[]{:S(2)}) %all-to-all-start.1) | async-done | bytes 1048608 | tf_op jit(solution)/shard_map/all_to_all | solution.py:116
  101.4 3.1 %shard_map.83 = f32[16,32,512]{2,1,0:T(8,128)} custom-call(f32[16,32,512]{2,1,0:T(8,128)} %copy-done.2), custom_call_target="tpu_custom_call" | custom-call | bytes 2097152 | tf_op jit(solution)/shard_map/pallas_call | solution.py:102
  104.5 6.6 %fusion.15 = f32[2,8,32,512]{3,2,0,1:T(8,128)S(1)} fusion(f32[8,512,512]{2,1,0:T(8,128)} %select_add_fusion, f32[2,8,32,512]{3,2,1,0:T(8,128)} %bitcast.131, f32[2,8,32,512]{3,2,1,0:T(8,128)} %bitcast.132), kind=kOutput, calls=%fused_computation.19 | convolution fusion | flops 805830656 | bytes 11534336 | tf_op jit(solution)/shard_map/terc,ecn->tern/dot_general | solution.py:76
  111.3 3.1 %collective-permute-start.5 = (f32[1,4,32,512]{3,2,0,1:T(8,128)S(1)}, f32[1,4,32,512]{3,2,0,1:T(8,128)S(1)}, u32[]{:S(2)}, u32[]{:S(2)}) collective-permute-start(f32[1,4,32,512]{3,2,0,1:T(8,128)S(1)} %get-tuple-element.15), channel_id=1, source_target_pairs={{0,4},{1,5},{2,6},{3,7},{4,8},{5,9},{6,10},{7,11},{8,12},{9,13},{1... | collective-permute-start | bytes 786440 | tf_op jit(solution)/shard_map/ppermute | solution.py:43
  114.4 3.0 %collective-permute-start.6 = (f32[1,4,32,512]{3,2,0,1:T(8,128)S(1)}, f32[1,4,32,512]{3,2,0,1:T(8,128)S(1)}, u32[]{:S(2)}, u32[]{:S(2)}) collective-permute-start(f32[1,4,32,512]{3,2,0,1:T(8,128)S(1)} %get-tuple-element.18), channel_id=1, source_target_pairs={{4,0},{5,1},{6,2},{7,3},{8,4},{9,5},{10,6},{11,7},{12,8},{13,9},{1... | collective-permute-start | bytes 786440 | tf_op jit(solution)/shard_map/ppermute | solution.py:43
  124.4 4.5 %collective-permute-done.9 = f32[1,4,32,512]{3,2,0,1:T(8,128)S(1)} collective-permute-done((f32[1,4,32,512]{3,2,0,1:T(8,128)S(1)}, f32[1,4,32,512]{3,2,0,1:T(8,128)S(1)}, u32[]{:S(2)}, u32[]{:S(2)}) %collective-permute-start.9) | collective-permute-done | bytes 262176 | tf_op jit(solution)/shard_map/ppermute | solution.py:43
  128.9 2.8 %collective-permute-done.7 = f32[1,4,32,512]{3,2,0,1:T(8,128)S(1)} collective-permute-done((f32[1,4,32,512]{3,2,0,1:T(8,128)S(1)}, f32[1,4,32,512]{3,2,0,1:T(8,128)S(1)}, u32[]{:S(2)}, u32[]{:S(2)}) %collective-permute-start.7) | collective-permute-done | bytes 262176 | tf_op jit(solution)/shard_map/ppermute | solution.py:43
  132.9 2.9 %fusion.6 = f32[2,8,32,512]{3,2,0,1:T(8,128)S(1)} fusion(f32[8,512,512]{2,1,0:T(8,128)S(1)} %bitcast.126, f32[2,8,32,512]{3,1,2,0:T(8,128)S(1)} %pad_maximum_fusion.1), kind=kOutput, calls=%fused_computation.16 | convolution fusion | flops 805306368 | bytes 10485760 | tf_op jit(solution)/shard_map/terc,ecn->tern/dot_general | solution.py:76
  136.2 29.9 %all_to_all.15.src_ref = f32[16,32,512]{2,1,0:T(8,128)} all-to-all(f32[16,32,512]{2,1,0:T(8,128)S(1)} %bitcast.129), channel_id=1, replica_groups=mesh['asset'=16,'earn'=4,'age'=4] {'asset'}, dimensions={0} | all-to-all | bytes 2097152 | tf_op jit(solution)/shard_map/all_to_all | solution.py:116
  166.2 3.1 %shard_map.84 = f32[16,32,512]{2,1,0:T(8,128)} custom-call(f32[16,32,512]{2,1,0:T(8,128)} %all_to_all.15.src_ref), custom_call_target="tpu_custom_call" | custom-call | bytes 2097152 | tf_op jit(solution)/shard_map/pallas_call | solution.py:102
  169.2 6.1 %fusion.24 = f32[2,8,32,512]{3,2,0,1:T(8,128)S(1)} fusion(f32[8,512,512]{2,1,0:T(8,128)} %copy-done, f32[2,8,32,512]{3,2,1,0:T(8,128)S(1)} %copy-done.3, f32[2,8,32,512]{3,2,1,0:T(8,128)} %bitcast.133), kind=kOutput, calls=%fused_computation.22 | convolution fusion | flops 805830656 | bytes 11534336 | tf_op jit(solution)/shard_map/terc,ecn->tern/dot_general | solution.py:76
  (86 shorter events, 25.8 us)
Async XLA Ops:
  0.0 36.5 %copy-start.4 = (s32[8,512]{1,0:T(8,128)S(1)}, s32[8,512]{1,0:T(8,128)}, u32[]{:S(2)}) copy-start(s32[8,512]{1,0:T(8,128)} %param.12) | copy-start | bytes 49156
  0.0 24.0 %copy-start.3 = (f32[2,8,32,512]{3,2,1,0:T(8,128)S(1)}, f32[2,8,32,512]{3,2,1,0:T(8,128)}, u32[]{:S(2)}) copy-start(f32[2,8,32,512]{3,2,1,0:T(8,128)} %param.9) | copy-start | bytes 3145732
  1.6 42.8 %collective-permute-start.4 = (f32[1,4,32,512]{3,1,2,0:T(4,128)S(1)}, f32[1,4,32,512]{3,1,2,0:T(4,128)}, u32[]{:S(2)}, u32[]{:S(2)}) collective-permute-start(f32[1,4,32,512]{3,1,2,0:T(4,128)S(1)} %copy.54), channel_id=1, source_target_pairs={{5,0},{6,1},{7,2},{9,4},{10,5},{11,6},{13,8},{14,9},{15,10},{21,16... | collective-permute-start | bytes 786440 | tf_op jit(solution)/shard_map/ppermute | solution.py:43
  3.7 18.7 %collective-permute-start.1 = (f32[1,4,32,512]{3,1,2,0:T(4,128)S(1)}, f32[1,4,32,512]{3,1,2,0:T(4,128)}, u32[]{:S(2)}, u32[]{:S(2)}) collective-permute-start(f32[1,4,32,512]{3,1,2,0:T(4,128)S(1)} %copy.51), channel_id=1, source_target_pairs={{4,0},{5,1},{6,2},{7,3},{8,4},{9,5},{10,6},{11,7},{12,8},{13,9},{1... | collective-permute-start | bytes 786440 | tf_op jit(solution)/shard_map/ppermute | solution.py:43
  6.5 37.9 %collective-permute-start.2 = (f32[1,4,32,512]{3,1,2,0:T(4,128)}, f32[1,4,32,512]{3,1,2,0:T(4,128)}, u32[]{:S(2)}, u32[]{:S(2)}) collective-permute-start(f32[1,4,32,512]{3,1,2,0:T(4,128)} %copy.52), channel_id=1, source_target_pairs={{1,4},{2,5},{3,6},{5,8},{6,9},{7,10},{9,12},{10,13},{11,14},{17,20... | collective-permute-start | bytes 786440 | tf_op jit(solution)/shard_map/ppermute | solution.py:43
  11.8 10.6 %collective-permute-start = (f32[1,4,32,512]{3,1,2,0:T(4,128)S(1)}, f32[1,4,32,512]{3,1,2,0:T(4,128)}, u32[]{:S(2)}, u32[]{:S(2)}) collective-permute-start(f32[1,4,32,512]{3,1,2,0:T(4,128)S(1)} %copy.49), channel_id=1, source_target_pairs={{0,4},{1,5},{2,6},{3,7},{4,8},{5,9},{6,10},{7,11},{8,12},{9,13},{1... | collective-permute-start | bytes 786440 | tf_op jit(solution)/shard_map/ppermute | solution.py:43
  15.8 28.6 %collective-permute-start.3 = (f32[1,8,32,512]{3,1,2,0:T(8,128)S(1)}, f32[1,8,32,512]{3,1,2,0:T(8,128)}, u32[]{:S(2)}, u32[]{:S(2)}) collective-permute-start(f32[1,8,32,512]{3,1,2,0:T(8,128)S(1)} %copy.53), channel_id=1, source_target_pairs={{1,0},{2,1},{3,2},{5,4},{6,5},{7,6},{9,8},{10,9},{11,10},{13,12},{... | collective-permute-start | bytes 1572872 | tf_op jit(solution)/shard_map/ppermute | solution.py:43
  25.3 40.5 %all-to-all-start = ((f32[16,32,512]{2,1,0:T(8,128)}), f32[16,32,512]{2,1,0:T(8,128)S(1)}, u32[]{:S(2)}, u32[]{:S(2)}) async-start(f32[16,32,512]{2,1,0:T(8,128)} %bitcast.32), calls=%async_computation | async-start | bytes 2097152 | tf_op jit(solution)/shard_map/all_to_all | solution.py:116
  44.3 25.9 %copy-start.5 = (s32[8,512]{1,0:T(8,128)S(1)}, s32[8,512]{1,0:T(8,128)}, u32[]{:S(2)}) copy-start(s32[8,512]{1,0:T(8,128)} %param.14) | copy-start | bytes 49156
  44.3 26.0 %copy-start.6 = (f32[4,8,512]{2,1,0:T(8,128)S(1)}, f32[4,8,512]{2,1,0:T(8,128)}, u32[]{:S(2)}) copy-start(f32[4,8,512]{2,1,0:T(8,128)} %param.15) | copy-start | bytes 196612
  65.8 34.6 %all-to-all-start.1 = ((f32[16,32,512]{2,1,0:T(8,128)}), f32[16,32,512]{2,1,0:T(8,128)S(1)}, u32[]{:S(2)}, u32[]{:S(2)}) async-start(f32[16,32,512]{2,1,0:T(8,128)} %bitcast.37), calls=%async_computation.1 | async-start | bytes 2097152 | tf_op jit(solution)/shard_map/all_to_all | solution.py:116
  104.5 18.9 %copy-start.9 = (s32[8]{0:T(128)S(1)}, s32[8]{0:T(128)}, u32[]{:S(2)}) copy-start(s32[8]{0:T(128)} %copy-done.7) | copy-start | bytes 100
  104.5 18.9 %copy-start.11 = (f32[8]{0:T(128)S(1)}, f32[8]{0:T(128)}, u32[]{:S(2)}) copy-start(f32[8]{0:T(128)} %get-tuple-element.41) | copy-start | bytes 100
  104.5 19.0 %copy-start.13 = (f32[8]{0:T(128)S(1)}, f32[8]{0:T(128)}, u32[]{:S(2)}) copy-start(f32[8]{0:T(128)} %get-tuple-element.42) | copy-start | bytes 100
  104.5 19.0 %copy-start.15 = (f32[8]{0:T(128)S(1)}, f32[8]{0:T(128)}, u32[]{:S(2)}) copy-start(f32[8]{0:T(128)} %get-tuple-element.43) | copy-start | bytes 100
  104.5 19.0 %copy-start.17 = (f32[8]{0:T(128)S(1)}, f32[8]{0:T(128)}, u32[]{:S(2)}) copy-start(f32[8]{0:T(128)} %get-tuple-element.44) | copy-start | bytes 100
  104.5 19.0 %copy-start.19 = (f32[8]{0:T(128)S(1)}, f32[8]{0:T(128)}, u32[]{:S(2)}) copy-start(f32[8]{0:T(128)} %get-tuple-element.45) | copy-start | bytes 100
  104.5 28.4 %slice-start = ((s8[8388608]{0:T(1024)(128)(4,1)}), s8[4194304]{0:T(1024)(128)(4,1)S(1)}, s32[]{:S(2)}) async-start(s8[8388608]{0:T(1024)(128)(4,1)} %bitcast.125), calls=%async_computation.3 | async-start | bytes 8388608
  111.1 21.7 %slice-start.1 = ((s8[8388608]{0:T(1024)(128)(4,1)}), s8[4194304]{0:T(1024)(128)(4,1)S(1)}, s32[]{:S(2)}) async-start(s8[8388608]{0:T(1024)(128)(4,1)} %bitcast.125), calls=%async_computation.4 | async-start | bytes 8388608
  111.3 12.0 %collective-permute-start.5 = (f32[1,4,32,512]{3,2,0,1:T(8,128)S(1)}, f32[1,4,32,512]{3,2,0,1:T(8,128)S(1)}, u32[]{:S(2)}, u32[]{:S(2)}) collective-permute-start(f32[1,4,32,512]{3,2,0,1:T(8,128)S(1)} %get-tuple-element.15), channel_id=1, source_target_pairs={{0,4},{1,5},{2,6},{3,7},{4,8},{5,9},{6,10},{7,11},{8,12},{9,13},{1... | collective-permute-start | bytes 786440 | tf_op jit(solution)/shard_map/ppermute | solution.py:43
  114.4 8.9 %collective-permute-start.6 = (f32[1,4,32,512]{3,2,0,1:T(8,128)S(1)}, f32[1,4,32,512]{3,2,0,1:T(8,128)S(1)}, u32[]{:S(2)}, u32[]{:S(2)}) collective-permute-start(f32[1,4,32,512]{3,2,0,1:T(8,128)S(1)} %get-tuple-element.18), channel_id=1, source_target_pairs={{4,0},{5,1},{6,2},{7,3},{8,4},{9,5},{10,6},{11,7},{12,8},{13,9},{1... | collective-permute-start | bytes 786440 | tf_op jit(solution)/shard_map/ppermute | solution.py:43
  117.5 14.2 %collective-permute-start.8 = (f32[1,8,32,512]{3,2,0,1:T(8,128)S(1)}, f32[1,8,32,512]{3,2,0,1:T(8,128)S(1)}, u32[]{:S(2)}, u32[]{:S(2)}) collective-permute-start(f32[1,8,32,512]{3,2,0,1:T(8,128)S(1)} %get-tuple-element.20), channel_id=1, source_target_pairs={{1,0},{2,1},{3,2},{5,4},{6,5},{7,6},{9,8},{10,9},{11,10},{13,12},{... | collective-permute-start | bytes 1572872 | tf_op jit(solution)/shard_map/ppermute | solution.py:43
  119.4 9.5 %collective-permute-start.9 = (f32[1,4,32,512]{3,2,0,1:T(8,128)S(1)}, f32[1,4,32,512]{3,2,0,1:T(8,128)S(1)}, u32[]{:S(2)}, u32[]{:S(2)}) collective-permute-start(f32[1,4,32,512]{3,2,0,1:T(8,128)S(1)} %get-tuple-element.16), channel_id=1, source_target_pairs={{5,0},{6,1},{7,2},{9,4},{10,5},{11,6},{13,8},{14,9},{15,10},{21,16... | collective-permute-start | bytes 786440 | tf_op jit(solution)/shard_map/ppermute | solution.py:43
  121.3 10.4 %collective-permute-start.7 = (f32[1,4,32,512]{3,2,0,1:T(8,128)S(1)}, f32[1,4,32,512]{3,2,0,1:T(8,128)S(1)}, u32[]{:S(2)}, u32[]{:S(2)}) collective-permute-start(f32[1,4,32,512]{3,2,0,1:T(8,128)S(1)} %get-tuple-element.17), channel_id=1, source_target_pairs={{1,4},{2,5},{3,6},{5,8},{6,9},{7,10},{9,12},{10,13},{11,14},{17,20... | collective-permute-start | bytes 786440 | tf_op jit(solution)/shard_map/ppermute | solution.py:43
  (10 other events, 69.2 us)

commit v14 on v11

--- a/solution.py
+++ b/solution.py
@@ -135,8 +135,11 @@
         (saved, illiquid_offset, illiquid_weight)
     )
     illiquid_map = lax.optimization_barrier(band_matrix(illiquid_offset, illiquid_weight))
-    adjusted = along_lanes(flipped(saved), illiquid_map)
-    current = flipped(utility) + DISCOUNT * adjusted
+    arrived = flipped(saved)
+    carried = flipped(utility)
+    current = jnp.concatenate(
+        [carried[t : t + 1] + DISCOUNT * along_lanes(arrived[t : t + 1], illiquid_map) for t in range(2)], axis=0
+    )
 
     expected = continuation(current, earn_prob, support_start)
     moved = along_lanes(expected, illiquid_map)

time: 167 us -> 171 us (1.024)
  the two profiles are of different devices: /device:TPU:34 before, /device:TPU:1 now
where the time goes in v14:
time: 171 us; the launch traced here: 170 us
  starting transfers between devices  44.1 us (26%)
  matrix products  31.7 us (19%)
  waiting for transfers between devices  30.7 us (18%)
  blocking collectives  27.8 us (16%)
  other arithmetic  14.5 us (8%)
  local copies, waits for them, and re-layouts  11.4 us (7%)
  Pallas kernels  9.21 us (5%)
    all_to_all x1, blocking collectives, flipped(): got = lax.all_to_all(flat, 'asset', 0, 0, tiled=True)  27.8 us
    dot_general x6, matrix products, along_lanes(): jnp.einsum('terc,ecn->tern', stacked, matrix, precision=lax.Precision.HIGH)  26.5 us
    ppermute x10, starting transfers between devices, moved(): return lax.ppermute(value, axes, pairs)  23.1 us
    all_to_all x2, starting transfers between devices, flipped(): got = lax.all_to_all(flat, 'asset', 0, 0, tiled=True)  21.1 us
    ppermute x10, waiting for transfers between devices, moved(): return lax.ppermute(value, axes, pairs)  17.5 us
    add x2, other arithmetic, band_matrix(): matrix + jnp.where(positions[None, :, None] == (offset + number)[:, None,...  14.1 us
    all_to_all x2, waiting for transfers between devices, flipped(): got = lax.all_to_all(flat, 'asset', 0, 0, tiled=True)  13.2 us
    pallas_call x3, Pallas kernels, regroup(): pl.pallas_call(_gather_kernel, in_specs=[pl.BlockSpec(memory_space=pltpu....  9.21 us
  transfers between devices with their start and end apart: 12, of which 3 were waited for; matrix products, arithmetic and copies ran while one was open for 21% of the time, Pallas kernels for 2%

profile of v14, /device:TPU:1, one launch (start us, length us, event | category | flops | bytes accessed | tf_op | source)
XLA Modules:
  0.0 169.9 jit_solution(5523338755833944934)
XLA Ops:
  0.0 2.7 %copy.33 = f32[512,512]{0,1:T(8,128)} copy(f32[512,512]{1,0:T(8,128)} %bitcast.137) | data formatting | bytes 2097152 | tf_op jit(solution)/shard_map/reshape | solution.py:115
  2.7 11.7 %all-to-all-start = ((f32[16,32,512]{2,1,0:T(8,128)}), f32[16,32,512]{2,1,0:T(8,128)S(1)}, u32[]{:S(2)}, u32[]{:S(2)}) async-start(f32[16,32,512]{2,1,0:T(8,128)} %bitcast.32), calls=%async_computation | async-start | bytes 2097152 | tf_op jit(solution)/shard_map/all_to_all | solution.py:116
  20.3 5.8 %collective-permute-start.2 = (f32[1,4,32,512]{3,1,2,0:T(4,128)}, f32[1,4,32,512]{3,1,2,0:T(4,128)}, u32[]{:S(2)}, u32[]{:S(2)}) collective-permute-start(f32[1,4,32,512]{3,1,2,0:T(4,128)} %copy.48), channel_id=1, source_target_pairs={{1,4},{2,5},{3,6},{5,8},{6,9},{7,10},{9,12},{10,13},{11,14},{17,20... | collective-permute-start | bytes 786440 | tf_op jit(solution)/shard_map/ppermute | solution.py:43
  26.9 3.1 %collective-permute-start = (f32[1,4,32,512]{3,1,2,0:T(4,128)}, f32[1,4,32,512]{3,1,2,0:T(4,128)}, u32[]{:S(2)}, u32[]{:S(2)}) collective-permute-start(f32[1,4,32,512]{3,1,2,0:T(4,128)} %copy.45), channel_id=1, source_target_pairs={{0,4},{1,5},{2,6},{3,7},{4,8},{5,9},{6,10},{7,11},{8,12},{9,13},{1... | collective-permute-start | bytes 786440 | tf_op jit(solution)/shard_map/ppermute | solution.py:43
  30.5 1.9 %collective-permute-start.3 = (f32[1,8,32,512]{3,1,2,0:T(8,128)S(1)}, f32[1,8,32,512]{3,1,2,0:T(8,128)S(1)}, u32[]{:S(2)}, u32[]{:S(2)}) collective-permute-start(f32[1,8,32,512]{3,1,2,0:T(8,128)S(1)} %copy.49), channel_id=1, source_target_pairs={{1,0},{2,1},{3,2},{5,4},{6,5},{7,6},{9,8},{10,9},{11,10},{13,12},{... | collective-permute-start | bytes 1572872 | tf_op jit(solution)/shard_map/ppermute | solution.py:43
  32.4 7.1 %select_add_fusion.1 = f32[8,512,512]{2,1,0:T(8,128)} fusion(f32[8,512]{1,0:T(8,128)S(1)} %get-tuple-element.27, s32[8,512]{1,0:T(8,128)S(1)} %get-tuple-element.33, f32[8,512]{1,0:T(8,128)S(1)} %get-tuple-element.28, s32[8,512]{1,0:T(8,128)S(1)} %get-tuple-element.34, f32[8,512]{1,0:T(8,128)S(1)} %get-tuple-element.26, s32[8,512]{1,0:T(8,128)S(1)} %get-tuple-element.32, ...), kind=kLoop, calls=%fused_computation.9 | loop fusion | flops 23068672 | bytes 8519680 | tf_op jit(solution)/shard_map/add | solution.py:22
  40.0 1.7 %convolution_bitcast_fusion.5 = f32[8,32,512]{2,0,1:T(8,128)S(1)} fusion(f32[1,4,32,512]{3,1,2,0:T(4,128)} %collective-permute-done.1, f32[1,8,32,512]{3,1,2,0:T(8,128)S(1)} %copy.46, f32[1,4,32,512]{3,1,2,0:T(4,128)} %collective-permute-done, f32[8]{0:T(128)S(1)} %get-tuple-element.36, s32[8]{0:T(128)S(1)} %get-tuple-element.43, ...), kind=kOutput, calls=%fused_computation.27 | convolution fusion | flops 13108992 | bytes 1573184 | tf_op jit(solution)/shard_map/ij,tjxy->tixy/dot_general | solution.py:72
  41.7 6.4 %convolution_bitcast_fusion.1 = f32[1,8,32,512]{3,2,1,0:T(8,128)S(1)} fusion(f32[8,512,512]{2,1,0:T(8,128)} %select_add_fusion.1, f32[8,32,512]{2,0,1:T(8,128)S(1)} %convolution_bitcast_fusion.5), kind=kOutput, calls=%fused_computation.23 | convolution fusion | flops 402653184 | bytes 9437184 | tf_op jit(solution)/shard_map/terc,ecn->tern/dot_general | solution.py:76
  48.2 1.6 convolution_bitcast_fusion.4
  49.8 2.5 %convolution_bitcast_fusion = f32[1,8,32,512]{3,2,1,0:T(8,128)S(1)} fusion(f32[8,512,512]{2,1,0:T(8,128)S(1)} %copy-done.1, f32[8,32,512]{2,0,1:T(8,128)S(1)} %convolution_bitcast_fusion.4), kind=kOutput, calls=%fused_computation.22 | convolution fusion | flops 402653184 | bytes 9437184 | tf_op jit(solution)/shard_map/terc,ecn->tern/dot_general | solution.py:76
  53.7 9.3 %all-to-all-start.1 = ((f32[16,32,512]{2,1,0:T(8,128)}), f32[16,32,512]{2,1,0:T(8,128)S(1)}, u32[]{:S(2)}, u32[]{:S(2)}) async-start(f32[16,32,512]{2,1,0:T(8,128)} %bitcast.36), calls=%async_computation.1 | async-start | bytes 2097152 | tf_op jit(solution)/shard_map/all_to_all | solution.py:116
  63.1 7.0 %select_add_fusion = f32[8,512,512]{2,1,0:T(8,128)} fusion(f32[8,512]{1,0:T(8,128)S(1)} %get-tuple-element.22, s32[8,512]{1,0:T(8,128)S(1)} %get-tuple-element.30, f32[8,512]{1,0:T(8,128)S(1)} %get-tuple-element.23, s32[8,512]{1,0:T(8,128)S(1)} %get-tuple-element.31, f32[8,512]{1,0:T(8,128)S(1)} %get-tuple-element.24, s32[8,512]{1,0:T(8,128)S(1)} %get-tuple-element.29, ...), kind=kLoop, calls=%fused_computation.4 | loop fusion | flops 23068672 | bytes 8519680 | tf_op jit(solution)/shard_map/add | solution.py:22
  70.1 3.1 %shard_map.82 = f32[16,32,512]{2,1,0:T(8,128)} custom-call(f32[16,32,512]{2,1,0:T(8,128)} %copy-done.5), custom_call_target="tpu_custom_call" | custom-call | bytes 2097152 | tf_op jit(solution)/shard_map/pallas_call | solution.py:102
  73.1 13.2 %all-to-all-done.1.src_ref = f32[16,32,512]{2,1,0:T(8,128)S(1)} async-done(((f32[16,32,512]{2,1,0:T(8,128)}), f32[16,32,512]{2,1,0:T(8,128)S(1)}, u32[]{:S(2)}, u32[]{:S(2)}) %all-to-all-start.1) | async-done | bytes 1048608 | tf_op jit(solution)/shard_map/all_to_all | solution.py:116
  87.3 3.1 %shard_map.83 = f32[16,32,512]{2,1,0:T(8,128)} custom-call(f32[16,32,512]{2,1,0:T(8,128)} %copy-done.6), custom_call_target="tpu_custom_call" | custom-call | bytes 2097152 | tf_op jit(solution)/shard_map/pallas_call | solution.py:102
  90.4 6.1 %fusion.19 = f32[1,8,32,512]{3,2,1,0:T(8,128)S(1)} fusion(f32[8,512,512]{2,1,0:T(8,128)} %select_add_fusion, f32[16,32,512]{2,1,0:T(8,128)} %shard_map.83, f32[16,32,512]{2,1,0:T(8,128)} %shard_map.82), kind=kOutput, calls=%fused_computation.29 | convolution fusion | flops 402915328 | bytes 9961472 | tf_op jit(solution)/shard_map/terc,ecn->tern/dot_general | solution.py:76
  96.5 3.6 %collective-permute-start.5 = (f32[1,4,32,512]{3,2,1,0:T(8,128)S(1)}, f32[1,4,32,512]{3,2,1,0:T(8,128)S(1)}, u32[]{:S(2)}, u32[]{:S(2)}) collective-permute-start(f32[1,4,32,512]{3,2,1,0:T(8,128)S(1)} %get-tuple-element.17), channel_id=1, source_target_pairs={{0,4},{1,5},{2,6},{3,7},{4,8},{5,9},{6,10},{7,11},{8,12},{9,13},{1... | collective-permute-start | bytes 786440 | tf_op jit(solution)/shard_map/ppermute | solution.py:43
  101.5 2.5 %fusion.18 = f32[1,8,32,512]{3,2,1,0:T(8,128)S(1)} fusion(f32[8,512,512]{2,1,0:T(8,128)S(1)} %copy-done, f32[16,32,512]{2,1,0:T(8,128)S(1)} %copy-done.3, f32[16,32,512]{2,1,0:T(8,128)S(1)} %copy-done.2), kind=kOutput, calls=%fused_computation.28 | convolution fusion | flops 402915328 | bytes 9961472 | tf_op jit(solution)/shard_map/terc,ecn->tern/dot_general | solution.py:76
  103.9 1.9 %collective-permute-start.8 = (f32[1,8,32,512]{3,2,1,0:T(8,128)S(1)}, f32[1,8,32,512]{3,2,1,0:T(8,128)S(1)}, u32[]{:S(2)}, u32[]{:S(2)}) collective-permute-start(f32[1,8,32,512]{3,2,1,0:T(8,128)S(1)} %fusion.18), channel_id=1, source_target_pairs={{1,0},{2,1},{3,2},{5,4},{6,5},{7,6},{9,8},{10,9},{11,10},{13,12},{... | collective-permute-start | bytes 1572872 | tf_op jit(solution)/shard_map/ppermute | solution.py:43
  110.5 16.8 %collective-permute-done.9 = f32[1,4,32,512]{3,2,1,0:T(8,128)S(1)} collective-permute-done((f32[1,4,32,512]{3,2,1,0:T(8,128)S(1)}, f32[1,4,32,512]{3,2,1,0:T(8,128)S(1)}, u32[]{:S(2)}, u32[]{:S(2)}) %collective-permute-start.9) | collective-permute-done | bytes 262176 | tf_op jit(solution)/shard_map/ppermute | solution.py:43
  128.4 2.9 %fusion.4 = f32[2,8,32,512]{3,2,0,1:T(8,128)S(1)} fusion(f32[8,512,512]{2,1,0:T(8,128)S(1)} %copy-done, f32[2,8,32,512]{3,1,2,0:T(8,128)S(1)} %pad_maximum_fusion.1), kind=kOutput, calls=%fused_computation.14 | convolution fusion | flops 805306368 | bytes 10485760 | tf_op jit(solution)/shard_map/terc,ecn->tern/dot_general | solution.py:76
  131.8 27.8 %all_to_all.15.src_ref = f32[16,32,512]{2,1,0:T(8,128)} all-to-all(f32[16,32,512]{2,1,0:T(8,128)S(1)} %bitcast.136), channel_id=1, replica_groups=mesh['asset'=16,'earn'=4,'age'=4] {'asset'}, dimensions={0} | all-to-all | bytes 2097152 | tf_op jit(solution)/shard_map/all_to_all | solution.py:116
  159.6 3.1 %shard_map.84 = f32[16,32,512]{2,1,0:T(8,128)} custom-call(f32[16,32,512]{2,1,0:T(8,128)} %all_to_all.15.src_ref), custom_call_target="tpu_custom_call" | custom-call | bytes 2097152 | tf_op jit(solution)/shard_map/pallas_call | solution.py:102
  162.7 6.1 %fusion.13 = f32[2,8,32,512]{3,2,0,1:T(8,128)S(1)} fusion(f32[8,512,512]{2,1,0:T(8,128)} %select_add_fusion.1, f32[2,8,32,512]{3,2,1,0:T(8,128)S(1)} %copy-done.7, f32[2,8,32,512]{3,2,1,0:T(8,128)} %bitcast.138), kind=kOutput, calls=%fused_computation.17 | convolution fusion | flops 805830656 | bytes 11534336 | tf_op jit(solution)/shard_map/terc,ecn->tern/dot_general | solution.py:76
  (70 shorter events, 18.4 us)
Async XLA Ops:
  0.0 30.1 %copy-start.4 = (f32[2,8,32,512]{3,2,1,0:T(8,128)S(1)}, f32[2,8,32,512]{3,2,1,0:T(8,128)}, u32[]{:S(2)}) copy-start(f32[2,8,32,512]{3,2,1,0:T(8,128)} %param.8) | copy-start | bytes 3145732
  0.0 32.4 %copy-start.8 = (s32[8,512]{1,0:T(8,128)S(1)}, s32[8,512]{1,0:T(8,128)}, u32[]{:S(2)}) copy-start(s32[8,512]{1,0:T(8,128)} %param.12) | copy-start | bytes 49156
  0.0 32.4 %copy-start.10 = (f32[4,8,512]{2,1,0:T(8,128)S(1)}, f32[4,8,512]{2,1,0:T(8,128)}, u32[]{:S(2)}) copy-start(f32[4,8,512]{2,1,0:T(8,128)} %param.13) | copy-start | bytes 196612
  2.7 51.0 %all-to-all-start = ((f32[16,32,512]{2,1,0:T(8,128)}), f32[16,32,512]{2,1,0:T(8,128)S(1)}, u32[]{:S(2)}, u32[]{:S(2)}) async-start(f32[16,32,512]{2,1,0:T(8,128)} %bitcast.32), calls=%async_computation | async-start | bytes 2097152 | tf_op jit(solution)/shard_map/all_to_all | solution.py:116
  14.4 25.1 %copy-start.13 = (s32[8]{0:T(128)S(1)}, s32[8]{0:T(128)}, u32[]{:S(2)}) copy-start(s32[8]{0:T(128)} %param.11) | copy-start | bytes 100
  14.4 25.4 %copy-start.12 = (f32[5,8]{1,0:T(8,128)S(1)}, f32[5,8]{1,0:T(8,128)}, u32[]{:S(2)}) copy-start(f32[5,8]{1,0:T(8,128)} %param.10) | copy-start | bytes 484
  15.9 32.2 %collective-permute-start.4 = (f32[1,4,32,512]{3,1,2,0:T(4,128)S(1)}, f32[1,4,32,512]{3,1,2,0:T(4,128)}, u32[]{:S(2)}, u32[]{:S(2)}) collective-permute-start(f32[1,4,32,512]{3,1,2,0:T(4,128)S(1)} %copy.50), channel_id=1, source_target_pairs={{5,0},{6,1},{7,2},{9,4},{10,5},{11,6},{13,8},{14,9},{15,10},{21,16... | collective-permute-start | bytes 786440 | tf_op jit(solution)/shard_map/ppermute | solution.py:43
  18.1 21.8 %collective-permute-start.1 = (f32[1,4,32,512]{3,1,2,0:T(4,128)}, f32[1,4,32,512]{3,1,2,0:T(4,128)}, u32[]{:S(2)}, u32[]{:S(2)}) collective-permute-start(f32[1,4,32,512]{3,1,2,0:T(4,128)} %copy.47), channel_id=1, source_target_pairs={{4,0},{5,1},{6,2},{7,3},{8,4},{9,5},{10,6},{11,7},{12,8},{13,9},{1... | collective-permute-start | bytes 786440 | tf_op jit(solution)/shard_map/ppermute | solution.py:43
  20.3 27.9 %collective-permute-start.2 = (f32[1,4,32,512]{3,1,2,0:T(4,128)}, f32[1,4,32,512]{3,1,2,0:T(4,128)}, u32[]{:S(2)}, u32[]{:S(2)}) collective-permute-start(f32[1,4,32,512]{3,1,2,0:T(4,128)} %copy.48), channel_id=1, source_target_pairs={{1,4},{2,5},{3,6},{5,8},{6,9},{7,10},{9,12},{10,13},{11,14},{17,20... | collective-permute-start | bytes 786440 | tf_op jit(solution)/shard_map/ppermute | solution.py:43
  26.9 13.0 %collective-permute-start = (f32[1,4,32,512]{3,1,2,0:T(4,128)}, f32[1,4,32,512]{3,1,2,0:T(4,128)}, u32[]{:S(2)}, u32[]{:S(2)}) collective-permute-start(f32[1,4,32,512]{3,1,2,0:T(4,128)} %copy.45), channel_id=1, source_target_pairs={{0,4},{1,5},{2,6},{3,7},{4,8},{5,9},{6,10},{7,11},{8,12},{9,13},{1... | collective-permute-start | bytes 786440 | tf_op jit(solution)/shard_map/ppermute | solution.py:43
  30.5 17.7 %collective-permute-start.3 = (f32[1,8,32,512]{3,1,2,0:T(8,128)S(1)}, f32[1,8,32,512]{3,1,2,0:T(8,128)S(1)}, u32[]{:S(2)}, u32[]{:S(2)}) collective-permute-start(f32[1,8,32,512]{3,1,2,0:T(8,128)S(1)} %copy.49), channel_id=1, source_target_pairs={{1,0},{2,1},{3,2},{5,4},{6,5},{7,6},{9,8},{10,9},{11,10},{13,12},{... | collective-permute-start | bytes 1572872 | tf_op jit(solution)/shard_map/ppermute | solution.py:43
  48.1 15.0 %copy-start.9 = (s32[8,512]{1,0:T(8,128)S(1)}, s32[8,512]{1,0:T(8,128)}, u32[]{:S(2)}) copy-start(s32[8,512]{1,0:T(8,128)} %param.14) | copy-start | bytes 49156
  48.1 15.0 %copy-start.11 = (f32[4,8,512]{2,1,0:T(8,128)S(1)}, f32[4,8,512]{2,1,0:T(8,128)}, u32[]{:S(2)}) copy-start(f32[4,8,512]{2,1,0:T(8,128)} %param.15) | copy-start | bytes 196612
  53.7 16.4 %copy-start.5 = (f32[16,32,512]{2,1,0:T(8,128)}, f32[16,32,512]{2,1,0:T(8,128)S(1)}, u32[]{:S(2)}) copy-start(f32[16,32,512]{2,1,0:T(8,128)S(1)} %all-to-all-done.src_ref) | copy-start | bytes 3145732
  53.7 32.6 %all-to-all-start.1 = ((f32[16,32,512]{2,1,0:T(8,128)}), f32[16,32,512]{2,1,0:T(8,128)S(1)}, u32[]{:S(2)}, u32[]{:S(2)}) async-start(f32[16,32,512]{2,1,0:T(8,128)} %bitcast.36), calls=%async_computation.1 | async-start | bytes 2097152 | tf_op jit(solution)/shard_map/all_to_all | solution.py:116
  73.1 28.3 %copy-start.2 = (f32[16,32,512]{2,1,0:T(8,128)S(1)}, f32[16,32,512]{2,1,0:T(8,128)}, u32[]{:S(2)}) copy-start(f32[16,32,512]{2,1,0:T(8,128)} %shard_map.82) | copy-start | bytes 3145732
  90.4 11.0 %copy-start = (f32[8,512,512]{2,1,0:T(8,128)S(1)}, f32[8,512,512]{2,1,0:T(8,128)}, u32[]{:S(2)}) copy-start(f32[8,512,512]{2,1,0:T(8,128)} %select_add_fusion) | copy-start | bytes 25165828
  90.4 11.1 %copy-start.3 = (f32[16,32,512]{2,1,0:T(8,128)S(1)}, f32[16,32,512]{2,1,0:T(8,128)}, u32[]{:S(2)}) copy-start(f32[16,32,512]{2,1,0:T(8,128)} %shard_map.83) | copy-start | bytes 3145732
  96.5 12.2 %collective-permute-start.5 = (f32[1,4,32,512]{3,2,1,0:T(8,128)S(1)}, f32[1,4,32,512]{3,2,1,0:T(8,128)S(1)}, u32[]{:S(2)}, u32[]{:S(2)}) collective-permute-start(f32[1,4,32,512]{3,2,1,0:T(8,128)S(1)} %get-tuple-element.17), channel_id=1, source_target_pairs={{0,4},{1,5},{2,6},{3,7},{4,8},{5,9},{6,10},{7,11},{8,12},{9,13},{1... | collective-permute-start | bytes 786440 | tf_op jit(solution)/shard_map/ppermute | solution.py:43
  100.1 8.6 %collective-permute-start.6 = (f32[1,4,32,512]{3,2,1,0:T(8,128)S(1)}, f32[1,4,32,512]{3,2,1,0:T(8,128)S(1)}, u32[]{:S(2)}, u32[]{:S(2)}) collective-permute-start(f32[1,4,32,512]{3,2,1,0:T(8,128)S(1)} %get-tuple-element.18), channel_id=1, source_target_pairs={{4,0},{5,1},{6,2},{7,3},{8,4},{9,5},{10,6},{11,7},{12,8},{13,9},{1... | collective-permute-start | bytes 786440 | tf_op jit(solution)/shard_map/ppermute | solution.py:43
  103.9 23.3 %collective-permute-start.8 = (f32[1,8,32,512]{3,2,1,0:T(8,128)S(1)}, f32[1,8,32,512]{3,2,1,0:T(8,128)S(1)}, u32[]{:S(2)}, u32[]{:S(2)}) collective-permute-start(f32[1,8,32,512]{3,2,1,0:T(8,128)S(1)} %fusion.18), channel_id=1, source_target_pairs={{1,0},{2,1},{3,2},{5,4},{6,5},{7,6},{9,8},{10,9},{11,10},{13,12},{... | collective-permute-start | bytes 1572872 | tf_op jit(solution)/shard_map/ppermute | solution.py:43
  105.9 4.6 %collective-permute-start.7 = (f32[1,4,32,512]{3,2,1,0:T(8,128)S(1)}, f32[1,4,32,512]{3,2,1,0:T(8,128)S(1)}, u32[]{:S(2)}, u32[]{:S(2)}) collective-permute-start(f32[1,4,32,512]{3,2,1,0:T(8,128)S(1)} %get-tuple-element.19), channel_id=1, source_target_pairs={{1,4},{2,5},{3,6},{5,8},{6,9},{7,10},{9,12},{10,13},{11,14},{17,20... | collective-permute-start | bytes 786440 | tf_op jit(solution)/shard_map/ppermute | solution.py:43
  107.2 20.0 %collective-permute-start.9 = (f32[1,4,32,512]{3,2,1,0:T(8,128)S(1)}, f32[1,4,32,512]{3,2,1,0:T(8,128)S(1)}, u32[]{:S(2)}, u32[]{:S(2)}) collective-permute-start(f32[1,4,32,512]{3,2,1,0:T(8,128)S(1)} %get-tuple-element.20), channel_id=1, source_target_pairs={{5,0},{6,1},{7,2},{9,4},{10,5},{11,6},{13,8},{14,9},{15,10},{21,16... | collective-permute-start | bytes 786440 | tf_op jit(solution)/shard_map/ppermute | solution.py:43
  128.4 34.3 %copy-start.7 = (f32[2,8,32,512]{3,2,1,0:T(8,128)S(1)}, f32[2,8,32,512]{3,2,1,0:T(8,128)}, u32[]{:S(2)}) copy-start(f32[2,8,32,512]{3,2,1,0:T(8,128)} %param.9) | copy-start | bytes 3145732
  (2 other events, 10.8 us)
